TPU v7x, 32 devices: a whole 2x2x4 slice. The times are simulated.
32 devices in a mesh: starts: 2 (over y), gx: 8 (over z, x), gy: 2 (over core).
Axes of the slice: x: 2, y: 2, z: 4, core: 2. Of those that a mesh axis runs over, the one named last changes fastest.
Arguments:
- chi_final: float32 [2, 64, 128, 256], P(None, ('starts', 'gx'), 'gy'), parts along dimension 1, may hold values from -30 to 30
- psi_late: float32 [2, 64, 128, 256], P(None, ('starts', 'gx'), 'gy'), parts along dimension 1, may hold values from -0.7 to 0.7
- psi_early: float32 [2, 64, 128, 256], P(None, ('starts', 'gx'), 'gy'), parts along dimension 1, may hold values from -0.7 to 0.7
- trap: float32 [32, 128, 256], P('gx', 'gy'), may hold values from 0 to 1
- controls: float32 [4, 64, 256], P('starts', 'gy'), parts along dimension 0, may hold values from -0.5 to 0.5
Outputs:
- chi_start: float32 [2, 64, 128, 256], P(None, ('starts', 'gx'), 'gy'), parts along dimension 1
- grad_rows: float32 [4, 64, 256], P('starts', 'gy'), parts along dimension 0
- adjoint_power: float32 [2], P('starts'), parts along dimension 0
There are 2 independent parts, one for each index of `starts`. A program takes and returns all parts, laid end to end along the dimension named above; an argument that names none is the same for every part. Nothing has to cross between parts.
All inputs are finite; a program needn't handle non-finite values.
Results may differ from a plain program's by a relative error of at most 0.0005.
Values sent between devices are 32-bit elements; how exact they have to be, the bound alone decides.
No kernel may reach another device: no remote copies, remote signals or barrier semaphores. Data moves between devices by JAX's collectives and lax.ppermute only.
A program may use at most 64 MiB of HBM per device.

v0:
```python
import math

import jax
import jax.numpy as jnp
from jax import lax
from jax.sharding import PartitionSpec as P

COUPLING = 1.0
STEP_SIZE = 0.2


def extended(block, sides, width):
    for axis, dim in sides:
        count = lax.axis_size(axis)
        forward = [(i, i + 1) for i in range(count - 1)]
        backward = [(target, source) for source, target in forward]
        low = lax.ppermute(
            lax.slice_in_dim(block, block.shape[dim] - width, None, axis=dim), axis, forward
        )
        high = lax.ppermute(lax.slice_in_dim(block, 0, width, axis=dim), axis, backward)
        block = jnp.concatenate([low, block, high], axis=dim)
    return block


def coefficients(psi, trap, control, profile):
    real_part = psi[0]
    imag_part = psi[1]
    fine_control = jnp.repeat(control, 2, axis=0)
    potential = trap + profile[:, None, None] * fine_control[None, :, :]
    weight = potential + 2.0 * COUPLING * (real_part * real_part + imag_part * imag_part)
    mix_a = COUPLING * (real_part * real_part - imag_part * imag_part)
    mix_b = 2.0 * COUPLING * real_part * imag_part
    return (weight, mix_a, mix_b)


def apply_coef(lapl, field, coef):
    weight, mix_a, mix_b = coef
    real_part = field[0]
    imag_part = field[1]
    upper = -0.5 * lapl[0] + (weight + mix_a) * real_part + mix_b * imag_part
    lower = -0.5 * lapl[1] + mix_b * real_part + (weight - mix_a) * imag_part
    return jnp.stack([-lower, upper])


def operator(field, coef):
    padded = extended(field, (("gx", 1), ("gy", 2)), 1)
    z_padded = jnp.pad(field, ((0, 0), (0, 0), (0, 0), (1, 1)))
    total = padded[:, 2:, 1:-1, :] + padded[:, :-2, 1:-1, :]
    total = total + padded[:, 1:-1, 2:, :] + padded[:, 1:-1, :-2, :]
    total = total + z_padded[:, :, :, 2:] + z_padded[:, :, :, :-2]
    lapl = total - 6.0 * field
    return apply_coef(lapl, field, coef)


def rk_step(field, coef):
    section_one = operator(field, coef)
    section_two = operator(field + 0.5 * STEP_SIZE * section_one, coef)
    section_three = operator(field + 0.5 * STEP_SIZE * section_two, coef)
    section_four = operator(field + STEP_SIZE * section_three, coef)
    return field + STEP_SIZE / 6.0 * (
        section_one + 2.0 * section_two + 2.0 * section_three + section_four
    )


def row_terms(field, psi, profile):
    intersection = field[0] * psi[1] - field[1] * psi[0]
    summed = jnp.sum(intersection * profile[:, None, None], axis=0)
    return summed.reshape(summed.shape[0] // 2, 2, summed.shape[1]).sum(axis=1)


def on_device(chi_final, psi_late, psi_early, trap, controls):
    planes = chi_final.shape[1]
    width_y = chi_final.shape[2]
    depth = chi_final.shape[3]
    total_x = planes * lax.axis_size("gx")
    total_y = width_y * lax.axis_size("gy")
    first = lax.axis_index("gx") * planes
    x_index = (first + jnp.arange(planes, dtype=jnp.int32)).astype(jnp.float32)
    profile = 1.0 + 0.5 * jnp.cos(2.0 * math.pi * x_index / float(total_x))
    coef_late = coefficients(psi_late, trap, controls[1], profile)
    coef_early = coefficients(psi_early, trap, controls[0], profile)
    chi_late = rk_step(chi_final, coef_late)
    chi_start = rk_step(chi_late, coef_early)
    rows = jnp.stack(
        [row_terms(chi_start, psi_early, profile), row_terms(chi_late, psi_late, profile)]
    )
    local_sq = jnp.sum(chi_start * chi_start)
    squares = lax.psum(local_sq, ("gx", "gy"))
    rows_sum = lax.psum(rows, "gx")
    power = squares / float(total_x * total_y * depth)
    grad_rows = rows_sum / jnp.sqrt(float(total_x) * (power + 1e-06))
    return (chi_start, grad_rows, jnp.reshape(power, (1,)))


def solution(mesh):
    placed = (
        P(None, ("starts", "gx"), "gy", None),
        P(None, ("starts", "gx"), "gy", None),
        P(None, ("starts", "gx"), "gy", None),
        P("gx", "gy", None),
        P("starts", "gy", None),
    )
    return jax.shard_map(
        on_device,
        mesh=mesh,
        in_specs=placed,
        out_specs=(P(None, ("starts", "gx"), "gy", None), P("starts", "gy", None), P("starts")),
        check_vma=False,
    )
```

profile of v0, /device:TPU:0, one launch (start us, length us, event | category | flops | bytes accessed | tf_op | source)
XLA Modules:
  0.0 232.7 jit_solution(15009674649921705698)
XLA Ops:
  8.3 1.3 collective-permute-start
  9.6 5.5 %collective-permute-start.1 = (f32[2,1,64,256]{3,2,1,0:T(8,128)S(1)}, f32[2,1,64,256]{3,2,1,0:T(8,128)S(1)}, u32[]{:S(2)}, u32[]{:S(2)}) collective-permute-start(f32[2,1,64,256]{3,2,1,0:T(8,128)S(1)} %get-tuple-element.62), channel_id=1, source_target_pairs={{0,2},{2,4},{4,6},{6,8},{8,10},{10,12},{12,14},{1,3},{3,5},{5,7},{... | collective-permute-start | bytes 393224 | tf_op jit(solution)/shard_map/ppermute | solution.py:17
  15.1 1.4 slice_bitcast_fusion.14
  16.5 3.1 %collective-permute-done.1 = f32[2,1,64,256]{3,2,1,0:T(8,128)S(1)} collective-permute-done((f32[2,1,64,256]{3,2,1,0:T(8,128)S(1)}, f32[2,1,64,256]{3,2,1,0:T(8,128)S(1)}, u32[]{:S(2)}, u32[]{:S(2)}) %collective-permute-start.1) | collective-permute-done | bytes 131104 | tf_op jit(solution)/shard_map/ppermute | solution.py:17
  19.7 1.3 collective-permute-start.2
  21.0 3.0 %collective-permute-start.3 = (f32[2,6,1,256]{3,2,1,0:T(1,128)S(1)}, f32[2,6,1,256]{3,2,1,0:T(1,128)S(1)}, u32[]{:S(2)}, u32[]{:S(2)}) collective-permute-start(f32[2,6,1,256]{3,2,1,0:T(1,128)S(1)} %get-tuple-element.46), channel_id=1, source_target_pairs={{0,1},{2,3},{4,5},{6,7},{8,9},{10,11},{12,13},{14,15},{16,17},{18,... | collective-permute-start | bytes 36872 | tf_op jit(solution)/shard_map/ppermute | solution.py:17
  25.7 4.4 %collective-permute-start.5 = (f32[2,1,64,256]{3,2,1,0:T(8,128)S(1)}, f32[2,1,64,256]{3,2,1,0:T(8,128)S(1)}, u32[]{:S(2)}, u32[]{:S(2)}) collective-permute-start(f32[2,1,64,256]{3,2,1,0:T(8,128)S(1)} %get-tuple-element.59), channel_id=1, source_target_pairs={{0,2},{2,4},{4,6},{6,8},{8,10},{10,12},{12,14},{1,3},{3,5},{5,7},{... | collective-permute-start | bytes 393224 | tf_op jit(solution)/shard_map/ppermute | solution.py:17
  30.1 1.3 collective-permute-start.4
  31.4 1.9 collective-permute-done.5
  33.3 4.1 %collective-permute-done.4 = f32[2,1,64,256]{3,2,1,0:T(8,128)S(1)} collective-permute-done((f32[2,1,64,256]{3,2,1,0:T(8,128)S(1)}, f32[2,1,64,256]{3,2,1,0:T(8,128)S(1)}, u32[]{:S(2)}, u32[]{:S(2)}) %collective-permute-start.4) | collective-permute-done | bytes 131104 | tf_op jit(solution)/shard_map/ppermute | solution.py:20
  37.5 1.3 collective-permute-start.6
  38.8 3.0 %collective-permute-start.7 = (f32[2,6,1,256]{3,2,1,0:T(1,128)S(1)}, f32[2,6,1,256]{3,2,1,0:T(1,128)S(1)}, u32[]{:S(2)}, u32[]{:S(2)}) collective-permute-start(f32[2,6,1,256]{3,2,1,0:T(1,128)S(1)} %get-tuple-element.44), channel_id=1, source_target_pairs={{0,1},{2,3},{4,5},{6,7},{8,9},{10,11},{12,13},{14,15},{16,17},{18,... | collective-permute-start | bytes 36872 | tf_op jit(solution)/shard_map/ppermute | solution.py:17
  43.3 4.5 %collective-permute-start.9 = (f32[2,1,64,256]{3,2,1,0:T(8,128)S(1)}, f32[2,1,64,256]{3,2,1,0:T(8,128)S(1)}, u32[]{:S(2)}, u32[]{:S(2)}) collective-permute-start(f32[2,1,64,256]{3,2,1,0:T(8,128)S(1)} %get-tuple-element.57), channel_id=1, source_target_pairs={{0,2},{2,4},{4,6},{6,8},{8,10},{10,12},{12,14},{1,3},{3,5},{5,7},{... | collective-permute-start | bytes 393224 | tf_op jit(solution)/shard_map/ppermute | solution.py:17
  47.9 1.3 collective-permute-start.8
  49.2 1.9 collective-permute-done.9
  51.1 4.1 %collective-permute-done.8 = f32[2,1,64,256]{3,2,1,0:T(8,128)S(1)} collective-permute-done((f32[2,1,64,256]{3,2,1,0:T(8,128)S(1)}, f32[2,1,64,256]{3,2,1,0:T(8,128)S(1)}, u32[]{:S(2)}, u32[]{:S(2)}) %collective-permute-start.8) | collective-permute-done | bytes 131104 | tf_op jit(solution)/shard_map/ppermute | solution.py:20
  55.2 1.3 collective-permute-start.10
  56.5 3.0 %collective-permute-start.11 = (f32[2,6,1,256]{3,2,1,0:T(1,128)S(1)}, f32[2,6,1,256]{3,2,1,0:T(1,128)S(1)}, u32[]{:S(2)}, u32[]{:S(2)}) collective-permute-start(f32[2,6,1,256]{3,2,1,0:T(1,128)S(1)} %get-tuple-element.42), channel_id=1, source_target_pairs={{0,1},{2,3},{4,5},{6,7},{8,9},{10,11},{12,13},{14,15},{16,17},{18,... | collective-permute-start | bytes 36872 | tf_op jit(solution)/shard_map/ppermute | solution.py:17
  61.0 4.0 %collective-permute-start.13 = (f32[2,1,64,256]{3,2,1,0:T(8,128)S(1)}, f32[2,1,64,256]{3,2,1,0:T(8,128)S(1)}, u32[]{:S(2)}, u32[]{:S(2)}) collective-permute-start(f32[2,1,64,256]{3,2,1,0:T(8,128)S(1)} %get-tuple-element.55), channel_id=1, source_target_pairs={{0,2},{2,4},{4,6},{6,8},{8,10},{10,12},{12,14},{1,3},{3,5},{5,7},{... | collective-permute-start | bytes 393224 | tf_op jit(solution)/shard_map/ppermute | solution.py:17
  65.0 1.3 collective-permute-start.12
  66.3 1.9 collective-permute-done.13
  68.2 4.1 %collective-permute-done.12 = f32[2,1,64,256]{3,2,1,0:T(8,128)S(1)} collective-permute-done((f32[2,1,64,256]{3,2,1,0:T(8,128)S(1)}, f32[2,1,64,256]{3,2,1,0:T(8,128)S(1)}, u32[]{:S(2)}, u32[]{:S(2)}) %collective-permute-start.12) | collective-permute-done | bytes 131104 | tf_op jit(solution)/shard_map/ppermute | solution.py:20
  72.4 1.3 collective-permute-start.14
  73.7 3.0 %collective-permute-start.15 = (f32[2,6,1,256]{3,2,1,0:T(1,128)S(1)}, f32[2,6,1,256]{3,2,1,0:T(1,128)S(1)}, u32[]{:S(2)}, u32[]{:S(2)}) collective-permute-start(f32[2,6,1,256]{3,2,1,0:T(1,128)S(1)} %get-tuple-element.40), channel_id=1, source_target_pairs={{0,1},{2,3},{4,5},{6,7},{8,9},{10,11},{12,13},{14,15},{16,17},{18,... | collective-permute-start | bytes 36872 | tf_op jit(solution)/shard_map/ppermute | solution.py:17
  78.2 4.0 %collective-permute-start.17 = (f32[2,1,64,256]{3,2,1,0:T(8,128)S(1)}, f32[2,1,64,256]{3,2,1,0:T(8,128)S(1)}, u32[]{:S(2)}, u32[]{:S(2)}) collective-permute-start(f32[2,1,64,256]{3,2,1,0:T(8,128)S(1)} %get-tuple-element.53), channel_id=1, source_target_pairs={{0,2},{2,4},{4,6},{6,8},{8,10},{10,12},{12,14},{1,3},{3,5},{5,7},{... | collective-permute-start | bytes 393224 | tf_op jit(solution)/shard_map/ppermute | solution.py:17
  82.3 1.3 collective-permute-start.16
  83.6 1.9 collective-permute-done.17
  85.5 4.1 %collective-permute-done.16 = f32[2,1,64,256]{3,2,1,0:T(8,128)S(1)} collective-permute-done((f32[2,1,64,256]{3,2,1,0:T(8,128)S(1)}, f32[2,1,64,256]{3,2,1,0:T(8,128)S(1)}, u32[]{:S(2)}, u32[]{:S(2)}) %collective-permute-start.16) | collective-permute-done | bytes 131104 | tf_op jit(solution)/shard_map/ppermute | solution.py:20
  91.6 4.2 %collective-permute-start.19 = (f32[2,6,1,256]{3,2,1,0:T(1,128)S(1)}, f32[2,6,1,256]{3,2,1,0:T(1,128)}, u32[]{:S(2)}, u32[]{:S(2)}) collective-permute-start(f32[2,6,1,256]{3,2,1,0:T(1,128)S(1)} %get-tuple-element.38), channel_id=1, source_target_pairs={{0,1},{2,3},{4,5},{6,7},{8,9},{10,11},{12,13},{14,15},{16,17},{18,... | collective-permute-start | bytes 36872 | tf_op jit(solution)/shard_map/ppermute | solution.py:17
  96.4 1.5 mul.427
  97.9 1.3 fusion.14
  100.0 4.0 %collective-permute-start.21 = (f32[2,1,64,256]{3,2,1,0:T(8,128)S(1)}, f32[2,1,64,256]{3,2,1,0:T(8,128)S(1)}, u32[]{:S(2)}, u32[]{:S(2)}) collective-permute-start(f32[2,1,64,256]{3,2,1,0:T(8,128)S(1)} %get-tuple-element.51), channel_id=1, source_target_pairs={{0,2},{2,4},{4,6},{6,8},{8,10},{10,12},{12,14},{1,3},{3,5},{5,7},{... | collective-permute-start | bytes 393224 | tf_op jit(solution)/shard_map/ppermute | solution.py:17
  103.9 1.3 collective-permute-start.20
  106.4 4.4 %collective-permute-done.20 = f32[2,1,64,256]{3,2,1,0:T(8,128)S(1)} collective-permute-done((f32[2,1,64,256]{3,2,1,0:T(8,128)S(1)}, f32[2,1,64,256]{3,2,1,0:T(8,128)S(1)}, u32[]{:S(2)}, u32[]{:S(2)}) %collective-permute-start.20) | collective-permute-done | bytes 131104 | tf_op jit(solution)/shard_map/ppermute | solution.py:20
  110.8 1.3 collective-permute-start.22
  112.1 3.0 %collective-permute-start.23 = (f32[2,6,1,256]{3,2,1,0:T(1,128)S(1)}, f32[2,6,1,256]{3,2,1,0:T(1,128)S(1)}, u32[]{:S(2)}, u32[]{:S(2)}) collective-permute-start(f32[2,6,1,256]{3,2,1,0:T(1,128)S(1)} %get-tuple-element.36), channel_id=1, source_target_pairs={{0,1},{2,3},{4,5},{6,7},{8,9},{10,11},{12,13},{14,15},{16,17},{18,... | collective-permute-start | bytes 36872 | tf_op jit(solution)/shard_map/ppermute | solution.py:17
  116.8 4.0 %collective-permute-start.25 = (f32[2,1,64,256]{3,2,1,0:T(8,128)S(1)}, f32[2,1,64,256]{3,2,1,0:T(8,128)S(1)}, u32[]{:S(2)}, u32[]{:S(2)}) collective-permute-start(f32[2,1,64,256]{3,2,1,0:T(8,128)S(1)} %get-tuple-element.49), channel_id=1, source_target_pairs={{0,2},{2,4},{4,6},{6,8},{8,10},{10,12},{12,14},{1,3},{3,5},{5,7},{... | collective-permute-start | bytes 393224 | tf_op jit(solution)/shard_map/ppermute | solution.py:17
  120.8 1.3 collective-permute-start.24
  122.1 1.9 collective-permute-done.25
  124.0 4.1 %collective-permute-done.24 = f32[2,1,64,256]{3,2,1,0:T(8,128)S(1)} collective-permute-done((f32[2,1,64,256]{3,2,1,0:T(8,128)S(1)}, f32[2,1,64,256]{3,2,1,0:T(8,128)S(1)}, u32[]{:S(2)}, u32[]{:S(2)}) %collective-permute-start.24) | collective-permute-done | bytes 131104 | tf_op jit(solution)/shard_map/ppermute | solution.py:20
  129.4 3.0 %collective-permute-start.27 = (f32[2,6,1,256]{3,2,1,0:T(1,128)S(1)}, f32[2,6,1,256]{3,2,1,0:T(1,128)S(1)}, u32[]{:S(2)}, u32[]{:S(2)}) collective-permute-start(f32[2,6,1,256]{3,2,1,0:T(1,128)S(1)} %get-tuple-element.34), channel_id=1, source_target_pairs={{0,1},{2,3},{4,5},{6,7},{8,9},{10,11},{12,13},{14,15},{16,17},{18,... | collective-permute-start | bytes 36872 | tf_op jit(solution)/shard_map/ppermute | solution.py:17
  134.1 3.8 %collective-permute-start.29 = (f32[2,1,64,256]{3,2,1,0:T(8,128)S(1)}, f32[2,1,64,256]{3,2,1,0:T(8,128)S(1)}, u32[]{:S(2)}, u32[]{:S(2)}) collective-permute-start(f32[2,1,64,256]{3,2,1,0:T(8,128)S(1)} %get-tuple-element.47), channel_id=1, source_target_pairs={{0,2},{2,4},{4,6},{6,8},{8,10},{10,12},{12,14},{1,3},{3,5},{5,7},{... | collective-permute-start | bytes 393224 | tf_op jit(solution)/shard_map/ppermute | solution.py:17
  139.2 1.9 collective-permute-done.29
  141.1 4.1 %collective-permute-done.28 = f32[2,1,64,256]{3,2,1,0:T(8,128)S(1)} collective-permute-done((f32[2,1,64,256]{3,2,1,0:T(8,128)S(1)}, f32[2,1,64,256]{3,2,1,0:T(8,128)S(1)}, u32[]{:S(2)}, u32[]{:S(2)}) %collective-permute-start.28) | collective-permute-done | bytes 131104 | tf_op jit(solution)/shard_map/ppermute | solution.py:20
  146.6 3.0 %collective-permute-start.31 = (f32[2,6,1,256]{3,2,1,0:T(1,128)S(1)}, f32[2,6,1,256]{3,2,1,0:T(1,128)S(1)}, u32[]{:S(2)}, u32[]{:S(2)}) collective-permute-start(f32[2,6,1,256]{3,2,1,0:T(1,128)S(1)} %get-tuple-element.32), channel_id=1, source_target_pairs={{0,1},{2,3},{4,5},{6,7},{8,9},{10,11},{12,13},{14,15},{16,17},{18,... | collective-permute-start | bytes 36872 | tf_op jit(solution)/shard_map/ppermute | solution.py:17
  153.7 32.3 %psum.15 = f32[]{:T(128)} all-reduce(f32[]{:T(128)} %get-tuple-element.5), channel_id=1, replica_groups=mesh['starts'=2,'gx'=8,'gy'=2] {'gx','gy'}, use_global_device_ids=true, to_apply=%region_6.7 | all-reduce | flops 1 | bytes 8 | tf_op jit(solution)/shard_map/psum | solution.py:88
  186.7 36.6 %all-reduce.10.cloned.1.call-done = f32[2,32,256]{2,1,0:T(8,128)} async-done(((f32[2,32,256]{2,1,0:T(8,128)}), f32[2,32,256]{2,1,0:T(8,128)}) %all-reduce.10.cloned.1.call-update) | async-done | bytes 65552 | tf_op jit(solution)/shard_map/psum | solution.py:89
  223.3 1.5 broadcast_divide_fusion
  (96 shorter events, 22.7 us)
Async XLA Ops:
  7.2 12.4 %copy-start = (f32[2,4,64,256]{3,2,1,0:T(8,128)S(1)}, f32[2,4,64,256]{3,2,1,0:T(8,128)}, u32[]{:S(2)}) copy-start(f32[2,4,64,256]{3,2,1,0:T(8,128)} %param.5) | copy-start | bytes 1572868
  7.2 216.1 %all-reduce.10.cloned.1.call-start = ((), (), s32[]{:S(2)}) async-start(), calls=%async_computation | async-start | bytes 131072 | tf_op jit(solution)/shard_map/psum | solution.py:89
  8.3 11.4 %collective-permute-start = (f32[2,1,64,256]{3,2,1,0:T(8,128)S(1)}, f32[2,1,64,256]{3,2,1,0:T(8,128)S(1)}, u32[]{:S(2)}, u32[]{:S(2)}) collective-permute-start(f32[2,1,64,256]{3,2,1,0:T(8,128)S(1)} %get-tuple-element.61), channel_id=1, source_target_pairs={{2,0},{4,2},{6,4},{8,6},{10,8},{12,10},{14,12},{3,1},{5,3},{7,5},{... | collective-permute-start | bytes 393224 | tf_op jit(solution)/shard_map/ppermute | solution.py:20
  9.6 10.0 %collective-permute-start.1 = (f32[2,1,64,256]{3,2,1,0:T(8,128)S(1)}, f32[2,1,64,256]{3,2,1,0:T(8,128)S(1)}, u32[]{:S(2)}, u32[]{:S(2)}) collective-permute-start(f32[2,1,64,256]{3,2,1,0:T(8,128)S(1)} %get-tuple-element.62), channel_id=1, source_target_pairs={{0,2},{2,4},{4,6},{6,8},{8,10},{10,12},{12,14},{1,3},{3,5},{5,7},{... | collective-permute-start | bytes 393224 | tf_op jit(solution)/shard_map/ppermute | solution.py:17
  19.7 4.5 %collective-permute-start.2 = (f32[2,6,1,256]{3,2,1,0:T(1,128)S(1)}, f32[2,6,1,256]{3,2,1,0:T(1,128)S(1)}, u32[]{:S(2)}, u32[]{:S(2)}) collective-permute-start(f32[2,6,1,256]{3,2,1,0:T(1,128)S(1)} %get-tuple-element.45), channel_id=1, source_target_pairs={{1,0},{3,2},{5,4},{7,6},{9,8},{11,10},{13,12},{15,14},{17,16},{19,... | collective-permute-start | bytes 36872 | tf_op jit(solution)/shard_map/ppermute | solution.py:20
  21.0 3.9 %collective-permute-start.3 = (f32[2,6,1,256]{3,2,1,0:T(1,128)S(1)}, f32[2,6,1,256]{3,2,1,0:T(1,128)S(1)}, u32[]{:S(2)}, u32[]{:S(2)}) collective-permute-start(f32[2,6,1,256]{3,2,1,0:T(1,128)S(1)} %get-tuple-element.46), channel_id=1, source_target_pairs={{0,1},{2,3},{4,5},{6,7},{8,9},{10,11},{12,13},{14,15},{16,17},{18,... | collective-permute-start | bytes 36872 | tf_op jit(solution)/shard_map/ppermute | solution.py:17
  24.2 1.1 copy-start.1
  24.2 1.1 copy-start.5
  25.7 7.6 %collective-permute-start.5 = (f32[2,1,64,256]{3,2,1,0:T(8,128)S(1)}, f32[2,1,64,256]{3,2,1,0:T(8,128)S(1)}, u32[]{:S(2)}, u32[]{:S(2)}) collective-permute-start(f32[2,1,64,256]{3,2,1,0:T(8,128)S(1)} %get-tuple-element.59), channel_id=1, source_target_pairs={{0,2},{2,4},{4,6},{6,8},{8,10},{10,12},{12,14},{1,3},{3,5},{5,7},{... | collective-permute-start | bytes 393224 | tf_op jit(solution)/shard_map/ppermute | solution.py:17
  30.1 7.4 %collective-permute-start.4 = (f32[2,1,64,256]{3,2,1,0:T(8,128)S(1)}, f32[2,1,64,256]{3,2,1,0:T(8,128)S(1)}, u32[]{:S(2)}, u32[]{:S(2)}) collective-permute-start(f32[2,1,64,256]{3,2,1,0:T(8,128)S(1)} %get-tuple-element.60), channel_id=1, source_target_pairs={{2,0},{4,2},{6,4},{8,6},{10,8},{12,10},{14,12},{3,1},{5,3},{7,5},{... | collective-permute-start | bytes 393224 | tf_op jit(solution)/shard_map/ppermute | solution.py:20
  37.5 4.3 %collective-permute-start.6 = (f32[2,6,1,256]{3,2,1,0:T(1,128)S(1)}, f32[2,6,1,256]{3,2,1,0:T(1,128)S(1)}, u32[]{:S(2)}, u32[]{:S(2)}) collective-permute-start(f32[2,6,1,256]{3,2,1,0:T(1,128)S(1)} %get-tuple-element.43), channel_id=1, source_target_pairs={{1,0},{3,2},{5,4},{7,6},{9,8},{11,10},{13,12},{15,14},{17,16},{19,... | collective-permute-start | bytes 36872 | tf_op jit(solution)/shard_map/ppermute | solution.py:20
  38.8 3.9 %collective-permute-start.7 = (f32[2,6,1,256]{3,2,1,0:T(1,128)S(1)}, f32[2,6,1,256]{3,2,1,0:T(1,128)S(1)}, u32[]{:S(2)}, u32[]{:S(2)}) collective-permute-start(f32[2,6,1,256]{3,2,1,0:T(1,128)S(1)} %get-tuple-element.44), channel_id=1, source_target_pairs={{0,1},{2,3},{4,5},{6,7},{8,9},{10,11},{12,13},{14,15},{16,17},{18,... | collective-permute-start | bytes 36872 | tf_op jit(solution)/shard_map/ppermute | solution.py:17
  43.3 7.8 %collective-permute-start.9 = (f32[2,1,64,256]{3,2,1,0:T(8,128)S(1)}, f32[2,1,64,256]{3,2,1,0:T(8,128)S(1)}, u32[]{:S(2)}, u32[]{:S(2)}) collective-permute-start(f32[2,1,64,256]{3,2,1,0:T(8,128)S(1)} %get-tuple-element.57), channel_id=1, source_target_pairs={{0,2},{2,4},{4,6},{6,8},{8,10},{10,12},{12,14},{1,3},{3,5},{5,7},{... | collective-permute-start | bytes 393224 | tf_op jit(solution)/shard_map/ppermute | solution.py:17
  47.9 7.4 %collective-permute-start.8 = (f32[2,1,64,256]{3,2,1,0:T(8,128)S(1)}, f32[2,1,64,256]{3,2,1,0:T(8,128)S(1)}, u32[]{:S(2)}, u32[]{:S(2)}) collective-permute-start(f32[2,1,64,256]{3,2,1,0:T(8,128)S(1)} %get-tuple-element.58), channel_id=1, source_target_pairs={{2,0},{4,2},{6,4},{8,6},{10,8},{12,10},{14,12},{3,1},{5,3},{7,5},{... | collective-permute-start | bytes 393224 | tf_op jit(solution)/shard_map/ppermute | solution.py:20
  55.2 4.3 %collective-permute-start.10 = (f32[2,6,1,256]{3,2,1,0:T(1,128)S(1)}, f32[2,6,1,256]{3,2,1,0:T(1,128)S(1)}, u32[]{:S(2)}, u32[]{:S(2)}) collective-permute-start(f32[2,6,1,256]{3,2,1,0:T(1,128)S(1)} %get-tuple-element.41), channel_id=1, source_target_pairs={{1,0},{3,2},{5,4},{7,6},{9,8},{11,10},{13,12},{15,14},{17,16},{19,... | collective-permute-start | bytes 36872 | tf_op jit(solution)/shard_map/ppermute | solution.py:20
  56.5 3.9 %collective-permute-start.11 = (f32[2,6,1,256]{3,2,1,0:T(1,128)S(1)}, f32[2,6,1,256]{3,2,1,0:T(1,128)S(1)}, u32[]{:S(2)}, u32[]{:S(2)}) collective-permute-start(f32[2,6,1,256]{3,2,1,0:T(1,128)S(1)} %get-tuple-element.42), channel_id=1, source_target_pairs={{0,1},{2,3},{4,5},{6,7},{8,9},{10,11},{12,13},{14,15},{16,17},{18,... | collective-permute-start | bytes 36872 | tf_op jit(solution)/shard_map/ppermute | solution.py:17
  61.0 7.2 %collective-permute-start.13 = (f32[2,1,64,256]{3,2,1,0:T(8,128)S(1)}, f32[2,1,64,256]{3,2,1,0:T(8,128)S(1)}, u32[]{:S(2)}, u32[]{:S(2)}) collective-permute-start(f32[2,1,64,256]{3,2,1,0:T(8,128)S(1)} %get-tuple-element.55), channel_id=1, source_target_pairs={{0,2},{2,4},{4,6},{6,8},{8,10},{10,12},{12,14},{1,3},{3,5},{5,7},{... | collective-permute-start | bytes 393224 | tf_op jit(solution)/shard_map/ppermute | solution.py:17
  65.0 7.4 %collective-permute-start.12 = (f32[2,1,64,256]{3,2,1,0:T(8,128)S(1)}, f32[2,1,64,256]{3,2,1,0:T(8,128)S(1)}, u32[]{:S(2)}, u32[]{:S(2)}) collective-permute-start(f32[2,1,64,256]{3,2,1,0:T(8,128)S(1)} %get-tuple-element.56), channel_id=1, source_target_pairs={{2,0},{4,2},{6,4},{8,6},{10,8},{12,10},{14,12},{3,1},{5,3},{7,5},{... | collective-permute-start | bytes 393224 | tf_op jit(solution)/shard_map/ppermute | solution.py:20
  72.4 4.3 %collective-permute-start.14 = (f32[2,6,1,256]{3,2,1,0:T(1,128)S(1)}, f32[2,6,1,256]{3,2,1,0:T(1,128)S(1)}, u32[]{:S(2)}, u32[]{:S(2)}) collective-permute-start(f32[2,6,1,256]{3,2,1,0:T(1,128)S(1)} %get-tuple-element.39), channel_id=1, source_target_pairs={{1,0},{3,2},{5,4},{7,6},{9,8},{11,10},{13,12},{15,14},{17,16},{19,... | collective-permute-start | bytes 36872 | tf_op jit(solution)/shard_map/ppermute | solution.py:20
  73.7 3.9 %collective-permute-start.15 = (f32[2,6,1,256]{3,2,1,0:T(1,128)S(1)}, f32[2,6,1,256]{3,2,1,0:T(1,128)S(1)}, u32[]{:S(2)}, u32[]{:S(2)}) collective-permute-start(f32[2,6,1,256]{3,2,1,0:T(1,128)S(1)} %get-tuple-element.40), channel_id=1, source_target_pairs={{0,1},{2,3},{4,5},{6,7},{8,9},{10,11},{12,13},{14,15},{16,17},{18,... | collective-permute-start | bytes 36872 | tf_op jit(solution)/shard_map/ppermute | solution.py:17
  78.2 7.2 %collective-permute-start.17 = (f32[2,1,64,256]{3,2,1,0:T(8,128)S(1)}, f32[2,1,64,256]{3,2,1,0:T(8,128)S(1)}, u32[]{:S(2)}, u32[]{:S(2)}) collective-permute-start(f32[2,1,64,256]{3,2,1,0:T(8,128)S(1)} %get-tuple-element.53), channel_id=1, source_target_pairs={{0,2},{2,4},{4,6},{6,8},{8,10},{10,12},{12,14},{1,3},{3,5},{5,7},{... | collective-permute-start | bytes 393224 | tf_op jit(solution)/shard_map/ppermute | solution.py:17
  82.2 13.5 %copy-start.8 = (f32[32,256]{1,0:T(8,128)S(1)}, f32[32,256]{1,0:T(8,128)}, u32[]{:S(2)}) copy-start(f32[32,256]{1,0:T(8,128)} %get-tuple-element.63) | copy-start | bytes 98308
  82.3 7.4 %collective-permute-start.16 = (f32[2,1,64,256]{3,2,1,0:T(8,128)S(1)}, f32[2,1,64,256]{3,2,1,0:T(8,128)S(1)}, u32[]{:S(2)}, u32[]{:S(2)}) collective-permute-start(f32[2,1,64,256]{3,2,1,0:T(8,128)S(1)} %get-tuple-element.54), channel_id=1, source_target_pairs={{2,0},{4,2},{6,4},{8,6},{10,8},{12,10},{14,12},{3,1},{5,3},{7,5},{... | collective-permute-start | bytes 393224 | tf_op jit(solution)/shard_map/ppermute | solution.py:20
  89.6 0.7 copy-start.6
  90.3 7.7 %collective-permute-start.18 = (f32[2,6,1,256]{3,2,1,0:T(1,128)}, f32[2,6,1,256]{3,2,1,0:T(1,128)}, u32[]{:S(2)}, u32[]{:S(2)}) collective-permute-start(f32[2,6,1,256]{3,2,1,0:T(1,128)} %get-tuple-element.37), channel_id=1, source_target_pairs={{1,0},{3,2},{5,4},{7,6},{9,8},{11,10},{13,12},{15,14},{17,16},{19,... | collective-permute-start | bytes 36872 | tf_op jit(solution)/shard_map/ppermute | solution.py:20
  91.6 6.4 %collective-permute-start.19 = (f32[2,6,1,256]{3,2,1,0:T(1,128)S(1)}, f32[2,6,1,256]{3,2,1,0:T(1,128)}, u32[]{:S(2)}, u32[]{:S(2)}) collective-permute-start(f32[2,6,1,256]{3,2,1,0:T(1,128)S(1)} %get-tuple-element.38), channel_id=1, source_target_pairs={{0,1},{2,3},{4,5},{6,7},{8,9},{10,11},{12,13},{14,15},{16,17},{18,... | collective-permute-start | bytes 36872 | tf_op jit(solution)/shard_map/ppermute | solution.py:17
  97.9 1.3 copy-start.3
  97.9 1.4 copy-start.7
  100.0 6.5 %collective-permute-start.21 = (f32[2,1,64,256]{3,2,1,0:T(8,128)S(1)}, f32[2,1,64,256]{3,2,1,0:T(8,128)S(1)}, u32[]{:S(2)}, u32[]{:S(2)}) collective-permute-start(f32[2,1,64,256]{3,2,1,0:T(8,128)S(1)} %get-tuple-element.51), channel_id=1, source_target_pairs={{0,2},{2,4},{4,6},{6,8},{8,10},{10,12},{12,14},{1,3},{3,5},{5,7},{... | collective-permute-start | bytes 393224 | tf_op jit(solution)/shard_map/ppermute | solution.py:17
  103.9 6.9 %collective-permute-start.20 = (f32[2,1,64,256]{3,2,1,0:T(8,128)S(1)}, f32[2,1,64,256]{3,2,1,0:T(8,128)S(1)}, u32[]{:S(2)}, u32[]{:S(2)}) collective-permute-start(f32[2,1,64,256]{3,2,1,0:T(8,128)S(1)} %get-tuple-element.52), channel_id=1, source_target_pairs={{2,0},{4,2},{6,4},{8,6},{10,8},{12,10},{14,12},{3,1},{5,3},{7,5},{... | collective-permute-start | bytes 393224 | tf_op jit(solution)/shard_map/ppermute | solution.py:20
  110.8 4.3 %collective-permute-start.22 = (f32[2,6,1,256]{3,2,1,0:T(1,128)S(1)}, f32[2,6,1,256]{3,2,1,0:T(1,128)S(1)}, u32[]{:S(2)}, u32[]{:S(2)}) collective-permute-start(f32[2,6,1,256]{3,2,1,0:T(1,128)S(1)} %get-tuple-element.35), channel_id=1, source_target_pairs={{1,0},{3,2},{5,4},{7,6},{9,8},{11,10},{13,12},{15,14},{17,16},{19,... | collective-permute-start | bytes 36872 | tf_op jit(solution)/shard_map/ppermute | solution.py:20
  112.1 3.9 %collective-permute-start.23 = (f32[2,6,1,256]{3,2,1,0:T(1,128)S(1)}, f32[2,6,1,256]{3,2,1,0:T(1,128)S(1)}, u32[]{:S(2)}, u32[]{:S(2)}) collective-permute-start(f32[2,6,1,256]{3,2,1,0:T(1,128)S(1)} %get-tuple-element.36), channel_id=1, source_target_pairs={{0,1},{2,3},{4,5},{6,7},{8,9},{10,11},{12,13},{14,15},{16,17},{18,... | collective-permute-start | bytes 36872 | tf_op jit(solution)/shard_map/ppermute | solution.py:17
  116.8 7.2 %collective-permute-start.25 = (f32[2,1,64,256]{3,2,1,0:T(8,128)S(1)}, f32[2,1,64,256]{3,2,1,0:T(8,128)S(1)}, u32[]{:S(2)}, u32[]{:S(2)}) collective-permute-start(f32[2,1,64,256]{3,2,1,0:T(8,128)S(1)} %get-tuple-element.49), channel_id=1, source_target_pairs={{0,2},{2,4},{4,6},{6,8},{8,10},{10,12},{12,14},{1,3},{3,5},{5,7},{... | collective-permute-start | bytes 393224 | tf_op jit(solution)/shard_map/ppermute | solution.py:17
  120.8 7.4 %collective-permute-start.24 = (f32[2,1,64,256]{3,2,1,0:T(8,128)S(1)}, f32[2,1,64,256]{3,2,1,0:T(8,128)S(1)}, u32[]{:S(2)}, u32[]{:S(2)}) collective-permute-start(f32[2,1,64,256]{3,2,1,0:T(8,128)S(1)} %get-tuple-element.50), channel_id=1, source_target_pairs={{2,0},{4,2},{6,4},{8,6},{10,8},{12,10},{14,12},{3,1},{5,3},{7,5},{... | collective-permute-start | bytes 393224 | tf_op jit(solution)/shard_map/ppermute | solution.py:20
  128.1 4.3 %collective-permute-start.26 = (f32[2,6,1,256]{3,2,1,0:T(1,128)S(1)}, f32[2,6,1,256]{3,2,1,0:T(1,128)S(1)}, u32[]{:S(2)}, u32[]{:S(2)}) collective-permute-start(f32[2,6,1,256]{3,2,1,0:T(1,128)S(1)} %get-tuple-element.33), channel_id=1, source_target_pairs={{1,0},{3,2},{5,4},{7,6},{9,8},{11,10},{13,12},{15,14},{17,16},{19,... | collective-permute-start | bytes 36872 | tf_op jit(solution)/shard_map/ppermute | solution.py:20
  129.4 3.9 %collective-permute-start.27 = (f32[2,6,1,256]{3,2,1,0:T(1,128)S(1)}, f32[2,6,1,256]{3,2,1,0:T(1,128)S(1)}, u32[]{:S(2)}, u32[]{:S(2)}) collective-permute-start(f32[2,6,1,256]{3,2,1,0:T(1,128)S(1)} %get-tuple-element.34), channel_id=1, source_target_pairs={{0,1},{2,3},{4,5},{6,7},{8,9},{10,11},{12,13},{14,15},{16,17},{18,... | collective-permute-start | bytes 36872 | tf_op jit(solution)/shard_map/ppermute | solution.py:17
  134.1 7.0 %collective-permute-start.29 = (f32[2,1,64,256]{3,2,1,0:T(8,128)S(1)}, f32[2,1,64,256]{3,2,1,0:T(8,128)S(1)}, u32[]{:S(2)}, u32[]{:S(2)}) collective-permute-start(f32[2,1,64,256]{3,2,1,0:T(8,128)S(1)} %get-tuple-element.47), channel_id=1, source_target_pairs={{0,2},{2,4},{4,6},{6,8},{8,10},{10,12},{12,14},{1,3},{3,5},{5,7},{... | collective-permute-start | bytes 393224 | tf_op jit(solution)/shard_map/ppermute | solution.py:17
  137.9 7.4 %collective-permute-start.28 = (f32[2,1,64,256]{3,2,1,0:T(8,128)S(1)}, f32[2,1,64,256]{3,2,1,0:T(8,128)S(1)}, u32[]{:S(2)}, u32[]{:S(2)}) collective-permute-start(f32[2,1,64,256]{3,2,1,0:T(8,128)S(1)} %get-tuple-element.48), channel_id=1, source_target_pairs={{2,0},{4,2},{6,4},{8,6},{10,8},{12,10},{14,12},{3,1},{5,3},{7,5},{... | collective-permute-start | bytes 393224 | tf_op jit(solution)/shard_map/ppermute | solution.py:20
  145.3 4.3 %collective-permute-start.30 = (f32[2,6,1,256]{3,2,1,0:T(1,128)S(1)}, f32[2,6,1,256]{3,2,1,0:T(1,128)S(1)}, u32[]{:S(2)}, u32[]{:S(2)}) collective-permute-start(f32[2,6,1,256]{3,2,1,0:T(1,128)S(1)} %get-tuple-element.31), channel_id=1, source_target_pairs={{1,0},{3,2},{5,4},{7,6},{9,8},{11,10},{13,12},{15,14},{17,16},{19,... | collective-permute-start | bytes 36872 | tf_op jit(solution)/shard_map/ppermute | solution.py:20
  146.6 3.9 %collective-permute-start.31 = (f32[2,6,1,256]{3,2,1,0:T(1,128)S(1)}, f32[2,6,1,256]{3,2,1,0:T(1,128)S(1)}, u32[]{:S(2)}, u32[]{:S(2)}) collective-permute-start(f32[2,6,1,256]{3,2,1,0:T(1,128)S(1)} %get-tuple-element.32), channel_id=1, source_target_pairs={{0,1},{2,3},{4,5},{6,7},{8,9},{10,11},{12,13},{14,15},{16,17},{18,... | collective-permute-start | bytes 36872 | tf_op jit(solution)/shard_map/ppermute | solution.py:17
  150.9 1.1 copy-start.2
  152.0 0.8 copy-start.4
Sparse Core Ops, SparseCore 0:
  153.8 69.3 all-reduce.9
where the time goes:
time: 234 us; the launch traced here: 233 us
  waiting for transfers between devices  87.1 us (37%)
  starting transfers between devices  80.2 us (34%)
  blocking collectives  32.3 us (14%)
  between operations  16.6 us (7%)
  other arithmetic  11 us (5%)
  local copies, waits for them, and re-layouts  5.59 us (2%)
    ppermute x16, starting transfers between devices, extended(): lax.ppermute(lax.slice_in_dim(block, block.shape[dim] - width, None, axis...  59.5 us
    psum x1, waiting for transfers between devices, on_device(): rows_sum = lax.psum(rows, 'gx')  36.6 us
    psum x1, blocking collectives, on_device(): squares = lax.psum(local_sq, ('gx', 'gy'))  32.3 us
    ppermute x16, waiting for transfers between devices, extended(): lax.ppermute(lax.slice_in_dim(block, 0, width, axis=dim), axis, backward)  29.1 us
    ppermute x16, waiting for transfers between devices, extended(): lax.ppermute(lax.slice_in_dim(block, block.shape[dim] - width, None, axis...  21.4 us
    ppermute x16, starting transfers between devices, extended(): lax.ppermute(lax.slice_in_dim(block, 0, width, axis=dim), axis, backward)  20.7 us
  transfers between devices with their start and end apart: 33, of which 23 were waited for; matrix products, arithmetic and copies ran while one was open for 2% of the time, Pallas kernels for 0%

commit v1 on v0

--- a/solution.py
+++ b/solution.py
@@ -9,17 +9,27 @@
 STEP_SIZE = 0.2
 
 
-def extended(block, sides, width):
-    for axis, dim in sides:
-        count = lax.axis_size(axis)
-        forward = [(i, i + 1) for i in range(count - 1)]
-        backward = [(target, source) for source, target in forward]
-        low = lax.ppermute(
-            lax.slice_in_dim(block, block.shape[dim] - width, None, axis=dim), axis, forward
-        )
-        high = lax.ppermute(lax.slice_in_dim(block, 0, width, axis=dim), axis, backward)
-        block = jnp.concatenate([low, block, high], axis=dim)
-    return block
+def halo(block, axis, dim, width):
+    count = lax.axis_size(axis)
+    forward = [(i, i + 1) for i in range(count - 1)]
+    backward = [(target, source) for source, target in forward]
+    low = lax.ppermute(
+        lax.slice_in_dim(block, block.shape[dim] - width, None, axis=dim), axis, forward
+    )
+    high = lax.ppermute(lax.slice_in_dim(block, 0, width, axis=dim), axis, backward)
+    return low, high
+
+
+def axis_sum(value, axis):
+    count = lax.axis_size(axis)
+    if count & (count - 1):
+        return lax.psum(value, axis)
+    step = 1
+    while step < count:
+        pairs = [(i, i ^ step) for i in range(count)]
+        value = value + lax.ppermute(value, axis, pairs)
+        step *= 2
+    return value
 
 
 def coefficients(psi, trap, control, profile):
@@ -43,10 +53,13 @@
 
 
 def operator(field, coef):
-    padded = extended(field, (("gx", 1), ("gy", 2)), 1)
+    x_low, x_high = halo(field, "gx", 1, 1)
+    y_low, y_high = halo(field, "gy", 2, 1)
+    x_padded = jnp.concatenate([x_low, field, x_high], axis=1)
+    y_padded = jnp.concatenate([y_low, field, y_high], axis=2)
     z_padded = jnp.pad(field, ((0, 0), (0, 0), (0, 0), (1, 1)))
-    total = padded[:, 2:, 1:-1, :] + padded[:, :-2, 1:-1, :]
-    total = total + padded[:, 1:-1, 2:, :] + padded[:, 1:-1, :-2, :]
+    total = x_padded[:, 2:] + x_padded[:, :-2]
+    total = total + y_padded[:, :, 2:] + y_padded[:, :, :-2]
     total = total + z_padded[:, :, :, 2:] + z_padded[:, :, :, :-2]
     lapl = total - 6.0 * field
     return apply_coef(lapl, field, coef)
@@ -80,13 +93,14 @@
     coef_late = coefficients(psi_late, trap, controls[1], profile)
     coef_early = coefficients(psi_early, trap, controls[0], profile)
     chi_late = rk_step(chi_final, coef_late)
+    rows_late = axis_sum(row_terms(chi_late, psi_late, profile), "gx")
     chi_start = rk_step(chi_late, coef_early)
-    rows = jnp.stack(
-        [row_terms(chi_start, psi_early, profile), row_terms(chi_late, psi_late, profile)]
-    )
+    rows_early = row_terms(chi_start, psi_early, profile)
     local_sq = jnp.sum(chi_start * chi_start)
-    squares = lax.psum(local_sq, ("gx", "gy"))
-    rows_sum = lax.psum(rows, "gx")
+    extra = jnp.zeros((1, rows_early.shape[1]), jnp.float32).at[0, 0].set(local_sq)
+    packed = axis_sum(jnp.concatenate([rows_early, extra], axis=0), "gx")
+    squares = axis_sum(packed[-1, 0], "gy")
+    rows_sum = jnp.stack([packed[:-1], rows_late])
     power = squares / float(total_x * total_y * depth)
     grad_rows = rows_sum / jnp.sqrt(float(total_x) * (power + 1e-06))
     return (chi_start, grad_rows, jnp.reshape(power, (1,)))

time: 234 us -> 135 us (0.58)
  waiting for transfers between devices: 87.1 us -> 16 us
  blocking collectives: 32.3 us -> 0 us
  starting transfers between devices: 80.2 us -> 98.1 us
  between operations: 16.6 us -> 5.14 us
    psum x1 -> x0, waiting for transfers between devices: 36.6 us -> none  [on_device(): rows_sum = lax.psum(rows, 'gx')]
    ppermute x32 -> x39, waiting for transfers between devices: 50.5 us -> 16 us  [the longest x7 11.6 us: axis_sum(): value = value + lax.ppermute(value, axis, pairs)]
    psum x1 -> x0, blocking collectives: 32.3 us -> none  [on_device(): squares = lax.psum(local_sq, ('gx', 'gy'))]
    ppermute x32 -> x39, starting transfers between devices: 80.2 us -> 98.1 us  [the longest x16 69 us: halo(): lax.ppermute(lax.slice_in_dim(block, block.shape[dim] - width, None, axis...]
  transfers between devices with their start and end apart: 33 -> 39, of which waited for: 23 -> 12; matrix products, arithmetic and copies ran while one was open for 2% -> 1% of each run, Pallas kernels for 0% -> 0%
where the time goes in v1:
time: 135 us; the launch traced here: 134 us
  starting transfers between devices  98.1 us (73%)
  waiting for transfers between devices  16 us (12%)
  other arithmetic  9.53 us (7%)
  between operations  5.14 us (4%)
  local copies, waits for them, and re-layouts  4.77 us (4%)
    ppermute x16, starting transfers between devices, halo(): lax.ppermute(lax.slice_in_dim(block, block.shape[dim] - width, None, axis...  69 us
    ppermute x16, starting transfers between devices, halo(): lax.ppermute(lax.slice_in_dim(block, 0, width, axis=dim), axis, backward)  20.7 us
    ppermute x7, waiting for transfers between devices, axis_sum(): value = value + lax.ppermute(value, axis, pairs)  11.6 us
    ppermute x7, starting transfers between devices, axis_sum(): value = value + lax.ppermute(value, axis, pairs)  8.35 us
    ppermute x16, waiting for transfers between devices, halo(): lax.ppermute(lax.slice_in_dim(block, block.shape[dim] - width, None, axis...  4.43 us
    sub x8, other arithmetic, operator(): lapl = total - 6.0 * field  3.8 us
  transfers between devices with their start and end apart: 39, of which 12 were waited for; matrix products, arithmetic and copies ran while one was open for 1% of the time, Pallas kernels for 0%

profile of v1, /device:TPU:0, one launch (start us, length us, event | category | flops | bytes accessed | tf_op | source)
XLA Modules:
  0.0 133.5 jit_solution(10786290396906709860)
XLA Ops:
  0.6 1.0 fusion.152
  1.7 1.3 collective-permute-start
  3.0 5.5 %collective-permute-start.1 = (f32[2,1,64,256]{3,2,1,0:T(8,128)S(1)}, f32[2,1,64,256]{3,2,1,0:T(8,128)S(1)}, u32[]{:S(2)}, u32[]{:S(2)}) collective-permute-start(f32[2,1,64,256]{3,2,1,0:T(8,128)S(1)} %get-tuple-element.72), channel_id=1, source_target_pairs={{0,2},{2,4},{4,6},{6,8},{8,10},{10,12},{12,14},{1,3},{3,5},{5,7},{... | collective-permute-start | bytes 393224 | tf_op jit(solution)/shard_map/ppermute | solution.py:16
  8.5 1.3 collective-permute-start.2
  9.8 3.0 %collective-permute-start.3 = (f32[2,4,1,256]{3,2,1,0:T(1,128)S(1)}, f32[2,4,1,256]{3,2,1,0:T(1,128)S(1)}, u32[]{:S(2)}, u32[]{:S(2)}) collective-permute-start(f32[2,4,1,256]{3,2,1,0:T(1,128)S(1)} %get-tuple-element.74), channel_id=1, source_target_pairs={{0,1},{2,3},{4,5},{6,7},{8,9},{10,11},{12,13},{14,15},{16,17},{18,... | collective-permute-start | bytes 24584 | tf_op jit(solution)/shard_map/ppermute | solution.py:16
  15.4 1.3 collective-permute-start.4
  16.7 5.4 %collective-permute-start.5 = (f32[2,1,64,256]{3,2,1,0:T(8,128)S(1)}, f32[2,1,64,256]{3,2,1,0:T(8,128)S(1)}, u32[]{:S(2)}, u32[]{:S(2)}) collective-permute-start(f32[2,1,64,256]{3,2,1,0:T(8,128)S(1)} %get-tuple-element.68), channel_id=1, source_target_pairs={{0,2},{2,4},{4,6},{6,8},{8,10},{10,12},{12,14},{1,3},{3,5},{5,7},{... | collective-permute-start | bytes 393224 | tf_op jit(solution)/shard_map/ppermute | solution.py:16
  22.2 1.3 collective-permute-start.6
  23.5 3.0 %collective-permute-start.7 = (f32[2,4,1,256]{3,2,1,0:T(1,128)S(1)}, f32[2,4,1,256]{3,2,1,0:T(1,128)S(1)}, u32[]{:S(2)}, u32[]{:S(2)}) collective-permute-start(f32[2,4,1,256]{3,2,1,0:T(1,128)S(1)} %get-tuple-element.70), channel_id=1, source_target_pairs={{0,1},{2,3},{4,5},{6,7},{8,9},{10,11},{12,13},{14,15},{16,17},{18,... | collective-permute-start | bytes 24584 | tf_op jit(solution)/shard_map/ppermute | solution.py:16
  26.5 0.8 collective-permute-done.7
  28.0 1.3 collective-permute-start.8
  29.3 5.4 %collective-permute-start.9 = (f32[2,1,64,256]{3,2,1,0:T(8,128)S(1)}, f32[2,1,64,256]{3,2,1,0:T(8,128)S(1)}, u32[]{:S(2)}, u32[]{:S(2)}) collective-permute-start(f32[2,1,64,256]{3,2,1,0:T(8,128)S(1)} %get-tuple-element.64), channel_id=1, source_target_pairs={{0,2},{2,4},{4,6},{6,8},{8,10},{10,12},{12,14},{1,3},{3,5},{5,7},{... | collective-permute-start | bytes 393224 | tf_op jit(solution)/shard_map/ppermute | solution.py:16
  34.7 1.3 collective-permute-start.10
  36.0 3.0 %collective-permute-start.11 = (f32[2,4,1,256]{3,2,1,0:T(1,128)S(1)}, f32[2,4,1,256]{3,2,1,0:T(1,128)S(1)}, u32[]{:S(2)}, u32[]{:S(2)}) collective-permute-start(f32[2,4,1,256]{3,2,1,0:T(1,128)S(1)} %get-tuple-element.66), channel_id=1, source_target_pairs={{0,1},{2,3},{4,5},{6,7},{8,9},{10,11},{12,13},{14,15},{16,17},{18,... | collective-permute-start | bytes 24584 | tf_op jit(solution)/shard_map/ppermute | solution.py:16
  39.1 0.8 collective-permute-done.11
  40.5 1.3 collective-permute-start.12
  41.8 5.4 %collective-permute-start.13 = (f32[2,1,64,256]{3,2,1,0:T(8,128)S(1)}, f32[2,1,64,256]{3,2,1,0:T(8,128)S(1)}, u32[]{:S(2)}, u32[]{:S(2)}) collective-permute-start(f32[2,1,64,256]{3,2,1,0:T(8,128)S(1)} %get-tuple-element.60), channel_id=1, source_target_pairs={{0,2},{2,4},{4,6},{6,8},{8,10},{10,12},{12,14},{1,3},{3,5},{5,7},{... | collective-permute-start | bytes 393224 | tf_op jit(solution)/shard_map/ppermute | solution.py:16
  47.3 1.3 collective-permute-start.14
  48.6 3.0 %collective-permute-start.15 = (f32[2,4,1,256]{3,2,1,0:T(1,128)S(1)}, f32[2,4,1,256]{3,2,1,0:T(1,128)S(1)}, u32[]{:S(2)}, u32[]{:S(2)}) collective-permute-start(f32[2,4,1,256]{3,2,1,0:T(1,128)S(1)} %get-tuple-element.62), channel_id=1, source_target_pairs={{0,1},{2,3},{4,5},{6,7},{8,9},{10,11},{12,13},{14,15},{16,17},{18,... | collective-permute-start | bytes 24584 | tf_op jit(solution)/shard_map/ppermute | solution.py:16
  51.7 0.8 collective-permute-done.15
  53.9 1.3 collective-permute-start.16
  55.2 6.1 %collective-permute-start.17 = (f32[2,1,64,256]{3,2,1,0:T(8,128)}, f32[2,1,64,256]{3,2,1,0:T(8,128)}, u32[]{:S(2)}, u32[]{:S(2)}) collective-permute-start(f32[2,1,64,256]{3,2,1,0:T(8,128)} %get-tuple-element.56), channel_id=1, source_target_pairs={{0,2},{2,4},{4,6},{6,8},{8,10},{10,12},{12,14},{1,3},{3,5},{5,7},{... | collective-permute-start | bytes 393224 | tf_op jit(solution)/shard_map/ppermute | solution.py:16
  61.3 1.3 collective-permute-start.18
  62.6 4.2 %collective-permute-start.19 = (f32[2,4,1,256]{3,2,1,0:T(1,128)S(1)}, f32[2,4,1,256]{3,2,1,0:T(1,128)}, u32[]{:S(2)}, u32[]{:S(2)}) collective-permute-start(f32[2,4,1,256]{3,2,1,0:T(1,128)S(1)} %get-tuple-element.58), channel_id=1, source_target_pairs={{0,1},{2,3},{4,5},{6,7},{8,9},{10,11},{12,13},{14,15},{16,17},{18,... | collective-permute-start | bytes 24584 | tf_op jit(solution)/shard_map/ppermute | solution.py:16
  67.2 1.3 %fusion.14 = f32[2,4,64,256]{3,2,1,0:T(8,128)S(1)} fusion(f32[2,4,64,256]{3,2,1,0:T(8,128)S(1)} %fusion.49, f32[2,4,1,256]{3,2,1,0:T(1,128)} %collective-permute-done.19, f32[2,4,1,256]{3,2,1,0:T(1,128)} %collective-permute-done.18, f32[2,1,64,256]{3,2,1,0:T(8,128)} %collective-permute-done.17, f32[2,1,64,256]{3,2,1,0:T(8,128)} %collective-permute-done.16), kind=kLoop, calls=%fused_computation.30 | loop fusion | flops 1441792 | bytes 1327104 | tf_op jit(solution)/shard_map/sub | solution.py:64
  69.2 1.3 collective-permute-start.20
  70.5 4.8 %collective-permute-start.21 = (f32[2,1,64,256]{3,2,1,0:T(8,128)S(1)}, f32[2,1,64,256]{3,2,1,0:T(8,128)S(1)}, u32[]{:S(2)}, u32[]{:S(2)}) collective-permute-start(f32[2,1,64,256]{3,2,1,0:T(8,128)S(1)} %get-tuple-element.52), channel_id=1, source_target_pairs={{0,2},{2,4},{4,6},{6,8},{8,10},{10,12},{12,14},{1,3},{3,5},{5,7},{... | collective-permute-start | bytes 393224 | tf_op jit(solution)/shard_map/ppermute | solution.py:16
  75.4 1.3 collective-permute-start.22
  76.7 3.0 %collective-permute-start.23 = (f32[2,4,1,256]{3,2,1,0:T(1,128)S(1)}, f32[2,4,1,256]{3,2,1,0:T(1,128)S(1)}, u32[]{:S(2)}, u32[]{:S(2)}) collective-permute-start(f32[2,4,1,256]{3,2,1,0:T(1,128)S(1)} %get-tuple-element.54), channel_id=1, source_target_pairs={{0,1},{2,3},{4,5},{6,7},{8,9},{10,11},{12,13},{14,15},{16,17},{18,... | collective-permute-start | bytes 24584 | tf_op jit(solution)/shard_map/ppermute | solution.py:16
  79.7 0.8 collective-permute-done.23
  81.3 1.3 collective-permute-start.24
  82.6 5.4 %collective-permute-start.25 = (f32[2,1,64,256]{3,2,1,0:T(8,128)S(1)}, f32[2,1,64,256]{3,2,1,0:T(8,128)S(1)}, u32[]{:S(2)}, u32[]{:S(2)}) collective-permute-start(f32[2,1,64,256]{3,2,1,0:T(8,128)S(1)} %get-tuple-element.48), channel_id=1, source_target_pairs={{0,2},{2,4},{4,6},{6,8},{8,10},{10,12},{12,14},{1,3},{3,5},{5,7},{... | collective-permute-start | bytes 393224 | tf_op jit(solution)/shard_map/ppermute | solution.py:16
  88.1 1.3 collective-permute-start.26
  89.4 3.0 %collective-permute-start.27 = (f32[2,4,1,256]{3,2,1,0:T(1,128)S(1)}, f32[2,4,1,256]{3,2,1,0:T(1,128)S(1)}, u32[]{:S(2)}, u32[]{:S(2)}) collective-permute-start(f32[2,4,1,256]{3,2,1,0:T(1,128)S(1)} %get-tuple-element.50), channel_id=1, source_target_pairs={{0,1},{2,3},{4,5},{6,7},{8,9},{10,11},{12,13},{14,15},{16,17},{18,... | collective-permute-start | bytes 24584 | tf_op jit(solution)/shard_map/ppermute | solution.py:16
  92.4 0.8 collective-permute-done.27
  94.0 1.3 collective-permute-start.28
  95.3 5.4 %collective-permute-start.29 = (f32[2,1,64,256]{3,2,1,0:T(8,128)S(1)}, f32[2,1,64,256]{3,2,1,0:T(8,128)S(1)}, u32[]{:S(2)}, u32[]{:S(2)}) collective-permute-start(f32[2,1,64,256]{3,2,1,0:T(8,128)S(1)} %get-tuple-element.44), channel_id=1, source_target_pairs={{0,2},{2,4},{4,6},{6,8},{8,10},{10,12},{12,14},{1,3},{3,5},{5,7},{... | collective-permute-start | bytes 393224 | tf_op jit(solution)/shard_map/ppermute | solution.py:16
  100.8 1.3 collective-permute-start.30
  102.1 3.0 %collective-permute-start.31 = (f32[2,4,1,256]{3,2,1,0:T(1,128)S(1)}, f32[2,4,1,256]{3,2,1,0:T(1,128)S(1)}, u32[]{:S(2)}, u32[]{:S(2)}) collective-permute-start(f32[2,4,1,256]{3,2,1,0:T(1,128)S(1)} %get-tuple-element.46), channel_id=1, source_target_pairs={{0,1},{2,3},{4,5},{6,7},{8,9},{10,11},{12,13},{14,15},{16,17},{18,... | collective-permute-start | bytes 24584 | tf_op jit(solution)/shard_map/ppermute | solution.py:16
  106.5 1.1 multiply_reduce_fusion
  109.8 3.0 %collective-permute-start.32 = (f32[33,256]{1,0:T(8,128)S(1)}, f32[33,256]{1,0:T(8,128)S(1)}, u32[]{:S(2)}, u32[]{:S(2)}) collective-permute-start(f32[33,256]{1,0:T(8,128)S(1)} %select_maximum_fusion), channel_id=1, source_target_pairs={{0,2},{2,0},{4,6},{6,4},{8,10},{10,8},{12,14},{14,12},{1,3},{3,1},... | collective-permute-start | bytes 101384 | tf_op jit(solution)/shard_map/ppermute | solution.py:30
  113.0 3.9 %collective-permute-done.35 = f32[32,256]{1,0:T(8,128)S(1)} collective-permute-done((f32[32,256]{1,0:T(8,128)S(1)}, f32[32,256]{1,0:T(8,128)S(1)}, u32[]{:S(2)}, u32[]{:S(2)}) %collective-permute-start.35) | collective-permute-done | bytes 32800 | tf_op jit(solution)/shard_map/ppermute | solution.py:30
  116.9 1.6 %collective-permute-start.36 = (f32[32,256]{1,0:T(8,128)S(1)}, f32[32,256]{1,0:T(8,128)S(1)}, u32[]{:S(2)}, u32[]{:S(2)}) collective-permute-start(f32[32,256]{1,0:T(8,128)S(1)} %add.450), channel_id=1, source_target_pairs={{0,4},{2,6},{4,0},{6,2},{8,12},{10,14},{12,8},{14,10},{1,5},{3,7},... | collective-permute-start | bytes 98312 | tf_op jit(solution)/shard_map/ppermute | solution.py:30
  119.0 1.8 %collective-permute-done.36 = f32[32,256]{1,0:T(8,128)S(1)} collective-permute-done((f32[32,256]{1,0:T(8,128)S(1)}, f32[32,256]{1,0:T(8,128)S(1)}, u32[]{:S(2)}, u32[]{:S(2)}) %collective-permute-start.36) | collective-permute-done | bytes 32800 | tf_op jit(solution)/shard_map/ppermute | solution.py:30
  120.8 2.6 %collective-permute-start.37 = (f32[32,256]{1,0:T(8,128)S(1)}, f32[32,256]{1,0:T(8,128)S(1)}, u32[]{:S(2)}, u32[]{:S(2)}) collective-permute-start(f32[32,256]{1,0:T(8,128)S(1)} %add.451), channel_id=1, source_target_pairs={{0,8},{2,10},{4,12},{6,14},{8,0},{10,2},{12,4},{14,6},{1,9},{3,11}... | collective-permute-start | bytes 98312 | tf_op jit(solution)/shard_map/ppermute | solution.py:30
  124.0 1.6 %collective-permute-done.37 = f32[32,256]{1,0:T(8,128)S(1)} collective-permute-done((f32[32,256]{1,0:T(8,128)S(1)}, f32[32,256]{1,0:T(8,128)S(1)}, u32[]{:S(2)}, u32[]{:S(2)}) %collective-permute-start.37) | collective-permute-done | bytes 32800 | tf_op jit(solution)/shard_map/ppermute | solution.py:30
  125.6 2.8 %collective-permute-done.34 = f32[33,256]{1,0:T(8,128)S(1)} collective-permute-done((f32[33,256]{1,0:T(8,128)S(1)}, f32[33,256]{1,0:T(8,128)S(1)}, u32[]{:S(2)}, u32[]{:S(2)}) %collective-permute-start.34) | collective-permute-done | bytes 33824 | tf_op jit(solution)/shard_map/ppermute | solution.py:30
  129.0 1.4 %collective-permute-done.38 = f32[]{:T(128)} collective-permute-done((f32[]{:T(128)}, f32[]{:T(128)}, u32[]{:S(2)}, u32[]{:S(2)}) %collective-permute-start.38) | collective-permute-done | bytes 36 | tf_op jit(solution)/shard_map/ppermute | solution.py:30
  (110 shorter events, 12.5 us)
Async XLA Ops:
  0.6 7.9 %copy-start = (f32[2,4,64,256]{3,2,1,0:T(8,128)S(1)}, f32[2,4,64,256]{3,2,1,0:T(8,128)}, u32[]{:S(2)}) copy-start(f32[2,4,64,256]{3,2,1,0:T(8,128)} %param.7) | copy-start | bytes 1572868
  1.7 12.2 %collective-permute-start = (f32[2,1,64,256]{3,2,1,0:T(8,128)S(1)}, f32[2,1,64,256]{3,2,1,0:T(8,128)S(1)}, u32[]{:S(2)}, u32[]{:S(2)}) collective-permute-start(f32[2,1,64,256]{3,2,1,0:T(8,128)S(1)} %get-tuple-element.71), channel_id=1, source_target_pairs={{2,0},{4,2},{6,4},{8,6},{10,8},{12,10},{14,12},{3,1},{5,3},{7,5},{... | collective-permute-start | bytes 393224 | tf_op jit(solution)/shard_map/ppermute | solution.py:19
  3.0 10.9 %collective-permute-start.1 = (f32[2,1,64,256]{3,2,1,0:T(8,128)S(1)}, f32[2,1,64,256]{3,2,1,0:T(8,128)S(1)}, u32[]{:S(2)}, u32[]{:S(2)}) collective-permute-start(f32[2,1,64,256]{3,2,1,0:T(8,128)S(1)} %get-tuple-element.72), channel_id=1, source_target_pairs={{0,2},{2,4},{4,6},{6,8},{8,10},{10,12},{12,14},{1,3},{3,5},{5,7},{... | collective-permute-start | bytes 393224 | tf_op jit(solution)/shard_map/ppermute | solution.py:16
  8.5 5.3 %collective-permute-start.2 = (f32[2,4,1,256]{3,2,1,0:T(1,128)S(1)}, f32[2,4,1,256]{3,2,1,0:T(1,128)S(1)}, u32[]{:S(2)}, u32[]{:S(2)}) collective-permute-start(f32[2,4,1,256]{3,2,1,0:T(1,128)S(1)} %get-tuple-element.73), channel_id=1, source_target_pairs={{1,0},{3,2},{5,4},{7,6},{9,8},{11,10},{13,12},{15,14},{17,16},{19,... | collective-permute-start | bytes 24584 | tf_op jit(solution)/shard_map/ppermute | solution.py:19
  9.8 4.0 %collective-permute-start.3 = (f32[2,4,1,256]{3,2,1,0:T(1,128)S(1)}, f32[2,4,1,256]{3,2,1,0:T(1,128)S(1)}, u32[]{:S(2)}, u32[]{:S(2)}) collective-permute-start(f32[2,4,1,256]{3,2,1,0:T(1,128)S(1)} %get-tuple-element.74), channel_id=1, source_target_pairs={{0,1},{2,3},{4,5},{6,7},{8,9},{10,11},{12,13},{14,15},{16,17},{18,... | collective-permute-start | bytes 24584 | tf_op jit(solution)/shard_map/ppermute | solution.py:16
  13.7 0.5 copy-start.6
  13.8 1.0 copy-start.1
  13.8 1.1 copy-start.5
  15.4 11.9 %collective-permute-start.4 = (f32[2,1,64,256]{3,2,1,0:T(8,128)S(1)}, f32[2,1,64,256]{3,2,1,0:T(8,128)S(1)}, u32[]{:S(2)}, u32[]{:S(2)}) collective-permute-start(f32[2,1,64,256]{3,2,1,0:T(8,128)S(1)} %get-tuple-element.67), channel_id=1, source_target_pairs={{2,0},{4,2},{6,4},{8,6},{10,8},{12,10},{14,12},{3,1},{5,3},{7,5},{... | collective-permute-start | bytes 393224 | tf_op jit(solution)/shard_map/ppermute | solution.py:19
  16.7 10.6 %collective-permute-start.5 = (f32[2,1,64,256]{3,2,1,0:T(8,128)S(1)}, f32[2,1,64,256]{3,2,1,0:T(8,128)S(1)}, u32[]{:S(2)}, u32[]{:S(2)}) collective-permute-start(f32[2,1,64,256]{3,2,1,0:T(8,128)S(1)} %get-tuple-element.68), channel_id=1, source_target_pairs={{0,2},{2,4},{4,6},{6,8},{8,10},{10,12},{12,14},{1,3},{3,5},{5,7},{... | collective-permute-start | bytes 393224 | tf_op jit(solution)/shard_map/ppermute | solution.py:16
  22.2 4.3 %collective-permute-start.6 = (f32[2,4,1,256]{3,2,1,0:T(1,128)S(1)}, f32[2,4,1,256]{3,2,1,0:T(1,128)S(1)}, u32[]{:S(2)}, u32[]{:S(2)}) collective-permute-start(f32[2,4,1,256]{3,2,1,0:T(1,128)S(1)} %get-tuple-element.69), channel_id=1, source_target_pairs={{1,0},{3,2},{5,4},{7,6},{9,8},{11,10},{13,12},{15,14},{17,16},{19,... | collective-permute-start | bytes 24584 | tf_op jit(solution)/shard_map/ppermute | solution.py:19
  23.5 3.8 %collective-permute-start.7 = (f32[2,4,1,256]{3,2,1,0:T(1,128)S(1)}, f32[2,4,1,256]{3,2,1,0:T(1,128)S(1)}, u32[]{:S(2)}, u32[]{:S(2)}) collective-permute-start(f32[2,4,1,256]{3,2,1,0:T(1,128)S(1)} %get-tuple-element.70), channel_id=1, source_target_pairs={{0,1},{2,3},{4,5},{6,7},{8,9},{10,11},{12,13},{14,15},{16,17},{18,... | collective-permute-start | bytes 24584 | tf_op jit(solution)/shard_map/ppermute | solution.py:16
  28.0 11.9 %collective-permute-start.8 = (f32[2,1,64,256]{3,2,1,0:T(8,128)S(1)}, f32[2,1,64,256]{3,2,1,0:T(8,128)S(1)}, u32[]{:S(2)}, u32[]{:S(2)}) collective-permute-start(f32[2,1,64,256]{3,2,1,0:T(8,128)S(1)} %get-tuple-element.63), channel_id=1, source_target_pairs={{2,0},{4,2},{6,4},{8,6},{10,8},{12,10},{14,12},{3,1},{5,3},{7,5},{... | collective-permute-start | bytes 393224 | tf_op jit(solution)/shard_map/ppermute | solution.py:19
  29.3 10.6 %collective-permute-start.9 = (f32[2,1,64,256]{3,2,1,0:T(8,128)S(1)}, f32[2,1,64,256]{3,2,1,0:T(8,128)S(1)}, u32[]{:S(2)}, u32[]{:S(2)}) collective-permute-start(f32[2,1,64,256]{3,2,1,0:T(8,128)S(1)} %get-tuple-element.64), channel_id=1, source_target_pairs={{0,2},{2,4},{4,6},{6,8},{8,10},{10,12},{12,14},{1,3},{3,5},{5,7},{... | collective-permute-start | bytes 393224 | tf_op jit(solution)/shard_map/ppermute | solution.py:16
  34.7 4.3 %collective-permute-start.10 = (f32[2,4,1,256]{3,2,1,0:T(1,128)S(1)}, f32[2,4,1,256]{3,2,1,0:T(1,128)S(1)}, u32[]{:S(2)}, u32[]{:S(2)}) collective-permute-start(f32[2,4,1,256]{3,2,1,0:T(1,128)S(1)} %get-tuple-element.65), channel_id=1, source_target_pairs={{1,0},{3,2},{5,4},{7,6},{9,8},{11,10},{13,12},{15,14},{17,16},{19,... | collective-permute-start | bytes 24584 | tf_op jit(solution)/shard_map/ppermute | solution.py:19
  36.0 3.8 %collective-permute-start.11 = (f32[2,4,1,256]{3,2,1,0:T(1,128)S(1)}, f32[2,4,1,256]{3,2,1,0:T(1,128)S(1)}, u32[]{:S(2)}, u32[]{:S(2)}) collective-permute-start(f32[2,4,1,256]{3,2,1,0:T(1,128)S(1)} %get-tuple-element.66), channel_id=1, source_target_pairs={{0,1},{2,3},{4,5},{6,7},{8,9},{10,11},{12,13},{14,15},{16,17},{18,... | collective-permute-start | bytes 24584 | tf_op jit(solution)/shard_map/ppermute | solution.py:16
  40.5 11.9 %collective-permute-start.12 = (f32[2,1,64,256]{3,2,1,0:T(8,128)S(1)}, f32[2,1,64,256]{3,2,1,0:T(8,128)S(1)}, u32[]{:S(2)}, u32[]{:S(2)}) collective-permute-start(f32[2,1,64,256]{3,2,1,0:T(8,128)S(1)} %get-tuple-element.59), channel_id=1, source_target_pairs={{2,0},{4,2},{6,4},{8,6},{10,8},{12,10},{14,12},{3,1},{5,3},{7,5},{... | collective-permute-start | bytes 393224 | tf_op jit(solution)/shard_map/ppermute | solution.py:19
  41.8 10.6 %collective-permute-start.13 = (f32[2,1,64,256]{3,2,1,0:T(8,128)S(1)}, f32[2,1,64,256]{3,2,1,0:T(8,128)S(1)}, u32[]{:S(2)}, u32[]{:S(2)}) collective-permute-start(f32[2,1,64,256]{3,2,1,0:T(8,128)S(1)} %get-tuple-element.60), channel_id=1, source_target_pairs={{0,2},{2,4},{4,6},{6,8},{8,10},{10,12},{12,14},{1,3},{3,5},{5,7},{... | collective-permute-start | bytes 393224 | tf_op jit(solution)/shard_map/ppermute | solution.py:16
  47.3 4.3 %collective-permute-start.14 = (f32[2,4,1,256]{3,2,1,0:T(1,128)S(1)}, f32[2,4,1,256]{3,2,1,0:T(1,128)S(1)}, u32[]{:S(2)}, u32[]{:S(2)}) collective-permute-start(f32[2,4,1,256]{3,2,1,0:T(1,128)S(1)} %get-tuple-element.61), channel_id=1, source_target_pairs={{1,0},{3,2},{5,4},{7,6},{9,8},{11,10},{13,12},{15,14},{17,16},{19,... | collective-permute-start | bytes 24584 | tf_op jit(solution)/shard_map/ppermute | solution.py:19
  48.6 3.8 %collective-permute-start.15 = (f32[2,4,1,256]{3,2,1,0:T(1,128)S(1)}, f32[2,4,1,256]{3,2,1,0:T(1,128)S(1)}, u32[]{:S(2)}, u32[]{:S(2)}) collective-permute-start(f32[2,4,1,256]{3,2,1,0:T(1,128)S(1)} %get-tuple-element.62), channel_id=1, source_target_pairs={{0,1},{2,3},{4,5},{6,7},{8,9},{10,11},{12,13},{14,15},{16,17},{18,... | collective-permute-start | bytes 24584 | tf_op jit(solution)/shard_map/ppermute | solution.py:16
  53.9 13.3 %collective-permute-start.16 = (f32[2,1,64,256]{3,2,1,0:T(8,128)}, f32[2,1,64,256]{3,2,1,0:T(8,128)}, u32[]{:S(2)}, u32[]{:S(2)}) collective-permute-start(f32[2,1,64,256]{3,2,1,0:T(8,128)} %get-tuple-element.55), channel_id=1, source_target_pairs={{2,0},{4,2},{6,4},{8,6},{10,8},{12,10},{14,12},{3,1},{5,3},{7,5},{... | collective-permute-start | bytes 393224 | tf_op jit(solution)/shard_map/ppermute | solution.py:19
  55.2 12.0 %collective-permute-start.17 = (f32[2,1,64,256]{3,2,1,0:T(8,128)}, f32[2,1,64,256]{3,2,1,0:T(8,128)}, u32[]{:S(2)}, u32[]{:S(2)}) collective-permute-start(f32[2,1,64,256]{3,2,1,0:T(8,128)} %get-tuple-element.56), channel_id=1, source_target_pairs={{0,2},{2,4},{4,6},{6,8},{8,10},{10,12},{12,14},{1,3},{3,5},{5,7},{... | collective-permute-start | bytes 393224 | tf_op jit(solution)/shard_map/ppermute | solution.py:16
  61.3 5.6 %collective-permute-start.18 = (f32[2,4,1,256]{3,2,1,0:T(1,128)S(1)}, f32[2,4,1,256]{3,2,1,0:T(1,128)}, u32[]{:S(2)}, u32[]{:S(2)}) collective-permute-start(f32[2,4,1,256]{3,2,1,0:T(1,128)S(1)} %get-tuple-element.57), channel_id=1, source_target_pairs={{1,0},{3,2},{5,4},{7,6},{9,8},{11,10},{13,12},{15,14},{17,16},{19,... | collective-permute-start | bytes 24584 | tf_op jit(solution)/shard_map/ppermute | solution.py:19
  62.6 4.5 %collective-permute-start.19 = (f32[2,4,1,256]{3,2,1,0:T(1,128)S(1)}, f32[2,4,1,256]{3,2,1,0:T(1,128)}, u32[]{:S(2)}, u32[]{:S(2)}) collective-permute-start(f32[2,4,1,256]{3,2,1,0:T(1,128)S(1)} %get-tuple-element.58), channel_id=1, source_target_pairs={{0,1},{2,3},{4,5},{6,7},{8,9},{10,11},{12,13},{14,15},{16,17},{18,... | collective-permute-start | bytes 24584 | tf_op jit(solution)/shard_map/ppermute | solution.py:16
  66.9 1.6 %copy-start.3 = (f32[2,4,64,256]{3,2,1,0:T(8,128)S(1)}, f32[2,4,64,256]{3,2,1,0:T(8,128)}, u32[]{:S(2)}) copy-start(f32[2,4,64,256]{3,2,1,0:T(8,128)} %param.9) | copy-start | bytes 1572868
  66.9 1.6 %copy-start.7 = (f32[4]{0:T(128)S(1)}, f32[4]{0:T(128)}, u32[]{:S(2)}) copy-start(f32[4]{0:T(128)} %copy-done.6) | copy-start | bytes 52
  69.2 11.3 %collective-permute-start.20 = (f32[2,1,64,256]{3,2,1,0:T(8,128)S(1)}, f32[2,1,64,256]{3,2,1,0:T(8,128)S(1)}, u32[]{:S(2)}, u32[]{:S(2)}) collective-permute-start(f32[2,1,64,256]{3,2,1,0:T(8,128)S(1)} %get-tuple-element.51), channel_id=1, source_target_pairs={{2,0},{4,2},{6,4},{8,6},{10,8},{12,10},{14,12},{3,1},{5,3},{7,5},{... | collective-permute-start | bytes 393224 | tf_op jit(solution)/shard_map/ppermute | solution.py:19
  70.5 10.0 %collective-permute-start.21 = (f32[2,1,64,256]{3,2,1,0:T(8,128)S(1)}, f32[2,1,64,256]{3,2,1,0:T(8,128)S(1)}, u32[]{:S(2)}, u32[]{:S(2)}) collective-permute-start(f32[2,1,64,256]{3,2,1,0:T(8,128)S(1)} %get-tuple-element.52), channel_id=1, source_target_pairs={{0,2},{2,4},{4,6},{6,8},{8,10},{10,12},{12,14},{1,3},{3,5},{5,7},{... | collective-permute-start | bytes 393224 | tf_op jit(solution)/shard_map/ppermute | solution.py:16
  75.4 4.3 %collective-permute-start.22 = (f32[2,4,1,256]{3,2,1,0:T(1,128)S(1)}, f32[2,4,1,256]{3,2,1,0:T(1,128)S(1)}, u32[]{:S(2)}, u32[]{:S(2)}) collective-permute-start(f32[2,4,1,256]{3,2,1,0:T(1,128)S(1)} %get-tuple-element.53), channel_id=1, source_target_pairs={{1,0},{3,2},{5,4},{7,6},{9,8},{11,10},{13,12},{15,14},{17,16},{19,... | collective-permute-start | bytes 24584 | tf_op jit(solution)/shard_map/ppermute | solution.py:19
  76.7 3.8 %collective-permute-start.23 = (f32[2,4,1,256]{3,2,1,0:T(1,128)S(1)}, f32[2,4,1,256]{3,2,1,0:T(1,128)S(1)}, u32[]{:S(2)}, u32[]{:S(2)}) collective-permute-start(f32[2,4,1,256]{3,2,1,0:T(1,128)S(1)} %get-tuple-element.54), channel_id=1, source_target_pairs={{0,1},{2,3},{4,5},{6,7},{8,9},{10,11},{12,13},{14,15},{16,17},{18,... | collective-permute-start | bytes 24584 | tf_op jit(solution)/shard_map/ppermute | solution.py:16
  81.3 11.9 %collective-permute-start.24 = (f32[2,1,64,256]{3,2,1,0:T(8,128)S(1)}, f32[2,1,64,256]{3,2,1,0:T(8,128)S(1)}, u32[]{:S(2)}, u32[]{:S(2)}) collective-permute-start(f32[2,1,64,256]{3,2,1,0:T(8,128)S(1)} %get-tuple-element.47), channel_id=1, source_target_pairs={{2,0},{4,2},{6,4},{8,6},{10,8},{12,10},{14,12},{3,1},{5,3},{7,5},{... | collective-permute-start | bytes 393224 | tf_op jit(solution)/shard_map/ppermute | solution.py:19
  82.6 10.6 %collective-permute-start.25 = (f32[2,1,64,256]{3,2,1,0:T(8,128)S(1)}, f32[2,1,64,256]{3,2,1,0:T(8,128)S(1)}, u32[]{:S(2)}, u32[]{:S(2)}) collective-permute-start(f32[2,1,64,256]{3,2,1,0:T(8,128)S(1)} %get-tuple-element.48), channel_id=1, source_target_pairs={{0,2},{2,4},{4,6},{6,8},{8,10},{10,12},{12,14},{1,3},{3,5},{5,7},{... | collective-permute-start | bytes 393224 | tf_op jit(solution)/shard_map/ppermute | solution.py:16
  88.1 4.3 %collective-permute-start.26 = (f32[2,4,1,256]{3,2,1,0:T(1,128)S(1)}, f32[2,4,1,256]{3,2,1,0:T(1,128)S(1)}, u32[]{:S(2)}, u32[]{:S(2)}) collective-permute-start(f32[2,4,1,256]{3,2,1,0:T(1,128)S(1)} %get-tuple-element.49), channel_id=1, source_target_pairs={{1,0},{3,2},{5,4},{7,6},{9,8},{11,10},{13,12},{15,14},{17,16},{19,... | collective-permute-start | bytes 24584 | tf_op jit(solution)/shard_map/ppermute | solution.py:19
  89.4 3.8 %collective-permute-start.27 = (f32[2,4,1,256]{3,2,1,0:T(1,128)S(1)}, f32[2,4,1,256]{3,2,1,0:T(1,128)S(1)}, u32[]{:S(2)}, u32[]{:S(2)}) collective-permute-start(f32[2,4,1,256]{3,2,1,0:T(1,128)S(1)} %get-tuple-element.50), channel_id=1, source_target_pairs={{0,1},{2,3},{4,5},{6,7},{8,9},{10,11},{12,13},{14,15},{16,17},{18,... | collective-permute-start | bytes 24584 | tf_op jit(solution)/shard_map/ppermute | solution.py:16
  94.0 11.9 %collective-permute-start.28 = (f32[2,1,64,256]{3,2,1,0:T(8,128)S(1)}, f32[2,1,64,256]{3,2,1,0:T(8,128)S(1)}, u32[]{:S(2)}, u32[]{:S(2)}) collective-permute-start(f32[2,1,64,256]{3,2,1,0:T(8,128)S(1)} %get-tuple-element.43), channel_id=1, source_target_pairs={{2,0},{4,2},{6,4},{8,6},{10,8},{12,10},{14,12},{3,1},{5,3},{7,5},{... | collective-permute-start | bytes 393224 | tf_op jit(solution)/shard_map/ppermute | solution.py:19
  95.3 10.6 %collective-permute-start.29 = (f32[2,1,64,256]{3,2,1,0:T(8,128)S(1)}, f32[2,1,64,256]{3,2,1,0:T(8,128)S(1)}, u32[]{:S(2)}, u32[]{:S(2)}) collective-permute-start(f32[2,1,64,256]{3,2,1,0:T(8,128)S(1)} %get-tuple-element.44), channel_id=1, source_target_pairs={{0,2},{2,4},{4,6},{6,8},{8,10},{10,12},{12,14},{1,3},{3,5},{5,7},{... | collective-permute-start | bytes 393224 | tf_op jit(solution)/shard_map/ppermute | solution.py:16
  100.8 5.0 %collective-permute-start.30 = (f32[2,4,1,256]{3,2,1,0:T(1,128)S(1)}, f32[2,4,1,256]{3,2,1,0:T(1,128)S(1)}, u32[]{:S(2)}, u32[]{:S(2)}) collective-permute-start(f32[2,4,1,256]{3,2,1,0:T(1,128)S(1)} %get-tuple-element.45), channel_id=1, source_target_pairs={{1,0},{3,2},{5,4},{7,6},{9,8},{11,10},{13,12},{15,14},{17,16},{19,... | collective-permute-start | bytes 24584 | tf_op jit(solution)/shard_map/ppermute | solution.py:19
  102.1 3.8 %collective-permute-start.31 = (f32[2,4,1,256]{3,2,1,0:T(1,128)S(1)}, f32[2,4,1,256]{3,2,1,0:T(1,128)S(1)}, u32[]{:S(2)}, u32[]{:S(2)}) collective-permute-start(f32[2,4,1,256]{3,2,1,0:T(1,128)S(1)} %get-tuple-element.46), channel_id=1, source_target_pairs={{0,1},{2,3},{4,5},{6,7},{8,9},{10,11},{12,13},{14,15},{16,17},{18,... | collective-permute-start | bytes 24584 | tf_op jit(solution)/shard_map/ppermute | solution.py:16
  106.5 1.1 copy-start.2
  107.6 0.8 copy-start.4
  109.8 8.7 %collective-permute-start.32 = (f32[33,256]{1,0:T(8,128)S(1)}, f32[33,256]{1,0:T(8,128)S(1)}, u32[]{:S(2)}, u32[]{:S(2)}) collective-permute-start(f32[33,256]{1,0:T(8,128)S(1)} %select_maximum_fusion), channel_id=1, source_target_pairs={{0,2},{2,0},{4,6},{6,4},{8,10},{10,8},{12,14},{14,12},{1,3},{3,1},... | collective-permute-start | bytes 101384 | tf_op jit(solution)/shard_map/ppermute | solution.py:30
  112.9 4.0 %collective-permute-start.35 = (f32[32,256]{1,0:T(8,128)S(1)}, f32[32,256]{1,0:T(8,128)S(1)}, u32[]{:S(2)}, u32[]{:S(2)}) collective-permute-start(f32[32,256]{1,0:T(8,128)S(1)} %reduce_sum.49), channel_id=1, source_target_pairs={{0,2},{2,0},{4,6},{6,4},{8,10},{10,8},{12,14},{14,12},{1,3},{3,1},... | collective-permute-start | bytes 98312 | tf_op jit(solution)/shard_map/ppermute | solution.py:30
  116.9 3.9 %collective-permute-start.36 = (f32[32,256]{1,0:T(8,128)S(1)}, f32[32,256]{1,0:T(8,128)S(1)}, u32[]{:S(2)}, u32[]{:S(2)}) collective-permute-start(f32[32,256]{1,0:T(8,128)S(1)} %add.450), channel_id=1, source_target_pairs={{0,4},{2,6},{4,0},{6,2},{8,12},{10,14},{12,8},{14,10},{1,5},{3,7},... | collective-permute-start | bytes 98312 | tf_op jit(solution)/shard_map/ppermute | solution.py:30
  118.5 4.9 %collective-permute-start.33 = (f32[33,256]{1,0:T(8,128)S(1)}, f32[33,256]{1,0:T(8,128)S(1)}, u32[]{:S(2)}, u32[]{:S(2)}) collective-permute-start(f32[33,256]{1,0:T(8,128)S(1)} %fusion.134), channel_id=1, source_target_pairs={{0,4},{2,6},{4,0},{6,2},{8,12},{10,14},{12,8},{14,10},{1,5},{3,7},... | collective-permute-start | bytes 101384 | tf_op jit(solution)/shard_map/ppermute | solution.py:30
  120.8 4.8 %collective-permute-start.37 = (f32[32,256]{1,0:T(8,128)S(1)}, f32[32,256]{1,0:T(8,128)S(1)}, u32[]{:S(2)}, u32[]{:S(2)}) collective-permute-start(f32[32,256]{1,0:T(8,128)S(1)} %add.451), channel_id=1, source_target_pairs={{0,8},{2,10},{4,12},{6,14},{8,0},{10,2},{12,4},{14,6},{1,9},{3,11}... | collective-permute-start | bytes 98312 | tf_op jit(solution)/shard_map/ppermute | solution.py:30
  123.4 5.0 %collective-permute-start.34 = (f32[33,256]{1,0:T(8,128)S(1)}, f32[33,256]{1,0:T(8,128)S(1)}, u32[]{:S(2)}, u32[]{:S(2)}) collective-permute-start(f32[33,256]{1,0:T(8,128)S(1)} %add.448), channel_id=1, source_target_pairs={{0,8},{2,10},{4,12},{6,14},{8,0},{10,2},{12,4},{14,6},{1,9},{3,11}... | collective-permute-start | bytes 101384 | tf_op jit(solution)/shard_map/ppermute | solution.py:30
  129.0 1.4 %collective-permute-start.38 = (f32[]{:T(128)}, f32[]{:T(128)}, u32[]{:S(2)}, u32[]{:S(2)}) collective-permute-start(f32[]{:T(128)} %bitcast.59), channel_id=1, source_target_pairs={{0,1},{1,0},{2,3},{3,2},{4,5},{5,4},{6,7},{7,6},{8,9},{9,8},{10,11... | collective-permute-start | bytes 20 | tf_op jit(solution)/shard_map/ppermute | solution.py:30

commit v2 on v1

v2 whole, which is shorter than its diff:
```python
import math

import jax
import jax.numpy as jnp
from jax import lax
from jax.sharding import PartitionSpec as P

COUPLING = 1.0
STEP_SIZE = 0.2
DEPTH = 4


def axis_sum(value, axis):
    count = lax.axis_size(axis)
    if count & (count - 1):
        return lax.psum(value, axis)
    step = 1
    while step < count:
        pairs = [(i, i ^ step) for i in range(count)]
        value = value + lax.ppermute(value, axis, pairs)
        step *= 2
    return value


def swap_y(value):
    return lax.ppermute(value, "gy", [(0, 1), (1, 0)])


def extend(block, w):
    nx = lax.axis_size("gx")
    ny = lax.axis_size("gy")
    iy = lax.axis_index("gy")
    X, Y = block.shape[1], block.shape[2]
    up = [(i, i + 1) for i in range(nx - 1)]
    down = [(i + 1, i) for i in range(nx - 1)]
    x_low = lax.ppermute(block[:, X - w:], "gx", up)
    x_high = lax.ppermute(block[:, :w], "gx", down)
    strip = lax.dynamic_slice_in_dim(block, (1 - iy) * (Y - w), w, axis=2)
    y_other = swap_y(strip)
    up_d = [(i * ny + j, (i + 1) * ny + (1 - j)) for i in range(nx - 1) for j in range(ny)]
    down_d = [((i + 1) * ny + j, i * ny + (1 - j)) for i in range(nx - 1) for j in range(ny)]
    c_low = lax.ppermute(strip[:, X - w:], ("gx", "gy"), up_d)
    c_high = lax.ppermute(strip[:, :w], ("gx", "gy"), down_d)
    main = jnp.concatenate([x_low, block, x_high], axis=1)
    side = jnp.concatenate([c_low, y_other, c_high], axis=1)
    zero = jnp.zeros_like(side)
    below = jnp.where(iy == 1, side, zero)
    above = jnp.where(iy == 0, side, zero)
    return jnp.concatenate([below, main, above], axis=2)


def crop(a, k):
    if k == 0:
        return a
    return a[..., k:a.shape[-3] - k, k:a.shape[-2] - k, :]


def coefficients(psi, trap, fine_control, profile):
    real_part = psi[0]
    imag_part = psi[1]
    potential = trap + profile[:, None, None] * fine_control[None, :, :]
    weight = potential + 2.0 * COUPLING * (real_part * real_part + imag_part * imag_part)
    mix_a = COUPLING * (real_part * real_part - imag_part * imag_part)
    mix_b = 2.0 * COUPLING * real_part * imag_part
    return (weight, mix_a, mix_b)


def apply_coef(lapl, field, coef):
    weight, mix_a, mix_b = coef
    real_part = field[0]
    imag_part = field[1]
    upper = -0.5 * lapl[0] + (weight + mix_a) * real_part + mix_b * imag_part
    lower = -0.5 * lapl[1] + mix_b * real_part + (weight - mix_a) * imag_part
    return jnp.stack([-lower, upper])


def operator(field, coef):
    center = crop(field, 1)
    z_padded = jnp.pad(center, ((0, 0), (0, 0), (0, 0), (1, 1)))
    total = field[:, 2:, 1:-1] + field[:, :-2, 1:-1]
    total = total + field[:, 1:-1, 2:] + field[:, 1:-1, :-2]
    total = total + z_padded[:, :, :, 2:] + z_padded[:, :, :, :-2]
    lapl = total - 6.0 * center
    return apply_coef(lapl, center, coef)


def rk_step(field, coef, inside):
    def masked(value, k):
        return jnp.where(crop(inside, k), value, 0.0)

    def cut(coef_k, k):
        return tuple(crop(c, k) for c in coef_k)

    section_one = operator(field, coef)
    stage_two = masked(crop(field, 1) + 0.5 * STEP_SIZE * section_one, 1)
    section_two = operator(stage_two, cut(coef, 1))
    stage_three = masked(crop(field, 2) + 0.5 * STEP_SIZE * section_two, 2)
    section_three = operator(stage_three, cut(coef, 2))
    stage_four = masked(crop(field, 3) + STEP_SIZE * section_three, 3)
    section_four = operator(stage_four, cut(coef, 3))
    return crop(field, 4) + STEP_SIZE / 6.0 * (
        crop(section_one, 3) + 2.0 * crop(section_two, 2) + 2.0 * crop(section_three, 1)
        + section_four
    )


def row_terms(field, psi, profile):
    intersection = field[0] * psi[1] - field[1] * psi[0]
    summed = jnp.sum(intersection * profile[:, None, None], axis=0)
    return summed.reshape(summed.shape[0] // 2, 2, summed.shape[1]).sum(axis=1)


def on_device(chi_final, psi_late, psi_early, trap, controls):
    w = DEPTH
    planes = chi_final.shape[1]
    width_y = chi_final.shape[2]
    depth = chi_final.shape[3]
    total_x = planes * lax.axis_size("gx")
    total_y = width_y * lax.axis_size("gy")
    ix = lax.axis_index("gx")
    iy = lax.axis_index("gy")

    late_ext = extend(jnp.concatenate([chi_final, psi_late, trap[None]], axis=0), w)
    early_ext = extend(psi_early, w)
    other_controls = swap_y(controls)
    all_controls = jnp.where(
        iy == 0,
        jnp.concatenate([controls, other_controls], axis=1),
        jnp.concatenate([other_controls, controls], axis=1),
    )
    fine = jnp.repeat(all_controls, 2, axis=1)
    fine = jnp.pad(fine, ((0, 0), (w, w), (0, 0)))
    fine = lax.dynamic_slice_in_dim(fine, iy * width_y + 1, width_y + 2 * w - 2, axis=1)

    x_global = ix * planes - w + jnp.arange(planes + 2 * w, dtype=jnp.int32)
    y_global = iy * width_y - w + jnp.arange(width_y + 2 * w, dtype=jnp.int32)
    inside = ((x_global >= 0) & (x_global < total_x))[:, None, None] & (
        (y_global >= 0) & (y_global < total_y)
    )[None, :, None]
    profile_ext = 1.0 + 0.5 * jnp.cos(2.0 * math.pi * x_global.astype(jnp.float32) / float(total_x))
    profile = profile_ext[w:w + planes]
    profile_3 = profile_ext[1:-1]

    coef_late = coefficients(crop(late_ext[2:4], 1), crop(late_ext[4], 1), fine[1], profile_3)
    coef_early = coefficients(crop(early_ext, 1), crop(late_ext[4], 1), fine[0], profile_3)

    chi_late = rk_step(late_ext[0:2], coef_late, inside)
    chi_start = rk_step(extend(chi_late, w), coef_early, inside)

    rows_late = row_terms(chi_late, psi_late, profile)
    rows_early = row_terms(chi_start, psi_early, profile)
    local_sq = jnp.sum(chi_start * chi_start)
    extra = jnp.zeros((1, rows_early.shape[1]), jnp.float32).at[0, 0].set(local_sq)
    packed = axis_sum(jnp.concatenate([rows_early, rows_late, extra], axis=0), "gx")
    squares = axis_sum(packed[-1, 0], "gy")
    half = rows_early.shape[0]
    rows_sum = jnp.stack([packed[:half], packed[half:2 * half]])
    power = squares / float(total_x * total_y * depth)
    grad_rows = rows_sum / jnp.sqrt(float(total_x) * (power + 1e-06))
    return (chi_start, grad_rows, jnp.reshape(power, (1,)))


def solution(mesh):
    placed = (
        P(None, ("starts", "gx"), "gy", None),
        P(None, ("starts", "gx"), "gy", None),
        P(None, ("starts", "gx"), "gy", None),
        P("gx", "gy", None),
        P("starts", "gy", None),
    )
    return jax.shard_map(
        on_device,
        mesh=mesh,
        in_specs=placed,
        out_specs=(P(None, ("starts", "gx"), "gy", None), P("starts", "gy", None), P("starts")),
        check_vma=False,
    )
```

time: 135 us -> 170 us (1.26)
  waiting for transfers between devices: 16 us -> 92.3 us
  starting transfers between devices: 98.1 us -> 46.3 us
  other arithmetic: 9.53 us -> 18.7 us
  local copies, waits for them, and re-layouts: 4.77 us -> 7.08 us
    ppermute x32 -> x16, waiting for transfers between devices: 4.47 us -> 84 us  [the longest x3 49.8 us: extend(): c_low = lax.ppermute(strip[:, X - w:], ('gx', 'gy'), up_d)]
    ppermute x32 -> x16, starting transfers between devices: 89.7 us -> 37.2 us  [the longest x3 15.2 us: extend(): x_low = lax.ppermute(block[:, X - w:], 'gx', up)]
    concatenate x1 -> x4, other arithmetic: 0.01 us -> 3.8 us  [the longest x2 2.35 us: extend(): return jnp.concatenate([below, main, above], axis=2)]
    ppermute x7 -> x4, waiting for transfers between devices: 11.6 us -> 8.27 us  [axis_sum(): value = value + lax.ppermute(value, axis, pairs)]
    another operation x10, other arithmetic: 1.61 us -> 4.16 us  [apply_coef(): return jnp.stack([-lower, upper])]
    select_n x0 -> x10, other arithmetic: none -> 2.35 us  [the longest x6 1.54 us: masked(): return jnp.where(crop(inside, k), value, 0.0)]
    ppermute x7 -> x4, starting transfers between devices: 8.35 us -> 9.08 us  [axis_sum(): value = value + lax.ppermute(value, axis, pairs)]
  transfers between devices with their start and end apart: 39 -> 20, of which waited for: 12 -> 11; matrix products, arithmetic and copies ran while one was open for 1% -> 9% of each run, Pallas kernels for 0% -> 0%
where the time goes in v2:
time: 170 us; the launch traced here: 169 us
  waiting for transfers between devices  92.3 us (54%)
  starting transfers between devices  46.3 us (27%)
  other arithmetic  18.7 us (11%)
  local copies, waits for them, and re-layouts  7.08 us (4%)
  between operations  5.06 us (3%)
    ppermute x3, waiting for transfers between devices, extend(): c_low = lax.ppermute(strip[:, X - w:], ('gx', 'gy'), up_d)  49.8 us
    ppermute x3, waiting for transfers between devices, extend(): x_low = lax.ppermute(block[:, X - w:], 'gx', up)  18.2 us
    ppermute x3, starting transfers between devices, extend(): x_low = lax.ppermute(block[:, X - w:], 'gx', up)  15.2 us
    ppermute x3, starting transfers between devices, extend(): c_low = lax.ppermute(strip[:, X - w:], ('gx', 'gy'), up_d)  13.4 us
    ppermute x3, waiting for transfers between devices, extend(): x_high = lax.ppermute(block[:, :w], 'gx', down)  10.3 us
    ppermute x4, starting transfers between devices, axis_sum(): value = value + lax.ppermute(value, axis, pairs)  9.08 us
    ppermute x4, waiting for transfers between devices, axis_sum(): value = value + lax.ppermute(value, axis, pairs)  8.27 us
    sub x8, other arithmetic, operator(): lapl = total - 6.0 * center  5.01 us
  transfers between devices with their start and end apart: 20, of which 11 were waited for; matrix products, arithmetic and copies ran while one was open for 9% of the time, Pallas kernels for 0%

profile of v2, /device:TPU:0, one launch (start us, length us, event | category | flops | bytes accessed | tf_op | source)
XLA Modules:
  0.0 169.5 jit_solution(17664766978618810267)
XLA Ops:
  0.7 1.4 pad_maximum_fusion.6
  2.1 0.7 constant_dynamic-slice_fusion.2
  2.8 4.9 %collective-permute-start = (f32[5,4,4,256]{3,2,1,0:T(4,128)}, f32[5,4,4,256]{3,2,1,0:T(4,128)}, u32[]{:S(2)}, u32[]{:S(2)}) collective-permute-start(f32[5,4,4,256]{3,2,1,0:T(4,128)} %constant_dynamic-slice_fusion.2), channel_id=1, source_target_pairs={{0,3},{1,2},{2,5},{3,4},{4,7},{5,6},{6,9},{7,8},{8,11},{9,10},{10,... | collective-permute-start | bytes 245768 | tf_op jit(solution)/shard_map/ppermute | solution.py:42
  7.7 0.7 collective-permute-start.1
  8.4 3.9 %collective-permute-start.3 = (f32[5,4,64,256]{3,2,1,0:T(8,128)S(1)}, f32[5,4,64,256]{3,2,1,0:T(8,128)}, u32[]{:S(2)}, u32[]{:S(2)}) collective-permute-start(f32[5,4,64,256]{3,2,1,0:T(8,128)S(1)} %pad_maximum_fusion.6), channel_id=1, source_target_pairs={{0,2},{2,4},{4,6},{6,8},{8,10},{10,12},{12,14},{1,3},{3,5},{5,7},{... | collective-permute-start | bytes 3932168 | tf_op jit(solution)/shard_map/ppermute | solution.py:36
  12.3 1.3 collective-permute-start.4
  13.6 3.6 %collective-permute-start.11 = (f32[2,4,4,256]{3,2,1,0:T(4,128)S(1)}, f32[2,4,4,256]{3,2,1,0:T(4,128)S(1)}, u32[]{:S(2)}, u32[]{:S(2)}) collective-permute-start(f32[2,4,4,256]{3,2,1,0:T(4,128)S(1)} %constant_dynamic-slice_fusion), channel_id=1, source_target_pairs={{0,3},{1,2},{2,5},{3,4},{4,7},{5,6},{6,9},{7,8},{8,11},{9,10},{10,... | collective-permute-start | bytes 98312 | tf_op jit(solution)/shard_map/ppermute | solution.py:42
  17.8 0.6 compare_reduce_fusion
  18.5 49.8 %collective-permute-done.11 = f32[2,4,4,256]{3,2,1,0:T(4,128)S(1)} collective-permute-done((f32[2,4,4,256]{3,2,1,0:T(4,128)S(1)}, f32[2,4,4,256]{3,2,1,0:T(4,128)S(1)}, u32[]{:S(2)}, u32[]{:S(2)}) %collective-permute-start.11) | collective-permute-done | bytes 32800 | tf_op jit(solution)/shard_map/ppermute | solution.py:42
  68.3 1.2 collective-permute-done.12
  69.5 1.3 collective-permute-start.13
  70.8 4.1 %collective-permute-done.13 = f32[2,4,4,256]{3,2,1,0:T(4,128)S(1)} collective-permute-done((f32[2,4,4,256]{3,2,1,0:T(4,128)S(1)}, f32[2,4,4,256]{3,2,1,0:T(4,128)S(1)}, u32[]{:S(2)}, u32[]{:S(2)}) %collective-permute-start.13) | collective-permute-done | bytes 32800 | tf_op jit(solution)/shard_map/ppermute | solution.py:43
  75.1 0.7 broadcast_select_fusion.3
  76.2 1.3 collective-permute-start.2
  77.5 0.8 broadcast_in_dim.66
  78.3 1.1 reshape.175
  79.5 5.4 %collective-permute-start.14 = (f32[2,4,64,256]{3,2,1,0:T(8,128)S(1)}, f32[2,4,64,256]{3,2,1,0:T(8,128)S(1)}, u32[]{:S(2)}, u32[]{:S(2)}) collective-permute-start(f32[2,4,64,256]{3,2,1,0:T(8,128)S(1)} %copy-done.2), channel_id=1, source_target_pairs={{0,2},{2,4},{4,6},{6,8},{8,10},{10,12},{12,14},{1,3},{3,5},{5,7},{... | collective-permute-start | bytes 1572872 | tf_op jit(solution)/shard_map/ppermute | solution.py:36
  84.8 0.9 constant_dynamic-update-slice_fusion.2
  85.7 1.3 collective-permute-start.15
  87.0 0.9 constant_dynamic-update-slice_fusion.1
  88.0 0.9 constant_dynamic-update-slice_fusion
  89.0 2.2 %pad_maximum_fusion = f32[5,12,72,256]{3,2,1,0:T(8,128)S(1)} fusion(f32[5,12,4,256]{3,2,1,0:T(4,128)S(1)} %get-tuple-element.44, f32[5,4,64,256]{3,2,1,0:T(8,128)} %collective-permute-done.4, f32[1,4,64,256]{3,2,1,0:T(8,128)S(1)} %bitcast.323, f32[2,4,64,256]{3,2,1,0:T(8,128)S(1)} %copy-done.1, f32[2,4,64,256]{3,2,1,0:T(8,128)S(1)} %copy-done, ...), kind=kLoop, calls=%fused_computation | loop fusion | flops 6635520 | bytes 8847360 | tf_op jit(solution)/shard_map/concatenate | solution.py:49
  91.4 0.8 fusion.8
  92.2 0.7 fusion.53
  93.7 0.8 fusion.20
  95.3 0.6 fusion.32
  97.3 4.9 %collective-permute-start.6 = (f32[2,4,4,256]{3,2,1,0:T(4,128)S(1)}, f32[2,4,4,256]{3,2,1,0:T(4,128)S(1)}, u32[]{:S(2)}, u32[]{:S(2)}) collective-permute-start(f32[2,4,4,256]{3,2,1,0:T(4,128)S(1)} %constant_dynamic-slice_fusion.1), channel_id=1, source_target_pairs={{0,3},{1,2},{2,5},{3,4},{4,7},{5,6},{6,9},{7,8},{8,11},{9,10},{10,... | collective-permute-start | bytes 98312 | tf_op jit(solution)/shard_map/ppermute | solution.py:42
  102.2 5.7 %collective-permute-done.14 = f32[2,4,64,256]{3,2,1,0:T(8,128)S(1)} collective-permute-done((f32[2,4,64,256]{3,2,1,0:T(8,128)S(1)}, f32[2,4,64,256]{3,2,1,0:T(8,128)S(1)}, u32[]{:S(2)}, u32[]{:S(2)}) %collective-permute-start.14) | collective-permute-done | bytes 524320 | tf_op jit(solution)/shard_map/ppermute | solution.py:36
  108.2 1.3 collective-permute-start.8
  109.5 1.3 collective-permute-start.10
  110.8 5.9 %collective-permute-start.9 = (f32[2,4,64,256]{3,2,1,0:T(8,128)S(1)}, f32[2,4,64,256]{3,2,1,0:T(8,128)S(1)}, u32[]{:S(2)}, u32[]{:S(2)}) collective-permute-start(f32[2,4,64,256]{3,2,1,0:T(8,128)S(1)} %fusion.89), channel_id=1, source_target_pairs={{0,2},{2,4},{4,6},{6,8},{8,10},{10,12},{12,14},{1,3},{3,5},{5,7},{... | collective-permute-start | bytes 1572872 | tf_op jit(solution)/shard_map/ppermute | solution.py:36
  116.8 10.3 %collective-permute-done.10 = f32[2,4,64,256]{3,2,1,0:T(8,128)S(1)} collective-permute-done((f32[2,4,64,256]{3,2,1,0:T(8,128)S(1)}, f32[2,4,64,256]{3,2,1,0:T(8,128)S(1)}, u32[]{:S(2)}, u32[]{:S(2)}) %collective-permute-start.10) | collective-permute-done | bytes 524320 | tf_op jit(solution)/shard_map/ppermute | solution.py:37
  127.1 12.4 %collective-permute-done.9 = f32[2,4,64,256]{3,2,1,0:T(8,128)S(1)} collective-permute-done((f32[2,4,64,256]{3,2,1,0:T(8,128)S(1)}, f32[2,4,64,256]{3,2,1,0:T(8,128)S(1)}, u32[]{:S(2)}, u32[]{:S(2)}) %collective-permute-start.9) | collective-permute-done | bytes 524320 | tf_op jit(solution)/shard_map/ppermute | solution.py:36
  139.8 0.8 fusion.11
  140.7 0.6 fusion.44
  142.1 0.8 fusion.23
  142.8 0.5 fusion.62
  143.7 0.5 fusion.35
  145.4 1.2 multiply_reduce_fusion
  148.4 2.5 %collective-permute-start.16 = (f32[65,256]{1,0:T(8,128)S(1)}, f32[65,256]{1,0:T(8,128)S(1)}, u32[]{:S(2)}, u32[]{:S(2)}) collective-permute-start(f32[65,256]{1,0:T(8,128)S(1)} %select_maximum_fusion), channel_id=1, source_target_pairs={{0,2},{2,0},{4,6},{6,4},{8,10},{10,8},{12,14},{14,12},{1,3},{3,1},... | collective-permute-start | bytes 199688 | tf_op jit(solution)/shard_map/ppermute | solution.py:20
  150.9 2.3 %collective-permute-done.16 = f32[65,256]{1,0:T(8,128)S(1)} collective-permute-done((f32[65,256]{1,0:T(8,128)S(1)}, f32[65,256]{1,0:T(8,128)S(1)}, u32[]{:S(2)}, u32[]{:S(2)}) %collective-permute-start.16) | collective-permute-done | bytes 66592 | tf_op jit(solution)/shard_map/ppermute | solution.py:20
  153.3 3.4 %collective-permute-start.17 = (f32[65,256]{1,0:T(8,128)S(1)}, f32[65,256]{1,0:T(8,128)S(1)}, u32[]{:S(2)}, u32[]{:S(2)}) collective-permute-start(f32[65,256]{1,0:T(8,128)S(1)} %fusion.144), channel_id=1, source_target_pairs={{0,4},{2,6},{4,0},{6,2},{8,12},{10,14},{12,8},{14,10},{1,5},{3,7},... | collective-permute-start | bytes 199688 | tf_op jit(solution)/shard_map/ppermute | solution.py:20
  156.7 2.3 %collective-permute-done.17 = f32[65,256]{1,0:T(8,128)S(1)} collective-permute-done((f32[65,256]{1,0:T(8,128)S(1)}, f32[65,256]{1,0:T(8,128)S(1)}, u32[]{:S(2)}, u32[]{:S(2)}) %collective-permute-start.17) | collective-permute-done | bytes 66592 | tf_op jit(solution)/shard_map/ppermute | solution.py:20
  159.1 3.1 %collective-permute-start.18 = (f32[65,256]{1,0:T(8,128)S(1)}, f32[65,256]{1,0:T(8,128)S(1)}, u32[]{:S(2)}, u32[]{:S(2)}) collective-permute-start(f32[65,256]{1,0:T(8,128)S(1)} %add.486), channel_id=1, source_target_pairs={{0,8},{2,10},{4,12},{6,14},{8,0},{10,2},{12,4},{14,6},{1,9},{3,11}... | collective-permute-start | bytes 199688 | tf_op jit(solution)/shard_map/ppermute | solution.py:20
  162.2 2.3 %collective-permute-done.18 = f32[65,256]{1,0:T(8,128)S(1)} collective-permute-done((f32[65,256]{1,0:T(8,128)S(1)}, f32[65,256]{1,0:T(8,128)S(1)}, u32[]{:S(2)}, u32[]{:S(2)}) %collective-permute-start.18) | collective-permute-done | bytes 66592 | tf_op jit(solution)/shard_map/ppermute | solution.py:20
  164.5 0.5 slice.747
  165.0 1.3 collective-permute-done.19
  167.7 0.6 maximum_divide_fusion
  (86 shorter events, 7.8 us)
Async XLA Ops:
  0.6 13.0 %copy-start.2 = (f32[2,4,64,256]{3,2,1,0:T(8,128)S(1)}, f32[2,4,64,256]{3,2,1,0:T(8,128)}, u32[]{:S(2)}) copy-start(f32[2,4,64,256]{3,2,1,0:T(8,128)} %param.9) | copy-start | bytes 1572868
  0.6 74.3 %copy-start.6 = (f32[2,32,256]{2,1,0:T(8,128)S(1)}, f32[2,32,256]{2,1,0:T(8,128)}, u32[]{:S(2)}) copy-start(f32[2,32,256]{2,1,0:T(8,128)} %param.11) | copy-start | bytes 196612
  2.8 76.7 %collective-permute-start = (f32[5,4,4,256]{3,2,1,0:T(4,128)}, f32[5,4,4,256]{3,2,1,0:T(4,128)}, u32[]{:S(2)}, u32[]{:S(2)}) collective-permute-start(f32[5,4,4,256]{3,2,1,0:T(4,128)} %constant_dynamic-slice_fusion.2), channel_id=1, source_target_pairs={{0,3},{1,2},{2,5},{3,4},{4,7},{5,6},{6,9},{7,8},{8,11},{9,10},{10,... | collective-permute-start | bytes 245768 | tf_op jit(solution)/shard_map/ppermute | solution.py:42
  7.7 78.0 %collective-permute-start.1 = (f32[5,4,4,256]{3,2,1,0:T(4,128)}, f32[5,4,4,256]{3,2,1,0:T(4,128)}, u32[]{:S(2)}, u32[]{:S(2)}) collective-permute-start(f32[5,4,4,256]{3,2,1,0:T(4,128)} %constant_dynamic-slice_fusion.2), channel_id=1, source_target_pairs={{0,1},{1,0},{2,3},{3,2},{4,5},{5,4},{6,7},{7,6},{8,9},{9,8},{10,11... | collective-permute-start | bytes 245768 | tf_op jit(solution)/shard_map/ppermute | solution.py:26
  8.4 80.6 %collective-permute-start.3 = (f32[5,4,64,256]{3,2,1,0:T(8,128)S(1)}, f32[5,4,64,256]{3,2,1,0:T(8,128)}, u32[]{:S(2)}, u32[]{:S(2)}) collective-permute-start(f32[5,4,64,256]{3,2,1,0:T(8,128)S(1)} %pad_maximum_fusion.6), channel_id=1, source_target_pairs={{0,2},{2,4},{4,6},{6,8},{8,10},{10,12},{12,14},{1,3},{3,5},{5,7},{... | collective-permute-start | bytes 3932168 | tf_op jit(solution)/shard_map/ppermute | solution.py:36
  12.3 76.7 %collective-permute-start.4 = (f32[5,4,64,256]{3,2,1,0:T(8,128)S(1)}, f32[5,4,64,256]{3,2,1,0:T(8,128)}, u32[]{:S(2)}, u32[]{:S(2)}) collective-permute-start(f32[5,4,64,256]{3,2,1,0:T(8,128)S(1)} %pad_maximum_fusion.6), channel_id=1, source_target_pairs={{2,0},{4,2},{6,4},{8,6},{10,8},{12,10},{14,12},{3,1},{5,3},{7,5},{... | collective-permute-start | bytes 3932168 | tf_op jit(solution)/shard_map/ppermute | solution.py:37
  13.6 54.6 %collective-permute-start.11 = (f32[2,4,4,256]{3,2,1,0:T(4,128)S(1)}, f32[2,4,4,256]{3,2,1,0:T(4,128)S(1)}, u32[]{:S(2)}, u32[]{:S(2)}) collective-permute-start(f32[2,4,4,256]{3,2,1,0:T(4,128)S(1)} %constant_dynamic-slice_fusion), channel_id=1, source_target_pairs={{0,3},{1,2},{2,5},{3,4},{4,7},{5,6},{6,9},{7,8},{8,11},{9,10},{10,... | collective-permute-start | bytes 98312 | tf_op jit(solution)/shard_map/ppermute | solution.py:42
  68.3 1.2 collective-permute-start.12
  69.5 5.4 %collective-permute-start.13 = (f32[2,4,4,256]{3,2,1,0:T(4,128)S(1)}, f32[2,4,4,256]{3,2,1,0:T(4,128)S(1)}, u32[]{:S(2)}, u32[]{:S(2)}) collective-permute-start(f32[2,4,4,256]{3,2,1,0:T(4,128)S(1)} %constant_dynamic-slice_fusion), channel_id=1, source_target_pairs={{2,1},{3,0},{4,3},{5,2},{6,5},{7,4},{8,7},{9,6},{10,9},{11,8},{12,... | collective-permute-start | bytes 98312 | tf_op jit(solution)/shard_map/ppermute | solution.py:43
  74.9 1.3 collective-permute-start.5
  75.8 13.2 %copy-start = (f32[2,4,64,256]{3,2,1,0:T(8,128)S(1)}, f32[2,4,64,256]{3,2,1,0:T(8,128)}, u32[]{:S(2)}) copy-start(f32[2,4,64,256]{3,2,1,0:T(8,128)} %param.7) | copy-start | bytes 1572868
  75.8 13.2 %copy-start.1 = (f32[2,4,64,256]{3,2,1,0:T(8,128)S(1)}, f32[2,4,64,256]{3,2,1,0:T(8,128)}, u32[]{:S(2)}) copy-start(f32[2,4,64,256]{3,2,1,0:T(8,128)} %param.8) | copy-start | bytes 1572868
  75.8 13.2 %copy-start.4 = (f32[4,64,256]{2,1,0:T(8,128)S(1)}, f32[4,64,256]{2,1,0:T(8,128)}, u32[]{:S(2)}) copy-start(f32[4,64,256]{2,1,0:T(8,128)} %param.10) | copy-start | bytes 786436
  76.2 11.8 %collective-permute-start.2 = (f32[5,4,4,256]{3,2,1,0:T(4,128)}, f32[5,4,4,256]{3,2,1,0:T(4,128)}, u32[]{:S(2)}, u32[]{:S(2)}) collective-permute-start(f32[5,4,4,256]{3,2,1,0:T(4,128)} %constant_dynamic-slice_fusion.2), channel_id=1, source_target_pairs={{2,1},{3,0},{4,3},{5,2},{6,5},{7,4},{8,7},{9,6},{10,9},{11,8},{12,... | collective-permute-start | bytes 245768 | tf_op jit(solution)/shard_map/ppermute | solution.py:43
  79.5 28.5 %collective-permute-start.14 = (f32[2,4,64,256]{3,2,1,0:T(8,128)S(1)}, f32[2,4,64,256]{3,2,1,0:T(8,128)S(1)}, u32[]{:S(2)}, u32[]{:S(2)}) collective-permute-start(f32[2,4,64,256]{3,2,1,0:T(8,128)S(1)} %copy-done.2), channel_id=1, source_target_pairs={{0,2},{2,4},{4,6},{6,8},{8,10},{10,12},{12,14},{1,3},{3,5},{5,7},{... | collective-permute-start | bytes 1572872 | tf_op jit(solution)/shard_map/ppermute | solution.py:36
  85.7 22.2 %collective-permute-start.15 = (f32[2,4,64,256]{3,2,1,0:T(8,128)S(1)}, f32[2,4,64,256]{3,2,1,0:T(8,128)S(1)}, u32[]{:S(2)}, u32[]{:S(2)}) collective-permute-start(f32[2,4,64,256]{3,2,1,0:T(8,128)S(1)} %copy-done.2), channel_id=1, source_target_pairs={{2,0},{4,2},{6,4},{8,6},{10,8},{12,10},{14,12},{3,1},{5,3},{7,5},{... | collective-permute-start | bytes 1572872 | tf_op jit(solution)/shard_map/ppermute | solution.py:37
  97.1 10.9 %copy-start.5 = (f32[2,12,4,256]{3,2,1,0:T(4,128)S(1)}, f32[2,12,4,256]{3,2,1,0:T(4,128)}, u32[]{:S(2)}) copy-start(f32[2,12,4,256]{3,2,1,0:T(4,128)} %get-tuple-element.46) | copy-start | bytes 294916
  97.3 19.3 %collective-permute-start.6 = (f32[2,4,4,256]{3,2,1,0:T(4,128)S(1)}, f32[2,4,4,256]{3,2,1,0:T(4,128)S(1)}, u32[]{:S(2)}, u32[]{:S(2)}) collective-permute-start(f32[2,4,4,256]{3,2,1,0:T(4,128)S(1)} %constant_dynamic-slice_fusion.1), channel_id=1, source_target_pairs={{0,3},{1,2},{2,5},{3,4},{4,7},{5,6},{6,9},{7,8},{8,11},{9,10},{10,... | collective-permute-start | bytes 98312 | tf_op jit(solution)/shard_map/ppermute | solution.py:42
  108.1 8.6 %collective-permute-start.7 = (f32[2,4,4,256]{3,2,1,0:T(4,128)S(1)}, f32[2,4,4,256]{3,2,1,0:T(4,128)S(1)}, u32[]{:S(2)}, u32[]{:S(2)}) collective-permute-start(f32[2,4,4,256]{3,2,1,0:T(4,128)S(1)} %constant_dynamic-slice_fusion.1), channel_id=1, source_target_pairs={{0,1},{1,0},{2,3},{3,2},{4,5},{5,4},{6,7},{7,6},{8,9},{9,8},{10,11... | collective-permute-start | bytes 98312 | tf_op jit(solution)/shard_map/ppermute | solution.py:26
  108.2 8.5 %collective-permute-start.8 = (f32[2,4,4,256]{3,2,1,0:T(4,128)S(1)}, f32[2,4,4,256]{3,2,1,0:T(4,128)S(1)}, u32[]{:S(2)}, u32[]{:S(2)}) collective-permute-start(f32[2,4,4,256]{3,2,1,0:T(4,128)S(1)} %constant_dynamic-slice_fusion.1), channel_id=1, source_target_pairs={{2,1},{3,0},{4,3},{5,2},{6,5},{7,4},{8,7},{9,6},{10,9},{11,8},{12,... | collective-permute-start | bytes 98312 | tf_op jit(solution)/shard_map/ppermute | solution.py:43
  109.5 17.6 %collective-permute-start.10 = (f32[2,4,64,256]{3,2,1,0:T(8,128)S(1)}, f32[2,4,64,256]{3,2,1,0:T(8,128)S(1)}, u32[]{:S(2)}, u32[]{:S(2)}) collective-permute-start(f32[2,4,64,256]{3,2,1,0:T(8,128)S(1)} %fusion.89), channel_id=1, source_target_pairs={{2,0},{4,2},{6,4},{8,6},{10,8},{12,10},{14,12},{3,1},{5,3},{7,5},{... | collective-permute-start | bytes 1572872 | tf_op jit(solution)/shard_map/ppermute | solution.py:37
  110.8 28.7 %collective-permute-start.9 = (f32[2,4,64,256]{3,2,1,0:T(8,128)S(1)}, f32[2,4,64,256]{3,2,1,0:T(8,128)S(1)}, u32[]{:S(2)}, u32[]{:S(2)}) collective-permute-start(f32[2,4,64,256]{3,2,1,0:T(8,128)S(1)} %fusion.89), channel_id=1, source_target_pairs={{0,2},{2,4},{4,6},{6,8},{8,10},{10,12},{12,14},{1,3},{3,5},{5,7},{... | collective-permute-start | bytes 1572872 | tf_op jit(solution)/shard_map/ppermute | solution.py:36
  146.6 6.7 %copy-start.3 = (f32[2,4,64,256]{3,2,1,0:T(8,128)}, f32[2,4,64,256]{3,2,1,0:T(8,128)S(1)}, u32[]{:S(2)}) copy-start(f32[2,4,64,256]{3,2,1,0:T(8,128)S(1)} %get-tuple-element.18) | copy-start | bytes 1572868
  148.4 4.9 %collective-permute-start.16 = (f32[65,256]{1,0:T(8,128)S(1)}, f32[65,256]{1,0:T(8,128)S(1)}, u32[]{:S(2)}, u32[]{:S(2)}) collective-permute-start(f32[65,256]{1,0:T(8,128)S(1)} %select_maximum_fusion), channel_id=1, source_target_pairs={{0,2},{2,0},{4,6},{6,4},{8,10},{10,8},{12,14},{14,12},{1,3},{3,1},... | collective-permute-start | bytes 199688 | tf_op jit(solution)/shard_map/ppermute | solution.py:20
  153.3 5.8 %collective-permute-start.17 = (f32[65,256]{1,0:T(8,128)S(1)}, f32[65,256]{1,0:T(8,128)S(1)}, u32[]{:S(2)}, u32[]{:S(2)}) collective-permute-start(f32[65,256]{1,0:T(8,128)S(1)} %fusion.144), channel_id=1, source_target_pairs={{0,4},{2,6},{4,0},{6,2},{8,12},{10,14},{12,8},{14,10},{1,5},{3,7},... | collective-permute-start | bytes 199688 | tf_op jit(solution)/shard_map/ppermute | solution.py:20
  159.1 5.4 %collective-permute-start.18 = (f32[65,256]{1,0:T(8,128)S(1)}, f32[65,256]{1,0:T(8,128)S(1)}, u32[]{:S(2)}, u32[]{:S(2)}) collective-permute-start(f32[65,256]{1,0:T(8,128)S(1)} %add.486), channel_id=1, source_target_pairs={{0,8},{2,10},{4,12},{6,14},{8,0},{10,2},{12,4},{14,6},{1,9},{3,11}... | collective-permute-start | bytes 199688 | tf_op jit(solution)/shard_map/ppermute | solution.py:20
  165.0 1.3 collective-permute-start.19

commit v3 on v2

--- a/solution.py
+++ b/solution.py
@@ -7,7 +7,7 @@
 
 COUPLING = 1.0
 STEP_SIZE = 0.2
-DEPTH = 4
+DEPTH = 2
 
 
 def axis_sum(value, axis):
@@ -31,22 +31,29 @@
     ny = lax.axis_size("gy")
     iy = lax.axis_index("gy")
     X, Y = block.shape[1], block.shape[2]
+    if ny == 2:
+        strip = lax.dynamic_slice_in_dim(block, (1 - iy) * (Y - w), w, axis=2)
+        other = swap_y(strip)
+        zero = jnp.zeros_like(other)
+        below = jnp.where(iy == 1, other, zero)
+        above = jnp.where(iy == 0, other, zero)
+    else:
+        below = lax.ppermute(block[:, :, Y - w:], "gy", [(j, j + 1) for j in range(ny - 1)])
+        above = lax.ppermute(block[:, :, :w], "gy", [(j + 1, j) for j in range(ny - 1)])
     up = [(i, i + 1) for i in range(nx - 1)]
     down = [(i + 1, i) for i in range(nx - 1)]
-    x_low = lax.ppermute(block[:, X - w:], "gx", up)
-    x_high = lax.ppermute(block[:, :w], "gx", down)
-    strip = lax.dynamic_slice_in_dim(block, (1 - iy) * (Y - w), w, axis=2)
-    y_other = swap_y(strip)
-    up_d = [(i * ny + j, (i + 1) * ny + (1 - j)) for i in range(nx - 1) for j in range(ny)]
-    down_d = [((i + 1) * ny + j, i * ny + (1 - j)) for i in range(nx - 1) for j in range(ny)]
-    c_low = lax.ppermute(strip[:, X - w:], ("gx", "gy"), up_d)
-    c_high = lax.ppermute(strip[:, :w], ("gx", "gy"), down_d)
-    main = jnp.concatenate([x_low, block, x_high], axis=1)
-    side = jnp.concatenate([c_low, y_other, c_high], axis=1)
-    zero = jnp.zeros_like(side)
-    below = jnp.where(iy == 1, side, zero)
-    above = jnp.where(iy == 0, side, zero)
-    return jnp.concatenate([below, main, above], axis=2)
+    if w == 1:
+        x_low = lax.ppermute(block[:, X - w:], "gx", up)
+        x_high = lax.ppermute(block[:, :w], "gx", down)
+        corner = jnp.zeros(x_low.shape[:2] + (w,) + x_low.shape[3:], block.dtype)
+        x_low = jnp.concatenate([corner, x_low, corner], axis=2)
+        x_high = jnp.concatenate([corner, x_high, corner], axis=2)
+        tall = jnp.concatenate([below, block, above], axis=2)
+    else:
+        tall = jnp.concatenate([below, block, above], axis=2)
+        x_low = lax.ppermute(tall[:, X - w:], "gx", up)
+        x_high = lax.ppermute(tall[:, :w], "gx", down)
+    return jnp.concatenate([x_low, tall, x_high], axis=1)
 
 
 def crop(a, k):
@@ -84,23 +91,22 @@
     return apply_coef(lapl, center, coef)
 
 
-def rk_step(field, coef, inside):
-    def masked(value, k):
-        return jnp.where(crop(inside, k), value, 0.0)
-
-    def cut(coef_k, k):
-        return tuple(crop(c, k) for c in coef_k)
-
-    section_one = operator(field, coef)
-    stage_two = masked(crop(field, 1) + 0.5 * STEP_SIZE * section_one, 1)
-    section_two = operator(stage_two, cut(coef, 1))
-    stage_three = masked(crop(field, 2) + 0.5 * STEP_SIZE * section_two, 2)
-    section_three = operator(stage_three, cut(coef, 2))
-    stage_four = masked(crop(field, 3) + STEP_SIZE * section_three, 3)
-    section_four = operator(stage_four, cut(coef, 3))
-    return crop(field, 4) + STEP_SIZE / 6.0 * (
-        crop(section_one, 3) + 2.0 * crop(section_two, 2) + 2.0 * crop(section_three, 1)
-        + section_four
+def rk_step(field, coef, inside, w):
+    weights = (0.5 * STEP_SIZE, 0.5 * STEP_SIZE, STEP_SIZE)
+    sections = []
+    stage, reach = field, w
+    for k in range(4):
+        if reach == 0:
+            stage, reach = extend(stage, w), w
+        section = operator(stage, tuple(crop(c, w - reach) for c in coef))
+        reach -= 1
+        sections.append(crop(section, reach))
+        if k < 3:
+            stage = crop(field, w - reach) + weights[k] * section
+            stage = jnp.where(crop(inside, w - reach), stage, 0.0)
+    section_one, section_two, section_three, section_four = sections
+    return crop(field, w) + STEP_SIZE / 6.0 * (
+        section_one + 2.0 * section_two + 2.0 * section_three + section_four
     )
 
 
@@ -120,17 +126,22 @@
     ix = lax.axis_index("gx")
     iy = lax.axis_index("gy")
 
-    late_ext = extend(jnp.concatenate([chi_final, psi_late, trap[None]], axis=0), w)
-    early_ext = extend(psi_early, w)
-    other_controls = swap_y(controls)
-    all_controls = jnp.where(
-        iy == 0,
-        jnp.concatenate([controls, other_controls], axis=1),
-        jnp.concatenate([other_controls, controls], axis=1),
-    )
-    fine = jnp.repeat(all_controls, 2, axis=1)
-    fine = jnp.pad(fine, ((0, 0), (w, w), (0, 0)))
-    fine = lax.dynamic_slice_in_dim(fine, iy * width_y + 1, width_y + 2 * w - 2, axis=1)
+    cd = w - 1
+    sources = jnp.concatenate([psi_late, psi_early, trap[None]], axis=0)
+    if cd > 0:
+        sources = extend(sources, cd)
+        other_controls = swap_y(controls)
+        all_controls = jnp.where(
+            iy == 0,
+            jnp.concatenate([controls, other_controls], axis=1),
+            jnp.concatenate([other_controls, controls], axis=1),
+        )
+        fine = jnp.repeat(all_controls, 2, axis=1)
+        fine = jnp.pad(fine, ((0, 0), (cd, cd), (0, 0)))
+        fine = lax.dynamic_slice_in_dim(fine, iy * width_y, width_y + 2 * cd, axis=1)
+    else:
+        fine = jnp.repeat(controls, 2, axis=1)
+    chi_ext = extend(chi_final, w)
 
     x_global = ix * planes - w + jnp.arange(planes + 2 * w, dtype=jnp.int32)
     y_global = iy * width_y - w + jnp.arange(width_y + 2 * w, dtype=jnp.int32)
@@ -139,13 +150,13 @@
     )[None, :, None]
     profile_ext = 1.0 + 0.5 * jnp.cos(2.0 * math.pi * x_global.astype(jnp.float32) / float(total_x))
     profile = profile_ext[w:w + planes]
-    profile_3 = profile_ext[1:-1]
+    profile_c = profile_ext[1:-1]
 
-    coef_late = coefficients(crop(late_ext[2:4], 1), crop(late_ext[4], 1), fine[1], profile_3)
-    coef_early = coefficients(crop(early_ext, 1), crop(late_ext[4], 1), fine[0], profile_3)
+    coef_late = coefficients(sources[0:2], sources[4], fine[1], profile_c)
+    coef_early = coefficients(sources[2:4], sources[4], fine[0], profile_c)
 
-    chi_late = rk_step(late_ext[0:2], coef_late, inside)
-    chi_start = rk_step(extend(chi_late, w), coef_early, inside)
+    chi_late = rk_step(chi_ext, coef_late, inside, w)
+    chi_start = rk_step(extend(chi_late, w), coef_early, inside, w)
 
     rows_late = row_terms(chi_late, psi_late, profile)
     rows_early = row_terms(chi_start, psi_early, profile)

time: 170 us -> 131 us (0.77)
  waiting for transfers between devices: 92.3 us -> 62.7 us
  starting transfers between devices: 46.3 us -> 39.6 us
  other arithmetic: 18.7 us -> 15.4 us
    ppermute x3 -> x1, waiting for transfers between devices: 18.2 us -> 0.01 us  [extend(): x_low = lax.ppermute(block[:, X - w:], 'gx', up)]
    ppermute x3 -> x1, waiting for transfers between devices: 10.3 us -> 0.01 us  [extend(): x_high = lax.ppermute(block[:, :w], 'gx', down)]
    ppermute x3 -> x1, starting transfers between devices: 15.2 us -> 4.89 us  [extend(): x_low = lax.ppermute(block[:, X - w:], 'gx', up)]
    ppermute x6 -> x8, starting transfers between devices: 17.3 us -> 25.6 us  [the longest x4 20.4 us: extend(): x_low = lax.ppermute(tall[:, X - w:], 'gx', up)]
    ppermute x6 -> x8, waiting for transfers between devices: 54 us -> 49.9 us  [the longest x4 28.7 us: extend(): x_low = lax.ppermute(tall[:, X - w:], 'gx', up)]
    another operation x10 -> x6, other arithmetic: 4.16 us -> 1.09 us  [apply_coef(): return jnp.stack([-lower, upper])]
    ppermute x3 -> x1, starting transfers between devices: 3.86 us -> 1.29 us  [extend(): x_high = lax.ppermute(block[:, :w], 'gx', down)]
    ppermute x4, starting transfers between devices: 9.08 us -> 6.83 us  [axis_sum(): value = value + lax.ppermute(value, axis, pairs)]
  transfers between devices with their start and end apart: 20 -> 20, of which waited for: 11 -> 15; matrix products, arithmetic and copies ran while one was open for 9% -> 6% of each run, Pallas kernels for 0% -> 0%
where the time goes in v3:
time: 131 us
  waiting for transfers between devices  62.7 us (48%)
  starting transfers between devices  39.6 us (30%)
  other arithmetic  15.4 us (12%)
  local copies, waits for them, and re-layouts  7.97 us (6%)
  between operations  5.06 us (4%)
    ppermute x4, waiting for transfers between devices, extend(): x_low = lax.ppermute(tall[:, X - w:], 'gx', up)  28.7 us
    ppermute x4, waiting for transfers between devices, extend(): x_high = lax.ppermute(tall[:, :w], 'gx', down)  21.2 us
    ppermute x4, starting transfers between devices, extend(): x_low = lax.ppermute(tall[:, X - w:], 'gx', up)  20.4 us
    ppermute x4, waiting for transfers between devices, axis_sum(): value = value + lax.ppermute(value, axis, pairs)  9.33 us
    ppermute x4, starting transfers between devices, axis_sum(): value = value + lax.ppermute(value, axis, pairs)  6.83 us
    ppermute x4, starting transfers between devices, extend(): x_high = lax.ppermute(tall[:, :w], 'gx', down)  5.17 us
    ppermute x1, starting transfers between devices, extend(): x_low = lax.ppermute(block[:, X - w:], 'gx', up)  4.89 us
    sub x8, other arithmetic, operator(): lapl = total - 6.0 * center  3.85 us
  transfers between devices with their start and end apart: 20, of which 15 were waited for; matrix products, arithmetic and copies ran while one was open for 6% of the time, Pallas kernels for 0%

profile of v3, /device:TPU:0, one launch (start us, length us, event | category | flops | bytes accessed | tf_op | source)
XLA Modules:
  0.0 130.7 jit_solution(12469823517008649378)
XLA Ops:
  0.6 0.9 constant_dynamic-slice_fusion.4
  1.5 0.6 collective-permute-start
  2.0 1.4 %pad_maximum_fusion = f32[5,4,64,256]{3,2,1,0:T(8,128)S(1)} fusion(f32[1,4,64,256]{3,2,1,0:T(8,128)} %bitcast.182, f32[2,4,64,256]{3,2,1,0:T(8,128)} %param.9, f32[2,4,64,256]{3,2,1,0:T(8,128)} %param.8), kind=kLoop, calls=%fused_computation.9 | loop fusion | flops 655360 | bytes 2621440 | tf_op jit(solution)/shard_map/concatenate | solution.py:130
  3.6 4.9 %collective-permute-start.3 = (f32[5,1,64,256]{3,2,1,0:T(8,128)S(1)}, f32[5,1,64,256]{3,2,1,0:T(8,128)S(1)}, u32[]{:S(2)}, u32[]{:S(2)}) collective-permute-start(f32[5,1,64,256]{3,2,1,0:T(8,128)S(1)} %get-tuple-element.43), channel_id=1, source_target_pairs={{0,2},{2,4},{4,6},{6,8},{8,10},{10,12},{12,14},{1,3},{3,5},{5,7},{... | collective-permute-start | bytes 983048 | tf_op jit(solution)/shard_map/ppermute | solution.py:46
  8.5 1.3 collective-permute-start.5
  10.0 0.6 slice_bitcast_fusion.11
  10.7 0.6 slice_bitcast_fusion.12
  11.3 0.6 slice.471
  11.9 0.6 slice.611
  12.7 1.3 collective-permute-start.1
  14.0 5.2 %collective-permute-start.2 = (f32[2,2,68,256]{3,2,1,0:T(8,128)S(1)}, f32[2,2,68,256]{3,2,1,0:T(8,128)S(1)}, u32[]{:S(2)}, u32[]{:S(2)}) collective-permute-start(f32[2,2,68,256]{3,2,1,0:T(8,128)S(1)} %get-tuple-element.51), channel_id=1, source_target_pairs={{0,2},{2,4},{4,6},{6,8},{8,10},{10,12},{12,14},{1,3},{3,5},{5,7},{... | collective-permute-start | bytes 835592 | tf_op jit(solution)/shard_map/ppermute | solution.py:54
  19.2 0.6 broadcast_select_fusion.1
  20.2 5.9 %collective-permute-done.1 = f32[2,2,68,256]{3,2,1,0:T(8,128)S(1)} collective-permute-done((f32[2,2,68,256]{3,2,1,0:T(8,128)S(1)}, f32[2,2,68,256]{3,2,1,0:T(8,128)S(1)}, u32[]{:S(2)}, u32[]{:S(2)}) %collective-permute-start.1) | collective-permute-done | bytes 278560 | tf_op jit(solution)/shard_map/ppermute | solution.py:55
  26.1 9.2 %collective-permute-done.2 = f32[2,2,68,256]{3,2,1,0:T(8,128)S(1)} collective-permute-done((f32[2,2,68,256]{3,2,1,0:T(8,128)S(1)}, f32[2,2,68,256]{3,2,1,0:T(8,128)S(1)}, u32[]{:S(2)}, u32[]{:S(2)}) %collective-permute-start.2) | collective-permute-done | bytes 278560 | tf_op jit(solution)/shard_map/ppermute | solution.py:54
  35.3 0.8 pad_maximum_fusion.1
  36.2 0.6 copy-done.6
  36.9 0.6 fusion.14
  41.1 0.5 copy-done.12
  41.8 1.2 collective-permute-done.7
  43.1 1.3 collective-permute-start.8
  44.4 5.0 %collective-permute-start.9 = (f32[2,2,68,256]{3,2,1,0:T(8,128)S(1)}, f32[2,2,68,256]{3,2,1,0:T(8,128)S(1)}, u32[]{:S(2)}, u32[]{:S(2)}) collective-permute-start(f32[2,2,68,256]{3,2,1,0:T(8,128)S(1)} %get-tuple-element.49), channel_id=1, source_target_pairs={{0,2},{2,4},{4,6},{6,8},{8,10},{10,12},{12,14},{1,3},{3,5},{5,7},{... | collective-permute-start | bytes 835592 | tf_op jit(solution)/shard_map/ppermute | solution.py:54
  49.4 5.4 %collective-permute-done.8 = f32[2,2,68,256]{3,2,1,0:T(8,128)S(1)} collective-permute-done((f32[2,2,68,256]{3,2,1,0:T(8,128)S(1)}, f32[2,2,68,256]{3,2,1,0:T(8,128)S(1)}, u32[]{:S(2)}, u32[]{:S(2)}) %collective-permute-start.8) | collective-permute-done | bytes 278560 | tf_op jit(solution)/shard_map/ppermute | solution.py:55
  54.8 6.5 %collective-permute-done.9 = f32[2,2,68,256]{3,2,1,0:T(8,128)S(1)} collective-permute-done((f32[2,2,68,256]{3,2,1,0:T(8,128)S(1)}, f32[2,2,68,256]{3,2,1,0:T(8,128)S(1)}, u32[]{:S(2)}, u32[]{:S(2)}) %collective-permute-start.9) | collective-permute-done | bytes 278560 | tf_op jit(solution)/shard_map/ppermute | solution.py:54
  61.5 0.6 fusion.17
  63.6 1.2 collective-permute-done.10
  64.9 1.3 collective-permute-start.11
  66.2 5.0 %collective-permute-start.12 = (f32[2,2,68,256]{3,2,1,0:T(8,128)S(1)}, f32[2,2,68,256]{3,2,1,0:T(8,128)S(1)}, u32[]{:S(2)}, u32[]{:S(2)}) collective-permute-start(f32[2,2,68,256]{3,2,1,0:T(8,128)S(1)} %get-tuple-element.47), channel_id=1, source_target_pairs={{0,2},{2,4},{4,6},{6,8},{8,10},{10,12},{12,14},{1,3},{3,5},{5,7},{... | collective-permute-start | bytes 835592 | tf_op jit(solution)/shard_map/ppermute | solution.py:54
  71.3 5.4 %collective-permute-done.11 = f32[2,2,68,256]{3,2,1,0:T(8,128)S(1)} collective-permute-done((f32[2,2,68,256]{3,2,1,0:T(8,128)S(1)}, f32[2,2,68,256]{3,2,1,0:T(8,128)S(1)}, u32[]{:S(2)}, u32[]{:S(2)}) %collective-permute-start.11) | collective-permute-done | bytes 278560 | tf_op jit(solution)/shard_map/ppermute | solution.py:55
  76.6 6.5 %collective-permute-done.12 = f32[2,2,68,256]{3,2,1,0:T(8,128)S(1)} collective-permute-done((f32[2,2,68,256]{3,2,1,0:T(8,128)S(1)}, f32[2,2,68,256]{3,2,1,0:T(8,128)S(1)}, u32[]{:S(2)}, u32[]{:S(2)}) %collective-permute-start.12) | collective-permute-done | bytes 278560 | tf_op jit(solution)/shard_map/ppermute | solution.py:54
  83.3 0.6 fusion.20
  85.9 1.2 collective-permute-done.13
  87.2 1.3 collective-permute-start.14
  88.5 5.2 %collective-permute-start.15 = (f32[2,2,68,256]{3,2,1,0:T(8,128)S(1)}, f32[2,2,68,256]{3,2,1,0:T(8,128)S(1)}, u32[]{:S(2)}, u32[]{:S(2)}) collective-permute-start(f32[2,2,68,256]{3,2,1,0:T(8,128)S(1)} %get-tuple-element.45), channel_id=1, source_target_pairs={{0,2},{2,4},{4,6},{6,8},{8,10},{10,12},{12,14},{1,3},{3,5},{5,7},{... | collective-permute-start | bytes 835592 | tf_op jit(solution)/shard_map/ppermute | solution.py:54
  93.7 0.6 compare_reduce_fusion
  94.4 4.6 %collective-permute-done.14 = f32[2,2,68,256]{3,2,1,0:T(8,128)S(1)} collective-permute-done((f32[2,2,68,256]{3,2,1,0:T(8,128)S(1)}, f32[2,2,68,256]{3,2,1,0:T(8,128)S(1)}, u32[]{:S(2)}, u32[]{:S(2)}) %collective-permute-start.14) | collective-permute-done | bytes 278560 | tf_op jit(solution)/shard_map/ppermute | solution.py:55
  98.9 6.5 %collective-permute-done.15 = f32[2,2,68,256]{3,2,1,0:T(8,128)S(1)} collective-permute-done((f32[2,2,68,256]{3,2,1,0:T(8,128)S(1)}, f32[2,2,68,256]{3,2,1,0:T(8,128)S(1)}, u32[]{:S(2)}, u32[]{:S(2)}) %collective-permute-start.15) | collective-permute-done | bytes 278560 | tf_op jit(solution)/shard_map/ppermute | solution.py:54
  105.6 0.6 fusion.23
  107.4 1.1 multiply_reduce_fusion
  108.9 0.5 copy-done.3
  110.9 2.5 %collective-permute-start.16 = (f32[65,256]{1,0:T(8,128)S(1)}, f32[65,256]{1,0:T(8,128)S(1)}, u32[]{:S(2)}, u32[]{:S(2)}) collective-permute-start(f32[65,256]{1,0:T(8,128)S(1)} %select_maximum_fusion), channel_id=1, source_target_pairs={{0,2},{2,0},{4,6},{6,4},{8,10},{10,8},{12,14},{14,12},{1,3},{3,1},... | collective-permute-start | bytes 199688 | tf_op jit(solution)/shard_map/ppermute | solution.py:20
  113.4 2.5 %collective-permute-done.16 = f32[65,256]{1,0:T(8,128)S(1)} collective-permute-done((f32[65,256]{1,0:T(8,128)S(1)}, f32[65,256]{1,0:T(8,128)S(1)}, u32[]{:S(2)}, u32[]{:S(2)}) %collective-permute-start.16) | collective-permute-done | bytes 66592 | tf_op jit(solution)/shard_map/ppermute | solution.py:20
  115.9 1.6 %collective-permute-start.17 = (f32[65,256]{1,0:T(8,128)S(1)}, f32[65,256]{1,0:T(8,128)S(1)}, u32[]{:S(2)}, u32[]{:S(2)}) collective-permute-start(f32[65,256]{1,0:T(8,128)S(1)} %fusion.126), channel_id=1, source_target_pairs={{0,4},{2,6},{4,0},{6,2},{8,12},{10,14},{12,8},{14,10},{1,5},{3,7},... | collective-permute-start | bytes 199688 | tf_op jit(solution)/shard_map/ppermute | solution.py:20
  117.5 2.8 %collective-permute-done.17 = f32[65,256]{1,0:T(8,128)S(1)} collective-permute-done((f32[65,256]{1,0:T(8,128)S(1)}, f32[65,256]{1,0:T(8,128)S(1)}, u32[]{:S(2)}, u32[]{:S(2)}) %collective-permute-start.17) | collective-permute-done | bytes 66592 | tf_op jit(solution)/shard_map/ppermute | solution.py:20
  120.3 2.7 %collective-permute-start.18 = (f32[65,256]{1,0:T(8,128)S(1)}, f32[65,256]{1,0:T(8,128)S(1)}, u32[]{:S(2)}, u32[]{:S(2)}) collective-permute-start(f32[65,256]{1,0:T(8,128)S(1)} %add.529), channel_id=1, source_target_pairs={{0,8},{2,10},{4,12},{6,14},{8,0},{10,2},{12,4},{14,6},{1,9},{3,11}... | collective-permute-start | bytes 199688 | tf_op jit(solution)/shard_map/ppermute | solution.py:20
  123.0 2.7 %collective-permute-done.18 = f32[65,256]{1,0:T(8,128)S(1)} collective-permute-done((f32[65,256]{1,0:T(8,128)S(1)}, f32[65,256]{1,0:T(8,128)S(1)}, u32[]{:S(2)}, u32[]{:S(2)}) %collective-permute-start.18) | collective-permute-done | bytes 66592 | tf_op jit(solution)/shard_map/ppermute | solution.py:20
  125.7 0.5 slice.692
  126.2 1.4 %collective-permute-done.19 = f32[]{:T(128)} collective-permute-done((f32[]{:T(128)}, f32[]{:T(128)}, u32[]{:S(2)}, u32[]{:S(2)}) %collective-permute-start.19) | collective-permute-done | bytes 36 | tf_op jit(solution)/shard_map/ppermute | solution.py:20
  128.9 0.6 maximum_divide_fusion
  (109 shorter events, 10.7 us)
Async XLA Ops:
  1.5 11.0 %collective-permute-start = (f32[2,4,2,256]{3,2,1,0:T(2,128)S(1)}, f32[2,4,2,256]{3,2,1,0:T(2,128)S(1)}, u32[]{:S(2)}, u32[]{:S(2)}) collective-permute-start(f32[2,4,2,256]{3,2,1,0:T(2,128)S(1)} %constant_dynamic-slice_fusion.4), channel_id=1, source_target_pairs={{0,1},{1,0},{2,3},{3,2},{4,5},{5,4},{6,7},{7,6},{8,9},{9,8},{10,11... | collective-permute-start | bytes 49160 | tf_op jit(solution)/shard_map/ppermute | solution.py:26
  3.4 6.4 %copy-start.9 = (f32[2,32,256]{2,1,0:T(8,128)S(1)}, f32[2,32,256]{2,1,0:T(8,128)}, u32[]{:S(2)}) copy-start(f32[2,32,256]{2,1,0:T(8,128)} %param.11) | copy-start | bytes 196612
  3.5 9.1 %copy-start = (f32[2,4,64,256]{3,2,1,0:T(8,128)S(1)}, f32[2,4,64,256]{3,2,1,0:T(8,128)}, u32[]{:S(2)}) copy-start(f32[2,4,64,256]{3,2,1,0:T(8,128)} %param.7) | copy-start | bytes 1572868
  3.5 10.5 %collective-permute-start.4 = (f32[5,4,1,256]{3,2,1,0:T(1,128)S(1)}, f32[5,4,1,256]{3,2,1,0:T(1,128)S(1)}, u32[]{:S(2)}, u32[]{:S(2)}) collective-permute-start(f32[5,4,1,256]{3,2,1,0:T(1,128)S(1)} %constant_dynamic-slice_fusion.3), channel_id=1, source_target_pairs={{0,1},{1,0},{2,3},{3,2},{4,5},{5,4},{6,7},{7,6},{8,9},{9,8},{10,11... | collective-permute-start | bytes 61448 | tf_op jit(solution)/shard_map/ppermute | solution.py:26
  3.6 33.9 %collective-permute-start.3 = (f32[5,1,64,256]{3,2,1,0:T(8,128)S(1)}, f32[5,1,64,256]{3,2,1,0:T(8,128)S(1)}, u32[]{:S(2)}, u32[]{:S(2)}) collective-permute-start(f32[5,1,64,256]{3,2,1,0:T(8,128)S(1)} %get-tuple-element.43), channel_id=1, source_target_pairs={{0,2},{2,4},{4,6},{6,8},{8,10},{10,12},{12,14},{1,3},{3,5},{5,7},{... | collective-permute-start | bytes 983048 | tf_op jit(solution)/shard_map/ppermute | solution.py:46
  8.5 29.0 %collective-permute-start.5 = (f32[5,1,64,256]{3,2,1,0:T(8,128)S(1)}, f32[5,1,64,256]{3,2,1,0:T(8,128)S(1)}, u32[]{:S(2)}, u32[]{:S(2)}) collective-permute-start(f32[5,1,64,256]{3,2,1,0:T(8,128)S(1)} %get-tuple-element.44), channel_id=1, source_target_pairs={{2,0},{4,2},{6,4},{8,6},{10,8},{12,10},{14,12},{3,1},{5,3},{7,5},{... | collective-permute-start | bytes 983048 | tf_op jit(solution)/shard_map/ppermute | solution.py:47
  9.8 10.0 %collective-permute-start.6 = (f32[2,32,256]{2,1,0:T(8,128)S(1)}, f32[2,32,256]{2,1,0:T(8,128)S(1)}, u32[]{:S(2)}, u32[]{:S(2)}) collective-permute-start(f32[2,32,256]{2,1,0:T(8,128)S(1)} %copy-done.9), channel_id=1, source_target_pairs={{0,1},{1,0},{2,3},{3,2},{4,5},{5,4},{6,7},{7,6},{8,9},{9,8},{10,11... | collective-permute-start | bytes 196616 | tf_op jit(solution)/shard_map/ppermute | solution.py:26
  12.5 7.3 %copy-start.5 = (f32[2,4,2,256]{3,2,1,0:T(2,128)}, f32[2,4,2,256]{3,2,1,0:T(2,128)S(1)}, u32[]{:S(2)}) copy-start(f32[2,4,2,256]{3,2,1,0:T(2,128)S(1)} %get-tuple-element.66) | copy-start | bytes 49156
  12.7 13.4 %collective-permute-start.1 = (f32[2,2,68,256]{3,2,1,0:T(8,128)S(1)}, f32[2,2,68,256]{3,2,1,0:T(8,128)S(1)}, u32[]{:S(2)}, u32[]{:S(2)}) collective-permute-start(f32[2,2,68,256]{3,2,1,0:T(8,128)S(1)} %get-tuple-element.52), channel_id=1, source_target_pairs={{2,0},{4,2},{6,4},{8,6},{10,8},{12,10},{14,12},{3,1},{5,3},{7,5},{... | collective-permute-start | bytes 835592 | tf_op jit(solution)/shard_map/ppermute | solution.py:55
  14.0 21.3 %collective-permute-start.2 = (f32[2,2,68,256]{3,2,1,0:T(8,128)S(1)}, f32[2,2,68,256]{3,2,1,0:T(8,128)S(1)}, u32[]{:S(2)}, u32[]{:S(2)}) collective-permute-start(f32[2,2,68,256]{3,2,1,0:T(8,128)S(1)} %get-tuple-element.51), channel_id=1, source_target_pairs={{0,2},{2,4},{4,6},{6,8},{8,10},{10,12},{12,14},{1,3},{3,5},{5,7},{... | collective-permute-start | bytes 835592 | tf_op jit(solution)/shard_map/ppermute | solution.py:54
  36.1 0.7 copy-start.6
  36.9 1.0 copy-start.1
  36.9 1.2 copy-start.2
  36.9 1.3 copy-start.4
  36.9 1.3 copy-start.7
  36.9 1.3 copy-start.8
  38.1 0.7 copy-start.13
  39.2 0.7 copy-start.10
  40.1 0.6 copy-start.11
  40.9 0.6 copy-start.12
  41.7 1.2 collective-permute-start.7
  43.1 11.7 %collective-permute-start.8 = (f32[2,2,68,256]{3,2,1,0:T(8,128)S(1)}, f32[2,2,68,256]{3,2,1,0:T(8,128)S(1)}, u32[]{:S(2)}, u32[]{:S(2)}) collective-permute-start(f32[2,2,68,256]{3,2,1,0:T(8,128)S(1)} %get-tuple-element.50), channel_id=1, source_target_pairs={{2,0},{4,2},{6,4},{8,6},{10,8},{12,10},{14,12},{3,1},{5,3},{7,5},{... | collective-permute-start | bytes 835592 | tf_op jit(solution)/shard_map/ppermute | solution.py:55
  44.4 16.9 %collective-permute-start.9 = (f32[2,2,68,256]{3,2,1,0:T(8,128)S(1)}, f32[2,2,68,256]{3,2,1,0:T(8,128)S(1)}, u32[]{:S(2)}, u32[]{:S(2)}) collective-permute-start(f32[2,2,68,256]{3,2,1,0:T(8,128)S(1)} %get-tuple-element.49), channel_id=1, source_target_pairs={{0,2},{2,4},{4,6},{6,8},{8,10},{10,12},{12,14},{1,3},{3,5},{5,7},{... | collective-permute-start | bytes 835592 | tf_op jit(solution)/shard_map/ppermute | solution.py:54
  63.6 1.2 collective-permute-start.10
  64.9 11.7 %collective-permute-start.11 = (f32[2,2,68,256]{3,2,1,0:T(8,128)S(1)}, f32[2,2,68,256]{3,2,1,0:T(8,128)S(1)}, u32[]{:S(2)}, u32[]{:S(2)}) collective-permute-start(f32[2,2,68,256]{3,2,1,0:T(8,128)S(1)} %get-tuple-element.48), channel_id=1, source_target_pairs={{2,0},{4,2},{6,4},{8,6},{10,8},{12,10},{14,12},{3,1},{5,3},{7,5},{... | collective-permute-start | bytes 835592 | tf_op jit(solution)/shard_map/ppermute | solution.py:55
  66.2 16.9 %collective-permute-start.12 = (f32[2,2,68,256]{3,2,1,0:T(8,128)S(1)}, f32[2,2,68,256]{3,2,1,0:T(8,128)S(1)}, u32[]{:S(2)}, u32[]{:S(2)}) collective-permute-start(f32[2,2,68,256]{3,2,1,0:T(8,128)S(1)} %get-tuple-element.47), channel_id=1, source_target_pairs={{0,2},{2,4},{4,6},{6,8},{8,10},{10,12},{12,14},{1,3},{3,5},{5,7},{... | collective-permute-start | bytes 835592 | tf_op jit(solution)/shard_map/ppermute | solution.py:54
  85.8 1.2 collective-permute-start.13
  87.2 11.7 %collective-permute-start.14 = (f32[2,2,68,256]{3,2,1,0:T(8,128)S(1)}, f32[2,2,68,256]{3,2,1,0:T(8,128)S(1)}, u32[]{:S(2)}, u32[]{:S(2)}) collective-permute-start(f32[2,2,68,256]{3,2,1,0:T(8,128)S(1)} %get-tuple-element.46), channel_id=1, source_target_pairs={{2,0},{4,2},{6,4},{8,6},{10,8},{12,10},{14,12},{3,1},{5,3},{7,5},{... | collective-permute-start | bytes 835592 | tf_op jit(solution)/shard_map/ppermute | solution.py:55
  88.5 16.9 %collective-permute-start.15 = (f32[2,2,68,256]{3,2,1,0:T(8,128)S(1)}, f32[2,2,68,256]{3,2,1,0:T(8,128)S(1)}, u32[]{:S(2)}, u32[]{:S(2)}) collective-permute-start(f32[2,2,68,256]{3,2,1,0:T(8,128)S(1)} %get-tuple-element.45), channel_id=1, source_target_pairs={{0,2},{2,4},{4,6},{6,8},{8,10},{10,12},{12,14},{1,3},{3,5},{5,7},{... | collective-permute-start | bytes 835592 | tf_op jit(solution)/shard_map/ppermute | solution.py:54
  108.6 0.8 copy-start.3
  110.9 5.0 %collective-permute-start.16 = (f32[65,256]{1,0:T(8,128)S(1)}, f32[65,256]{1,0:T(8,128)S(1)}, u32[]{:S(2)}, u32[]{:S(2)}) collective-permute-start(f32[65,256]{1,0:T(8,128)S(1)} %select_maximum_fusion), channel_id=1, source_target_pairs={{0,2},{2,0},{4,6},{6,4},{8,10},{10,8},{12,14},{14,12},{1,3},{3,1},... | collective-permute-start | bytes 199688 | tf_op jit(solution)/shard_map/ppermute | solution.py:20
  115.9 4.4 %collective-permute-start.17 = (f32[65,256]{1,0:T(8,128)S(1)}, f32[65,256]{1,0:T(8,128)S(1)}, u32[]{:S(2)}, u32[]{:S(2)}) collective-permute-start(f32[65,256]{1,0:T(8,128)S(1)} %fusion.126), channel_id=1, source_target_pairs={{0,4},{2,6},{4,0},{6,2},{8,12},{10,14},{12,8},{14,10},{1,5},{3,7},... | collective-permute-start | bytes 199688 | tf_op jit(solution)/shard_map/ppermute | solution.py:20
  120.3 5.3 %collective-permute-start.18 = (f32[65,256]{1,0:T(8,128)S(1)}, f32[65,256]{1,0:T(8,128)S(1)}, u32[]{:S(2)}, u32[]{:S(2)}) collective-permute-start(f32[65,256]{1,0:T(8,128)S(1)} %add.529), channel_id=1, source_target_pairs={{0,8},{2,10},{4,12},{6,14},{8,0},{10,2},{12,4},{14,6},{1,9},{3,11}... | collective-permute-start | bytes 199688 | tf_op jit(solution)/shard_map/ppermute | solution.py:20
  126.2 1.4 %collective-permute-start.19 = (f32[]{:T(128)}, f32[]{:T(128)}, u32[]{:S(2)}, u32[]{:S(2)}) collective-permute-start(f32[]{:T(128)} %bitcast.41), channel_id=1, source_target_pairs={{0,1},{1,0},{2,3},{3,2},{4,5},{5,4},{6,7},{7,6},{8,9},{9,8},{10,11... | collective-permute-start | bytes 20 | tf_op jit(solution)/shard_map/ppermute | solution.py:20

commit v4 on v3

--- a/solution.py
+++ b/solution.py
@@ -22,8 +22,13 @@
     return value
 
 
+def send(value, axis, pairs):
+    flat = value.reshape(-1, value.shape[-1])
+    return lax.ppermute(flat, axis, pairs).reshape(value.shape)
+
+
 def swap_y(value):
-    return lax.ppermute(value, "gy", [(0, 1), (1, 0)])
+    return send(value, "gy", [(0, 1), (1, 0)])
 
 
 def extend(block, w):
@@ -38,21 +43,21 @@
         below = jnp.where(iy == 1, other, zero)
         above = jnp.where(iy == 0, other, zero)
     else:
-        below = lax.ppermute(block[:, :, Y - w:], "gy", [(j, j + 1) for j in range(ny - 1)])
-        above = lax.ppermute(block[:, :, :w], "gy", [(j + 1, j) for j in range(ny - 1)])
+        below = send(block[:, :, Y - w:], "gy", [(j, j + 1) for j in range(ny - 1)])
+        above = send(block[:, :, :w], "gy", [(j + 1, j) for j in range(ny - 1)])
     up = [(i, i + 1) for i in range(nx - 1)]
     down = [(i + 1, i) for i in range(nx - 1)]
     if w == 1:
-        x_low = lax.ppermute(block[:, X - w:], "gx", up)
-        x_high = lax.ppermute(block[:, :w], "gx", down)
+        x_low = send(block[:, X - w:], "gx", up)
+        x_high = send(block[:, :w], "gx", down)
         corner = jnp.zeros(x_low.shape[:2] + (w,) + x_low.shape[3:], block.dtype)
         x_low = jnp.concatenate([corner, x_low, corner], axis=2)
         x_high = jnp.concatenate([corner, x_high, corner], axis=2)
         tall = jnp.concatenate([below, block, above], axis=2)
     else:
         tall = jnp.concatenate([below, block, above], axis=2)
-        x_low = lax.ppermute(tall[:, X - w:], "gx", up)
-        x_high = lax.ppermute(tall[:, :w], "gx", down)
+        x_low = send(tall[:, X - w:], "gx", up)
+        x_high = send(tall[:, :w], "gx", down)
     return jnp.concatenate([x_low, tall, x_high], axis=1)
 
 

time: 131 us -> 165 us (1.26)
  local copies, waits for them, and re-layouts: 7.97 us -> 44.4 us
  waiting for transfers between devices: 62.7 us -> 48.5 us
  other arithmetic: 15.4 us -> 20.2 us
  starting transfers between devices: 39.6 us -> 44.4 us
    reshape x0 -> x21, local copies, waits for them, and re-layouts: none -> 16 us  [the longest x8 8.34 us: send(): return lax.ppermute(flat, axis, pairs).reshape(value.shape)]
    unnamed x28 -> x178, local copies, waits for them, and re-layouts: 3.02 us -> 18.2 us
    ppermute x16, waiting for transfers between devices: 53.4 us -> 40 us  [send(): return lax.ppermute(flat, axis, pairs).reshape(value.shape)]
    concatenate x5, other arithmetic: 1.58 us -> 5.51 us  [extend(): return jnp.concatenate([x_low, tall, x_high], axis=1)]
    ppermute x4, starting transfers between devices: 6.83 us -> 9.82 us  [axis_sum(): value = value + lax.ppermute(value, axis, pairs)]
    slice x5, local copies, waits for them, and re-layouts: 0.21 us -> 2.69 us  [the longest x4 1.79 us: extend(): x_low = send(tall[:, X - w:], 'gx', up)]
    concatenate x4, other arithmetic: 0.24 us -> 2.33 us  [extend(): tall = jnp.concatenate([below, block, above], axis=2)]
    ppermute x16, starting transfers between devices: 32.8 us -> 34.5 us  [send(): return lax.ppermute(flat, axis, pairs).reshape(value.shape)]
  transfers between devices with their start and end apart: 20 -> 20, of which waited for: 15 -> 15; matrix products, arithmetic and copies ran while one was open for 6% -> 11% of each run, Pallas kernels for 0% -> 0%
where the time goes in v4:
time: 165 us; the launch traced here: 163 us
  waiting for transfers between devices  48.5 us (29%)
  local copies, waits for them, and re-layouts  44.4 us (27%)
  starting transfers between devices  44.4 us (27%)
  other arithmetic  20.2 us (12%)
  between operations  5.63 us (3%)
    ppermute x16, waiting for transfers between devices, send(): return lax.ppermute(flat, axis, pairs).reshape(value.shape)  40 us
    ppermute x16, starting transfers between devices, send(): return lax.ppermute(flat, axis, pairs).reshape(value.shape)  34.5 us
    unnamed x178, local copies, waits for them, and re-layouts  18.2 us
    ppermute x4, starting transfers between devices, axis_sum(): value = value + lax.ppermute(value, axis, pairs)  9.82 us
    ppermute x4, waiting for transfers between devices, axis_sum(): value = value + lax.ppermute(value, axis, pairs)  8.56 us
    reshape x8, local copies, waits for them, and re-layouts, send(): return lax.ppermute(flat, axis, pairs).reshape(value.shape)  8.34 us
    reshape x13, local copies, waits for them, and re-layouts, send(): flat = value.reshape(-1, value.shape[-1])  7.69 us
    concatenate x5, other arithmetic, extend(): return jnp.concatenate([x_low, tall, x_high], axis=1)  5.51 us
  transfers between devices with their start and end apart: 20, of which 15 were waited for; matrix products, arithmetic and copies ran while one was open for 11% of the time, Pallas kernels for 0%

profile of v4, /device:TPU:0, one launch (start us, length us, event | category | flops | bytes accessed | tf_op | source)
XLA Modules:
  0.0 163.1 jit_solution(17504406319476680202)
XLA Ops:
  2.1 1.4 pad_maximum_fusion
  4.6 5.6 %collective-permute-start.3 = (f32[320,256]{1,0:T(8,128)}, f32[320,256]{1,0:T(8,128)}, u32[]{:S(2)}, u32[]{:S(2)}) collective-permute-start(f32[320,256]{1,0:T(8,128)} %bitcast.1), channel_id=1, source_target_pairs={{0,2},{2,4},{4,6},{6,8},{8,10},{10,12},{12,14},{1,3},{3,5},{5,7},{... | collective-permute-start | bytes 983048 | tf_op jit(solution)/shard_map/ppermute | solution.py:27
  10.2 1.3 collective-permute-start.5
  14.4 1.3 collective-permute-start.1
  15.8 5.2 %collective-permute-start.2 = (f32[272,256]{1,0:T(8,128)S(1)}, f32[272,256]{1,0:T(8,128)S(1)}, u32[]{:S(2)}, u32[]{:S(2)}) collective-permute-start(f32[272,256]{1,0:T(8,128)S(1)} %reshape.307), channel_id=1, source_target_pairs={{0,2},{2,4},{4,6},{6,8},{8,10},{10,12},{12,14},{1,3},{3,5},{5,7},{... | collective-permute-start | bytes 835592 | tf_op jit(solution)/shard_map/ppermute | solution.py:27
  23.2 4.4 %collective-permute-done.1 = f32[272,256]{1,0:T(8,128)S(1)} collective-permute-done((f32[272,256]{1,0:T(8,128)S(1)}, f32[272,256]{1,0:T(8,128)S(1)}, u32[]{:S(2)}, u32[]{:S(2)}) %collective-permute-start.1) | collective-permute-done | bytes 278560 | tf_op jit(solution)/shard_map/ppermute | solution.py:27
  27.6 8.1 %collective-permute-done.2 = f32[272,256]{1,0:T(8,128)S(1)} collective-permute-done((f32[272,256]{1,0:T(8,128)S(1)}, f32[272,256]{1,0:T(8,128)S(1)}, u32[]{:S(2)}, u32[]{:S(2)}) %collective-permute-start.2) | collective-permute-done | bytes 278560 | tf_op jit(solution)/shard_map/ppermute | solution.py:27
  37.9 1.4 maximum_maximum_fusion
  42.6 1.1 copy-done.1
  44.8 1.2 collective-permute-done.7
  46.0 1.1 pad_maximum_fusion.34
  48.0 1.7 %reshape.318 = f32[272,256]{1,0:T(8,128)} reshape(f32[2,2,68,256]{3,2,1,0:T(8,128)} %get-tuple-element.50) | data formatting | bytes 557056 | tf_op jit(solution)/shard_map/reshape | solution.py:26
  49.7 1.3 collective-permute-start.8
  50.9 1.7 %reshape.320 = f32[272,256]{1,0:T(8,128)} reshape(f32[2,2,68,256]{3,2,1,0:T(8,128)} %get-tuple-element.49) | data formatting | bytes 557056 | tf_op jit(solution)/shard_map/reshape | solution.py:26
  52.6 5.7 %collective-permute-start.9 = (f32[272,256]{1,0:T(8,128)}, f32[272,256]{1,0:T(8,128)}, u32[]{:S(2)}, u32[]{:S(2)}) collective-permute-start(f32[272,256]{1,0:T(8,128)} %reshape.320), channel_id=1, source_target_pairs={{0,2},{2,4},{4,6},{6,8},{8,10},{10,12},{12,14},{1,3},{3,5},{5,7},{... | collective-permute-start | bytes 835592 | tf_op jit(solution)/shard_map/ppermute | solution.py:27
  58.4 3.0 %collective-permute-done.8 = f32[272,256]{1,0:T(8,128)} collective-permute-done((f32[272,256]{1,0:T(8,128)}, f32[272,256]{1,0:T(8,128)}, u32[]{:S(2)}, u32[]{:S(2)}) %collective-permute-start.8) | collective-permute-done | bytes 278560 | tf_op jit(solution)/shard_map/ppermute | solution.py:27
  61.3 1.7 %reshape.319 = f32[2,2,68,256]{3,2,1,0:T(8,128)} reshape(f32[272,256]{1,0:T(8,128)} %collective-permute-done.8) | data formatting | bytes 557056 | tf_op jit(solution)/shard_map/reshape | solution.py:27
  63.0 4.4 %collective-permute-done.9 = f32[272,256]{1,0:T(8,128)} collective-permute-done((f32[272,256]{1,0:T(8,128)}, f32[272,256]{1,0:T(8,128)}, u32[]{:S(2)}, u32[]{:S(2)}) %collective-permute-start.9) | collective-permute-done | bytes 278560 | tf_op jit(solution)/shard_map/ppermute | solution.py:27
  67.5 1.7 %reshape.321 = f32[2,2,68,256]{3,2,1,0:T(8,128)} reshape(f32[272,256]{1,0:T(8,128)} %collective-permute-done.9) | data formatting | bytes 557056 | tf_op jit(solution)/shard_map/reshape | solution.py:27
  69.2 1.3 pad_maximum_fusion.2
  70.6 0.9 copy-done.29
  76.6 1.1 collective-permute-done.10
  77.9 1.3 collective-permute-start.11
  80.0 5.0 %collective-permute-start.12 = (f32[272,256]{1,0:T(8,128)}, f32[272,256]{1,0:T(8,128)S(1)}, u32[]{:S(2)}, u32[]{:S(2)}) collective-permute-start(f32[272,256]{1,0:T(8,128)} %reshape.325), channel_id=1, source_target_pairs={{0,2},{2,4},{4,6},{6,8},{8,10},{10,12},{12,14},{1,3},{3,5},{5,7},{... | collective-permute-start | bytes 835592 | tf_op jit(solution)/shard_map/ppermute | solution.py:27
  85.6 3.7 %collective-permute-done.11 = f32[272,256]{1,0:T(8,128)S(1)} collective-permute-done((f32[272,256]{1,0:T(8,128)S(1)}, f32[272,256]{1,0:T(8,128)S(1)}, u32[]{:S(2)}, u32[]{:S(2)}) %collective-permute-start.11) | collective-permute-done | bytes 278560 | tf_op jit(solution)/shard_map/ppermute | solution.py:27
  90.0 6.1 %collective-permute-done.12 = f32[272,256]{1,0:T(8,128)S(1)} collective-permute-done((f32[272,256]{1,0:T(8,128)}, f32[272,256]{1,0:T(8,128)S(1)}, u32[]{:S(2)}, u32[]{:S(2)}) %collective-permute-start.12) | collective-permute-done | bytes 278560 | tf_op jit(solution)/shard_map/ppermute | solution.py:27
  96.9 1.3 pad_maximum_fusion.3
  98.4 0.9 copy-done.6
  106.5 1.1 collective-permute-done.13
  107.7 1.1 pad_maximum_fusion.36
  109.6 1.7 %reshape.328 = f32[272,256]{1,0:T(8,128)} reshape(f32[2,2,68,256]{3,2,1,0:T(8,128)} %get-tuple-element.46) | data formatting | bytes 557056 | tf_op jit(solution)/shard_map/reshape | solution.py:26
  111.3 1.3 collective-permute-start.14
  112.6 1.7 %reshape.330 = f32[272,256]{1,0:T(8,128)} reshape(f32[2,2,68,256]{3,2,1,0:T(8,128)} %get-tuple-element.45) | data formatting | bytes 557056 | tf_op jit(solution)/shard_map/reshape | solution.py:26
  114.3 5.6 %collective-permute-start.15 = (f32[272,256]{1,0:T(8,128)}, f32[272,256]{1,0:T(8,128)}, u32[]{:S(2)}, u32[]{:S(2)}) collective-permute-start(f32[272,256]{1,0:T(8,128)} %reshape.330), channel_id=1, source_target_pairs={{0,2},{2,4},{4,6},{6,8},{8,10},{10,12},{12,14},{1,3},{3,5},{5,7},{... | collective-permute-start | bytes 835592 | tf_op jit(solution)/shard_map/ppermute | solution.py:27
  120.5 2.3 %collective-permute-done.14 = f32[272,256]{1,0:T(8,128)} collective-permute-done((f32[272,256]{1,0:T(8,128)}, f32[272,256]{1,0:T(8,128)}, u32[]{:S(2)}, u32[]{:S(2)}) %collective-permute-start.14) | collective-permute-done | bytes 278560 | tf_op jit(solution)/shard_map/ppermute | solution.py:27
  122.9 1.7 %reshape.329 = f32[2,2,68,256]{3,2,1,0:T(8,128)} reshape(f32[272,256]{1,0:T(8,128)} %collective-permute-done.14) | data formatting | bytes 557056 | tf_op jit(solution)/shard_map/reshape | solution.py:27
  124.6 4.4 %collective-permute-done.15 = f32[272,256]{1,0:T(8,128)} collective-permute-done((f32[272,256]{1,0:T(8,128)}, f32[272,256]{1,0:T(8,128)}, u32[]{:S(2)}, u32[]{:S(2)}) %collective-permute-start.15) | collective-permute-done | bytes 278560 | tf_op jit(solution)/shard_map/ppermute | solution.py:27
  129.0 1.7 %reshape.331 = f32[2,2,68,256]{3,2,1,0:T(8,128)} reshape(f32[272,256]{1,0:T(8,128)} %collective-permute-done.15) | data formatting | bytes 557056 | tf_op jit(solution)/shard_map/reshape | solution.py:27
  130.7 1.3 pad_maximum_fusion.4
  132.2 0.9 copy-done.27
  137.8 1.1 multiply_reduce_fusion
  141.2 2.5 %collective-permute-start.16 = (f32[65,256]{1,0:T(8,128)S(1)}, f32[65,256]{1,0:T(8,128)S(1)}, u32[]{:S(2)}, u32[]{:S(2)}) collective-permute-start(f32[65,256]{1,0:T(8,128)S(1)} %select_maximum_fusion), channel_id=1, source_target_pairs={{0,2},{2,0},{4,6},{6,4},{8,10},{10,8},{12,14},{14,12},{1,3},{3,1},... | collective-permute-start | bytes 199688 | tf_op jit(solution)/shard_map/ppermute | solution.py:20
  143.7 2.5 %collective-permute-done.16 = f32[65,256]{1,0:T(8,128)S(1)} collective-permute-done((f32[65,256]{1,0:T(8,128)S(1)}, f32[65,256]{1,0:T(8,128)S(1)}, u32[]{:S(2)}, u32[]{:S(2)}) %collective-permute-start.16) | collective-permute-done | bytes 66592 | tf_op jit(solution)/shard_map/ppermute | solution.py:20
  146.2 3.7 %collective-permute-start.17 = (f32[65,256]{1,0:T(8,128)S(1)}, f32[65,256]{1,0:T(8,128)S(1)}, u32[]{:S(2)}, u32[]{:S(2)}) collective-permute-start(f32[65,256]{1,0:T(8,128)S(1)} %fusion.126), channel_id=1, source_target_pairs={{0,4},{2,6},{4,0},{6,2},{8,12},{10,14},{12,8},{14,10},{1,5},{3,7},... | collective-permute-start | bytes 199688 | tf_op jit(solution)/shard_map/ppermute | solution.py:20
  149.9 2.3 %collective-permute-done.17 = f32[65,256]{1,0:T(8,128)S(1)} collective-permute-done((f32[65,256]{1,0:T(8,128)S(1)}, f32[65,256]{1,0:T(8,128)S(1)}, u32[]{:S(2)}, u32[]{:S(2)}) %collective-permute-start.17) | collective-permute-done | bytes 66592 | tf_op jit(solution)/shard_map/ppermute | solution.py:20
  152.3 3.5 %collective-permute-start.18 = (f32[65,256]{1,0:T(8,128)S(1)}, f32[65,256]{1,0:T(8,128)S(1)}, u32[]{:S(2)}, u32[]{:S(2)}) collective-permute-start(f32[65,256]{1,0:T(8,128)S(1)} %add.529), channel_id=1, source_target_pairs={{0,8},{2,10},{4,12},{6,14},{8,0},{10,2},{12,4},{14,6},{1,9},{3,11}... | collective-permute-start | bytes 199688 | tf_op jit(solution)/shard_map/ppermute | solution.py:20
  155.8 2.3 %collective-permute-done.18 = f32[65,256]{1,0:T(8,128)S(1)} collective-permute-done((f32[65,256]{1,0:T(8,128)S(1)}, f32[65,256]{1,0:T(8,128)S(1)}, u32[]{:S(2)}, u32[]{:S(2)}) %collective-permute-start.18) | collective-permute-done | bytes 66592 | tf_op jit(solution)/shard_map/ppermute | solution.py:20
  158.7 1.4 collective-permute-done.19
  (290 shorter events, 38.1 us)
Async XLA Ops:
  1.5 12.7 %collective-permute-start = (f32[16,256]{1,0:T(8,128)S(1)}, f32[16,256]{1,0:T(8,128)S(1)}, u32[]{:S(2)}, u32[]{:S(2)}) collective-permute-start(f32[16,256]{1,0:T(8,128)S(1)} %reshape.304), channel_id=1, source_target_pairs={{0,1},{1,0},{2,3},{3,2},{4,5},{5,4},{6,7},{7,6},{8,9},{9,8},{10,11... | collective-permute-start | bytes 49160 | tf_op jit(solution)/shard_map/ppermute | solution.py:27
  3.5 8.0 %copy-start.84 = (f32[2,32,256]{2,1,0:T(8,128)S(1)}, f32[2,32,256]{2,1,0:T(8,128)}, u32[]{:S(2)}) copy-start(f32[2,32,256]{2,1,0:T(8,128)} %param.11) | copy-start | bytes 196612
  3.5 10.8 %copy-start = (f32[2,4,64,256]{3,2,1,0:T(8,128)S(1)}, f32[2,4,64,256]{3,2,1,0:T(8,128)}, u32[]{:S(2)}) copy-start(f32[2,4,64,256]{3,2,1,0:T(8,128)} %param.7) | copy-start | bytes 1572868
  3.6 12.2 %collective-permute-start.4 = (f32[20,256]{1,0:T(8,128)S(1)}, f32[20,256]{1,0:T(8,128)S(1)}, u32[]{:S(2)}, u32[]{:S(2)}) collective-permute-start(f32[20,256]{1,0:T(8,128)S(1)} %reshape.311), channel_id=1, source_target_pairs={{0,1},{1,0},{2,3},{3,2},{4,5},{5,4},{6,7},{7,6},{8,9},{9,8},{10,11... | collective-permute-start | bytes 61448 | tf_op jit(solution)/shard_map/ppermute | solution.py:27
  4.6 32.7 %collective-permute-start.3 = (f32[320,256]{1,0:T(8,128)}, f32[320,256]{1,0:T(8,128)}, u32[]{:S(2)}, u32[]{:S(2)}) collective-permute-start(f32[320,256]{1,0:T(8,128)} %bitcast.1), channel_id=1, source_target_pairs={{0,2},{2,4},{4,6},{6,8},{8,10},{10,12},{12,14},{1,3},{3,5},{5,7},{... | collective-permute-start | bytes 983048 | tf_op jit(solution)/shard_map/ppermute | solution.py:27
  10.2 27.1 %collective-permute-start.5 = (f32[320,256]{1,0:T(8,128)}, f32[320,256]{1,0:T(8,128)}, u32[]{:S(2)}, u32[]{:S(2)}) collective-permute-start(f32[320,256]{1,0:T(8,128)} %bitcast.3), channel_id=1, source_target_pairs={{2,0},{4,2},{6,4},{8,6},{10,8},{12,10},{14,12},{3,1},{5,3},{7,5},{... | collective-permute-start | bytes 983048 | tf_op jit(solution)/shard_map/ppermute | solution.py:27
  11.4 10.8 %collective-permute-start.6 = (f32[64,256]{1,0:T(8,128)S(1)}, f32[64,256]{1,0:T(8,128)S(1)}, u32[]{:S(2)}, u32[]{:S(2)}) collective-permute-start(f32[64,256]{1,0:T(8,128)S(1)} %bitcast.190), channel_id=1, source_target_pairs={{0,1},{1,0},{2,3},{3,2},{4,5},{5,4},{6,7},{7,6},{8,9},{9,8},{10,11... | collective-permute-start | bytes 196616 | tf_op jit(solution)/shard_map/ppermute | solution.py:27
  14.2 21.5 %copy-start.78 = (f32[2,4,2,256]{3,2,1,0:T(2,128)}, f32[2,4,2,256]{3,2,1,0:T(2,128)S(1)}, u32[]{:S(2)}) copy-start(f32[2,4,2,256]{3,2,1,0:T(2,128)S(1)} %select_n.144) | copy-start | bytes 49156
  14.4 13.2 %collective-permute-start.1 = (f32[272,256]{1,0:T(8,128)S(1)}, f32[272,256]{1,0:T(8,128)S(1)}, u32[]{:S(2)}, u32[]{:S(2)}) collective-permute-start(f32[272,256]{1,0:T(8,128)S(1)} %reshape.305), channel_id=1, source_target_pairs={{2,0},{4,2},{6,4},{8,6},{10,8},{12,10},{14,12},{3,1},{5,3},{7,5},{... | collective-permute-start | bytes 835592 | tf_op jit(solution)/shard_map/ppermute | solution.py:27
  15.8 20.0 %collective-permute-start.2 = (f32[272,256]{1,0:T(8,128)S(1)}, f32[272,256]{1,0:T(8,128)S(1)}, u32[]{:S(2)}, u32[]{:S(2)}) collective-permute-start(f32[272,256]{1,0:T(8,128)S(1)} %reshape.307), channel_id=1, source_target_pairs={{0,2},{2,4},{4,6},{6,8},{8,10},{10,12},{12,14},{1,3},{3,5},{5,7},{... | collective-permute-start | bytes 835592 | tf_op jit(solution)/shard_map/ppermute | solution.py:27
  39.7 2.0 %copy-start.74 = (f32[6,66,256]{2,1,0:T(8,128)}, f32[6,66,256]{2,1,0:T(8,128)S(1)}, u32[]{:S(2)}) copy-start(f32[6,66,256]{2,1,0:T(8,128)S(1)} %get-tuple-element.40) | copy-start | bytes 1216516
  39.8 2.7 %copy-start.24 = (f32[1,6,66,256]{3,2,1,0:T(8,128)}, f32[1,6,66,256]{3,2,1,0:T(8,128)S(1)}, u32[]{:S(2)}) copy-start(f32[1,6,66,256]{3,2,1,0:T(8,128)S(1)} %get-tuple-element.28) | copy-start | bytes 1216516
  39.8 2.7 %copy-start.58 = (f32[6,66,256]{2,1,0:T(8,128)}, f32[6,66,256]{2,1,0:T(8,128)S(1)}, u32[]{:S(2)}) copy-start(f32[6,66,256]{2,1,0:T(8,128)S(1)} %get-tuple-element.42) | copy-start | bytes 1216516
  44.7 1.2 collective-permute-start.7
  49.7 11.7 %collective-permute-start.8 = (f32[272,256]{1,0:T(8,128)}, f32[272,256]{1,0:T(8,128)}, u32[]{:S(2)}, u32[]{:S(2)}) collective-permute-start(f32[272,256]{1,0:T(8,128)} %reshape.318), channel_id=1, source_target_pairs={{2,0},{4,2},{6,4},{8,6},{10,8},{12,10},{14,12},{3,1},{5,3},{7,5},{... | collective-permute-start | bytes 835592 | tf_op jit(solution)/shard_map/ppermute | solution.py:27
  52.6 14.8 %collective-permute-start.9 = (f32[272,256]{1,0:T(8,128)}, f32[272,256]{1,0:T(8,128)}, u32[]{:S(2)}, u32[]{:S(2)}) collective-permute-start(f32[272,256]{1,0:T(8,128)} %reshape.320), channel_id=1, source_target_pairs={{0,2},{2,4},{4,6},{6,8},{8,10},{10,12},{12,14},{1,3},{3,5},{5,7},{... | collective-permute-start | bytes 835592 | tf_op jit(solution)/shard_map/ppermute | solution.py:27
  73.1 1.7 %copy-start.8 = (f32[1,6,66,256]{3,2,1,0:T(8,128)}, f32[1,6,66,256]{3,2,1,0:T(8,128)S(1)}, u32[]{:S(2)}) copy-start(f32[1,6,66,256]{3,2,1,0:T(8,128)S(1)} %get-tuple-element.31) | copy-start | bytes 1216516
  73.1 1.7 %copy-start.11 = (f32[1,6,66,256]{3,2,1,0:T(8,128)}, f32[1,6,66,256]{3,2,1,0:T(8,128)S(1)}, u32[]{:S(2)}) copy-start(f32[1,6,66,256]{3,2,1,0:T(8,128)S(1)} %get-tuple-element.32) | copy-start | bytes 1216516
  74.5 1.5 copy-start.19
  74.5 1.6 copy-start.31
  74.5 1.6 copy-start.35
  74.8 1.6 copy-start.42
  74.8 1.6 copy-start.45
  76.5 1.2 collective-permute-start.10
  77.9 11.4 %collective-permute-start.11 = (f32[272,256]{1,0:T(8,128)S(1)}, f32[272,256]{1,0:T(8,128)S(1)}, u32[]{:S(2)}, u32[]{:S(2)}) collective-permute-start(f32[272,256]{1,0:T(8,128)S(1)} %reshape.323), channel_id=1, source_target_pairs={{2,0},{4,2},{6,4},{8,6},{10,8},{12,10},{14,12},{3,1},{5,3},{7,5},{... | collective-permute-start | bytes 835592 | tf_op jit(solution)/shard_map/ppermute | solution.py:27
  80.0 16.2 %collective-permute-start.12 = (f32[272,256]{1,0:T(8,128)}, f32[272,256]{1,0:T(8,128)S(1)}, u32[]{:S(2)}, u32[]{:S(2)}) collective-permute-start(f32[272,256]{1,0:T(8,128)} %reshape.325), channel_id=1, source_target_pairs={{0,2},{2,4},{4,6},{6,8},{8,10},{10,12},{12,14},{1,3},{3,5},{5,7},{... | collective-permute-start | bytes 835592 | tf_op jit(solution)/shard_map/ppermute | solution.py:27
  100.4 2.9 %copy-start.22 = (f32[1,6,66,256]{3,2,1,0:T(8,128)}, f32[1,6,66,256]{3,2,1,0:T(8,128)S(1)}, u32[]{:S(2)}) copy-start(f32[1,6,66,256]{3,2,1,0:T(8,128)S(1)} %get-tuple-element.23) | copy-start | bytes 1216516
  101.2 2.2 %copy-start.56 = (f32[6,66,256]{2,1,0:T(8,128)}, f32[6,66,256]{2,1,0:T(8,128)S(1)}, u32[]{:S(2)}) copy-start(f32[6,66,256]{2,1,0:T(8,128)S(1)} %get-tuple-element.39) | copy-start | bytes 1216516
  103.0 1.5 copy-start.46
  103.3 2.3 %copy-start.72 = (f32[1,4,64,256]{3,2,1,0:T(8,128)}, f32[1,4,64,256]{3,2,1,0:T(8,128)S(1)}, u32[]{:S(2)}) copy-start(f32[1,4,64,256]{3,2,1,0:T(8,128)S(1)} %get-tuple-element.19) | copy-start | bytes 786436
  103.3 1.5 copy-start.3
  103.3 1.7 %copy-start.9 = (f32[1,6,66,256]{3,2,1,0:T(8,128)S(1)}, f32[1,6,66,256]{3,2,1,0:T(8,128)}, u32[]{:S(2)}) copy-start(f32[1,6,66,256]{3,2,1,0:T(8,128)} %copy-done.8) | copy-start | bytes 1216516
  103.3 1.9 %copy-start.12 = (f32[1,6,66,256]{3,2,1,0:T(8,128)S(1)}, f32[1,6,66,256]{3,2,1,0:T(8,128)}, u32[]{:S(2)}) copy-start(f32[1,6,66,256]{3,2,1,0:T(8,128)} %copy-done.11) | copy-start | bytes 1216516
  103.3 1.9 %copy-start.32 = (f32[1,4,64,256]{3,2,1,0:T(8,128)S(1)}, f32[1,4,64,256]{3,2,1,0:T(8,128)}, u32[]{:S(2)}) copy-start(f32[1,4,64,256]{3,2,1,0:T(8,128)} %copy-done.30) | copy-start | bytes 786436
  103.9 1.6 copy-start.70
  106.4 1.2 collective-permute-start.13
  111.3 11.6 %collective-permute-start.14 = (f32[272,256]{1,0:T(8,128)}, f32[272,256]{1,0:T(8,128)}, u32[]{:S(2)}, u32[]{:S(2)}) collective-permute-start(f32[272,256]{1,0:T(8,128)} %reshape.328), channel_id=1, source_target_pairs={{2,0},{4,2},{6,4},{8,6},{10,8},{12,10},{14,12},{3,1},{5,3},{7,5},{... | collective-permute-start | bytes 835592 | tf_op jit(solution)/shard_map/ppermute | solution.py:27
  114.3 14.7 %collective-permute-start.15 = (f32[272,256]{1,0:T(8,128)}, f32[272,256]{1,0:T(8,128)}, u32[]{:S(2)}, u32[]{:S(2)}) collective-permute-start(f32[272,256]{1,0:T(8,128)} %reshape.330), channel_id=1, source_target_pairs={{0,2},{2,4},{4,6},{6,8},{8,10},{10,12},{12,14},{1,3},{3,5},{5,7},{... | collective-permute-start | bytes 835592 | tf_op jit(solution)/shard_map/ppermute | solution.py:27
  135.0 1.5 copy-start.51
  135.0 1.6 copy-start.53
  135.0 1.7 %copy-start.71 = (f32[1,4,64,256]{3,2,1,0:T(8,128)S(1)}, f32[1,4,64,256]{3,2,1,0:T(8,128)}, u32[]{:S(2)}) copy-start(f32[1,4,64,256]{3,2,1,0:T(8,128)} %copy-done.70) | copy-start | bytes 786436
  135.0 1.8 %copy-start.73 = (f32[1,4,64,256]{3,2,1,0:T(8,128)S(1)}, f32[1,4,64,256]{3,2,1,0:T(8,128)}, u32[]{:S(2)}) copy-start(f32[1,4,64,256]{3,2,1,0:T(8,128)} %copy-done.72) | copy-start | bytes 786436
  136.0 1.6 copy-start.17
  136.1 1.7 %copy-start.21 = (f32[1,6,66,256]{3,2,1,0:T(8,128)S(1)}, f32[1,6,66,256]{3,2,1,0:T(8,128)}, u32[]{:S(2)}) copy-start(f32[1,6,66,256]{3,2,1,0:T(8,128)} %copy-done.18) | copy-start | bytes 1216516
  141.2 5.0 %collective-permute-start.16 = (f32[65,256]{1,0:T(8,128)S(1)}, f32[65,256]{1,0:T(8,128)S(1)}, u32[]{:S(2)}, u32[]{:S(2)}) collective-permute-start(f32[65,256]{1,0:T(8,128)S(1)} %select_maximum_fusion), channel_id=1, source_target_pairs={{0,2},{2,0},{4,6},{6,4},{8,10},{10,8},{12,14},{14,12},{1,3},{3,1},... | collective-permute-start | bytes 199688 | tf_op jit(solution)/shard_map/ppermute | solution.py:20
  146.2 6.1 %collective-permute-start.17 = (f32[65,256]{1,0:T(8,128)S(1)}, f32[65,256]{1,0:T(8,128)S(1)}, u32[]{:S(2)}, u32[]{:S(2)}) collective-permute-start(f32[65,256]{1,0:T(8,128)S(1)} %fusion.126), channel_id=1, source_target_pairs={{0,4},{2,6},{4,0},{6,2},{8,12},{10,14},{12,8},{14,10},{1,5},{3,7},... | collective-permute-start | bytes 199688 | tf_op jit(solution)/shard_map/ppermute | solution.py:20
  152.3 5.9 %collective-permute-start.18 = (f32[65,256]{1,0:T(8,128)S(1)}, f32[65,256]{1,0:T(8,128)S(1)}, u32[]{:S(2)}, u32[]{:S(2)}) collective-permute-start(f32[65,256]{1,0:T(8,128)S(1)} %add.529), channel_id=1, source_target_pairs={{0,8},{2,10},{4,12},{6,14},{8,0},{10,2},{12,4},{14,6},{1,9},{3,11}... | collective-permute-start | bytes 199688 | tf_op jit(solution)/shard_map/ppermute | solution.py:20
  158.7 1.4 collective-permute-start.19
  (61 other events, 67.9 us)

commit v5 on v1

--- a/solution.py
+++ b/solution.py
@@ -7,17 +7,6 @@
 
 COUPLING = 1.0
 STEP_SIZE = 0.2
-
-
-def halo(block, axis, dim, width):
-    count = lax.axis_size(axis)
-    forward = [(i, i + 1) for i in range(count - 1)]
-    backward = [(target, source) for source, target in forward]
-    low = lax.ppermute(
-        lax.slice_in_dim(block, block.shape[dim] - width, None, axis=dim), axis, forward
-    )
-    high = lax.ppermute(lax.slice_in_dim(block, 0, width, axis=dim), axis, backward)
-    return low, high
 
 
 def axis_sum(value, axis):
@@ -30,6 +19,22 @@
         value = value + lax.ppermute(value, axis, pairs)
         step *= 2
     return value
+
+
+def y_extended(block):
+    ny = lax.axis_size("gy")
+    iy = lax.axis_index("gy")
+    Y = block.shape[2]
+    if ny == 2:
+        strip = lax.dynamic_slice_in_dim(block, (1 - iy) * (Y - 1), 1, axis=2)
+        other = lax.ppermute(strip, "gy", [(0, 1), (1, 0)])
+        zero = jnp.zeros_like(other)
+        below = jnp.where(iy == 1, other, zero)
+        above = jnp.where(iy == 0, other, zero)
+    else:
+        below = lax.ppermute(block[:, :, Y - 1:], "gy", [(j, j + 1) for j in range(ny - 1)])
+        above = lax.ppermute(block[:, :, :1], "gy", [(j + 1, j) for j in range(ny - 1)])
+    return jnp.concatenate([below, block, above], axis=2)
 
 
 def coefficients(psi, trap, control, profile):
@@ -52,24 +57,59 @@
     return jnp.stack([-lower, upper])
 
 
-def operator(field, coef):
-    x_low, x_high = halo(field, "gx", 1, 1)
-    y_low, y_high = halo(field, "gy", 2, 1)
+def operator(tall, x_low, x_high, coef):
+    field = tall[:, :, 1:-1]
     x_padded = jnp.concatenate([x_low, field, x_high], axis=1)
-    y_padded = jnp.concatenate([y_low, field, y_high], axis=2)
     z_padded = jnp.pad(field, ((0, 0), (0, 0), (0, 0), (1, 1)))
     total = x_padded[:, 2:] + x_padded[:, :-2]
-    total = total + y_padded[:, :, 2:] + y_padded[:, :, :-2]
+    total = total + tall[:, :, 2:] + tall[:, :, :-2]
     total = total + z_padded[:, :, :, 2:] + z_padded[:, :, :, :-2]
     lapl = total - 6.0 * field
     return apply_coef(lapl, field, coef)
 
 
+def cut(coef, lo, hi):
+    return tuple(c[lo:hi] for c in coef)
+
+
+def across(plane):
+    return jnp.stack([0.5 * plane[1], -0.5 * plane[0]])
+
+
+def stage_pair(stage, base, base_low, base_high, coef, weight):
+    nx = lax.axis_size("gx")
+    ix = lax.axis_index("gx")
+    X = stage.shape[1]
+    up = [(i, i + 1) for i in range(nx - 1)]
+    down = [(i + 1, i) for i in range(nx - 1)]
+    tall = y_extended(stage)
+    zero_plane = jnp.zeros_like(stage[:, :1])
+    part_top = operator(tall[:, X - 1:], stage[:, X - 2:X - 1], zero_plane, cut(coef, X - 1, X))
+    part_bottom = operator(tall[:, :1], zero_plane, stage[:, 1:2], cut(coef, 0, 1))
+    from_low = lax.ppermute(jnp.concatenate([stage[:, X - 1:], part_top]), "gx", up)
+    from_high = lax.ppermute(jnp.concatenate([stage[:, :1], part_bottom]), "gx", down)
+    stage_low, part_low = from_low[:2], from_low[2:]
+    stage_high, part_high = from_high[:2], from_high[2:]
+    if base_low is None:
+        base_low, base_high = stage_low, stage_high
+    section = operator(tall, stage_low, stage_high, coef)
+    section_low = part_low + across(stage[:, :1])
+    section_high = part_high + across(stage[:, X - 1:])
+    nxt = base + weight * section
+    nxt_low = jnp.where(ix > 0, base_low + weight * section_low, 0.0)
+    nxt_high = jnp.where(ix < nx - 1, base_high + weight * section_high, 0.0)
+    section_next = operator(y_extended(nxt), nxt_low, nxt_high, coef)
+    return section, section_next, base_low, base_high
+
+
 def rk_step(field, coef):
-    section_one = operator(field, coef)
-    section_two = operator(field + 0.5 * STEP_SIZE * section_one, coef)
-    section_three = operator(field + 0.5 * STEP_SIZE * section_two, coef)
-    section_four = operator(field + STEP_SIZE * section_three, coef)
+    section_one, section_two, low, high = stage_pair(
+        field, field, None, None, coef, 0.5 * STEP_SIZE
+    )
+    stage_three = field + 0.5 * STEP_SIZE * section_two
+    section_three, section_four, _, _ = stage_pair(
+        stage_three, field, low, high, coef, STEP_SIZE
+    )
     return field + STEP_SIZE / 6.0 * (
         section_one + 2.0 * section_two + 2.0 * section_three + section_four
     )
@@ -93,14 +133,15 @@
     coef_late = coefficients(psi_late, trap, controls[1], profile)
     coef_early = coefficients(psi_early, trap, controls[0], profile)
     chi_late = rk_step(chi_final, coef_late)
-    rows_late = axis_sum(row_terms(chi_late, psi_late, profile), "gx")
     chi_start = rk_step(chi_late, coef_early)
+    rows_late = row_terms(chi_late, psi_late, profile)
     rows_early = row_terms(chi_start, psi_early, profile)
     local_sq = jnp.sum(chi_start * chi_start)
     extra = jnp.zeros((1, rows_early.shape[1]), jnp.float32).at[0, 0].set(local_sq)
-    packed = axis_sum(jnp.concatenate([rows_early, extra], axis=0), "gx")
+    packed = axis_sum(jnp.concatenate([rows_early, rows_late, extra], axis=0), "gx")
     squares = axis_sum(packed[-1, 0], "gy")
-    rows_sum = jnp.stack([packed[:-1], rows_late])
+    half = rows_early.shape[0]
+    rows_sum = jnp.stack([packed[:half], packed[half:2 * half]])
     power = squares / float(total_x * total_y * depth)
     grad_rows = rows_sum / jnp.sqrt(float(total_x) * (power + 1e-06))
     return (chi_start, grad_rows, jnp.reshape(power, (1,)))

time: 135 us -> 111 us (0.82)
  starting transfers between devices: 98.1 us -> 33.1 us
  waiting for transfers between devices: 16 us -> 57.7 us
  other arithmetic: 9.53 us -> 11.4 us
  local copies, waits for them, and re-layouts: 4.77 us -> 3.16 us
    ppermute x32 -> x16, starting transfers between devices: 89.7 us -> 26.2 us  [the longest x4 19.5 us: stage_pair(): lax.ppermute(jnp.concatenate([stage[:, X - 1:], part_top]), 'gx', up)]
    ppermute x32 -> x16, waiting for transfers between devices: 4.47 us -> 48.4 us  [the longest x4 27.3 us: stage_pair(): lax.ppermute(jnp.concatenate([stage[:, X - 1:], part_top]), 'gx', up)]
    ppermute x7 -> x4, waiting for transfers between devices: 11.6 us -> 9.31 us  [axis_sum(): value = value + lax.ppermute(value, axis, pairs)]
    slice x16 -> x4, local copies, waits for them, and re-layouts: 2 us -> 0.07 us  [stage_pair(): stage[:, :1]]
    ppermute x7 -> x4, starting transfers between devices: 8.35 us -> 6.83 us  [axis_sum(): value = value + lax.ppermute(value, axis, pairs)]
    sub x8 -> x12, other arithmetic: 3.8 us -> 3.63 us  [operator(): lapl = total - 6.0 * field]
  transfers between devices with their start and end apart: 39 -> 20, of which waited for: 12 -> 18; matrix products, arithmetic and copies ran while one was open for 1% -> 3% of each run, Pallas kernels for 0% -> 0%
where the time goes in v5:
time: 111 us; the launch traced here: 110 us
  waiting for transfers between devices  57.7 us (52%)
  starting transfers between devices  33.1 us (30%)
  other arithmetic  11.4 us (10%)
  between operations  5.07 us (5%)
  local copies, waits for them, and re-layouts  3.16 us (3%)
    ppermute x4, waiting for transfers between devices, stage_pair(): lax.ppermute(jnp.concatenate([stage[:, X - 1:], part_top]), 'gx', up)  27.3 us
    ppermute x4, starting transfers between devices, stage_pair(): lax.ppermute(jnp.concatenate([stage[:, X - 1:], part_top]), 'gx', up)  19.5 us
    ppermute x4, waiting for transfers between devices, stage_pair(): lax.ppermute(jnp.concatenate([stage[:, :1], part_bottom]), 'gx', down)  14.2 us
    ppermute x4, waiting for transfers between devices, axis_sum(): value = value + lax.ppermute(value, axis, pairs)  9.31 us
    ppermute x8, waiting for transfers between devices, y_extended(): other = lax.ppermute(strip, 'gy', [(0, 1), (1, 0)])  6.84 us
    ppermute x4, starting transfers between devices, axis_sum(): value = value + lax.ppermute(value, axis, pairs)  6.83 us
    ppermute x4, starting transfers between devices, stage_pair(): lax.ppermute(jnp.concatenate([stage[:, :1], part_bottom]), 'gx', down)  5.17 us
    sub x12, other arithmetic, operator(): lapl = total - 6.0 * field  3.63 us
  transfers between devices with their start and end apart: 20, of which 18 were waited for; matrix products, arithmetic and copies ran while one was open for 3% of the time, Pallas kernels for 0%

profile of v5, /device:TPU:0, one launch (start us, length us, event | category | flops | bytes accessed | tf_op | source)
XLA Modules:
  0.0 110.4 jit_solution(4804152437812111379)
XLA Ops:
  0.6 0.9 constant_dynamic-slice_fusion.7
  1.6 0.6 collective-permute-start
  2.2 0.8 slice_bitcast_fusion.20
  3.1 1.3 %multiply_add_fusion.6 = (f32[4,64,256]{2,1,0:T(8,128)S(1)}, f32[4,64,256]{2,1,0:T(8,128)S(1)}, f32[4,64,256]{2,1,0:T(8,128)S(1)}, f32[4,64,256]{2,1,0:T(8,128)S(1)}) fusion(f32[4,64,256]{2,1,0:T(8,128)} %param.10, f32[2,4,64,256]{3,2,1,0:T(8,128)} %param.8, f32[64,256]{1,0:T(8,128)S(1)} %mul.851, f32[4]{0:T(128)S(1)} %multiply_add_fusion.7, ...), kind=kLoop, calls=%fused_computation.256 | loop fusion | flops 1114112 | bytes 2490384 | tf_op jit(solution)/shard_map/add | solution.py:45
  4.9 1.3 %collective-permute-start.1 = (f32[4,1,64,256]{3,2,1,0:T(8,128)S(1)}, f32[4,1,64,256]{3,2,1,0:T(8,128)S(1)}, u32[]{:S(2)}, u32[]{:S(2)}) collective-permute-start(f32[4,1,64,256]{3,2,1,0:T(8,128)S(1)} %pad_maximum_fusion.38), channel_id=1, source_target_pairs={{2,0},{4,2},{6,4},{8,6},{10,8},{12,10},{14,12},{3,1},{5,3},{7,5},{... | collective-permute-start | bytes 786440 | tf_op jit(solution)/shard_map/ppermute | solution.py:90
  6.2 5.0 %collective-permute-start.2 = (f32[4,1,64,256]{3,2,1,0:T(8,128)S(1)}, f32[4,1,64,256]{3,2,1,0:T(8,128)S(1)}, u32[]{:S(2)}, u32[]{:S(2)}) collective-permute-start(f32[4,1,64,256]{3,2,1,0:T(8,128)S(1)} %pad_maximum_fusion.39), channel_id=1, source_target_pairs={{0,2},{2,4},{4,6},{6,8},{8,10},{10,12},{12,14},{1,3},{3,5},{5,7},{... | collective-permute-start | bytes 786440 | tf_op jit(solution)/shard_map/ppermute | solution.py:89
  11.3 4.9 %collective-permute-done.1 = f32[4,1,64,256]{3,2,1,0:T(8,128)S(1)} collective-permute-done((f32[4,1,64,256]{3,2,1,0:T(8,128)S(1)}, f32[4,1,64,256]{3,2,1,0:T(8,128)S(1)}, u32[]{:S(2)}, u32[]{:S(2)}) %collective-permute-start.1) | collective-permute-done | bytes 262176 | tf_op jit(solution)/shard_map/ppermute | solution.py:90
  16.3 5.8 %collective-permute-done.2 = f32[4,1,64,256]{3,2,1,0:T(8,128)S(1)} collective-permute-done((f32[4,1,64,256]{3,2,1,0:T(8,128)S(1)}, f32[4,1,64,256]{3,2,1,0:T(8,128)S(1)}, u32[]{:S(2)}, u32[]{:S(2)}) %collective-permute-start.2) | collective-permute-done | bytes 262176 | tf_op jit(solution)/shard_map/ppermute | solution.py:89
  22.1 0.4 fusion.2
  22.8 1.1 %collective-permute-done.3 = f32[2,4,1,256]{3,2,1,0:T(1,128)S(1)} collective-permute-done((f32[2,4,1,256]{3,2,1,0:T(1,128)S(1)}, f32[2,4,1,256]{3,2,1,0:T(1,128)S(1)}, u32[]{:S(2)}, u32[]{:S(2)}) %collective-permute-start.3) | collective-permute-done | bytes 8224 | tf_op jit(solution)/shard_map/ppermute | solution.py:30
  24.0 0.3 fusion.5
  24.8 1.0 collective-permute-done.4
  26.2 1.3 %collective-permute-start.5 = (f32[4,1,64,256]{3,2,1,0:T(8,128)S(1)}, f32[4,1,64,256]{3,2,1,0:T(8,128)S(1)}, u32[]{:S(2)}, u32[]{:S(2)}) collective-permute-start(f32[4,1,64,256]{3,2,1,0:T(8,128)S(1)} %pad_maximum_fusion.40), channel_id=1, source_target_pairs={{2,0},{4,2},{6,4},{8,6},{10,8},{12,10},{14,12},{3,1},{5,3},{7,5},{... | collective-permute-start | bytes 786440 | tf_op jit(solution)/shard_map/ppermute | solution.py:90
  27.5 5.0 %collective-permute-start.6 = (f32[4,1,64,256]{3,2,1,0:T(8,128)S(1)}, f32[4,1,64,256]{3,2,1,0:T(8,128)S(1)}, u32[]{:S(2)}, u32[]{:S(2)}) collective-permute-start(f32[4,1,64,256]{3,2,1,0:T(8,128)S(1)} %pad_maximum_fusion.41), channel_id=1, source_target_pairs={{0,2},{2,4},{4,6},{6,8},{8,10},{10,12},{12,14},{1,3},{3,5},{5,7},{... | collective-permute-start | bytes 786440 | tf_op jit(solution)/shard_map/ppermute | solution.py:89
  32.5 4.6 %collective-permute-done.5 = f32[4,1,64,256]{3,2,1,0:T(8,128)S(1)} collective-permute-done((f32[4,1,64,256]{3,2,1,0:T(8,128)S(1)}, f32[4,1,64,256]{3,2,1,0:T(8,128)S(1)}, u32[]{:S(2)}, u32[]{:S(2)}) %collective-permute-start.5) | collective-permute-done | bytes 262176 | tf_op jit(solution)/shard_map/ppermute | solution.py:90
  37.2 5.7 %collective-permute-done.6 = f32[4,1,64,256]{3,2,1,0:T(8,128)S(1)} collective-permute-done((f32[4,1,64,256]{3,2,1,0:T(8,128)S(1)}, f32[4,1,64,256]{3,2,1,0:T(8,128)S(1)}, u32[]{:S(2)}, u32[]{:S(2)}) %collective-permute-start.6) | collective-permute-done | bytes 262176 | tf_op jit(solution)/shard_map/ppermute | solution.py:89
  43.0 0.3 fusion.8
  43.8 1.1 collective-permute-done.7
  44.9 0.3 fusion.11
  45.9 1.0 collective-permute-done.8
  47.2 4.4 %collective-permute-start.10 = (f32[4,1,64,256]{3,2,1,0:T(8,128)S(1)}, f32[4,1,64,256]{3,2,1,0:T(8,128)S(1)}, u32[]{:S(2)}, u32[]{:S(2)}) collective-permute-start(f32[4,1,64,256]{3,2,1,0:T(8,128)S(1)} %pad_maximum_fusion.43), channel_id=1, source_target_pairs={{0,2},{2,4},{4,6},{6,8},{8,10},{10,12},{12,14},{1,3},{3,5},{5,7},{... | collective-permute-start | bytes 786440 | tf_op jit(solution)/shard_map/ppermute | solution.py:89
  51.7 1.3 %collective-permute-start.9 = (f32[4,1,64,256]{3,2,1,0:T(8,128)S(1)}, f32[4,1,64,256]{3,2,1,0:T(8,128)S(1)}, u32[]{:S(2)}, u32[]{:S(2)}) collective-permute-start(f32[4,1,64,256]{3,2,1,0:T(8,128)S(1)} %pad_maximum_fusion.42), channel_id=1, source_target_pairs={{2,0},{4,2},{6,4},{8,6},{10,8},{12,10},{14,12},{3,1},{5,3},{7,5},{... | collective-permute-start | bytes 786440 | tf_op jit(solution)/shard_map/ppermute | solution.py:90
  53.0 10.1 %collective-permute-done.10 = f32[4,1,64,256]{3,2,1,0:T(8,128)S(1)} collective-permute-done((f32[4,1,64,256]{3,2,1,0:T(8,128)S(1)}, f32[4,1,64,256]{3,2,1,0:T(8,128)S(1)}, u32[]{:S(2)}, u32[]{:S(2)}) %collective-permute-start.10) | collective-permute-done | bytes 262176 | tf_op jit(solution)/shard_map/ppermute | solution.py:89
  63.2 0.4 fusion.14
  64.1 1.2 %collective-permute-done.11 = f32[2,4,1,256]{3,2,1,0:T(1,128)S(1)} collective-permute-done((f32[2,4,1,256]{3,2,1,0:T(1,128)S(1)}, f32[2,4,1,256]{3,2,1,0:T(1,128)S(1)}, u32[]{:S(2)}, u32[]{:S(2)}) %collective-permute-start.11) | collective-permute-done | bytes 8224 | tf_op jit(solution)/shard_map/ppermute | solution.py:30
  65.3 0.3 fusion.17
  65.8 0.3 multiply_add_fusion.1
  66.3 1.0 collective-permute-done.12
  67.7 1.3 %collective-permute-start.13 = (f32[4,1,64,256]{3,2,1,0:T(8,128)S(1)}, f32[4,1,64,256]{3,2,1,0:T(8,128)S(1)}, u32[]{:S(2)}, u32[]{:S(2)}) collective-permute-start(f32[4,1,64,256]{3,2,1,0:T(8,128)S(1)} %pad_maximum_fusion.44), channel_id=1, source_target_pairs={{2,0},{4,2},{6,4},{8,6},{10,8},{12,10},{14,12},{3,1},{5,3},{7,5},{... | collective-permute-start | bytes 786440 | tf_op jit(solution)/shard_map/ppermute | solution.py:90
  69.0 5.0 %collective-permute-start.14 = (f32[4,1,64,256]{3,2,1,0:T(8,128)S(1)}, f32[4,1,64,256]{3,2,1,0:T(8,128)S(1)}, u32[]{:S(2)}, u32[]{:S(2)}) collective-permute-start(f32[4,1,64,256]{3,2,1,0:T(8,128)S(1)} %pad_maximum_fusion.45), channel_id=1, source_target_pairs={{0,2},{2,4},{4,6},{6,8},{8,10},{10,12},{12,14},{1,3},{3,5},{5,7},{... | collective-permute-start | bytes 786440 | tf_op jit(solution)/shard_map/ppermute | solution.py:89
  74.1 4.6 %collective-permute-done.13 = f32[4,1,64,256]{3,2,1,0:T(8,128)S(1)} collective-permute-done((f32[4,1,64,256]{3,2,1,0:T(8,128)S(1)}, f32[4,1,64,256]{3,2,1,0:T(8,128)S(1)}, u32[]{:S(2)}, u32[]{:S(2)}) %collective-permute-start.13) | collective-permute-done | bytes 262176 | tf_op jit(solution)/shard_map/ppermute | solution.py:90
  78.7 5.7 %collective-permute-done.14 = f32[4,1,64,256]{3,2,1,0:T(8,128)S(1)} collective-permute-done((f32[4,1,64,256]{3,2,1,0:T(8,128)S(1)}, f32[4,1,64,256]{3,2,1,0:T(8,128)S(1)}, u32[]{:S(2)}, u32[]{:S(2)}) %collective-permute-start.14) | collective-permute-done | bytes 262176 | tf_op jit(solution)/shard_map/ppermute | solution.py:89
  84.5 0.3 fusion.20
  85.0 0.3 multiply_add_fusion
  85.4 0.6 compare_reduce_fusion
  86.1 0.5 collective-permute-done.15
  86.6 0.3 fusion.23
  87.1 1.1 multiply_reduce_fusion
  88.5 0.5 copy-done.3
  90.5 2.5 %collective-permute-start.16 = (f32[65,256]{1,0:T(8,128)S(1)}, f32[65,256]{1,0:T(8,128)S(1)}, u32[]{:S(2)}, u32[]{:S(2)}) collective-permute-start(f32[65,256]{1,0:T(8,128)S(1)} %select_maximum_fusion), channel_id=1, source_target_pairs={{0,2},{2,0},{4,6},{6,4},{8,10},{10,8},{12,14},{14,12},{1,3},{3,1},... | collective-permute-start | bytes 199688 | tf_op jit(solution)/shard_map/ppermute | solution.py:19
  93.1 2.6 %collective-permute-done.16 = f32[65,256]{1,0:T(8,128)S(1)} collective-permute-done((f32[65,256]{1,0:T(8,128)S(1)}, f32[65,256]{1,0:T(8,128)S(1)}, u32[]{:S(2)}, u32[]{:S(2)}) %collective-permute-start.16) | collective-permute-done | bytes 66592 | tf_op jit(solution)/shard_map/ppermute | solution.py:19
  95.7 1.6 %collective-permute-start.17 = (f32[65,256]{1,0:T(8,128)S(1)}, f32[65,256]{1,0:T(8,128)S(1)}, u32[]{:S(2)}, u32[]{:S(2)}) collective-permute-start(f32[65,256]{1,0:T(8,128)S(1)} %fusion.256), channel_id=1, source_target_pairs={{0,4},{2,6},{4,0},{6,2},{8,12},{10,14},{12,8},{14,10},{1,5},{3,7},... | collective-permute-start | bytes 199688 | tf_op jit(solution)/shard_map/ppermute | solution.py:19
  97.3 2.8 %collective-permute-done.17 = f32[65,256]{1,0:T(8,128)S(1)} collective-permute-done((f32[65,256]{1,0:T(8,128)S(1)}, f32[65,256]{1,0:T(8,128)S(1)}, u32[]{:S(2)}, u32[]{:S(2)}) %collective-permute-start.17) | collective-permute-done | bytes 66592 | tf_op jit(solution)/shard_map/ppermute | solution.py:19
  100.1 2.7 %collective-permute-start.18 = (f32[65,256]{1,0:T(8,128)S(1)}, f32[65,256]{1,0:T(8,128)S(1)}, u32[]{:S(2)}, u32[]{:S(2)}) collective-permute-start(f32[65,256]{1,0:T(8,128)S(1)} %add.806), channel_id=1, source_target_pairs={{0,8},{2,10},{4,12},{6,14},{8,0},{10,2},{12,4},{14,6},{1,9},{3,11}... | collective-permute-start | bytes 199688 | tf_op jit(solution)/shard_map/ppermute | solution.py:19
  102.8 2.7 %collective-permute-done.18 = f32[65,256]{1,0:T(8,128)S(1)} collective-permute-done((f32[65,256]{1,0:T(8,128)S(1)}, f32[65,256]{1,0:T(8,128)S(1)}, u32[]{:S(2)}, u32[]{:S(2)}) %collective-permute-start.18) | collective-permute-done | bytes 66592 | tf_op jit(solution)/shard_map/ppermute | solution.py:19
  105.5 0.5 slice.1100
  106.0 1.3 %collective-permute-done.19 = f32[]{:T(128)} collective-permute-done((f32[]{:T(128)}, f32[]{:T(128)}, u32[]{:S(2)}, u32[]{:S(2)}) %collective-permute-start.19) | collective-permute-done | bytes 36 | tf_op jit(solution)/shard_map/ppermute | solution.py:19
  108.6 0.6 maximum_divide_fusion
  (97 shorter events, 5.9 us)
Async XLA Ops:
  0.6 2.5 %copy-start.1 = (f32[2,4,64,256]{3,2,1,0:T(8,128)S(1)}, f32[2,4,64,256]{3,2,1,0:T(8,128)}, u32[]{:S(2)}) copy-start(f32[2,4,64,256]{3,2,1,0:T(8,128)} %param.9) | copy-start | bytes 1572868
  1.6 3.0 %collective-permute-start = (f32[2,4,1,256]{3,2,1,0:T(1,128)S(1)}, f32[2,4,1,256]{3,2,1,0:T(1,128)S(1)}, u32[]{:S(2)}, u32[]{:S(2)}) collective-permute-start(f32[2,4,1,256]{3,2,1,0:T(1,128)S(1)} %constant_dynamic-slice_fusion.7), channel_id=1, source_target_pairs={{0,1},{1,0},{2,3},{3,2},{4,5},{5,4},{6,7},{7,6},{8,9},{9,8},{10,11... | collective-permute-start | bytes 24584 | tf_op jit(solution)/shard_map/ppermute | solution.py:30
  3.1 1.3 %copy-start = (f32[2,4,64,256]{3,2,1,0:T(8,128)S(1)}, f32[2,4,64,256]{3,2,1,0:T(8,128)}, u32[]{:S(2)}) copy-start(f32[2,4,64,256]{3,2,1,0:T(8,128)} %param.7) | copy-start | bytes 1572868
  4.9 11.4 %collective-permute-start.1 = (f32[4,1,64,256]{3,2,1,0:T(8,128)S(1)}, f32[4,1,64,256]{3,2,1,0:T(8,128)S(1)}, u32[]{:S(2)}, u32[]{:S(2)}) collective-permute-start(f32[4,1,64,256]{3,2,1,0:T(8,128)S(1)} %pad_maximum_fusion.38), channel_id=1, source_target_pairs={{2,0},{4,2},{6,4},{8,6},{10,8},{12,10},{14,12},{3,1},{5,3},{7,5},{... | collective-permute-start | bytes 786440 | tf_op jit(solution)/shard_map/ppermute | solution.py:90
  6.2 15.8 %collective-permute-start.2 = (f32[4,1,64,256]{3,2,1,0:T(8,128)S(1)}, f32[4,1,64,256]{3,2,1,0:T(8,128)S(1)}, u32[]{:S(2)}, u32[]{:S(2)}) collective-permute-start(f32[4,1,64,256]{3,2,1,0:T(8,128)S(1)} %pad_maximum_fusion.39), channel_id=1, source_target_pairs={{0,2},{2,4},{4,6},{6,8},{8,10},{10,12},{12,14},{1,3},{3,5},{5,7},{... | collective-permute-start | bytes 786440 | tf_op jit(solution)/shard_map/ppermute | solution.py:89
  22.7 1.2 %collective-permute-start.3 = (f32[2,4,1,256]{3,2,1,0:T(1,128)S(1)}, f32[2,4,1,256]{3,2,1,0:T(1,128)S(1)}, u32[]{:S(2)}, u32[]{:S(2)}) collective-permute-start(f32[2,4,1,256]{3,2,1,0:T(1,128)S(1)} %constant_dynamic-slice_fusion.6), channel_id=1, source_target_pairs={{0,1},{1,0},{2,3},{3,2},{4,5},{5,4},{6,7},{7,6},{8,9},{9,8},{10,11... | collective-permute-start | bytes 24584 | tf_op jit(solution)/shard_map/ppermute | solution.py:30
  24.6 1.2 %collective-permute-start.4 = (f32[2,4,1,256]{3,2,1,0:T(1,128)S(1)}, f32[2,4,1,256]{3,2,1,0:T(1,128)S(1)}, u32[]{:S(2)}, u32[]{:S(2)}) collective-permute-start(f32[2,4,1,256]{3,2,1,0:T(1,128)S(1)} %constant_dynamic-slice_fusion.5), channel_id=1, source_target_pairs={{0,1},{1,0},{2,3},{3,2},{4,5},{5,4},{6,7},{7,6},{8,9},{9,8},{10,11... | collective-permute-start | bytes 24584 | tf_op jit(solution)/shard_map/ppermute | solution.py:30
  26.2 11.0 %collective-permute-start.5 = (f32[4,1,64,256]{3,2,1,0:T(8,128)S(1)}, f32[4,1,64,256]{3,2,1,0:T(8,128)S(1)}, u32[]{:S(2)}, u32[]{:S(2)}) collective-permute-start(f32[4,1,64,256]{3,2,1,0:T(8,128)S(1)} %pad_maximum_fusion.40), channel_id=1, source_target_pairs={{2,0},{4,2},{6,4},{8,6},{10,8},{12,10},{14,12},{3,1},{5,3},{7,5},{... | collective-permute-start | bytes 786440 | tf_op jit(solution)/shard_map/ppermute | solution.py:90
  27.5 15.4 %collective-permute-start.6 = (f32[4,1,64,256]{3,2,1,0:T(8,128)S(1)}, f32[4,1,64,256]{3,2,1,0:T(8,128)S(1)}, u32[]{:S(2)}, u32[]{:S(2)}) collective-permute-start(f32[4,1,64,256]{3,2,1,0:T(8,128)S(1)} %pad_maximum_fusion.41), channel_id=1, source_target_pairs={{0,2},{2,4},{4,6},{6,8},{8,10},{10,12},{12,14},{1,3},{3,5},{5,7},{... | collective-permute-start | bytes 786440 | tf_op jit(solution)/shard_map/ppermute | solution.py:89
  43.6 1.2 %collective-permute-start.7 = (f32[2,4,1,256]{3,2,1,0:T(1,128)S(1)}, f32[2,4,1,256]{3,2,1,0:T(1,128)S(1)}, u32[]{:S(2)}, u32[]{:S(2)}) collective-permute-start(f32[2,4,1,256]{3,2,1,0:T(1,128)S(1)} %constant_dynamic-slice_fusion.4), channel_id=1, source_target_pairs={{0,1},{1,0},{2,3},{3,2},{4,5},{5,4},{6,7},{7,6},{8,9},{9,8},{10,11... | collective-permute-start | bytes 24584 | tf_op jit(solution)/shard_map/ppermute | solution.py:30
  45.7 1.2 %collective-permute-start.8 = (f32[2,4,1,256]{3,2,1,0:T(1,128)S(1)}, f32[2,4,1,256]{3,2,1,0:T(1,128)S(1)}, u32[]{:S(2)}, u32[]{:S(2)}) collective-permute-start(f32[2,4,1,256]{3,2,1,0:T(1,128)S(1)} %constant_dynamic-slice_fusion.3), channel_id=1, source_target_pairs={{0,1},{1,0},{2,3},{3,2},{4,5},{5,4},{6,7},{7,6},{8,9},{9,8},{10,11... | collective-permute-start | bytes 24584 | tf_op jit(solution)/shard_map/ppermute | solution.py:30
  47.2 15.9 %collective-permute-start.10 = (f32[4,1,64,256]{3,2,1,0:T(8,128)S(1)}, f32[4,1,64,256]{3,2,1,0:T(8,128)S(1)}, u32[]{:S(2)}, u32[]{:S(2)}) collective-permute-start(f32[4,1,64,256]{3,2,1,0:T(8,128)S(1)} %pad_maximum_fusion.43), channel_id=1, source_target_pairs={{0,2},{2,4},{4,6},{6,8},{8,10},{10,12},{12,14},{1,3},{3,5},{5,7},{... | collective-permute-start | bytes 786440 | tf_op jit(solution)/shard_map/ppermute | solution.py:89
  51.7 11.5 %collective-permute-start.9 = (f32[4,1,64,256]{3,2,1,0:T(8,128)S(1)}, f32[4,1,64,256]{3,2,1,0:T(8,128)S(1)}, u32[]{:S(2)}, u32[]{:S(2)}) collective-permute-start(f32[4,1,64,256]{3,2,1,0:T(8,128)S(1)} %pad_maximum_fusion.42), channel_id=1, source_target_pairs={{2,0},{4,2},{6,4},{8,6},{10,8},{12,10},{14,12},{3,1},{5,3},{7,5},{... | collective-permute-start | bytes 786440 | tf_op jit(solution)/shard_map/ppermute | solution.py:90
  64.0 1.2 %collective-permute-start.11 = (f32[2,4,1,256]{3,2,1,0:T(1,128)S(1)}, f32[2,4,1,256]{3,2,1,0:T(1,128)S(1)}, u32[]{:S(2)}, u32[]{:S(2)}) collective-permute-start(f32[2,4,1,256]{3,2,1,0:T(1,128)S(1)} %constant_dynamic-slice_fusion.2), channel_id=1, source_target_pairs={{0,1},{1,0},{2,3},{3,2},{4,5},{5,4},{6,7},{7,6},{8,9},{9,8},{10,11... | collective-permute-start | bytes 24584 | tf_op jit(solution)/shard_map/ppermute | solution.py:30
  66.1 1.2 %collective-permute-start.12 = (f32[2,4,1,256]{3,2,1,0:T(1,128)S(1)}, f32[2,4,1,256]{3,2,1,0:T(1,128)S(1)}, u32[]{:S(2)}, u32[]{:S(2)}) collective-permute-start(f32[2,4,1,256]{3,2,1,0:T(1,128)S(1)} %constant_dynamic-slice_fusion.1), channel_id=1, source_target_pairs={{0,1},{1,0},{2,3},{3,2},{4,5},{5,4},{6,7},{7,6},{8,9},{9,8},{10,11... | collective-permute-start | bytes 24584 | tf_op jit(solution)/shard_map/ppermute | solution.py:30
  67.7 11.0 %collective-permute-start.13 = (f32[4,1,64,256]{3,2,1,0:T(8,128)S(1)}, f32[4,1,64,256]{3,2,1,0:T(8,128)S(1)}, u32[]{:S(2)}, u32[]{:S(2)}) collective-permute-start(f32[4,1,64,256]{3,2,1,0:T(8,128)S(1)} %pad_maximum_fusion.44), channel_id=1, source_target_pairs={{2,0},{4,2},{6,4},{8,6},{10,8},{12,10},{14,12},{3,1},{5,3},{7,5},{... | collective-permute-start | bytes 786440 | tf_op jit(solution)/shard_map/ppermute | solution.py:90
  69.0 15.5 %collective-permute-start.14 = (f32[4,1,64,256]{3,2,1,0:T(8,128)S(1)}, f32[4,1,64,256]{3,2,1,0:T(8,128)S(1)}, u32[]{:S(2)}, u32[]{:S(2)}) collective-permute-start(f32[4,1,64,256]{3,2,1,0:T(8,128)S(1)} %pad_maximum_fusion.45), channel_id=1, source_target_pairs={{0,2},{2,4},{4,6},{6,8},{8,10},{10,12},{12,14},{1,3},{3,5},{5,7},{... | collective-permute-start | bytes 786440 | tf_op jit(solution)/shard_map/ppermute | solution.py:89
  85.3 1.2 %collective-permute-start.15 = (f32[2,4,1,256]{3,2,1,0:T(1,128)S(1)}, f32[2,4,1,256]{3,2,1,0:T(1,128)S(1)}, u32[]{:S(2)}, u32[]{:S(2)}) collective-permute-start(f32[2,4,1,256]{3,2,1,0:T(1,128)S(1)} %constant_dynamic-slice_fusion), channel_id=1, source_target_pairs={{0,1},{1,0},{2,3},{3,2},{4,5},{5,4},{6,7},{7,6},{8,9},{9,8},{10,11... | collective-permute-start | bytes 24584 | tf_op jit(solution)/shard_map/ppermute | solution.py:30
  87.1 1.1 copy-start.2
  88.2 0.8 copy-start.3
  90.5 5.1 %collective-permute-start.16 = (f32[65,256]{1,0:T(8,128)S(1)}, f32[65,256]{1,0:T(8,128)S(1)}, u32[]{:S(2)}, u32[]{:S(2)}) collective-permute-start(f32[65,256]{1,0:T(8,128)S(1)} %select_maximum_fusion), channel_id=1, source_target_pairs={{0,2},{2,0},{4,6},{6,4},{8,10},{10,8},{12,14},{14,12},{1,3},{3,1},... | collective-permute-start | bytes 199688 | tf_op jit(solution)/shard_map/ppermute | solution.py:19
  95.7 4.4 %collective-permute-start.17 = (f32[65,256]{1,0:T(8,128)S(1)}, f32[65,256]{1,0:T(8,128)S(1)}, u32[]{:S(2)}, u32[]{:S(2)}) collective-permute-start(f32[65,256]{1,0:T(8,128)S(1)} %fusion.256), channel_id=1, source_target_pairs={{0,4},{2,6},{4,0},{6,2},{8,12},{10,14},{12,8},{14,10},{1,5},{3,7},... | collective-permute-start | bytes 199688 | tf_op jit(solution)/shard_map/ppermute | solution.py:19
  100.1 5.3 %collective-permute-start.18 = (f32[65,256]{1,0:T(8,128)S(1)}, f32[65,256]{1,0:T(8,128)S(1)}, u32[]{:S(2)}, u32[]{:S(2)}) collective-permute-start(f32[65,256]{1,0:T(8,128)S(1)} %add.806), channel_id=1, source_target_pairs={{0,8},{2,10},{4,12},{6,14},{8,0},{10,2},{12,4},{14,6},{1,9},{3,11}... | collective-permute-start | bytes 199688 | tf_op jit(solution)/shard_map/ppermute | solution.py:19
  106.0 1.3 %collective-permute-start.19 = (f32[]{:T(128)}, f32[]{:T(128)}, u32[]{:S(2)}, u32[]{:S(2)}) collective-permute-start(f32[]{:T(128)} %bitcast.111), channel_id=1, source_target_pairs={{0,1},{1,0},{2,3},{3,2},{4,5},{5,4},{6,7},{7,6},{8,9},{9,8},{10,11... | collective-permute-start | bytes 20 | tf_op jit(solution)/shard_map/ppermute | solution.py:19

commit v6 on v5

--- a/solution.py
+++ b/solution.py
@@ -19,6 +19,26 @@
         value = value + lax.ppermute(value, axis, pairs)
         step *= 2
     return value
+
+
+def gx_total(value):
+    count = lax.axis_size("gx")
+    if count > 8 or count % 2:
+        return axis_sum(value, "gx")
+    pair = value + lax.ppermute(value, "gx", [(i, i ^ 1) for i in range(count)])
+    groups = count // 2
+    if groups == 1:
+        return pair
+    fetched = [pair] + [
+        lax.ppermute(pair, "gx", [(i, i ^ (2 * k)) for i in range(count)])
+        for k in range(1, groups)
+    ]
+    stacked = jnp.stack(fetched)
+    mine = lax.axis_index("gx") // 2
+    total = lax.dynamic_index_in_dim(stacked, mine, keepdims=False)
+    for j in range(1, groups):
+        total = total + lax.dynamic_index_in_dim(stacked, mine ^ j, keepdims=False)
+    return total
 
 
 def y_extended(block):
@@ -136,10 +156,10 @@
     chi_start = rk_step(chi_late, coef_early)
     rows_late = row_terms(chi_late, psi_late, profile)
     rows_early = row_terms(chi_start, psi_early, profile)
-    local_sq = jnp.sum(chi_start * chi_start)
+    local_sq = axis_sum(jnp.sum(chi_start * chi_start), "gy")
     extra = jnp.zeros((1, rows_early.shape[1]), jnp.float32).at[0, 0].set(local_sq)
-    packed = axis_sum(jnp.concatenate([rows_early, rows_late, extra], axis=0), "gx")
-    squares = axis_sum(packed[-1, 0], "gy")
+    packed = gx_total(jnp.concatenate([rows_early, rows_late, extra], axis=0))
+    squares = packed[-1, 0]
     half = rows_early.shape[0]
     rows_sum = jnp.stack([packed[:half], packed[half:2 * half]])
     power = squares / float(total_x * total_y * depth)

time: 111 us -> 111 us (level)
    ppermute x4 -> x1, waiting for transfers between devices: 9.31 us -> 0.9 us  [axis_sum(): value = value + lax.ppermute(value, axis, pairs)]
    ppermute x0 -> x4, waiting for transfers between devices: none -> 7.77 us  [the longest x3 5.15 us: gx_total(): lax.ppermute(pair, 'gx', [(i, i ^ 2 * k) for i in range(count)])]
    ppermute x0 -> x4, starting transfers between devices: none -> 6.99 us  [the longest x3 4.45 us: gx_total(): lax.ppermute(pair, 'gx', [(i, i ^ 2 * k) for i in range(count)])]
    ppermute x4 -> x1, starting transfers between devices: 6.83 us -> 0.23 us  [axis_sum(): value = value + lax.ppermute(value, axis, pairs)]
  transfers between devices with their start and end apart: 20 -> 21, of which waited for: 18 -> 18; matrix products, arithmetic and copies ran while one was open for 3% -> 3% of each run, Pallas kernels for 0% -> 0%
where the time goes in v6:
time: 111 us; the launch traced here: 110 us
  waiting for transfers between devices  57 us (51%)
  starting transfers between devices  33.5 us (30%)
  other arithmetic  11.5 us (10%)
  between operations  5.03 us (5%)
  local copies, waits for them, and re-layouts  3.16 us (3%)
    ppermute x4, waiting for transfers between devices, stage_pair(): lax.ppermute(jnp.concatenate([stage[:, X - 1:], part_top]), 'gx', up)  27.3 us
    ppermute x4, starting transfers between devices, stage_pair(): lax.ppermute(jnp.concatenate([stage[:, X - 1:], part_top]), 'gx', up)  19.5 us
    ppermute x4, waiting for transfers between devices, stage_pair(): lax.ppermute(jnp.concatenate([stage[:, :1], part_bottom]), 'gx', down)  14.2 us
    ppermute x8, waiting for transfers between devices, y_extended(): other = lax.ppermute(strip, 'gy', [(0, 1), (1, 0)])  6.84 us
    ppermute x4, starting transfers between devices, stage_pair(): lax.ppermute(jnp.concatenate([stage[:, :1], part_bottom]), 'gx', down)  5.17 us
    ppermute x3, waiting for transfers between devices, gx_total(): lax.ppermute(pair, 'gx', [(i, i ^ 2 * k) for i in range(count)])  5.15 us
    ppermute x3, starting transfers between devices, gx_total(): lax.ppermute(pair, 'gx', [(i, i ^ 2 * k) for i in range(count)])  4.45 us
    sub x12, other arithmetic, operator(): lapl = total - 6.0 * field  3.63 us
  transfers between devices with their start and end apart: 21, of which 18 were waited for; matrix products, arithmetic and copies ran while one was open for 3% of the time, Pallas kernels for 0%

profile of v6, /device:TPU:0, one launch (start us, length us, event | category | flops | bytes accessed | tf_op | source)
XLA Modules:
  0.0 110.2 jit_solution(14018674975570431028)
XLA Ops:
  0.6 0.9 constant_dynamic-slice_fusion.7
  1.6 0.6 collective-permute-start
  2.2 0.8 slice_bitcast_fusion.18
  3.1 1.3 %multiply_add_fusion.6 = (f32[4,64,256]{2,1,0:T(8,128)S(1)}, f32[4,64,256]{2,1,0:T(8,128)S(1)}, f32[4,64,256]{2,1,0:T(8,128)S(1)}, f32[4,64,256]{2,1,0:T(8,128)S(1)}) fusion(f32[4,64,256]{2,1,0:T(8,128)} %param.10, f32[2,4,64,256]{3,2,1,0:T(8,128)} %param.8, f32[64,256]{1,0:T(8,128)S(1)} %mul.852, f32[4]{0:T(128)S(1)} %multiply_add_fusion.7, ...), kind=kLoop, calls=%fused_computation.257 | loop fusion | flops 1114112 | bytes 2490384 | tf_op jit(solution)/shard_map/add | solution.py:65
  4.9 1.3 %collective-permute-start.1 = (f32[4,1,64,256]{3,2,1,0:T(8,128)S(1)}, f32[4,1,64,256]{3,2,1,0:T(8,128)S(1)}, u32[]{:S(2)}, u32[]{:S(2)}) collective-permute-start(f32[4,1,64,256]{3,2,1,0:T(8,128)S(1)} %pad_maximum_fusion.39), channel_id=1, source_target_pairs={{2,0},{4,2},{6,4},{8,6},{10,8},{12,10},{14,12},{3,1},{5,3},{7,5},{... | collective-permute-start | bytes 786440 | tf_op jit(solution)/shard_map/ppermute | solution.py:110
  6.2 5.0 %collective-permute-start.2 = (f32[4,1,64,256]{3,2,1,0:T(8,128)S(1)}, f32[4,1,64,256]{3,2,1,0:T(8,128)S(1)}, u32[]{:S(2)}, u32[]{:S(2)}) collective-permute-start(f32[4,1,64,256]{3,2,1,0:T(8,128)S(1)} %pad_maximum_fusion.40), channel_id=1, source_target_pairs={{0,2},{2,4},{4,6},{6,8},{8,10},{10,12},{12,14},{1,3},{3,5},{5,7},{... | collective-permute-start | bytes 786440 | tf_op jit(solution)/shard_map/ppermute | solution.py:109
  11.3 4.9 %collective-permute-done.1 = f32[4,1,64,256]{3,2,1,0:T(8,128)S(1)} collective-permute-done((f32[4,1,64,256]{3,2,1,0:T(8,128)S(1)}, f32[4,1,64,256]{3,2,1,0:T(8,128)S(1)}, u32[]{:S(2)}, u32[]{:S(2)}) %collective-permute-start.1) | collective-permute-done | bytes 262176 | tf_op jit(solution)/shard_map/ppermute | solution.py:110
  16.3 5.8 %collective-permute-done.2 = f32[4,1,64,256]{3,2,1,0:T(8,128)S(1)} collective-permute-done((f32[4,1,64,256]{3,2,1,0:T(8,128)S(1)}, f32[4,1,64,256]{3,2,1,0:T(8,128)S(1)}, u32[]{:S(2)}, u32[]{:S(2)}) %collective-permute-start.2) | collective-permute-done | bytes 262176 | tf_op jit(solution)/shard_map/ppermute | solution.py:109
  22.1 0.4 fusion.2
  22.8 1.1 %collective-permute-done.3 = f32[2,4,1,256]{3,2,1,0:T(1,128)S(1)} collective-permute-done((f32[2,4,1,256]{3,2,1,0:T(1,128)S(1)}, f32[2,4,1,256]{3,2,1,0:T(1,128)S(1)}, u32[]{:S(2)}, u32[]{:S(2)}) %collective-permute-start.3) | collective-permute-done | bytes 8224 | tf_op jit(solution)/shard_map/ppermute | solution.py:50
  24.0 0.3 fusion.5
  24.8 1.0 collective-permute-done.4
  26.2 1.3 %collective-permute-start.5 = (f32[4,1,64,256]{3,2,1,0:T(8,128)S(1)}, f32[4,1,64,256]{3,2,1,0:T(8,128)S(1)}, u32[]{:S(2)}, u32[]{:S(2)}) collective-permute-start(f32[4,1,64,256]{3,2,1,0:T(8,128)S(1)} %pad_maximum_fusion.41), channel_id=1, source_target_pairs={{2,0},{4,2},{6,4},{8,6},{10,8},{12,10},{14,12},{3,1},{5,3},{7,5},{... | collective-permute-start | bytes 786440 | tf_op jit(solution)/shard_map/ppermute | solution.py:110
  27.5 5.0 %collective-permute-start.6 = (f32[4,1,64,256]{3,2,1,0:T(8,128)S(1)}, f32[4,1,64,256]{3,2,1,0:T(8,128)S(1)}, u32[]{:S(2)}, u32[]{:S(2)}) collective-permute-start(f32[4,1,64,256]{3,2,1,0:T(8,128)S(1)} %pad_maximum_fusion.42), channel_id=1, source_target_pairs={{0,2},{2,4},{4,6},{6,8},{8,10},{10,12},{12,14},{1,3},{3,5},{5,7},{... | collective-permute-start | bytes 786440 | tf_op jit(solution)/shard_map/ppermute | solution.py:109
  32.5 4.6 %collective-permute-done.5 = f32[4,1,64,256]{3,2,1,0:T(8,128)S(1)} collective-permute-done((f32[4,1,64,256]{3,2,1,0:T(8,128)S(1)}, f32[4,1,64,256]{3,2,1,0:T(8,128)S(1)}, u32[]{:S(2)}, u32[]{:S(2)}) %collective-permute-start.5) | collective-permute-done | bytes 262176 | tf_op jit(solution)/shard_map/ppermute | solution.py:110
  37.2 5.7 %collective-permute-done.6 = f32[4,1,64,256]{3,2,1,0:T(8,128)S(1)} collective-permute-done((f32[4,1,64,256]{3,2,1,0:T(8,128)S(1)}, f32[4,1,64,256]{3,2,1,0:T(8,128)S(1)}, u32[]{:S(2)}, u32[]{:S(2)}) %collective-permute-start.6) | collective-permute-done | bytes 262176 | tf_op jit(solution)/shard_map/ppermute | solution.py:109
  43.0 0.3 fusion.8
  43.8 1.1 collective-permute-done.7
  44.9 0.3 fusion.11
  45.9 1.0 collective-permute-done.8
  47.2 4.4 %collective-permute-start.10 = (f32[4,1,64,256]{3,2,1,0:T(8,128)S(1)}, f32[4,1,64,256]{3,2,1,0:T(8,128)S(1)}, u32[]{:S(2)}, u32[]{:S(2)}) collective-permute-start(f32[4,1,64,256]{3,2,1,0:T(8,128)S(1)} %pad_maximum_fusion.44), channel_id=1, source_target_pairs={{0,2},{2,4},{4,6},{6,8},{8,10},{10,12},{12,14},{1,3},{3,5},{5,7},{... | collective-permute-start | bytes 786440 | tf_op jit(solution)/shard_map/ppermute | solution.py:109
  51.7 1.3 %collective-permute-start.9 = (f32[4,1,64,256]{3,2,1,0:T(8,128)S(1)}, f32[4,1,64,256]{3,2,1,0:T(8,128)S(1)}, u32[]{:S(2)}, u32[]{:S(2)}) collective-permute-start(f32[4,1,64,256]{3,2,1,0:T(8,128)S(1)} %pad_maximum_fusion.43), channel_id=1, source_target_pairs={{2,0},{4,2},{6,4},{8,6},{10,8},{12,10},{14,12},{3,1},{5,3},{7,5},{... | collective-permute-start | bytes 786440 | tf_op jit(solution)/shard_map/ppermute | solution.py:110
  53.0 10.1 %collective-permute-done.10 = f32[4,1,64,256]{3,2,1,0:T(8,128)S(1)} collective-permute-done((f32[4,1,64,256]{3,2,1,0:T(8,128)S(1)}, f32[4,1,64,256]{3,2,1,0:T(8,128)S(1)}, u32[]{:S(2)}, u32[]{:S(2)}) %collective-permute-start.10) | collective-permute-done | bytes 262176 | tf_op jit(solution)/shard_map/ppermute | solution.py:109
  63.2 0.4 fusion.14
  63.7 0.3 multiply_add_fusion.2
  64.1 1.2 %collective-permute-done.11 = f32[2,4,1,256]{3,2,1,0:T(1,128)S(1)} collective-permute-done((f32[2,4,1,256]{3,2,1,0:T(1,128)S(1)}, f32[2,4,1,256]{3,2,1,0:T(1,128)S(1)}, u32[]{:S(2)}, u32[]{:S(2)}) %collective-permute-start.11) | collective-permute-done | bytes 8224 | tf_op jit(solution)/shard_map/ppermute | solution.py:50
  65.3 0.3 fusion.17
  66.3 1.0 collective-permute-done.12
  67.7 1.3 %collective-permute-start.13 = (f32[4,1,64,256]{3,2,1,0:T(8,128)S(1)}, f32[4,1,64,256]{3,2,1,0:T(8,128)S(1)}, u32[]{:S(2)}, u32[]{:S(2)}) collective-permute-start(f32[4,1,64,256]{3,2,1,0:T(8,128)S(1)} %pad_maximum_fusion.45), channel_id=1, source_target_pairs={{2,0},{4,2},{6,4},{8,6},{10,8},{12,10},{14,12},{3,1},{5,3},{7,5},{... | collective-permute-start | bytes 786440 | tf_op jit(solution)/shard_map/ppermute | solution.py:110
  69.0 5.0 %collective-permute-start.14 = (f32[4,1,64,256]{3,2,1,0:T(8,128)S(1)}, f32[4,1,64,256]{3,2,1,0:T(8,128)S(1)}, u32[]{:S(2)}, u32[]{:S(2)}) collective-permute-start(f32[4,1,64,256]{3,2,1,0:T(8,128)S(1)} %pad_maximum_fusion.46), channel_id=1, source_target_pairs={{0,2},{2,4},{4,6},{6,8},{8,10},{10,12},{12,14},{1,3},{3,5},{5,7},{... | collective-permute-start | bytes 786440 | tf_op jit(solution)/shard_map/ppermute | solution.py:109
  74.1 4.6 %collective-permute-done.13 = f32[4,1,64,256]{3,2,1,0:T(8,128)S(1)} collective-permute-done((f32[4,1,64,256]{3,2,1,0:T(8,128)S(1)}, f32[4,1,64,256]{3,2,1,0:T(8,128)S(1)}, u32[]{:S(2)}, u32[]{:S(2)}) %collective-permute-start.13) | collective-permute-done | bytes 262176 | tf_op jit(solution)/shard_map/ppermute | solution.py:110
  78.7 5.7 %collective-permute-done.14 = f32[4,1,64,256]{3,2,1,0:T(8,128)S(1)} collective-permute-done((f32[4,1,64,256]{3,2,1,0:T(8,128)S(1)}, f32[4,1,64,256]{3,2,1,0:T(8,128)S(1)}, u32[]{:S(2)}, u32[]{:S(2)}) %collective-permute-start.14) | collective-permute-done | bytes 262176 | tf_op jit(solution)/shard_map/ppermute | solution.py:109
  84.5 0.3 fusion.20
  85.4 0.6 compare_reduce_fusion
  86.1 0.5 collective-permute-done.15
  86.6 0.3 fusion.23
  87.1 1.1 multiply_reduce_fusion
  88.5 0.5 copy-done.3
  89.5 0.9 collective-permute-done.16
  92.3 2.5 %collective-permute-start.17 = (f32[65,256]{1,0:T(8,128)S(1)}, f32[65,256]{1,0:T(8,128)S(1)}, u32[]{:S(2)}, u32[]{:S(2)}) collective-permute-start(f32[65,256]{1,0:T(8,128)S(1)} %select_maximum_fusion), channel_id=1, source_target_pairs={{0,2},{2,0},{4,6},{6,4},{8,10},{10,8},{12,14},{14,12},{1,3},{3,1},... | collective-permute-start | bytes 199688 | tf_op jit(solution)/shard_map/ppermute | solution.py:28
  94.8 2.6 %collective-permute-done.17 = f32[65,256]{1,0:T(8,128)S(1)} collective-permute-done((f32[65,256]{1,0:T(8,128)S(1)}, f32[65,256]{1,0:T(8,128)S(1)}, u32[]{:S(2)}, u32[]{:S(2)}) %collective-permute-start.17) | collective-permute-done | bytes 66592 | tf_op jit(solution)/shard_map/ppermute | solution.py:28
  97.5 2.7 %collective-permute-start.20 = (f32[65,256]{1,0:T(8,128)S(1)}, f32[65,256]{1,0:T(8,128)S(1)}, u32[]{:S(2)}, u32[]{:S(2)}) collective-permute-start(f32[65,256]{1,0:T(8,128)S(1)} %fusion.256), channel_id=1, source_target_pairs={{0,12},{2,14},{4,8},{6,10},{8,4},{10,6},{12,0},{14,2},{1,13},{3,15... | collective-permute-start | bytes 199688 | tf_op jit(solution)/shard_map/ppermute | solution.py:33
  100.1 0.4 collective-permute-start.19
  100.6 1.3 %collective-permute-start.18 = (f32[65,256]{1,0:T(8,128)S(1)}, f32[65,256]{1,0:T(8,128)S(1)}, u32[]{:S(2)}, u32[]{:S(2)}) collective-permute-start(f32[65,256]{1,0:T(8,128)S(1)} %fusion.256), channel_id=1, source_target_pairs={{0,4},{2,6},{4,0},{6,2},{8,12},{10,14},{12,8},{14,10},{1,5},{3,7},... | collective-permute-start | bytes 199688 | tf_op jit(solution)/shard_map/ppermute | solution.py:33
  101.9 2.6 %collective-permute-done.20 = f32[65,256]{1,0:T(8,128)S(1)} collective-permute-done((f32[65,256]{1,0:T(8,128)S(1)}, f32[65,256]{1,0:T(8,128)S(1)}, u32[]{:S(2)}, u32[]{:S(2)}) %collective-permute-start.20) | collective-permute-done | bytes 66592 | tf_op jit(solution)/shard_map/ppermute | solution.py:33
  104.5 2.5 %collective-permute-done.19 = f32[65,256]{1,0:T(8,128)S(1)} collective-permute-done((f32[65,256]{1,0:T(8,128)S(1)}, f32[65,256]{1,0:T(8,128)S(1)}, u32[]{:S(2)}, u32[]{:S(2)}) %collective-permute-start.19) | collective-permute-done | bytes 66592 | tf_op jit(solution)/shard_map/ppermute | solution.py:33
  107.2 0.5 slice.1102
  108.4 0.6 maximum_divide_fusion
  (100 shorter events, 6.5 us)
Async XLA Ops:
  0.6 2.5 %copy-start.1 = (f32[2,4,64,256]{3,2,1,0:T(8,128)S(1)}, f32[2,4,64,256]{3,2,1,0:T(8,128)}, u32[]{:S(2)}) copy-start(f32[2,4,64,256]{3,2,1,0:T(8,128)} %param.9) | copy-start | bytes 1572868
  1.6 3.0 %collective-permute-start = (f32[2,4,1,256]{3,2,1,0:T(1,128)S(1)}, f32[2,4,1,256]{3,2,1,0:T(1,128)S(1)}, u32[]{:S(2)}, u32[]{:S(2)}) collective-permute-start(f32[2,4,1,256]{3,2,1,0:T(1,128)S(1)} %constant_dynamic-slice_fusion.7), channel_id=1, source_target_pairs={{0,1},{1,0},{2,3},{3,2},{4,5},{5,4},{6,7},{7,6},{8,9},{9,8},{10,11... | collective-permute-start | bytes 24584 | tf_op jit(solution)/shard_map/ppermute | solution.py:50
  3.1 1.3 %copy-start = (f32[2,4,64,256]{3,2,1,0:T(8,128)S(1)}, f32[2,4,64,256]{3,2,1,0:T(8,128)}, u32[]{:S(2)}) copy-start(f32[2,4,64,256]{3,2,1,0:T(8,128)} %param.7) | copy-start | bytes 1572868
  4.9 11.4 %collective-permute-start.1 = (f32[4,1,64,256]{3,2,1,0:T(8,128)S(1)}, f32[4,1,64,256]{3,2,1,0:T(8,128)S(1)}, u32[]{:S(2)}, u32[]{:S(2)}) collective-permute-start(f32[4,1,64,256]{3,2,1,0:T(8,128)S(1)} %pad_maximum_fusion.39), channel_id=1, source_target_pairs={{2,0},{4,2},{6,4},{8,6},{10,8},{12,10},{14,12},{3,1},{5,3},{7,5},{... | collective-permute-start | bytes 786440 | tf_op jit(solution)/shard_map/ppermute | solution.py:110
  6.2 15.8 %collective-permute-start.2 = (f32[4,1,64,256]{3,2,1,0:T(8,128)S(1)}, f32[4,1,64,256]{3,2,1,0:T(8,128)S(1)}, u32[]{:S(2)}, u32[]{:S(2)}) collective-permute-start(f32[4,1,64,256]{3,2,1,0:T(8,128)S(1)} %pad_maximum_fusion.40), channel_id=1, source_target_pairs={{0,2},{2,4},{4,6},{6,8},{8,10},{10,12},{12,14},{1,3},{3,5},{5,7},{... | collective-permute-start | bytes 786440 | tf_op jit(solution)/shard_map/ppermute | solution.py:109
  22.7 1.2 %collective-permute-start.3 = (f32[2,4,1,256]{3,2,1,0:T(1,128)S(1)}, f32[2,4,1,256]{3,2,1,0:T(1,128)S(1)}, u32[]{:S(2)}, u32[]{:S(2)}) collective-permute-start(f32[2,4,1,256]{3,2,1,0:T(1,128)S(1)} %constant_dynamic-slice_fusion.6), channel_id=1, source_target_pairs={{0,1},{1,0},{2,3},{3,2},{4,5},{5,4},{6,7},{7,6},{8,9},{9,8},{10,11... | collective-permute-start | bytes 24584 | tf_op jit(solution)/shard_map/ppermute | solution.py:50
  24.6 1.2 %collective-permute-start.4 = (f32[2,4,1,256]{3,2,1,0:T(1,128)S(1)}, f32[2,4,1,256]{3,2,1,0:T(1,128)S(1)}, u32[]{:S(2)}, u32[]{:S(2)}) collective-permute-start(f32[2,4,1,256]{3,2,1,0:T(1,128)S(1)} %constant_dynamic-slice_fusion.5), channel_id=1, source_target_pairs={{0,1},{1,0},{2,3},{3,2},{4,5},{5,4},{6,7},{7,6},{8,9},{9,8},{10,11... | collective-permute-start | bytes 24584 | tf_op jit(solution)/shard_map/ppermute | solution.py:50
  26.2 11.0 %collective-permute-start.5 = (f32[4,1,64,256]{3,2,1,0:T(8,128)S(1)}, f32[4,1,64,256]{3,2,1,0:T(8,128)S(1)}, u32[]{:S(2)}, u32[]{:S(2)}) collective-permute-start(f32[4,1,64,256]{3,2,1,0:T(8,128)S(1)} %pad_maximum_fusion.41), channel_id=1, source_target_pairs={{2,0},{4,2},{6,4},{8,6},{10,8},{12,10},{14,12},{3,1},{5,3},{7,5},{... | collective-permute-start | bytes 786440 | tf_op jit(solution)/shard_map/ppermute | solution.py:110
  27.5 15.4 %collective-permute-start.6 = (f32[4,1,64,256]{3,2,1,0:T(8,128)S(1)}, f32[4,1,64,256]{3,2,1,0:T(8,128)S(1)}, u32[]{:S(2)}, u32[]{:S(2)}) collective-permute-start(f32[4,1,64,256]{3,2,1,0:T(8,128)S(1)} %pad_maximum_fusion.42), channel_id=1, source_target_pairs={{0,2},{2,4},{4,6},{6,8},{8,10},{10,12},{12,14},{1,3},{3,5},{5,7},{... | collective-permute-start | bytes 786440 | tf_op jit(solution)/shard_map/ppermute | solution.py:109
  43.6 1.2 %collective-permute-start.7 = (f32[2,4,1,256]{3,2,1,0:T(1,128)S(1)}, f32[2,4,1,256]{3,2,1,0:T(1,128)S(1)}, u32[]{:S(2)}, u32[]{:S(2)}) collective-permute-start(f32[2,4,1,256]{3,2,1,0:T(1,128)S(1)} %constant_dynamic-slice_fusion.4), channel_id=1, source_target_pairs={{0,1},{1,0},{2,3},{3,2},{4,5},{5,4},{6,7},{7,6},{8,9},{9,8},{10,11... | collective-permute-start | bytes 24584 | tf_op jit(solution)/shard_map/ppermute | solution.py:50
  45.7 1.2 %collective-permute-start.8 = (f32[2,4,1,256]{3,2,1,0:T(1,128)S(1)}, f32[2,4,1,256]{3,2,1,0:T(1,128)S(1)}, u32[]{:S(2)}, u32[]{:S(2)}) collective-permute-start(f32[2,4,1,256]{3,2,1,0:T(1,128)S(1)} %constant_dynamic-slice_fusion.3), channel_id=1, source_target_pairs={{0,1},{1,0},{2,3},{3,2},{4,5},{5,4},{6,7},{7,6},{8,9},{9,8},{10,11... | collective-permute-start | bytes 24584 | tf_op jit(solution)/shard_map/ppermute | solution.py:50
  47.2 15.9 %collective-permute-start.10 = (f32[4,1,64,256]{3,2,1,0:T(8,128)S(1)}, f32[4,1,64,256]{3,2,1,0:T(8,128)S(1)}, u32[]{:S(2)}, u32[]{:S(2)}) collective-permute-start(f32[4,1,64,256]{3,2,1,0:T(8,128)S(1)} %pad_maximum_fusion.44), channel_id=1, source_target_pairs={{0,2},{2,4},{4,6},{6,8},{8,10},{10,12},{12,14},{1,3},{3,5},{5,7},{... | collective-permute-start | bytes 786440 | tf_op jit(solution)/shard_map/ppermute | solution.py:109
  51.7 11.5 %collective-permute-start.9 = (f32[4,1,64,256]{3,2,1,0:T(8,128)S(1)}, f32[4,1,64,256]{3,2,1,0:T(8,128)S(1)}, u32[]{:S(2)}, u32[]{:S(2)}) collective-permute-start(f32[4,1,64,256]{3,2,1,0:T(8,128)S(1)} %pad_maximum_fusion.43), channel_id=1, source_target_pairs={{2,0},{4,2},{6,4},{8,6},{10,8},{12,10},{14,12},{3,1},{5,3},{7,5},{... | collective-permute-start | bytes 786440 | tf_op jit(solution)/shard_map/ppermute | solution.py:110
  64.0 1.2 %collective-permute-start.11 = (f32[2,4,1,256]{3,2,1,0:T(1,128)S(1)}, f32[2,4,1,256]{3,2,1,0:T(1,128)S(1)}, u32[]{:S(2)}, u32[]{:S(2)}) collective-permute-start(f32[2,4,1,256]{3,2,1,0:T(1,128)S(1)} %constant_dynamic-slice_fusion.2), channel_id=1, source_target_pairs={{0,1},{1,0},{2,3},{3,2},{4,5},{5,4},{6,7},{7,6},{8,9},{9,8},{10,11... | collective-permute-start | bytes 24584 | tf_op jit(solution)/shard_map/ppermute | solution.py:50
  66.1 1.2 %collective-permute-start.12 = (f32[2,4,1,256]{3,2,1,0:T(1,128)S(1)}, f32[2,4,1,256]{3,2,1,0:T(1,128)S(1)}, u32[]{:S(2)}, u32[]{:S(2)}) collective-permute-start(f32[2,4,1,256]{3,2,1,0:T(1,128)S(1)} %constant_dynamic-slice_fusion.1), channel_id=1, source_target_pairs={{0,1},{1,0},{2,3},{3,2},{4,5},{5,4},{6,7},{7,6},{8,9},{9,8},{10,11... | collective-permute-start | bytes 24584 | tf_op jit(solution)/shard_map/ppermute | solution.py:50
  67.7 11.0 %collective-permute-start.13 = (f32[4,1,64,256]{3,2,1,0:T(8,128)S(1)}, f32[4,1,64,256]{3,2,1,0:T(8,128)S(1)}, u32[]{:S(2)}, u32[]{:S(2)}) collective-permute-start(f32[4,1,64,256]{3,2,1,0:T(8,128)S(1)} %pad_maximum_fusion.45), channel_id=1, source_target_pairs={{2,0},{4,2},{6,4},{8,6},{10,8},{12,10},{14,12},{3,1},{5,3},{7,5},{... | collective-permute-start | bytes 786440 | tf_op jit(solution)/shard_map/ppermute | solution.py:110
  69.0 15.5 %collective-permute-start.14 = (f32[4,1,64,256]{3,2,1,0:T(8,128)S(1)}, f32[4,1,64,256]{3,2,1,0:T(8,128)S(1)}, u32[]{:S(2)}, u32[]{:S(2)}) collective-permute-start(f32[4,1,64,256]{3,2,1,0:T(8,128)S(1)} %pad_maximum_fusion.46), channel_id=1, source_target_pairs={{0,2},{2,4},{4,6},{6,8},{8,10},{10,12},{12,14},{1,3},{3,5},{5,7},{... | collective-permute-start | bytes 786440 | tf_op jit(solution)/shard_map/ppermute | solution.py:109
  85.3 1.2 %collective-permute-start.15 = (f32[2,4,1,256]{3,2,1,0:T(1,128)S(1)}, f32[2,4,1,256]{3,2,1,0:T(1,128)S(1)}, u32[]{:S(2)}, u32[]{:S(2)}) collective-permute-start(f32[2,4,1,256]{3,2,1,0:T(1,128)S(1)} %constant_dynamic-slice_fusion), channel_id=1, source_target_pairs={{0,1},{1,0},{2,3},{3,2},{4,5},{5,4},{6,7},{7,6},{8,9},{9,8},{10,11... | collective-permute-start | bytes 24584 | tf_op jit(solution)/shard_map/ppermute | solution.py:50
  87.1 1.1 copy-start.2
  88.2 0.8 copy-start.3
  89.0 1.3 %collective-permute-start.16 = (f32[]{:T(128)}, f32[]{:T(128)}, u32[]{:S(2)}, u32[]{:S(2)}) collective-permute-start(f32[]{:T(128)} %get-tuple-element.17), channel_id=1, source_target_pairs={{0,1},{1,0},{2,3},{3,2},{4,5},{5,4},{6,7},{7,6},{8,9},{9,8},{10,11... | collective-permute-start | bytes 20 | tf_op jit(solution)/shard_map/ppermute | solution.py:19
  92.3 5.2 %collective-permute-start.17 = (f32[65,256]{1,0:T(8,128)S(1)}, f32[65,256]{1,0:T(8,128)S(1)}, u32[]{:S(2)}, u32[]{:S(2)}) collective-permute-start(f32[65,256]{1,0:T(8,128)S(1)} %select_maximum_fusion), channel_id=1, source_target_pairs={{0,2},{2,0},{4,6},{6,4},{8,10},{10,8},{12,14},{14,12},{1,3},{3,1},... | collective-permute-start | bytes 199688 | tf_op jit(solution)/shard_map/ppermute | solution.py:28
  97.5 7.1 %collective-permute-start.20 = (f32[65,256]{1,0:T(8,128)S(1)}, f32[65,256]{1,0:T(8,128)S(1)}, u32[]{:S(2)}, u32[]{:S(2)}) collective-permute-start(f32[65,256]{1,0:T(8,128)S(1)} %fusion.256), channel_id=1, source_target_pairs={{0,12},{2,14},{4,8},{6,10},{8,4},{10,6},{12,0},{14,2},{1,13},{3,15... | collective-permute-start | bytes 199688 | tf_op jit(solution)/shard_map/ppermute | solution.py:33
  100.1 6.9 %collective-permute-start.19 = (f32[65,256]{1,0:T(8,128)S(1)}, f32[65,256]{1,0:T(8,128)S(1)}, u32[]{:S(2)}, u32[]{:S(2)}) collective-permute-start(f32[65,256]{1,0:T(8,128)S(1)} %fusion.256), channel_id=1, source_target_pairs={{0,8},{2,10},{4,12},{6,14},{8,0},{10,2},{12,4},{14,6},{1,9},{3,11}... | collective-permute-start | bytes 199688 | tf_op jit(solution)/shard_map/ppermute | solution.py:33
  100.6 6.5 %collective-permute-start.18 = (f32[65,256]{1,0:T(8,128)S(1)}, f32[65,256]{1,0:T(8,128)S(1)}, u32[]{:S(2)}, u32[]{:S(2)}) collective-permute-start(f32[65,256]{1,0:T(8,128)S(1)} %fusion.256), channel_id=1, source_target_pairs={{0,4},{2,6},{4,0},{6,2},{8,12},{10,14},{12,8},{14,10},{1,5},{3,7},... | collective-permute-start | bytes 199688 | tf_op jit(solution)/shard_map/ppermute | solution.py:33

commit v7 on v6

--- a/solution.py
+++ b/solution.py
@@ -88,10 +88,6 @@
     return apply_coef(lapl, field, coef)
 
 
-def cut(coef, lo, hi):
-    return tuple(c[lo:hi] for c in coef)
-
-
 def across(plane):
     return jnp.stack([0.5 * plane[1], -0.5 * plane[0]])
 
@@ -104,21 +100,21 @@
     down = [(i + 1, i) for i in range(nx - 1)]
     tall = y_extended(stage)
     zero_plane = jnp.zeros_like(stage[:, :1])
-    part_top = operator(tall[:, X - 1:], stage[:, X - 2:X - 1], zero_plane, cut(coef, X - 1, X))
-    part_bottom = operator(tall[:, :1], zero_plane, stage[:, 1:2], cut(coef, 0, 1))
+    part_top = operator(tall[:, X - 1:], stage[:, X - 2:X - 1], zero_plane, coef["top"])
+    part_bottom = operator(tall[:, :1], zero_plane, stage[:, 1:2], coef["bottom"])
     from_low = lax.ppermute(jnp.concatenate([stage[:, X - 1:], part_top]), "gx", up)
     from_high = lax.ppermute(jnp.concatenate([stage[:, :1], part_bottom]), "gx", down)
     stage_low, part_low = from_low[:2], from_low[2:]
     stage_high, part_high = from_high[:2], from_high[2:]
     if base_low is None:
         base_low, base_high = stage_low, stage_high
-    section = operator(tall, stage_low, stage_high, coef)
+    section = operator(tall, stage_low, stage_high, coef["all"])
     section_low = part_low + across(stage[:, :1])
     section_high = part_high + across(stage[:, X - 1:])
     nxt = base + weight * section
     nxt_low = jnp.where(ix > 0, base_low + weight * section_low, 0.0)
     nxt_high = jnp.where(ix < nx - 1, base_high + weight * section_high, 0.0)
-    section_next = operator(y_extended(nxt), nxt_low, nxt_high, coef)
+    section_next = operator(y_extended(nxt), nxt_low, nxt_high, coef["all"])
     return section, section_next, base_low, base_high
 
 
@@ -150,13 +146,20 @@
     first = lax.axis_index("gx") * planes
     x_index = (first + jnp.arange(planes, dtype=jnp.int32)).astype(jnp.float32)
     profile = 1.0 + 0.5 * jnp.cos(2.0 * math.pi * x_index / float(total_x))
-    coef_late = coefficients(psi_late, trap, controls[1], profile)
-    coef_early = coefficients(psi_early, trap, controls[0], profile)
+    def coefficient_set(psi, control):
+        return {
+            "all": coefficients(psi, trap, control, profile),
+            "top": coefficients(psi[:, planes - 1:], trap[planes - 1:], control, profile[planes - 1:]),
+            "bottom": coefficients(psi[:, :1], trap[:1], control, profile[:1]),
+        }
+
+    coef_late = coefficient_set(psi_late, controls[1])
+    coef_early = coefficient_set(psi_early, controls[0])
     chi_late = rk_step(chi_final, coef_late)
     chi_start = rk_step(chi_late, coef_early)
+    local_sq = axis_sum(jnp.sum(chi_start * chi_start), "gy")
     rows_late = row_terms(chi_late, psi_late, profile)
     rows_early = row_terms(chi_start, psi_early, profile)
-    local_sq = axis_sum(jnp.sum(chi_start * chi_start), "gy")
     extra = jnp.zeros((1, rows_early.shape[1]), jnp.float32).at[0, 0].set(local_sq)
     packed = gx_total(jnp.concatenate([rows_early, rows_late, extra], axis=0))
     squares = packed[-1, 0]

time: 111 us -> 122 us (1.099)
  local copies, waits for them, and re-layouts: 3.16 us -> 12.7 us
  other arithmetic: 11.5 us -> 14.1 us
  waiting for transfers between devices: 57 us -> 54.8 us
    ppermute x4, waiting for transfers between devices: 27.3 us -> 21.7 us  [stage_pair(): lax.ppermute(jnp.concatenate([stage[:, X - 1:], part_top]), 'gx', up)]
    ppermute x4, waiting for transfers between devices: 14.2 us -> 18.2 us  [stage_pair(): lax.ppermute(jnp.concatenate([stage[:, :1], part_bottom]), 'gx', down)]
    unnamed x8 -> x34, local copies, waits for them, and re-layouts: 0.54 us -> 3.63 us
    mul x2 -> x6, local copies, waits for them, and re-layouts: 0.09 us -> 3 us  [coefficients(): potential = trap + profile[:, None, None] * fine_control[None, :, :]]
    broadcast_in_dim x2 -> x6, local copies, waits for them, and re-layouts: 0.05 us -> 1.57 us  [coefficients(): fine_control = jnp.repeat(control, 2, axis=0)]
    add x1 -> x0, other arithmetic: 1.33 us -> none  [coefficients(): potential + 2.0 * COUPLING * (real_part * real_part + imag_part * imag_part)]
    mul x0 -> x1, other arithmetic: none -> 1.3 us  [coefficients(): potential = trap + profile[:, None, None] * fine_control[None, :, :]]
    ppermute x8, waiting for transfers between devices: 6.84 us -> 5.55 us  [y_extended(): other = lax.ppermute(strip, 'gy', [(0, 1), (1, 0)])]
  transfers between devices with their start and end apart: 21 -> 21, of which waited for: 18 -> 17; matrix products, arithmetic and copies ran while one was open for 3% -> 8% of each run, Pallas kernels for 0% -> 0%
where the time goes in v7:
time: 122 us; the launch traced here: 121 us
  waiting for transfers between devices  54.8 us (45%)
  starting transfers between devices  34.5 us (28%)
  other arithmetic  14.1 us (12%)
  local copies, waits for them, and re-layouts  12.7 us (10%)
  between operations  5.18 us (4%)
    ppermute x4, waiting for transfers between devices, stage_pair(): lax.ppermute(jnp.concatenate([stage[:, X - 1:], part_top]), 'gx', up)  21.7 us
    ppermute x4, starting transfers between devices, stage_pair(): lax.ppermute(jnp.concatenate([stage[:, X - 1:], part_top]), 'gx', up)  20.2 us
    ppermute x4, waiting for transfers between devices, stage_pair(): lax.ppermute(jnp.concatenate([stage[:, :1], part_bottom]), 'gx', down)  18.2 us
    ppermute x8, waiting for transfers between devices, y_extended(): other = lax.ppermute(strip, 'gy', [(0, 1), (1, 0)])  5.55 us
    ppermute x3, waiting for transfers between devices, gx_total(): lax.ppermute(pair, 'gx', [(i, i ^ 2 * k) for i in range(count)])  5.52 us
    ppermute x4, starting transfers between devices, stage_pair(): lax.ppermute(jnp.concatenate([stage[:, :1], part_bottom]), 'gx', down)  5.17 us
    sub x12, other arithmetic, operator(): lapl = total - 6.0 * field  4.58 us
    ppermute x3, starting transfers between devices, gx_total(): lax.ppermute(pair, 'gx', [(i, i ^ 2 * k) for i in range(count)])  4.45 us
  transfers between devices with their start and end apart: 21, of which 17 were waited for; matrix products, arithmetic and copies ran while one was open for 8% of the time, Pallas kernels for 0%

profile of v7, /device:TPU:0, one launch (start us, length us, event | category | flops | bytes accessed | tf_op | source)
XLA Modules:
  0.0 121.2 jit_solution(13358797060043142544)
XLA Ops:
  0.6 0.9 constant_dynamic-slice_fusion.7
  1.6 0.6 collective-permute-start
  2.1 1.0 fusion.261
  3.2 0.6 fusion.263
  4.0 1.3 %broadcast_multiply_fusion.2 = (f32[32,256]{1,0:T(8,128)S(1)}, f32[32,256]{1,0:T(8,128)S(1)}, f32[32,256]{1,0:T(8,128)S(1)}, f32[32,256]{1,0:T(8,128)S(1)}) fusion(f32[]{:T(128)} %bitcast.3, f32[2,32,256]{2,1,0:T(8,128)S(1)} %copy-done.13, f32[]{:T(128)} %bitcast.14), kind=kLoop, calls=%fused_computation.514 | loop fusion | flops 32768 | bytes 196616 | tf_op jit(solution)/shard_map/mul | solution.py:64
  5.7 0.8 copy-done.1
  6.8 1.3 %collective-permute-start.1 = (f32[4,1,64,256]{3,2,1,0:T(8,128)S(1)}, f32[4,1,64,256]{3,2,1,0:T(8,128)S(1)}, u32[]{:S(2)}, u32[]{:S(2)}) collective-permute-start(f32[4,1,64,256]{3,2,1,0:T(8,128)S(1)} %pad_maximum_fusion.39), channel_id=1, source_target_pairs={{2,0},{4,2},{6,4},{8,6},{10,8},{12,10},{14,12},{3,1},{5,3},{7,5},{... | collective-permute-start | bytes 786440 | tf_op jit(solution)/shard_map/ppermute | solution.py:106
  8.1 5.0 %collective-permute-start.2 = (f32[4,1,64,256]{3,2,1,0:T(8,128)S(1)}, f32[4,1,64,256]{3,2,1,0:T(8,128)S(1)}, u32[]{:S(2)}, u32[]{:S(2)}) collective-permute-start(f32[4,1,64,256]{3,2,1,0:T(8,128)S(1)} %pad_maximum_fusion.40), channel_id=1, source_target_pairs={{0,2},{2,4},{4,6},{6,8},{8,10},{10,12},{12,14},{1,3},{3,5},{5,7},{... | collective-permute-start | bytes 786440 | tf_op jit(solution)/shard_map/ppermute | solution.py:105
  13.1 0.6 slice_bitcast_fusion.14
  13.8 4.3 %collective-permute-done.1 = f32[4,1,64,256]{3,2,1,0:T(8,128)S(1)} collective-permute-done((f32[4,1,64,256]{3,2,1,0:T(8,128)S(1)}, f32[4,1,64,256]{3,2,1,0:T(8,128)S(1)}, u32[]{:S(2)}, u32[]{:S(2)}) %collective-permute-start.1) | collective-permute-done | bytes 262176 | tf_op jit(solution)/shard_map/ppermute | solution.py:106
  18.1 0.7 copy-done.10
  18.8 5.1 %collective-permute-done.2 = f32[4,1,64,256]{3,2,1,0:T(8,128)S(1)} collective-permute-done((f32[4,1,64,256]{3,2,1,0:T(8,128)S(1)}, f32[4,1,64,256]{3,2,1,0:T(8,128)S(1)}, u32[]{:S(2)}, u32[]{:S(2)}) %collective-permute-start.2) | collective-permute-done | bytes 262176 | tf_op jit(solution)/shard_map/ppermute | solution.py:105
  24.9 1.1 collective-permute-done.3
  26.9 1.0 collective-permute-done.4
  28.2 1.3 %collective-permute-start.5 = (f32[4,1,64,256]{3,2,1,0:T(8,128)S(1)}, f32[4,1,64,256]{3,2,1,0:T(8,128)S(1)}, u32[]{:S(2)}, u32[]{:S(2)}) collective-permute-start(f32[4,1,64,256]{3,2,1,0:T(8,128)S(1)} %pad_maximum_fusion.41), channel_id=1, source_target_pairs={{2,0},{4,2},{6,4},{8,6},{10,8},{12,10},{14,12},{3,1},{5,3},{7,5},{... | collective-permute-start | bytes 786440 | tf_op jit(solution)/shard_map/ppermute | solution.py:106
  29.6 5.1 %collective-permute-start.6 = (f32[4,1,64,256]{3,2,1,0:T(8,128)S(1)}, f32[4,1,64,256]{3,2,1,0:T(8,128)S(1)}, u32[]{:S(2)}, u32[]{:S(2)}) collective-permute-start(f32[4,1,64,256]{3,2,1,0:T(8,128)S(1)} %pad_maximum_fusion.42), channel_id=1, source_target_pairs={{0,2},{2,4},{4,6},{6,8},{8,10},{10,12},{12,14},{1,3},{3,5},{5,7},{... | collective-permute-start | bytes 786440 | tf_op jit(solution)/shard_map/ppermute | solution.py:105
  34.7 4.5 %collective-permute-done.5 = f32[4,1,64,256]{3,2,1,0:T(8,128)S(1)} collective-permute-done((f32[4,1,64,256]{3,2,1,0:T(8,128)S(1)}, f32[4,1,64,256]{3,2,1,0:T(8,128)S(1)}, u32[]{:S(2)}, u32[]{:S(2)}) %collective-permute-start.5) | collective-permute-done | bytes 262176 | tf_op jit(solution)/shard_map/ppermute | solution.py:106
  39.2 0.7 fusion.173
  39.9 5.1 %collective-permute-done.6 = f32[4,1,64,256]{3,2,1,0:T(8,128)S(1)} collective-permute-done((f32[4,1,64,256]{3,2,1,0:T(8,128)S(1)}, f32[4,1,64,256]{3,2,1,0:T(8,128)S(1)}, u32[]{:S(2)}, u32[]{:S(2)}) %collective-permute-start.6) | collective-permute-done | bytes 262176 | tf_op jit(solution)/shard_map/ppermute | solution.py:105
  45.0 0.7 fusion.170
  46.3 0.6 constant_dynamic-slice_fusion.4
  47.0 0.7 mul.1574
  47.7 0.7 mul.1592
  48.4 1.4 %broadcast_in_dim.44 = f32[32,2,256]{2,1,0:T(2,128)} broadcast(f32[32,256]{1,0:T(8,128)} %get-tuple-element.133), dimensions={0,2} | broadcast | bytes 98304 | tf_op jit(solution)/shard_map/broadcast_in_dim | solution.py:63
  49.8 1.5 %mul.1609 = f32[64,256]{1,0:T(8,128)} reshape(f32[32,2,256]{2,1,0:T(2,128)} %broadcast_in_dim.44) | data formatting | bytes 131072 | tf_op jit(solution)/shard_map/mul | solution.py:64
  51.4 1.3 %fusion.11 = f32[2,4,64,256]{3,2,1,0:T(8,128)S(1)} fusion(f32[2,4,64,256]{3,2,1,0:T(8,128)S(1)} %multiply_add_fusion.3, f32[2,4,1,256]{3,2,1,0:T(1,128)S(1)} %get-tuple-element.148, f32[2,4,1,256]{3,2,1,0:T(1,128)S(1)} %get-tuple-element.147, f32[2,1,64,256]{3,2,1,0:T(8,128)} %get-tuple-element.125, f32[2,1,64,256]{3,2,1,0:T(8,128)S(1)} %copy-done.12), kind=kLoop, calls=%fused_computation.27 | loop fusion | flops 1441792 | bytes 1327104 | tf_op jit(solution)/shard_map/sub | solution.py:87
  53.7 0.8 collective-permute-done.8
  54.8 0.8 copy-done.2
  55.8 1.3 %collective-permute-start.9 = (f32[4,1,64,256]{3,2,1,0:T(8,128)S(1)}, f32[4,1,64,256]{3,2,1,0:T(8,128)S(1)}, u32[]{:S(2)}, u32[]{:S(2)}) collective-permute-start(f32[4,1,64,256]{3,2,1,0:T(8,128)S(1)} %pad_maximum_fusion.43), channel_id=1, source_target_pairs={{2,0},{4,2},{6,4},{8,6},{10,8},{12,10},{14,12},{3,1},{5,3},{7,5},{... | collective-permute-start | bytes 786440 | tf_op jit(solution)/shard_map/ppermute | solution.py:106
  57.2 5.0 %collective-permute-start.10 = (f32[4,1,64,256]{3,2,1,0:T(8,128)S(1)}, f32[4,1,64,256]{3,2,1,0:T(8,128)S(1)}, u32[]{:S(2)}, u32[]{:S(2)}) collective-permute-start(f32[4,1,64,256]{3,2,1,0:T(8,128)S(1)} %pad_maximum_fusion.44), channel_id=1, source_target_pairs={{0,2},{2,4},{4,6},{6,8},{8,10},{10,12},{12,14},{1,3},{3,5},{5,7},{... | collective-permute-start | bytes 786440 | tf_op jit(solution)/shard_map/ppermute | solution.py:105
  62.2 4.8 %collective-permute-done.9 = f32[4,1,64,256]{3,2,1,0:T(8,128)S(1)} collective-permute-done((f32[4,1,64,256]{3,2,1,0:T(8,128)S(1)}, f32[4,1,64,256]{3,2,1,0:T(8,128)S(1)}, u32[]{:S(2)}, u32[]{:S(2)}) %collective-permute-start.9) | collective-permute-done | bytes 262176 | tf_op jit(solution)/shard_map/ppermute | solution.py:106
  67.0 5.8 %collective-permute-done.10 = f32[4,1,64,256]{3,2,1,0:T(8,128)S(1)} collective-permute-done((f32[4,1,64,256]{3,2,1,0:T(8,128)S(1)}, f32[4,1,64,256]{3,2,1,0:T(8,128)S(1)}, u32[]{:S(2)}, u32[]{:S(2)}) %collective-permute-start.10) | collective-permute-done | bytes 262176 | tf_op jit(solution)/shard_map/ppermute | solution.py:105
  74.4 1.1 collective-permute-done.11
  76.6 1.0 collective-permute-done.12
  78.0 1.3 %collective-permute-start.13 = (f32[4,1,64,256]{3,2,1,0:T(8,128)S(1)}, f32[4,1,64,256]{3,2,1,0:T(8,128)S(1)}, u32[]{:S(2)}, u32[]{:S(2)}) collective-permute-start(f32[4,1,64,256]{3,2,1,0:T(8,128)S(1)} %pad_maximum_fusion.45), channel_id=1, source_target_pairs={{2,0},{4,2},{6,4},{8,6},{10,8},{12,10},{14,12},{3,1},{5,3},{7,5},{... | collective-permute-start | bytes 786440 | tf_op jit(solution)/shard_map/ppermute | solution.py:106
  79.3 5.0 %collective-permute-start.14 = (f32[4,1,64,256]{3,2,1,0:T(8,128)S(1)}, f32[4,1,64,256]{3,2,1,0:T(8,128)S(1)}, u32[]{:S(2)}, u32[]{:S(2)}) collective-permute-start(f32[4,1,64,256]{3,2,1,0:T(8,128)S(1)} %pad_maximum_fusion.46), channel_id=1, source_target_pairs={{0,2},{2,4},{4,6},{6,8},{8,10},{10,12},{12,14},{1,3},{3,5},{5,7},{... | collective-permute-start | bytes 786440 | tf_op jit(solution)/shard_map/ppermute | solution.py:105
  84.4 4.6 %collective-permute-done.13 = f32[4,1,64,256]{3,2,1,0:T(8,128)S(1)} collective-permute-done((f32[4,1,64,256]{3,2,1,0:T(8,128)S(1)}, f32[4,1,64,256]{3,2,1,0:T(8,128)S(1)}, u32[]{:S(2)}, u32[]{:S(2)}) %collective-permute-start.13) | collective-permute-done | bytes 262176 | tf_op jit(solution)/shard_map/ppermute | solution.py:106
  89.0 5.7 %collective-permute-done.14 = f32[4,1,64,256]{3,2,1,0:T(8,128)S(1)} collective-permute-done((f32[4,1,64,256]{3,2,1,0:T(8,128)S(1)}, f32[4,1,64,256]{3,2,1,0:T(8,128)S(1)}, u32[]{:S(2)}, u32[]{:S(2)}) %collective-permute-start.14) | collective-permute-done | bytes 262176 | tf_op jit(solution)/shard_map/ppermute | solution.py:105
  95.7 0.6 compare_reduce_fusion
  97.3 1.1 multiply_reduce_fusion
  99.7 1.3 %collective-permute-done.16 = f32[]{:T(128)} collective-permute-done((f32[]{:T(128)}, f32[]{:T(128)}, u32[]{:S(2)}, u32[]{:S(2)}) %collective-permute-start.16) | collective-permute-done | bytes 36 | tf_op jit(solution)/shard_map/ppermute | solution.py:19
  103.0 2.5 %collective-permute-start.17 = (f32[65,256]{1,0:T(8,128)S(1)}, f32[65,256]{1,0:T(8,128)S(1)}, u32[]{:S(2)}, u32[]{:S(2)}) collective-permute-start(f32[65,256]{1,0:T(8,128)S(1)} %select_maximum_fusion), channel_id=1, source_target_pairs={{0,2},{2,0},{4,6},{6,4},{8,10},{10,8},{12,14},{14,12},{1,3},{3,1},... | collective-permute-start | bytes 199688 | tf_op jit(solution)/shard_map/ppermute | solution.py:28
  105.5 2.6 %collective-permute-done.17 = f32[65,256]{1,0:T(8,128)S(1)} collective-permute-done((f32[65,256]{1,0:T(8,128)S(1)}, f32[65,256]{1,0:T(8,128)S(1)}, u32[]{:S(2)}, u32[]{:S(2)}) %collective-permute-start.17) | collective-permute-done | bytes 66592 | tf_op jit(solution)/shard_map/ppermute | solution.py:28
  108.1 1.6 %collective-permute-start.18 = (f32[65,256]{1,0:T(8,128)S(1)}, f32[65,256]{1,0:T(8,128)S(1)}, u32[]{:S(2)}, u32[]{:S(2)}) collective-permute-start(f32[65,256]{1,0:T(8,128)S(1)} %fusion.254), channel_id=1, source_target_pairs={{0,4},{2,6},{4,0},{6,2},{8,12},{10,14},{12,8},{14,10},{1,5},{3,7},... | collective-permute-start | bytes 199688 | tf_op jit(solution)/shard_map/ppermute | solution.py:33
  109.7 1.1 collective-permute-start.19
  110.8 1.7 %collective-permute-start.20 = (f32[65,256]{1,0:T(8,128)S(1)}, f32[65,256]{1,0:T(8,128)S(1)}, u32[]{:S(2)}, u32[]{:S(2)}) collective-permute-start(f32[65,256]{1,0:T(8,128)S(1)} %fusion.254), channel_id=1, source_target_pairs={{0,12},{2,14},{4,8},{6,10},{8,4},{10,6},{12,0},{14,2},{1,13},{3,15... | collective-permute-start | bytes 199688 | tf_op jit(solution)/shard_map/ppermute | solution.py:33
  112.6 5.5 %collective-permute-done.19 = f32[65,256]{1,0:T(8,128)S(1)} collective-permute-done((f32[65,256]{1,0:T(8,128)S(1)}, f32[65,256]{1,0:T(8,128)S(1)}, u32[]{:S(2)}, u32[]{:S(2)}) %collective-permute-start.19) | collective-permute-done | bytes 66592 | tf_op jit(solution)/shard_map/ppermute | solution.py:33
  119.4 0.6 maximum_divide_fusion
  (134 shorter events, 12.1 us)
Async XLA Ops:
  0.6 2.5 %copy-start = (f32[2,4,64,256]{3,2,1,0:T(8,128)S(1)}, f32[2,4,64,256]{3,2,1,0:T(8,128)}, u32[]{:S(2)}) copy-start(f32[2,4,64,256]{3,2,1,0:T(8,128)} %param.7) | copy-start | bytes 1572868
  1.6 3.9 %collective-permute-start = (f32[2,4,1,256]{3,2,1,0:T(1,128)S(1)}, f32[2,4,1,256]{3,2,1,0:T(1,128)S(1)}, u32[]{:S(2)}, u32[]{:S(2)}) collective-permute-start(f32[2,4,1,256]{3,2,1,0:T(1,128)S(1)} %constant_dynamic-slice_fusion.7), channel_id=1, source_target_pairs={{0,1},{1,0},{2,3},{3,2},{4,5},{5,4},{6,7},{7,6},{8,9},{9,8},{10,11... | collective-permute-start | bytes 24584 | tf_op jit(solution)/shard_map/ppermute | solution.py:50
  3.1 0.8 copy-start.13
  5.5 1.0 copy-start.1
  5.5 1.1 copy-start.7
  6.8 11.4 %collective-permute-start.1 = (f32[4,1,64,256]{3,2,1,0:T(8,128)S(1)}, f32[4,1,64,256]{3,2,1,0:T(8,128)S(1)}, u32[]{:S(2)}, u32[]{:S(2)}) collective-permute-start(f32[4,1,64,256]{3,2,1,0:T(8,128)S(1)} %pad_maximum_fusion.39), channel_id=1, source_target_pairs={{2,0},{4,2},{6,4},{8,6},{10,8},{12,10},{14,12},{3,1},{5,3},{7,5},{... | collective-permute-start | bytes 786440 | tf_op jit(solution)/shard_map/ppermute | solution.py:106
  8.1 15.8 %collective-permute-start.2 = (f32[4,1,64,256]{3,2,1,0:T(8,128)S(1)}, f32[4,1,64,256]{3,2,1,0:T(8,128)S(1)}, u32[]{:S(2)}, u32[]{:S(2)}) collective-permute-start(f32[4,1,64,256]{3,2,1,0:T(8,128)S(1)} %pad_maximum_fusion.40), channel_id=1, source_target_pairs={{0,2},{2,4},{4,6},{6,8},{8,10},{10,12},{12,14},{1,3},{3,5},{5,7},{... | collective-permute-start | bytes 786440 | tf_op jit(solution)/shard_map/ppermute | solution.py:105
  18.1 0.7 copy-start.10
  24.5 21.6 %copy-start.3 = (f32[4,64,256]{2,1,0:T(8,128)}, f32[4,64,256]{2,1,0:T(8,128)S(1)}, u32[]{:S(2)}) copy-start(f32[4,64,256]{2,1,0:T(8,128)S(1)} %get-tuple-element.34) | copy-start | bytes 786436
  24.7 21.4 %copy-start.5 = (f32[4,64,256]{2,1,0:T(8,128)}, f32[4,64,256]{2,1,0:T(8,128)S(1)}, u32[]{:S(2)}) copy-start(f32[4,64,256]{2,1,0:T(8,128)S(1)} %get-tuple-element.38) | copy-start | bytes 786436
  24.8 1.2 %collective-permute-start.3 = (f32[2,4,1,256]{3,2,1,0:T(1,128)S(1)}, f32[2,4,1,256]{3,2,1,0:T(1,128)S(1)}, u32[]{:S(2)}, u32[]{:S(2)}) collective-permute-start(f32[2,4,1,256]{3,2,1,0:T(1,128)S(1)} %constant_dynamic-slice_fusion.6), channel_id=1, source_target_pairs={{0,1},{1,0},{2,3},{3,2},{4,5},{5,4},{6,7},{7,6},{8,9},{9,8},{10,11... | collective-permute-start | bytes 24584 | tf_op jit(solution)/shard_map/ppermute | solution.py:50
  26.7 1.2 %collective-permute-start.4 = (f32[2,4,1,256]{3,2,1,0:T(1,128)S(1)}, f32[2,4,1,256]{3,2,1,0:T(1,128)S(1)}, u32[]{:S(2)}, u32[]{:S(2)}) collective-permute-start(f32[2,4,1,256]{3,2,1,0:T(1,128)S(1)} %constant_dynamic-slice_fusion.5), channel_id=1, source_target_pairs={{0,1},{1,0},{2,3},{3,2},{4,5},{5,4},{6,7},{7,6},{8,9},{9,8},{10,11... | collective-permute-start | bytes 24584 | tf_op jit(solution)/shard_map/ppermute | solution.py:50
  28.2 11.0 %collective-permute-start.5 = (f32[4,1,64,256]{3,2,1,0:T(8,128)S(1)}, f32[4,1,64,256]{3,2,1,0:T(8,128)S(1)}, u32[]{:S(2)}, u32[]{:S(2)}) collective-permute-start(f32[4,1,64,256]{3,2,1,0:T(8,128)S(1)} %pad_maximum_fusion.41), channel_id=1, source_target_pairs={{2,0},{4,2},{6,4},{8,6},{10,8},{12,10},{14,12},{3,1},{5,3},{7,5},{... | collective-permute-start | bytes 786440 | tf_op jit(solution)/shard_map/ppermute | solution.py:106
  29.6 9.7 %copy-start.11 = (f32[4,1,64,256]{3,2,1,0:T(8,128)S(1)}, f32[4,1,64,256]{3,2,1,0:T(8,128)}, u32[]{:S(2)}) copy-start(f32[4,1,64,256]{3,2,1,0:T(8,128)} %copy-done.10) | copy-start | bytes 786436
  29.6 15.4 %collective-permute-start.6 = (f32[4,1,64,256]{3,2,1,0:T(8,128)S(1)}, f32[4,1,64,256]{3,2,1,0:T(8,128)S(1)}, u32[]{:S(2)}, u32[]{:S(2)}) collective-permute-start(f32[4,1,64,256]{3,2,1,0:T(8,128)S(1)} %pad_maximum_fusion.42), channel_id=1, source_target_pairs={{0,2},{2,4},{4,6},{6,8},{8,10},{10,12},{12,14},{1,3},{3,5},{5,7},{... | collective-permute-start | bytes 786440 | tf_op jit(solution)/shard_map/ppermute | solution.py:105
  46.9 4.4 %collective-permute-start.7 = (f32[2,4,1,256]{3,2,1,0:T(1,128)}, f32[2,4,1,256]{3,2,1,0:T(1,128)S(1)}, u32[]{:S(2)}, u32[]{:S(2)}) collective-permute-start(f32[2,4,1,256]{3,2,1,0:T(1,128)} %constant_dynamic-slice_fusion.4), channel_id=1, source_target_pairs={{0,1},{1,0},{2,3},{3,2},{4,5},{5,4},{6,7},{7,6},{8,9},{9,8},{10,11... | collective-permute-start | bytes 24584 | tf_op jit(solution)/shard_map/ppermute | solution.py:50
  48.4 3.0 %copy-start.12 = (f32[2,1,64,256]{3,2,1,0:T(8,128)S(1)}, f32[2,1,64,256]{3,2,1,0:T(8,128)}, u32[]{:S(2)}) copy-start(f32[2,1,64,256]{3,2,1,0:T(8,128)} %get-tuple-element.123) | copy-start | bytes 393220
  51.4 1.3 %copy-start.4 = (f32[4,64,256]{2,1,0:T(8,128)S(1)}, f32[4,64,256]{2,1,0:T(8,128)}, u32[]{:S(2)}) copy-start(f32[4,64,256]{2,1,0:T(8,128)} %copy-done.3) | copy-start | bytes 786436
  51.4 1.3 %copy-start.6 = (f32[4,64,256]{2,1,0:T(8,128)S(1)}, f32[4,64,256]{2,1,0:T(8,128)}, u32[]{:S(2)}) copy-start(f32[4,64,256]{2,1,0:T(8,128)} %copy-done.5) | copy-start | bytes 786436
  53.1 1.4 %collective-permute-start.8 = (f32[2,4,1,256]{3,2,1,0:T(1,128)S(1)}, f32[2,4,1,256]{3,2,1,0:T(1,128)S(1)}, u32[]{:S(2)}, u32[]{:S(2)}) collective-permute-start(f32[2,4,1,256]{3,2,1,0:T(1,128)S(1)} %constant_dynamic-slice_fusion.3), channel_id=1, source_target_pairs={{0,1},{1,0},{2,3},{3,2},{4,5},{5,4},{6,7},{7,6},{8,9},{9,8},{10,11... | collective-permute-start | bytes 24584 | tf_op jit(solution)/shard_map/ppermute | solution.py:50
  54.5 1.0 copy-start.2
  54.6 1.1 copy-start.8
  54.6 1.1 copy-start.15
  54.6 1.1 copy-start.16
  55.8 11.2 %collective-permute-start.9 = (f32[4,1,64,256]{3,2,1,0:T(8,128)S(1)}, f32[4,1,64,256]{3,2,1,0:T(8,128)S(1)}, u32[]{:S(2)}, u32[]{:S(2)}) collective-permute-start(f32[4,1,64,256]{3,2,1,0:T(8,128)S(1)} %pad_maximum_fusion.43), channel_id=1, source_target_pairs={{2,0},{4,2},{6,4},{8,6},{10,8},{12,10},{14,12},{3,1},{5,3},{7,5},{... | collective-permute-start | bytes 786440 | tf_op jit(solution)/shard_map/ppermute | solution.py:106
  57.2 15.6 %collective-permute-start.10 = (f32[4,1,64,256]{3,2,1,0:T(8,128)S(1)}, f32[4,1,64,256]{3,2,1,0:T(8,128)S(1)}, u32[]{:S(2)}, u32[]{:S(2)}) collective-permute-start(f32[4,1,64,256]{3,2,1,0:T(8,128)S(1)} %pad_maximum_fusion.44), channel_id=1, source_target_pairs={{0,2},{2,4},{4,6},{6,8},{8,10},{10,12},{12,14},{1,3},{3,5},{5,7},{... | collective-permute-start | bytes 786440 | tf_op jit(solution)/shard_map/ppermute | solution.py:105
  72.8 0.8 copy-start.14
  74.3 1.2 %collective-permute-start.11 = (f32[2,4,1,256]{3,2,1,0:T(1,128)S(1)}, f32[2,4,1,256]{3,2,1,0:T(1,128)S(1)}, u32[]{:S(2)}, u32[]{:S(2)}) collective-permute-start(f32[2,4,1,256]{3,2,1,0:T(1,128)S(1)} %constant_dynamic-slice_fusion.2), channel_id=1, source_target_pairs={{0,1},{1,0},{2,3},{3,2},{4,5},{5,4},{6,7},{7,6},{8,9},{9,8},{10,11... | collective-permute-start | bytes 24584 | tf_op jit(solution)/shard_map/ppermute | solution.py:50
  76.4 1.2 %collective-permute-start.12 = (f32[2,4,1,256]{3,2,1,0:T(1,128)S(1)}, f32[2,4,1,256]{3,2,1,0:T(1,128)S(1)}, u32[]{:S(2)}, u32[]{:S(2)}) collective-permute-start(f32[2,4,1,256]{3,2,1,0:T(1,128)S(1)} %constant_dynamic-slice_fusion.1), channel_id=1, source_target_pairs={{0,1},{1,0},{2,3},{3,2},{4,5},{5,4},{6,7},{7,6},{8,9},{9,8},{10,11... | collective-permute-start | bytes 24584 | tf_op jit(solution)/shard_map/ppermute | solution.py:50
  78.0 11.0 %collective-permute-start.13 = (f32[4,1,64,256]{3,2,1,0:T(8,128)S(1)}, f32[4,1,64,256]{3,2,1,0:T(8,128)S(1)}, u32[]{:S(2)}, u32[]{:S(2)}) collective-permute-start(f32[4,1,64,256]{3,2,1,0:T(8,128)S(1)} %pad_maximum_fusion.45), channel_id=1, source_target_pairs={{2,0},{4,2},{6,4},{8,6},{10,8},{12,10},{14,12},{3,1},{5,3},{7,5},{... | collective-permute-start | bytes 786440 | tf_op jit(solution)/shard_map/ppermute | solution.py:106
  79.3 15.5 %collective-permute-start.14 = (f32[4,1,64,256]{3,2,1,0:T(8,128)S(1)}, f32[4,1,64,256]{3,2,1,0:T(8,128)S(1)}, u32[]{:S(2)}, u32[]{:S(2)}) collective-permute-start(f32[4,1,64,256]{3,2,1,0:T(8,128)S(1)} %pad_maximum_fusion.46), channel_id=1, source_target_pairs={{0,2},{2,4},{4,6},{6,8},{8,10},{10,12},{12,14},{1,3},{3,5},{5,7},{... | collective-permute-start | bytes 786440 | tf_op jit(solution)/shard_map/ppermute | solution.py:105
  95.6 1.2 %collective-permute-start.15 = (f32[2,4,1,256]{3,2,1,0:T(1,128)S(1)}, f32[2,4,1,256]{3,2,1,0:T(1,128)S(1)}, u32[]{:S(2)}, u32[]{:S(2)}) collective-permute-start(f32[2,4,1,256]{3,2,1,0:T(1,128)S(1)} %constant_dynamic-slice_fusion), channel_id=1, source_target_pairs={{0,1},{1,0},{2,3},{3,2},{4,5},{5,4},{6,7},{7,6},{8,9},{9,8},{10,11... | collective-permute-start | bytes 24584 | tf_op jit(solution)/shard_map/ppermute | solution.py:50
  98.5 0.8 copy-start.9
  99.5 1.5 %collective-permute-start.16 = (f32[]{:T(128)}, f32[]{:T(128)}, u32[]{:S(2)}, u32[]{:S(2)}) collective-permute-start(f32[]{:T(128)} %get-tuple-element.17), channel_id=1, source_target_pairs={{0,1},{1,0},{2,3},{3,2},{4,5},{5,4},{6,7},{7,6},{8,9},{9,8},{10,11... | collective-permute-start | bytes 20 | tf_op jit(solution)/shard_map/ppermute | solution.py:19
  103.0 5.1 %collective-permute-start.17 = (f32[65,256]{1,0:T(8,128)S(1)}, f32[65,256]{1,0:T(8,128)S(1)}, u32[]{:S(2)}, u32[]{:S(2)}) collective-permute-start(f32[65,256]{1,0:T(8,128)S(1)} %select_maximum_fusion), channel_id=1, source_target_pairs={{0,2},{2,0},{4,6},{6,4},{8,10},{10,8},{12,14},{14,12},{1,3},{3,1},... | collective-permute-start | bytes 199688 | tf_op jit(solution)/shard_map/ppermute | solution.py:28
  108.1 4.5 %collective-permute-start.18 = (f32[65,256]{1,0:T(8,128)S(1)}, f32[65,256]{1,0:T(8,128)S(1)}, u32[]{:S(2)}, u32[]{:S(2)}) collective-permute-start(f32[65,256]{1,0:T(8,128)S(1)} %fusion.254), channel_id=1, source_target_pairs={{0,4},{2,6},{4,0},{6,2},{8,12},{10,14},{12,8},{14,10},{1,5},{3,7},... | collective-permute-start | bytes 199688 | tf_op jit(solution)/shard_map/ppermute | solution.py:33
  109.7 8.3 %collective-permute-start.19 = (f32[65,256]{1,0:T(8,128)S(1)}, f32[65,256]{1,0:T(8,128)S(1)}, u32[]{:S(2)}, u32[]{:S(2)}) collective-permute-start(f32[65,256]{1,0:T(8,128)S(1)} %fusion.254), channel_id=1, source_target_pairs={{0,8},{2,10},{4,12},{6,14},{8,0},{10,2},{12,4},{14,6},{1,9},{3,11}... | collective-permute-start | bytes 199688 | tf_op jit(solution)/shard_map/ppermute | solution.py:33
  110.8 7.2 %collective-permute-start.20 = (f32[65,256]{1,0:T(8,128)S(1)}, f32[65,256]{1,0:T(8,128)S(1)}, u32[]{:S(2)}, u32[]{:S(2)}) collective-permute-start(f32[65,256]{1,0:T(8,128)S(1)} %fusion.254), channel_id=1, source_target_pairs={{0,12},{2,14},{4,8},{6,10},{8,4},{10,6},{12,0},{14,2},{1,13},{3,15... | collective-permute-start | bytes 199688 | tf_op jit(solution)/shard_map/ppermute | solution.py:33

commit v8 on v6

--- a/solution.py
+++ b/solution.py
@@ -96,13 +96,18 @@
     return jnp.stack([0.5 * plane[1], -0.5 * plane[0]])
 
 
-def stage_pair(stage, base, base_low, base_high, coef, weight):
+def zero_extended(block):
+    zero = jnp.zeros_like(block[:, :, :1])
+    return jnp.concatenate([zero, block, zero], axis=2)
+
+
+def stage_pair(stage, base, base_low, base_high, coef, weight, extend_y):
     nx = lax.axis_size("gx")
     ix = lax.axis_index("gx")
     X = stage.shape[1]
     up = [(i, i + 1) for i in range(nx - 1)]
     down = [(i + 1, i) for i in range(nx - 1)]
-    tall = y_extended(stage)
+    tall = extend_y(stage)
     zero_plane = jnp.zeros_like(stage[:, :1])
     part_top = operator(tall[:, X - 1:], stage[:, X - 2:X - 1], zero_plane, cut(coef, X - 1, X))
     part_bottom = operator(tall[:, :1], zero_plane, stage[:, 1:2], cut(coef, 0, 1))
@@ -118,20 +123,57 @@
     nxt = base + weight * section
     nxt_low = jnp.where(ix > 0, base_low + weight * section_low, 0.0)
     nxt_high = jnp.where(ix < nx - 1, base_high + weight * section_high, 0.0)
-    section_next = operator(y_extended(nxt), nxt_low, nxt_high, coef)
+    section_next = operator(extend_y(nxt), nxt_low, nxt_high, coef)
     return section, section_next, base_low, base_high
 
 
-def rk_step(field, coef):
+CHAIN = 40
+
+
+def rk_chain(field, coef, extend_y):
     section_one, section_two, low, high = stage_pair(
-        field, field, None, None, coef, 0.5 * STEP_SIZE
+        field, field, None, None, coef, 0.5 * STEP_SIZE, extend_y
     )
     stage_three = field + 0.5 * STEP_SIZE * section_two
     section_three, section_four, _, _ = stage_pair(
-        stage_three, field, low, high, coef, STEP_SIZE
+        stage_three, field, low, high, coef, STEP_SIZE, extend_y
     )
     return field + STEP_SIZE / 6.0 * (
         section_one + 2.0 * section_two + 2.0 * section_three + section_four
+    )
+
+
+def rk_step(field, coef):
+    rows = field.shape[2]
+    half = rows // 2
+    if lax.axis_size("gy") != 2 or rows % 2 or CHAIN > rows or CHAIN - half < 4:
+        return rk_chain(field, coef, y_extended)
+    iy = lax.axis_index("gy")
+    spare = CHAIN - half
+    chains = []
+    for start, keep, extend_y in (
+        ((1 - iy) * (rows - CHAIN), (1 - iy) * spare, y_extended),
+        (iy * (rows - CHAIN), iy * spare, zero_extended),
+    ):
+        part = lax.dynamic_slice_in_dim(field, start, CHAIN, axis=2)
+        part_coef = tuple(lax.dynamic_slice_in_dim(c, start, CHAIN, axis=1) for c in coef)
+        chains.append((part, part_coef, extend_y, keep))
+    (fa, ca, ea, ka), (fb, cb, eb, kb) = chains
+    a1, a2, a_low, a_high = stage_pair(fa, fa, None, None, ca, 0.5 * STEP_SIZE, ea)
+    fb, a1 = lax.optimization_barrier((fb, a1))
+    b1, b2, b_low, b_high = stage_pair(fb, fb, None, None, cb, 0.5 * STEP_SIZE, eb)
+    a3, a4, _, _ = stage_pair(fa + 0.5 * STEP_SIZE * a2, fa, a_low, a_high, ca, STEP_SIZE, ea)
+    b_three, a3 = lax.optimization_barrier((fb + 0.5 * STEP_SIZE * b2, a3))
+    b3, b4, _, _ = stage_pair(b_three, fb, b_low, b_high, cb, STEP_SIZE, eb)
+    kept = []
+    for f, s1, s2, s3, s4, keep in ((fa, a1, a2, a3, a4, ka), (fb, b1, b2, b3, b4, kb)):
+        out = f + STEP_SIZE / 6.0 * (s1 + 2.0 * s2 + 2.0 * s3 + s4)
+        kept.append(lax.dynamic_slice_in_dim(out, keep, half, axis=2))
+    near, far = kept
+    return jnp.where(
+        iy == 0,
+        jnp.concatenate([far, near], axis=2),
+        jnp.concatenate([near, far], axis=2),
     )
 
 

time: 111 us -> 152 us (1.37)
  starting transfers between devices: 33.5 us -> 59.4 us
  other arithmetic: 11.5 us -> 20 us
  local copies, waits for them, and re-layouts: 3.16 us -> 8.4 us
    ppermute x4 -> x8, starting transfers between devices: 19.5 us -> 40.3 us  [stage_pair(): lax.ppermute(jnp.concatenate([stage[:, X - 1:], part_top]), 'gx', up)]
    ppermute x4 -> x8, starting transfers between devices: 5.17 us -> 10.3 us  [stage_pair(): lax.ppermute(jnp.concatenate([stage[:, :1], part_bottom]), 'gx', down)]
    ppermute x8, waiting for transfers between devices: 6.84 us -> 2.71 us  [y_extended(): other = lax.ppermute(strip, 'gy', [(0, 1), (1, 0)])]
    ppermute x4 -> x8, waiting for transfers between devices: 14.2 us -> 17.5 us  [stage_pair(): lax.ppermute(jnp.concatenate([stage[:, :1], part_bottom]), 'gx', down)]
    unnamed x8 -> x32, local copies, waits for them, and re-layouts: 0.54 us -> 3.48 us
    sub x12 -> x28, other arithmetic: 3.63 us -> 6.46 us  [operator(): lapl = total - 6.0 * field]
    select_n x4 -> x8, other arithmetic: 0.16 us -> 2.03 us  [stage_pair(): nxt_high = jnp.where(ix < nx - 1, base_high + weight * section_high, 0.0)]
    another operation x16 -> x20, other arithmetic: 1.58 us -> 3.36 us  [apply_coef(): return jnp.stack([-lower, upper])]
  transfers between devices with their start and end apart: 21 -> 29, of which waited for: 18 -> 23; matrix products, arithmetic and copies ran while one was open for 3% -> 7% of each run, Pallas kernels for 0% -> 0%
where the time goes in v8:
time: 152 us; the launch traced here: 151 us
  starting transfers between devices  59.4 us (39%)
  waiting for transfers between devices  58.1 us (38%)
  other arithmetic  20 us (13%)
  local copies, waits for them, and re-layouts  8.4 us (6%)
  between operations  5.44 us (4%)
    ppermute x8, starting transfers between devices, stage_pair(): lax.ppermute(jnp.concatenate([stage[:, X - 1:], part_top]), 'gx', up)  40.3 us
    ppermute x8, waiting for transfers between devices, stage_pair(): lax.ppermute(jnp.concatenate([stage[:, X - 1:], part_top]), 'gx', up)  27.7 us
    ppermute x8, waiting for transfers between devices, stage_pair(): lax.ppermute(jnp.concatenate([stage[:, :1], part_bottom]), 'gx', down)  17.5 us
    ppermute x8, starting transfers between devices, stage_pair(): lax.ppermute(jnp.concatenate([stage[:, :1], part_bottom]), 'gx', down)  10.3 us
    sub x28, other arithmetic, operator(): lapl = total - 6.0 * field  6.46 us
    ppermute x3, waiting for transfers between devices, gx_total(): lax.ppermute(pair, 'gx', [(i, i ^ 2 * k) for i in range(count)])  6.15 us
    ppermute x3, starting transfers between devices, gx_total(): lax.ppermute(pair, 'gx', [(i, i ^ 2 * k) for i in range(count)])  4.85 us
    unnamed x32, local copies, waits for them, and re-layouts  3.48 us
  transfers between devices with their start and end apart: 29, of which 23 were waited for; matrix products, arithmetic and copies ran while one was open for 7% of the time, Pallas kernels for 0%

profile of v8, /device:TPU:0, one launch (start us, length us, event | category | flops | bytes accessed | tf_op | source)
XLA Modules:
  0.0 151.4 jit_solution(4962488434546327530)
XLA Ops:
  2.1 1.2 constant_dynamic-slice_fusion.15
  5.9 0.9 copy-done.6
  7.0 0.9 copy-done
  9.2 1.3 fusion.304
  10.5 1.5 %fusion.557 = (f32[1,1,40,256]{3,2,1,0:T(8,128)S(1)}, f32[1,1,40,256]{3,2,1,0:T(8,128)S(1)}, f32[1,1,40,256]{3,2,1,0:T(8,128)}, f32[1,1,40,256]{3,2,1,0:T(8,128)}) fusion(f32[2,1,40,256]{3,2,1,0:T(8,128)S(1)} %get-tuple-element.133, f32[2,4,64,256]{3,2,1,0:T(8,128)S(1)} %copy-done, s32[]{:T(128)S(6)} %select_n.214, s32[]{:T(128)S(6)} %add.1642, ...), kind=kLoop, calls=%fused_computation.961 | loop fusion | flops 266240 | bytes 737292 | tf_op jit(solution)/shard_map/stack | solution.py:77
  12.7 1.3 collective-permute-start.1
  15.3 1.0 pad_maximum_fusion.62
  16.3 5.1 %collective-permute-start.2 = (f32[4,1,40,256]{3,2,1,0:T(8,128)S(1)}, f32[4,1,40,256]{3,2,1,0:T(8,128)S(1)}, u32[]{:S(2)}, u32[]{:S(2)}) collective-permute-start(f32[4,1,40,256]{3,2,1,0:T(8,128)S(1)} %pad_maximum_fusion.62), channel_id=1, source_target_pairs={{0,2},{2,4},{4,6},{6,8},{8,10},{10,12},{12,14},{1,3},{3,5},{5,7},{... | collective-permute-start | bytes 491528 | tf_op jit(solution)/shard_map/ppermute | solution.py:114
  21.4 0.9 collective-permute-done.1
  22.3 1.0 fusion.407
  23.2 2.6 %collective-permute-done.2 = f32[4,1,40,256]{3,2,1,0:T(8,128)S(1)} collective-permute-done((f32[4,1,40,256]{3,2,1,0:T(8,128)S(1)}, f32[4,1,40,256]{3,2,1,0:T(8,128)S(1)}, u32[]{:S(2)}, u32[]{:S(2)}) %collective-permute-start.2) | collective-permute-done | bytes 163872 | tf_op jit(solution)/shard_map/ppermute | solution.py:114
  27.4 1.3 collective-permute-start.3
  28.7 5.0 %collective-permute-start.4 = (f32[4,1,40,256]{3,2,1,0:T(8,128)S(1)}, f32[4,1,40,256]{3,2,1,0:T(8,128)S(1)}, u32[]{:S(2)}, u32[]{:S(2)}) collective-permute-start(f32[4,1,40,256]{3,2,1,0:T(8,128)S(1)} %pad_maximum_fusion.64), channel_id=1, source_target_pairs={{0,2},{2,4},{4,6},{6,8},{8,10},{10,12},{12,14},{1,3},{3,5},{5,7},{... | collective-permute-start | bytes 491528 | tf_op jit(solution)/shard_map/ppermute | solution.py:114
  34.0 2.6 %collective-permute-done.3 = f32[4,1,40,256]{3,2,1,0:T(8,128)S(1)} collective-permute-done((f32[4,1,40,256]{3,2,1,0:T(8,128)S(1)}, f32[4,1,40,256]{3,2,1,0:T(8,128)S(1)}, u32[]{:S(2)}, u32[]{:S(2)}) %collective-permute-start.3) | collective-permute-done | bytes 163872 | tf_op jit(solution)/shard_map/ppermute | solution.py:115
  36.7 4.2 %collective-permute-done.4 = f32[4,1,40,256]{3,2,1,0:T(8,128)S(1)} collective-permute-done((f32[4,1,40,256]{3,2,1,0:T(8,128)S(1)}, f32[4,1,40,256]{3,2,1,0:T(8,128)S(1)}, u32[]{:S(2)}, u32[]{:S(2)}) %collective-permute-start.4) | collective-permute-done | bytes 163872 | tf_op jit(solution)/shard_map/ppermute | solution.py:114
  42.8 1.3 collective-permute-start.7
  44.2 5.0 %collective-permute-start.8 = (f32[4,1,40,256]{3,2,1,0:T(8,128)S(1)}, f32[4,1,40,256]{3,2,1,0:T(8,128)S(1)}, u32[]{:S(2)}, u32[]{:S(2)}) collective-permute-start(f32[4,1,40,256]{3,2,1,0:T(8,128)S(1)} %pad_maximum_fusion.66), channel_id=1, source_target_pairs={{0,2},{2,4},{4,6},{6,8},{8,10},{10,12},{12,14},{1,3},{3,5},{5,7},{... | collective-permute-start | bytes 491528 | tf_op jit(solution)/shard_map/ppermute | solution.py:114
  49.2 2.5 %collective-permute-done.7 = f32[4,1,40,256]{3,2,1,0:T(8,128)S(1)} collective-permute-done((f32[4,1,40,256]{3,2,1,0:T(8,128)S(1)}, f32[4,1,40,256]{3,2,1,0:T(8,128)S(1)}, u32[]{:S(2)}, u32[]{:S(2)}) %collective-permute-start.7) | collective-permute-done | bytes 163872 | tf_op jit(solution)/shard_map/ppermute | solution.py:115
  51.7 0.9 fusion.395
  52.7 2.8 %collective-permute-done.8 = f32[4,1,40,256]{3,2,1,0:T(8,128)S(1)} collective-permute-done((f32[4,1,40,256]{3,2,1,0:T(8,128)S(1)}, f32[4,1,40,256]{3,2,1,0:T(8,128)S(1)}, u32[]{:S(2)}, u32[]{:S(2)}) %collective-permute-start.8) | collective-permute-done | bytes 163872 | tf_op jit(solution)/shard_map/ppermute | solution.py:114
  56.4 1.3 collective-permute-start.9
  57.8 5.0 %collective-permute-start.10 = (f32[4,1,40,256]{3,2,1,0:T(8,128)S(1)}, f32[4,1,40,256]{3,2,1,0:T(8,128)S(1)}, u32[]{:S(2)}, u32[]{:S(2)}) collective-permute-start(f32[4,1,40,256]{3,2,1,0:T(8,128)S(1)} %pad_maximum_fusion.68), channel_id=1, source_target_pairs={{0,2},{2,4},{4,6},{6,8},{8,10},{10,12},{12,14},{1,3},{3,5},{5,7},{... | collective-permute-start | bytes 491528 | tf_op jit(solution)/shard_map/ppermute | solution.py:114
  63.1 2.6 %collective-permute-done.9 = f32[4,1,40,256]{3,2,1,0:T(8,128)S(1)} collective-permute-done((f32[4,1,40,256]{3,2,1,0:T(8,128)S(1)}, f32[4,1,40,256]{3,2,1,0:T(8,128)S(1)}, u32[]{:S(2)}, u32[]{:S(2)}) %collective-permute-start.9) | collective-permute-done | bytes 163872 | tf_op jit(solution)/shard_map/ppermute | solution.py:115
  65.7 3.6 %collective-permute-done.10 = f32[4,1,40,256]{3,2,1,0:T(8,128)S(1)} collective-permute-done((f32[4,1,40,256]{3,2,1,0:T(8,128)S(1)}, f32[4,1,40,256]{3,2,1,0:T(8,128)S(1)}, u32[]{:S(2)}, u32[]{:S(2)}) %collective-permute-start.10) | collective-permute-done | bytes 163872 | tf_op jit(solution)/shard_map/ppermute | solution.py:114
  70.7 1.1 collective-permute-done.12
  72.0 1.3 collective-permute-start.13
  73.4 5.0 %collective-permute-start.14 = (f32[4,1,40,256]{3,2,1,0:T(8,128)S(1)}, f32[4,1,40,256]{3,2,1,0:T(8,128)S(1)}, u32[]{:S(2)}, u32[]{:S(2)}) collective-permute-start(f32[4,1,40,256]{3,2,1,0:T(8,128)S(1)} %pad_maximum_fusion.70), channel_id=1, source_target_pairs={{0,2},{2,4},{4,6},{6,8},{8,10},{10,12},{12,14},{1,3},{3,5},{5,7},{... | collective-permute-start | bytes 491528 | tf_op jit(solution)/shard_map/ppermute | solution.py:114
  78.4 2.5 %collective-permute-done.13 = f32[4,1,40,256]{3,2,1,0:T(8,128)S(1)} collective-permute-done((f32[4,1,40,256]{3,2,1,0:T(8,128)S(1)}, f32[4,1,40,256]{3,2,1,0:T(8,128)S(1)}, u32[]{:S(2)}, u32[]{:S(2)}) %collective-permute-start.13) | collective-permute-done | bytes 163872 | tf_op jit(solution)/shard_map/ppermute | solution.py:115
  80.9 3.7 %collective-permute-done.14 = f32[4,1,40,256]{3,2,1,0:T(8,128)S(1)} collective-permute-done((f32[4,1,40,256]{3,2,1,0:T(8,128)S(1)}, f32[4,1,40,256]{3,2,1,0:T(8,128)S(1)}, u32[]{:S(2)}, u32[]{:S(2)}) %collective-permute-start.14) | collective-permute-done | bytes 163872 | tf_op jit(solution)/shard_map/ppermute | solution.py:114
  85.4 1.3 collective-permute-start.15
  86.8 5.0 %collective-permute-start.16 = (f32[4,1,40,256]{3,2,1,0:T(8,128)S(1)}, f32[4,1,40,256]{3,2,1,0:T(8,128)S(1)}, u32[]{:S(2)}, u32[]{:S(2)}) collective-permute-start(f32[4,1,40,256]{3,2,1,0:T(8,128)S(1)} %pad_maximum_fusion.72), channel_id=1, source_target_pairs={{0,2},{2,4},{4,6},{6,8},{8,10},{10,12},{12,14},{1,3},{3,5},{5,7},{... | collective-permute-start | bytes 491528 | tf_op jit(solution)/shard_map/ppermute | solution.py:114
  92.1 2.0 %collective-permute-done.15 = f32[4,1,40,256]{3,2,1,0:T(8,128)S(1)} collective-permute-done((f32[4,1,40,256]{3,2,1,0:T(8,128)S(1)}, f32[4,1,40,256]{3,2,1,0:T(8,128)S(1)}, u32[]{:S(2)}, u32[]{:S(2)}) %collective-permute-start.15) | collective-permute-done | bytes 163872 | tf_op jit(solution)/shard_map/ppermute | solution.py:115
  94.2 3.7 %collective-permute-done.16 = f32[4,1,40,256]{3,2,1,0:T(8,128)S(1)} collective-permute-done((f32[4,1,40,256]{3,2,1,0:T(8,128)S(1)}, f32[4,1,40,256]{3,2,1,0:T(8,128)S(1)}, u32[]{:S(2)}, u32[]{:S(2)}) %collective-permute-start.16) | collective-permute-done | bytes 163872 | tf_op jit(solution)/shard_map/ppermute | solution.py:114
  99.9 1.3 collective-permute-start.19
  101.2 5.0 %collective-permute-start.20 = (f32[4,1,40,256]{3,2,1,0:T(8,128)S(1)}, f32[4,1,40,256]{3,2,1,0:T(8,128)S(1)}, u32[]{:S(2)}, u32[]{:S(2)}) collective-permute-start(f32[4,1,40,256]{3,2,1,0:T(8,128)S(1)} %pad_maximum_fusion.74), channel_id=1, source_target_pairs={{0,2},{2,4},{4,6},{6,8},{8,10},{10,12},{12,14},{1,3},{3,5},{5,7},{... | collective-permute-start | bytes 491528 | tf_op jit(solution)/shard_map/ppermute | solution.py:114
  106.2 2.5 %collective-permute-done.19 = f32[4,1,40,256]{3,2,1,0:T(8,128)S(1)} collective-permute-done((f32[4,1,40,256]{3,2,1,0:T(8,128)S(1)}, f32[4,1,40,256]{3,2,1,0:T(8,128)S(1)}, u32[]{:S(2)}, u32[]{:S(2)}) %collective-permute-start.19) | collective-permute-done | bytes 163872 | tf_op jit(solution)/shard_map/ppermute | solution.py:115
  108.8 3.6 %collective-permute-done.20 = f32[4,1,40,256]{3,2,1,0:T(8,128)S(1)} collective-permute-done((f32[4,1,40,256]{3,2,1,0:T(8,128)S(1)}, f32[4,1,40,256]{3,2,1,0:T(8,128)S(1)}, u32[]{:S(2)}, u32[]{:S(2)}) %collective-permute-start.20) | collective-permute-done | bytes 163872 | tf_op jit(solution)/shard_map/ppermute | solution.py:114
  113.3 1.3 collective-permute-start.21
  114.8 5.2 %collective-permute-start.22 = (f32[4,1,40,256]{3,2,1,0:T(8,128)S(1)}, f32[4,1,40,256]{3,2,1,0:T(8,128)S(1)}, u32[]{:S(2)}, u32[]{:S(2)}) collective-permute-start(f32[4,1,40,256]{3,2,1,0:T(8,128)S(1)} %pad_maximum_fusion.76), channel_id=1, source_target_pairs={{0,2},{2,4},{4,6},{6,8},{8,10},{10,12},{12,14},{1,3},{3,5},{5,7},{... | collective-permute-start | bytes 491528 | tf_op jit(solution)/shard_map/ppermute | solution.py:114
  120.3 1.8 %collective-permute-done.21 = f32[4,1,40,256]{3,2,1,0:T(8,128)S(1)} collective-permute-done((f32[4,1,40,256]{3,2,1,0:T(8,128)S(1)}, f32[4,1,40,256]{3,2,1,0:T(8,128)S(1)}, u32[]{:S(2)}, u32[]{:S(2)}) %collective-permute-start.21) | collective-permute-done | bytes 163872 | tf_op jit(solution)/shard_map/ppermute | solution.py:115
  122.1 3.6 %collective-permute-done.22 = f32[4,1,40,256]{3,2,1,0:T(8,128)S(1)} collective-permute-done((f32[4,1,40,256]{3,2,1,0:T(8,128)S(1)}, f32[4,1,40,256]{3,2,1,0:T(8,128)S(1)}, u32[]{:S(2)}, u32[]{:S(2)}) %collective-permute-start.22) | collective-permute-done | bytes 163872 | tf_op jit(solution)/shard_map/ppermute | solution.py:114
  128.8 1.4 collective-permute-done.24
  132.1 2.5 %collective-permute-start.25 = (f32[65,256]{1,0:T(8,128)S(1)}, f32[65,256]{1,0:T(8,128)S(1)}, u32[]{:S(2)}, u32[]{:S(2)}) collective-permute-start(f32[65,256]{1,0:T(8,128)S(1)} %select_maximum_fusion), channel_id=1, source_target_pairs={{0,2},{2,0},{4,6},{6,4},{8,10},{10,8},{12,14},{14,12},{1,3},{3,1},... | collective-permute-start | bytes 199688 | tf_op jit(solution)/shard_map/ppermute | solution.py:28
  134.6 2.6 %collective-permute-done.25 = f32[65,256]{1,0:T(8,128)S(1)} collective-permute-done((f32[65,256]{1,0:T(8,128)S(1)}, f32[65,256]{1,0:T(8,128)S(1)}, u32[]{:S(2)}, u32[]{:S(2)}) %collective-permute-start.25) | collective-permute-done | bytes 66592 | tf_op jit(solution)/shard_map/ppermute | solution.py:28
  137.3 2.3 %collective-permute-start.26 = (f32[65,256]{1,0:T(8,128)S(1)}, f32[65,256]{1,0:T(8,128)S(1)}, u32[]{:S(2)}, u32[]{:S(2)}) collective-permute-start(f32[65,256]{1,0:T(8,128)S(1)} %fusion.574), channel_id=1, source_target_pairs={{0,4},{2,6},{4,0},{6,2},{8,12},{10,14},{12,8},{14,10},{1,5},{3,7},... | collective-permute-start | bytes 199688 | tf_op jit(solution)/shard_map/ppermute | solution.py:33
  139.5 2.6 %collective-permute-start.27 = (f32[65,256]{1,0:T(8,128)S(1)}, f32[65,256]{1,0:T(8,128)S(1)}, u32[]{:S(2)}, u32[]{:S(2)}) collective-permute-start(f32[65,256]{1,0:T(8,128)S(1)} %fusion.574), channel_id=1, source_target_pairs={{0,8},{2,10},{4,12},{6,14},{8,0},{10,2},{12,4},{14,6},{1,9},{3,11}... | collective-permute-start | bytes 199688 | tf_op jit(solution)/shard_map/ppermute | solution.py:33
  142.1 4.4 %collective-permute-done.27 = f32[65,256]{1,0:T(8,128)S(1)} collective-permute-done((f32[65,256]{1,0:T(8,128)S(1)}, f32[65,256]{1,0:T(8,128)S(1)}, u32[]{:S(2)}, u32[]{:S(2)}) %collective-permute-start.27) | collective-permute-done | bytes 66592 | tf_op jit(solution)/shard_map/ppermute | solution.py:33
  146.5 1.8 %collective-permute-done.28 = f32[65,256]{1,0:T(8,128)S(1)} collective-permute-done((f32[65,256]{1,0:T(8,128)S(1)}, f32[65,256]{1,0:T(8,128)S(1)}, u32[]{:S(2)}, u32[]{:S(2)}) %collective-permute-start.28) | collective-permute-done | bytes 66592 | tf_op jit(solution)/shard_map/ppermute | solution.py:33
  (194 shorter events, 22.8 us)
Async XLA Ops:
  1.5 7.0 %collective-permute-start = (f32[2,4,1,256]{3,2,1,0:T(1,128)S(1)}, f32[2,4,1,256]{3,2,1,0:T(1,128)}, u32[]{:S(2)}, u32[]{:S(2)}) collective-permute-start(f32[2,4,1,256]{3,2,1,0:T(1,128)S(1)} %constant_dynamic-slice_fusion.13), channel_id=1, source_target_pairs={{0,1},{1,0},{2,3},{3,2},{4,5},{5,4},{6,7},{7,6},{8,9},{9,8},{10,11... | collective-permute-start | bytes 24584 | tf_op jit(solution)/shard_map/ppermute | solution.py:50
  2.1 1.2 copy-start.13
  3.2 1.5 copy-start.1
  3.3 2.6 %copy-start.14 = (f32[4]{0:T(128)}, f32[4]{0:T(128)S(1)}, u32[]{:S(2)}) copy-start(f32[4]{0:T(128)S(1)} %multiply_add_fusion.4) | copy-start | bytes 52
  4.7 1.1 copy-start.2
  5.8 0.9 copy-start.6
  5.9 1.0 copy-start.7
  5.9 1.0 copy-start.8
  6.8 1.0 copy-start
  10.5 1.5 %copy-start.5 = (f32[2,1,40,256]{3,2,1,0:T(8,128)S(1)}, f32[2,1,40,256]{3,2,1,0:T(8,128)}, u32[]{:S(2)}) copy-start(f32[2,1,40,256]{3,2,1,0:T(8,128)} %get-tuple-element.151) | copy-start | bytes 245764
  12.7 9.5 %collective-permute-start.1 = (f32[4,1,40,256]{3,2,1,0:T(8,128)}, f32[4,1,40,256]{3,2,1,0:T(8,128)}, u32[]{:S(2)}, u32[]{:S(2)}) collective-permute-start(f32[4,1,40,256]{3,2,1,0:T(8,128)} %pad_maximum_fusion.61), channel_id=1, source_target_pairs={{2,0},{4,2},{6,4},{8,6},{10,8},{12,10},{14,12},{3,1},{5,3},{7,5},{... | collective-permute-start | bytes 491528 | tf_op jit(solution)/shard_map/ppermute | solution.py:115
  15.3 6.9 %copy-start.11 = (f32[1,1,40,256]{3,2,1,0:T(8,128)S(1)}, f32[1,1,40,256]{3,2,1,0:T(8,128)}, u32[]{:S(2)}) copy-start(f32[1,1,40,256]{3,2,1,0:T(8,128)} %get-tuple-element.147) | copy-start | bytes 122884
  15.3 6.9 %copy-start.12 = (f32[1,1,40,256]{3,2,1,0:T(8,128)S(1)}, f32[1,1,40,256]{3,2,1,0:T(8,128)}, u32[]{:S(2)}) copy-start(f32[1,1,40,256]{3,2,1,0:T(8,128)} %get-tuple-element.148) | copy-start | bytes 122884
  16.3 9.5 %collective-permute-start.2 = (f32[4,1,40,256]{3,2,1,0:T(8,128)S(1)}, f32[4,1,40,256]{3,2,1,0:T(8,128)S(1)}, u32[]{:S(2)}, u32[]{:S(2)}) collective-permute-start(f32[4,1,40,256]{3,2,1,0:T(8,128)S(1)} %pad_maximum_fusion.62), channel_id=1, source_target_pairs={{0,2},{2,4},{4,6},{6,8},{8,10},{10,12},{12,14},{1,3},{3,5},{5,7},{... | collective-permute-start | bytes 491528 | tf_op jit(solution)/shard_map/ppermute | solution.py:114
  22.3 3.6 %copy-start.9 = (f32[1,1,40,256]{3,2,1,0:T(8,128)S(1)}, f32[1,1,40,256]{3,2,1,0:T(8,128)}, u32[]{:S(2)}) copy-start(f32[1,1,40,256]{3,2,1,0:T(8,128)} %get-tuple-element.149) | copy-start | bytes 122884
  22.3 3.6 %copy-start.10 = (f32[1,1,40,256]{3,2,1,0:T(8,128)S(1)}, f32[1,1,40,256]{3,2,1,0:T(8,128)}, u32[]{:S(2)}) copy-start(f32[1,1,40,256]{3,2,1,0:T(8,128)} %get-tuple-element.150) | copy-start | bytes 122884
  25.8 1.0 copy-start.3
  27.0 6.7 %collective-permute-start.5 = (f32[2,4,1,256]{3,2,1,0:T(1,128)S(1)}, f32[2,4,1,256]{3,2,1,0:T(1,128)S(1)}, u32[]{:S(2)}, u32[]{:S(2)}) collective-permute-start(f32[2,4,1,256]{3,2,1,0:T(1,128)S(1)} %constant_dynamic-slice_fusion.12), channel_id=1, source_target_pairs={{0,1},{1,0},{2,3},{3,2},{4,5},{5,4},{6,7},{7,6},{8,9},{9,8},{10,11... | collective-permute-start | bytes 24584 | tf_op jit(solution)/shard_map/ppermute | solution.py:50
  27.4 9.2 %collective-permute-start.3 = (f32[4,1,40,256]{3,2,1,0:T(8,128)S(1)}, f32[4,1,40,256]{3,2,1,0:T(8,128)S(1)}, u32[]{:S(2)}, u32[]{:S(2)}) collective-permute-start(f32[4,1,40,256]{3,2,1,0:T(8,128)S(1)} %pad_maximum_fusion.63), channel_id=1, source_target_pairs={{2,0},{4,2},{6,4},{8,6},{10,8},{12,10},{14,12},{3,1},{5,3},{7,5},{... | collective-permute-start | bytes 491528 | tf_op jit(solution)/shard_map/ppermute | solution.py:115
  28.7 12.1 %collective-permute-start.4 = (f32[4,1,40,256]{3,2,1,0:T(8,128)S(1)}, f32[4,1,40,256]{3,2,1,0:T(8,128)S(1)}, u32[]{:S(2)}, u32[]{:S(2)}) collective-permute-start(f32[4,1,40,256]{3,2,1,0:T(8,128)S(1)} %pad_maximum_fusion.64), channel_id=1, source_target_pairs={{0,2},{2,4},{4,6},{6,8},{8,10},{10,12},{12,14},{1,3},{3,5},{5,7},{... | collective-permute-start | bytes 491528 | tf_op jit(solution)/shard_map/ppermute | solution.py:114
  41.4 1.2 collective-permute-start.6
  42.8 8.9 %collective-permute-start.7 = (f32[4,1,40,256]{3,2,1,0:T(8,128)S(1)}, f32[4,1,40,256]{3,2,1,0:T(8,128)S(1)}, u32[]{:S(2)}, u32[]{:S(2)}) collective-permute-start(f32[4,1,40,256]{3,2,1,0:T(8,128)S(1)} %pad_maximum_fusion.65), channel_id=1, source_target_pairs={{2,0},{4,2},{6,4},{8,6},{10,8},{12,10},{14,12},{3,1},{5,3},{7,5},{... | collective-permute-start | bytes 491528 | tf_op jit(solution)/shard_map/ppermute | solution.py:115
  44.2 11.2 %collective-permute-start.8 = (f32[4,1,40,256]{3,2,1,0:T(8,128)S(1)}, f32[4,1,40,256]{3,2,1,0:T(8,128)S(1)}, u32[]{:S(2)}, u32[]{:S(2)}) collective-permute-start(f32[4,1,40,256]{3,2,1,0:T(8,128)S(1)} %pad_maximum_fusion.66), channel_id=1, source_target_pairs={{0,2},{2,4},{4,6},{6,8},{8,10},{10,12},{12,14},{1,3},{3,5},{5,7},{... | collective-permute-start | bytes 491528 | tf_op jit(solution)/shard_map/ppermute | solution.py:114
  56.0 6.8 %collective-permute-start.11 = (f32[2,4,1,256]{3,2,1,0:T(1,128)S(1)}, f32[2,4,1,256]{3,2,1,0:T(1,128)S(1)}, u32[]{:S(2)}, u32[]{:S(2)}) collective-permute-start(f32[2,4,1,256]{3,2,1,0:T(1,128)S(1)} %constant_dynamic-slice_fusion.10), channel_id=1, source_target_pairs={{0,1},{1,0},{2,3},{3,2},{4,5},{5,4},{6,7},{7,6},{8,9},{9,8},{10,11... | collective-permute-start | bytes 24584 | tf_op jit(solution)/shard_map/ppermute | solution.py:50
  56.4 9.2 %collective-permute-start.9 = (f32[4,1,40,256]{3,2,1,0:T(8,128)S(1)}, f32[4,1,40,256]{3,2,1,0:T(8,128)S(1)}, u32[]{:S(2)}, u32[]{:S(2)}) collective-permute-start(f32[4,1,40,256]{3,2,1,0:T(8,128)S(1)} %pad_maximum_fusion.67), channel_id=1, source_target_pairs={{2,0},{4,2},{6,4},{8,6},{10,8},{12,10},{14,12},{3,1},{5,3},{7,5},{... | collective-permute-start | bytes 491528 | tf_op jit(solution)/shard_map/ppermute | solution.py:115
  57.8 11.6 %collective-permute-start.10 = (f32[4,1,40,256]{3,2,1,0:T(8,128)S(1)}, f32[4,1,40,256]{3,2,1,0:T(8,128)S(1)}, u32[]{:S(2)}, u32[]{:S(2)}) collective-permute-start(f32[4,1,40,256]{3,2,1,0:T(8,128)S(1)} %pad_maximum_fusion.68), channel_id=1, source_target_pairs={{0,2},{2,4},{4,6},{6,8},{8,10},{10,12},{12,14},{1,3},{3,5},{5,7},{... | collective-permute-start | bytes 491528 | tf_op jit(solution)/shard_map/ppermute | solution.py:114
  70.5 1.2 collective-permute-start.12
  72.0 8.9 %collective-permute-start.13 = (f32[4,1,40,256]{3,2,1,0:T(8,128)S(1)}, f32[4,1,40,256]{3,2,1,0:T(8,128)S(1)}, u32[]{:S(2)}, u32[]{:S(2)}) collective-permute-start(f32[4,1,40,256]{3,2,1,0:T(8,128)S(1)} %pad_maximum_fusion.69), channel_id=1, source_target_pairs={{2,0},{4,2},{6,4},{8,6},{10,8},{12,10},{14,12},{3,1},{5,3},{7,5},{... | collective-permute-start | bytes 491528 | tf_op jit(solution)/shard_map/ppermute | solution.py:115
  73.4 11.2 %collective-permute-start.14 = (f32[4,1,40,256]{3,2,1,0:T(8,128)S(1)}, f32[4,1,40,256]{3,2,1,0:T(8,128)S(1)}, u32[]{:S(2)}, u32[]{:S(2)}) collective-permute-start(f32[4,1,40,256]{3,2,1,0:T(8,128)S(1)} %pad_maximum_fusion.70), channel_id=1, source_target_pairs={{0,2},{2,4},{4,6},{6,8},{8,10},{10,12},{12,14},{1,3},{3,5},{5,7},{... | collective-permute-start | bytes 491528 | tf_op jit(solution)/shard_map/ppermute | solution.py:114
  85.4 8.8 %collective-permute-start.15 = (f32[4,1,40,256]{3,2,1,0:T(8,128)S(1)}, f32[4,1,40,256]{3,2,1,0:T(8,128)S(1)}, u32[]{:S(2)}, u32[]{:S(2)}) collective-permute-start(f32[4,1,40,256]{3,2,1,0:T(8,128)S(1)} %pad_maximum_fusion.71), channel_id=1, source_target_pairs={{2,0},{4,2},{6,4},{8,6},{10,8},{12,10},{14,12},{3,1},{5,3},{7,5},{... | collective-permute-start | bytes 491528 | tf_op jit(solution)/shard_map/ppermute | solution.py:115
  86.7 5.1 %collective-permute-start.17 = (f32[2,4,1,256]{3,2,1,0:T(1,128)S(1)}, f32[2,4,1,256]{3,2,1,0:T(1,128)S(1)}, u32[]{:S(2)}, u32[]{:S(2)}) collective-permute-start(f32[2,4,1,256]{3,2,1,0:T(1,128)S(1)} %constant_dynamic-slice_fusion.5), channel_id=1, source_target_pairs={{0,1},{1,0},{2,3},{3,2},{4,5},{5,4},{6,7},{7,6},{8,9},{9,8},{10,11... | collective-permute-start | bytes 24584 | tf_op jit(solution)/shard_map/ppermute | solution.py:50
  86.8 11.0 %collective-permute-start.16 = (f32[4,1,40,256]{3,2,1,0:T(8,128)S(1)}, f32[4,1,40,256]{3,2,1,0:T(8,128)S(1)}, u32[]{:S(2)}, u32[]{:S(2)}) collective-permute-start(f32[4,1,40,256]{3,2,1,0:T(8,128)S(1)} %pad_maximum_fusion.72), channel_id=1, source_target_pairs={{0,2},{2,4},{4,6},{6,8},{8,10},{10,12},{12,14},{1,3},{3,5},{5,7},{... | collective-permute-start | bytes 491528 | tf_op jit(solution)/shard_map/ppermute | solution.py:114
  98.4 1.2 collective-permute-start.18
  99.9 8.9 %collective-permute-start.19 = (f32[4,1,40,256]{3,2,1,0:T(8,128)S(1)}, f32[4,1,40,256]{3,2,1,0:T(8,128)S(1)}, u32[]{:S(2)}, u32[]{:S(2)}) collective-permute-start(f32[4,1,40,256]{3,2,1,0:T(8,128)S(1)} %pad_maximum_fusion.73), channel_id=1, source_target_pairs={{2,0},{4,2},{6,4},{8,6},{10,8},{12,10},{14,12},{3,1},{5,3},{7,5},{... | collective-permute-start | bytes 491528 | tf_op jit(solution)/shard_map/ppermute | solution.py:115
  101.2 11.2 %collective-permute-start.20 = (f32[4,1,40,256]{3,2,1,0:T(8,128)S(1)}, f32[4,1,40,256]{3,2,1,0:T(8,128)S(1)}, u32[]{:S(2)}, u32[]{:S(2)}) collective-permute-start(f32[4,1,40,256]{3,2,1,0:T(8,128)S(1)} %pad_maximum_fusion.74), channel_id=1, source_target_pairs={{0,2},{2,4},{4,6},{6,8},{8,10},{10,12},{12,14},{1,3},{3,5},{5,7},{... | collective-permute-start | bytes 491528 | tf_op jit(solution)/shard_map/ppermute | solution.py:114
  113.3 8.8 %collective-permute-start.21 = (f32[4,1,40,256]{3,2,1,0:T(8,128)S(1)}, f32[4,1,40,256]{3,2,1,0:T(8,128)S(1)}, u32[]{:S(2)}, u32[]{:S(2)}) collective-permute-start(f32[4,1,40,256]{3,2,1,0:T(8,128)S(1)} %pad_maximum_fusion.75), channel_id=1, source_target_pairs={{2,0},{4,2},{6,4},{8,6},{10,8},{12,10},{14,12},{3,1},{5,3},{7,5},{... | collective-permute-start | bytes 491528 | tf_op jit(solution)/shard_map/ppermute | solution.py:115
  114.7 5.3 %collective-permute-start.23 = (f32[2,4,1,256]{3,2,1,0:T(1,128)S(1)}, f32[2,4,1,256]{3,2,1,0:T(1,128)S(1)}, u32[]{:S(2)}, u32[]{:S(2)}) collective-permute-start(f32[2,4,1,256]{3,2,1,0:T(1,128)S(1)} %constant_dynamic-slice_fusion.3), channel_id=1, source_target_pairs={{0,1},{1,0},{2,3},{3,2},{4,5},{5,4},{6,7},{7,6},{8,9},{9,8},{10,11... | collective-permute-start | bytes 24584 | tf_op jit(solution)/shard_map/ppermute | solution.py:50
  114.8 11.0 %collective-permute-start.22 = (f32[4,1,40,256]{3,2,1,0:T(8,128)S(1)}, f32[4,1,40,256]{3,2,1,0:T(8,128)S(1)}, u32[]{:S(2)}, u32[]{:S(2)}) collective-permute-start(f32[4,1,40,256]{3,2,1,0:T(8,128)S(1)} %pad_maximum_fusion.76), channel_id=1, source_target_pairs={{0,2},{2,4},{4,6},{6,8},{8,10},{10,12},{12,14},{1,3},{3,5},{5,7},{... | collective-permute-start | bytes 491528 | tf_op jit(solution)/shard_map/ppermute | solution.py:114
  127.6 0.8 copy-start.4
  127.6 0.6 copy-start.15
  128.7 1.5 collective-permute-start.24
  132.1 5.1 %collective-permute-start.25 = (f32[65,256]{1,0:T(8,128)S(1)}, f32[65,256]{1,0:T(8,128)S(1)}, u32[]{:S(2)}, u32[]{:S(2)}) collective-permute-start(f32[65,256]{1,0:T(8,128)S(1)} %select_maximum_fusion), channel_id=1, source_target_pairs={{0,2},{2,0},{4,6},{6,4},{8,10},{10,8},{12,14},{14,12},{1,3},{3,1},... | collective-permute-start | bytes 199688 | tf_op jit(solution)/shard_map/ppermute | solution.py:28
  137.3 4.8 %collective-permute-start.26 = (f32[65,256]{1,0:T(8,128)S(1)}, f32[65,256]{1,0:T(8,128)S(1)}, u32[]{:S(2)}, u32[]{:S(2)}) collective-permute-start(f32[65,256]{1,0:T(8,128)S(1)} %fusion.574), channel_id=1, source_target_pairs={{0,4},{2,6},{4,0},{6,2},{8,12},{10,14},{12,8},{14,10},{1,5},{3,7},... | collective-permute-start | bytes 199688 | tf_op jit(solution)/shard_map/ppermute | solution.py:33
  139.5 7.0 %collective-permute-start.27 = (f32[65,256]{1,0:T(8,128)S(1)}, f32[65,256]{1,0:T(8,128)S(1)}, u32[]{:S(2)}, u32[]{:S(2)}) collective-permute-start(f32[65,256]{1,0:T(8,128)S(1)} %fusion.574), channel_id=1, source_target_pairs={{0,8},{2,10},{4,12},{6,14},{8,0},{10,2},{12,4},{14,6},{1,9},{3,11}... | collective-permute-start | bytes 199688 | tf_op jit(solution)/shard_map/ppermute | solution.py:33
  142.1 6.2 %collective-permute-start.28 = (f32[65,256]{1,0:T(8,128)S(1)}, f32[65,256]{1,0:T(8,128)S(1)}, u32[]{:S(2)}, u32[]{:S(2)}) collective-permute-start(f32[65,256]{1,0:T(8,128)S(1)} %fusion.574), channel_id=1, source_target_pairs={{0,12},{2,14},{4,8},{6,10},{8,4},{10,6},{12,0},{14,2},{1,13},{3,15... | collective-permute-start | bytes 199688 | tf_op jit(solution)/shard_map/ppermute | solution.py:33

commit v9 on v6

--- a/solution.py
+++ b/solution.py
@@ -96,13 +96,36 @@
     return jnp.stack([0.5 * plane[1], -0.5 * plane[0]])
 
 
-def stage_pair(stage, base, base_low, base_high, coef, weight):
+def with_partner_row(block, row):
+    iy = lax.axis_index("gy")
+    zero = jnp.zeros_like(row)
+    below = jnp.where(iy == 1, row, zero)
+    above = jnp.where(iy == 0, row, zero)
+    return jnp.concatenate([below, block, above], axis=2)
+
+
+def edge_rows(block, offset=0):
+    iy = lax.axis_index("gy")
+    Y = block.shape[2]
+    start = (1 - iy) * (Y - 1 - offset) + iy * offset
+    return lax.dynamic_slice_in_dim(block, start, 1, axis=2)
+
+
+def partner_coef(coef):
+    rows = jnp.stack([edge_rows(c[:, None])[:, 0] for c in coef])
+    got = lax.ppermute(rows, "gy", [(0, 1), (1, 0)])
+    return tuple(got[k] for k in range(len(coef)))
+
+
+def stage_pair(stage, base, base_low, base_high, coef, weight, tall=None, ahead=None):
     nx = lax.axis_size("gx")
     ix = lax.axis_index("gx")
+    iy = lax.axis_index("gy")
     X = stage.shape[1]
     up = [(i, i + 1) for i in range(nx - 1)]
     down = [(i + 1, i) for i in range(nx - 1)]
-    tall = y_extended(stage)
+    if tall is None:
+        tall = y_extended(stage)
     zero_plane = jnp.zeros_like(stage[:, :1])
     part_top = operator(tall[:, X - 1:], stage[:, X - 2:X - 1], zero_plane, cut(coef, X - 1, X))
     part_bottom = operator(tall[:, :1], zero_plane, stage[:, 1:2], cut(coef, 0, 1))
@@ -118,17 +141,39 @@
     nxt = base + weight * section
     nxt_low = jnp.where(ix > 0, base_low + weight * section_low, 0.0)
     nxt_high = jnp.where(ix < nx - 1, base_high + weight * section_high, 0.0)
-    section_next = operator(y_extended(nxt), nxt_low, nxt_high, coef)
-    return section, section_next, base_low, base_high
+    if ahead is None:
+        section_next = operator(y_extended(nxt), nxt_low, nxt_high, coef)
+        return section, section_next, base_low, base_high, None
+    next_weight, coef_partner = ahead
+    mine = edge_rows(nxt)
+    pack = jnp.concatenate(
+        [mine, edge_rows(nxt, 1), edge_rows(nxt_low), edge_rows(nxt_high)], axis=1
+    )
+    got = lax.ppermute(pack, "gy", [(0, 1), (1, 0)])
+    their, their_inner = got[:, :X], got[:, X:2 * X]
+    their_low, their_high = got[:, 2 * X:2 * X + 1], got[:, 2 * X + 1:2 * X + 2]
+    section_next = operator(with_partner_row(nxt, their), nxt_low, nxt_high, coef)
+    slab = jnp.where(
+        iy == 0,
+        jnp.concatenate([mine, their, their_inner], axis=2),
+        jnp.concatenate([their_inner, their, mine], axis=2),
+    )
+    their_section = operator(slab, their_low, their_high, coef_partner)
+    their_base = jnp.where(iy == 1, tall[:, :, :1], tall[:, :, -1:])
+    their_next = their_base + next_weight * their_section
+    return section, section_next, base_low, base_high, their_next
 
 
 def rk_step(field, coef):
-    section_one, section_two, low, high = stage_pair(
-        field, field, None, None, coef, 0.5 * STEP_SIZE
+    fast = lax.axis_size("gy") == 2 and field.shape[2] >= 3
+    ahead = (0.5 * STEP_SIZE, partner_coef(coef)) if fast else None
+    section_one, section_two, low, high, their_three = stage_pair(
+        field, field, None, None, coef, 0.5 * STEP_SIZE, ahead=ahead
     )
     stage_three = field + 0.5 * STEP_SIZE * section_two
-    section_three, section_four, _, _ = stage_pair(
-        stage_three, field, low, high, coef, STEP_SIZE
+    tall_three = with_partner_row(stage_three, their_three) if fast else None
+    section_three, section_four, _, _, _ = stage_pair(
+        stage_three, field, low, high, coef, STEP_SIZE, tall=tall_three
     )
     return field + STEP_SIZE / 6.0 * (
         section_one + 2.0 * section_two + 2.0 * section_three + section_four

time: 111 us -> 109 us (0.982)
  waiting for transfers between devices: 57 us -> 54.4 us
    ppermute x8 -> x4, waiting for transfers between devices: 6.84 us -> 2.62 us  [y_extended(): other = lax.ppermute(strip, 'gy', [(0, 1), (1, 0)])]
    ppermute x0 -> x4, waiting for transfers between devices: none -> 1.78 us  [the longest x2 1.75 us: stage_pair(): got = lax.ppermute(pack, 'gy', [(0, 1), (1, 0)])]
    sub x12 -> x14, other arithmetic: 3.63 us -> 3.83 us  [operator(): lapl = total - 6.0 * field]
  transfers between devices with their start and end apart: 21 -> 21, of which waited for: 18 -> 16; matrix products, arithmetic and copies ran while one was open for 3% -> 5% of each run, Pallas kernels for 0% -> 0%
where the time goes in v9:
time: 109 us
  waiting for transfers between devices  54.4 us (50%)
  starting transfers between devices  34.1 us (31%)
  other arithmetic  12 us (11%)
  between operations  5.2 us (5%)
  local copies, waits for them, and re-layouts  3.27 us (3%)
    ppermute x4, waiting for transfers between devices, stage_pair(): lax.ppermute(jnp.concatenate([stage[:, X - 1:], part_top]), 'gx', up)  27.3 us
    ppermute x4, starting transfers between devices, stage_pair(): lax.ppermute(jnp.concatenate([stage[:, X - 1:], part_top]), 'gx', up)  20 us
    ppermute x4, waiting for transfers between devices, stage_pair(): lax.ppermute(jnp.concatenate([stage[:, :1], part_bottom]), 'gx', down)  13.9 us
    ppermute x4, starting transfers between devices, stage_pair(): lax.ppermute(jnp.concatenate([stage[:, :1], part_bottom]), 'gx', down)  5.17 us
    ppermute x3, waiting for transfers between devices, gx_total(): lax.ppermute(pair, 'gx', [(i, i ^ 2 * k) for i in range(count)])  5.13 us
    ppermute x3, starting transfers between devices, gx_total(): lax.ppermute(pair, 'gx', [(i, i ^ 2 * k) for i in range(count)])  4.45 us
    sub x14, other arithmetic, operator(): lapl = total - 6.0 * field  3.83 us
    ppermute x4, waiting for transfers between devices, y_extended(): other = lax.ppermute(strip, 'gy', [(0, 1), (1, 0)])  2.62 us
  transfers between devices with their start and end apart: 21, of which 16 were waited for; matrix products, arithmetic and copies ran while one was open for 5% of the time, Pallas kernels for 0%

profile of v9, /device:TPU:0, one launch (start us, length us, event | category | flops | bytes accessed | tf_op | source)
XLA Modules:
  0.0 109.0 jit_solution(11604637036792674906)
XLA Ops:
  0.6 0.9 constant_dynamic-slice_fusion.17
  1.6 0.6 collective-permute-start
  2.2 0.8 slice_bitcast_fusion.18
  3.1 1.3 %multiply_add_fusion.6 = (f32[4,64,256]{2,1,0:T(8,128)S(1)}, f32[4,64,256]{2,1,0:T(8,128)S(1)}, f32[4,64,256]{2,1,0:T(8,128)S(1)}, f32[4,64,256]{2,1,0:T(8,128)S(1)}) fusion(f32[4,64,256]{2,1,0:T(8,128)} %param.10, f32[2,4,64,256]{3,2,1,0:T(8,128)} %param.8, f32[64,256]{1,0:T(8,128)S(1)} %mul.964, f32[4]{0:T(128)S(1)} %multiply_add_fusion.7, ...), kind=kLoop, calls=%fused_computation.257 | loop fusion | flops 1114112 | bytes 2490384 | tf_op jit(solution)/shard_map/add | solution.py:65
  5.1 1.3 %collective-permute-start.1 = (f32[4,1,64,256]{3,2,1,0:T(8,128)S(1)}, f32[4,1,64,256]{3,2,1,0:T(8,128)S(1)}, u32[]{:S(2)}, u32[]{:S(2)}) collective-permute-start(f32[4,1,64,256]{3,2,1,0:T(8,128)S(1)} %pad_maximum_fusion.39), channel_id=1, source_target_pairs={{2,0},{4,2},{6,4},{8,6},{10,8},{12,10},{14,12},{3,1},{5,3},{7,5},{... | collective-permute-start | bytes 786440 | tf_op jit(solution)/shard_map/ppermute | solution.py:133
  6.5 5.5 %collective-permute-start.2 = (f32[4,1,64,256]{3,2,1,0:T(8,128)S(1)}, f32[4,1,64,256]{3,2,1,0:T(8,128)S(1)}, u32[]{:S(2)}, u32[]{:S(2)}) collective-permute-start(f32[4,1,64,256]{3,2,1,0:T(8,128)S(1)} %pad_maximum_fusion.40), channel_id=1, source_target_pairs={{0,2},{2,4},{4,6},{6,8},{8,10},{10,12},{12,14},{1,3},{3,5},{5,7},{... | collective-permute-start | bytes 786440 | tf_op jit(solution)/shard_map/ppermute | solution.py:132
  12.0 4.5 %collective-permute-done.1 = f32[4,1,64,256]{3,2,1,0:T(8,128)S(1)} collective-permute-done((f32[4,1,64,256]{3,2,1,0:T(8,128)S(1)}, f32[4,1,64,256]{3,2,1,0:T(8,128)S(1)}, u32[]{:S(2)}, u32[]{:S(2)}) %collective-permute-start.1) | collective-permute-done | bytes 262176 | tf_op jit(solution)/shard_map/ppermute | solution.py:133
  16.5 5.7 %collective-permute-done.2 = f32[4,1,64,256]{3,2,1,0:T(8,128)S(1)} collective-permute-done((f32[4,1,64,256]{3,2,1,0:T(8,128)S(1)}, f32[4,1,64,256]{3,2,1,0:T(8,128)S(1)}, u32[]{:S(2)}, u32[]{:S(2)}) %collective-permute-start.2) | collective-permute-done | bytes 262176 | tf_op jit(solution)/shard_map/ppermute | solution.py:132
  22.3 0.4 fusion.2
  23.1 1.2 %collective-permute-done.3 = f32[2,10,1,256]{3,2,1,0:T(1,128)S(1)} collective-permute-done((f32[2,10,1,256]{3,2,1,0:T(1,128)S(1)}, f32[2,10,1,256]{3,2,1,0:T(1,128)S(1)}, u32[]{:S(2)}, u32[]{:S(2)}) %collective-permute-start.3) | collective-permute-done | bytes 20512 | tf_op jit(solution)/shard_map/ppermute | solution.py:152
  24.5 0.3 fusion.5
  25.5 1.3 %collective-permute-start.5 = (f32[4,1,64,256]{3,2,1,0:T(8,128)S(1)}, f32[4,1,64,256]{3,2,1,0:T(8,128)S(1)}, u32[]{:S(2)}, u32[]{:S(2)}) collective-permute-start(f32[4,1,64,256]{3,2,1,0:T(8,128)S(1)} %pad_maximum_fusion.41), channel_id=1, source_target_pairs={{2,0},{4,2},{6,4},{8,6},{10,8},{12,10},{14,12},{3,1},{5,3},{7,5},{... | collective-permute-start | bytes 786440 | tf_op jit(solution)/shard_map/ppermute | solution.py:133
  26.8 5.0 %collective-permute-start.6 = (f32[4,1,64,256]{3,2,1,0:T(8,128)S(1)}, f32[4,1,64,256]{3,2,1,0:T(8,128)S(1)}, u32[]{:S(2)}, u32[]{:S(2)}) collective-permute-start(f32[4,1,64,256]{3,2,1,0:T(8,128)S(1)} %pad_maximum_fusion.42), channel_id=1, source_target_pairs={{0,2},{2,4},{4,6},{6,8},{8,10},{10,12},{12,14},{1,3},{3,5},{5,7},{... | collective-permute-start | bytes 786440 | tf_op jit(solution)/shard_map/ppermute | solution.py:132
  31.9 4.6 %collective-permute-done.5 = f32[4,1,64,256]{3,2,1,0:T(8,128)S(1)} collective-permute-done((f32[4,1,64,256]{3,2,1,0:T(8,128)S(1)}, f32[4,1,64,256]{3,2,1,0:T(8,128)S(1)}, u32[]{:S(2)}, u32[]{:S(2)}) %collective-permute-start.5) | collective-permute-done | bytes 262176 | tf_op jit(solution)/shard_map/ppermute | solution.py:133
  36.5 5.7 %collective-permute-done.6 = f32[4,1,64,256]{3,2,1,0:T(8,128)S(1)} collective-permute-done((f32[4,1,64,256]{3,2,1,0:T(8,128)S(1)}, f32[4,1,64,256]{3,2,1,0:T(8,128)S(1)}, u32[]{:S(2)}, u32[]{:S(2)}) %collective-permute-start.6) | collective-permute-done | bytes 262176 | tf_op jit(solution)/shard_map/ppermute | solution.py:132
  42.3 0.4 fusion.8
  43.1 1.1 %collective-permute-done.7 = f32[2,4,1,256]{3,2,1,0:T(1,128)S(1)} collective-permute-done((f32[2,4,1,256]{3,2,1,0:T(1,128)S(1)}, f32[2,4,1,256]{3,2,1,0:T(1,128)S(1)}, u32[]{:S(2)}, u32[]{:S(2)}) %collective-permute-start.7) | collective-permute-done | bytes 8224 | tf_op jit(solution)/shard_map/ppermute | solution.py:50
  44.2 0.3 fusion.11
  45.2 1.0 collective-permute-done.8
  46.6 4.4 %collective-permute-start.10 = (f32[4,1,64,256]{3,2,1,0:T(8,128)S(1)}, f32[4,1,64,256]{3,2,1,0:T(8,128)S(1)}, u32[]{:S(2)}, u32[]{:S(2)}) collective-permute-start(f32[4,1,64,256]{3,2,1,0:T(8,128)S(1)} %pad_maximum_fusion.44), channel_id=1, source_target_pairs={{0,2},{2,4},{4,6},{6,8},{8,10},{10,12},{12,14},{1,3},{3,5},{5,7},{... | collective-permute-start | bytes 786440 | tf_op jit(solution)/shard_map/ppermute | solution.py:132
  51.0 1.3 %collective-permute-start.9 = (f32[4,1,64,256]{3,2,1,0:T(8,128)S(1)}, f32[4,1,64,256]{3,2,1,0:T(8,128)S(1)}, u32[]{:S(2)}, u32[]{:S(2)}) collective-permute-start(f32[4,1,64,256]{3,2,1,0:T(8,128)S(1)} %pad_maximum_fusion.43), channel_id=1, source_target_pairs={{2,0},{4,2},{6,4},{8,6},{10,8},{12,10},{14,12},{3,1},{5,3},{7,5},{... | collective-permute-start | bytes 786440 | tf_op jit(solution)/shard_map/ppermute | solution.py:133
  52.3 10.1 %collective-permute-done.10 = f32[4,1,64,256]{3,2,1,0:T(8,128)S(1)} collective-permute-done((f32[4,1,64,256]{3,2,1,0:T(8,128)S(1)}, f32[4,1,64,256]{3,2,1,0:T(8,128)S(1)}, u32[]{:S(2)}, u32[]{:S(2)}) %collective-permute-start.10) | collective-permute-done | bytes 262176 | tf_op jit(solution)/shard_map/ppermute | solution.py:132
  62.5 0.3 fusion.14
  63.1 0.3 multiply_add_fusion.2
  63.5 0.6 collective-permute-start.12
  64.1 0.6 collective-permute-done.11
  65.0 0.3 fusion.17
  65.5 0.3 multiply_add_fusion.1
  66.2 1.3 %collective-permute-start.13 = (f32[4,1,64,256]{3,2,1,0:T(8,128)S(1)}, f32[4,1,64,256]{3,2,1,0:T(8,128)S(1)}, u32[]{:S(2)}, u32[]{:S(2)}) collective-permute-start(f32[4,1,64,256]{3,2,1,0:T(8,128)S(1)} %pad_maximum_fusion.45), channel_id=1, source_target_pairs={{2,0},{4,2},{6,4},{8,6},{10,8},{12,10},{14,12},{3,1},{5,3},{7,5},{... | collective-permute-start | bytes 786440 | tf_op jit(solution)/shard_map/ppermute | solution.py:133
  67.5 5.0 %collective-permute-start.14 = (f32[4,1,64,256]{3,2,1,0:T(8,128)S(1)}, f32[4,1,64,256]{3,2,1,0:T(8,128)S(1)}, u32[]{:S(2)}, u32[]{:S(2)}) collective-permute-start(f32[4,1,64,256]{3,2,1,0:T(8,128)S(1)} %pad_maximum_fusion.46), channel_id=1, source_target_pairs={{0,2},{2,4},{4,6},{6,8},{8,10},{10,12},{12,14},{1,3},{3,5},{5,7},{... | collective-permute-start | bytes 786440 | tf_op jit(solution)/shard_map/ppermute | solution.py:132
  72.6 4.8 %collective-permute-done.13 = f32[4,1,64,256]{3,2,1,0:T(8,128)S(1)} collective-permute-done((f32[4,1,64,256]{3,2,1,0:T(8,128)S(1)}, f32[4,1,64,256]{3,2,1,0:T(8,128)S(1)}, u32[]{:S(2)}, u32[]{:S(2)}) %collective-permute-start.13) | collective-permute-done | bytes 262176 | tf_op jit(solution)/shard_map/ppermute | solution.py:133
  77.4 5.7 %collective-permute-done.14 = f32[4,1,64,256]{3,2,1,0:T(8,128)S(1)} collective-permute-done((f32[4,1,64,256]{3,2,1,0:T(8,128)S(1)}, f32[4,1,64,256]{3,2,1,0:T(8,128)S(1)}, u32[]{:S(2)}, u32[]{:S(2)}) %collective-permute-start.14) | collective-permute-done | bytes 262176 | tf_op jit(solution)/shard_map/ppermute | solution.py:132
  83.2 0.4 fusion.20
  84.1 0.6 compare_reduce_fusion
  84.8 0.5 collective-permute-done.15
  85.3 0.3 fusion.23
  85.9 1.1 multiply_reduce_fusion
  87.2 0.5 copy-done.3
  88.2 1.1 collective-permute-done.16
  91.2 2.5 %collective-permute-start.17 = (f32[65,256]{1,0:T(8,128)S(1)}, f32[65,256]{1,0:T(8,128)S(1)}, u32[]{:S(2)}, u32[]{:S(2)}) collective-permute-start(f32[65,256]{1,0:T(8,128)S(1)} %select_maximum_fusion), channel_id=1, source_target_pairs={{0,2},{2,0},{4,6},{6,4},{8,10},{10,8},{12,14},{14,12},{1,3},{3,1},... | collective-permute-start | bytes 199688 | tf_op jit(solution)/shard_map/ppermute | solution.py:28
  93.7 2.6 %collective-permute-done.17 = f32[65,256]{1,0:T(8,128)S(1)} collective-permute-done((f32[65,256]{1,0:T(8,128)S(1)}, f32[65,256]{1,0:T(8,128)S(1)}, u32[]{:S(2)}, u32[]{:S(2)}) %collective-permute-start.17) | collective-permute-done | bytes 66592 | tf_op jit(solution)/shard_map/ppermute | solution.py:28
  96.3 2.7 %collective-permute-start.20 = (f32[65,256]{1,0:T(8,128)S(1)}, f32[65,256]{1,0:T(8,128)S(1)}, u32[]{:S(2)}, u32[]{:S(2)}) collective-permute-start(f32[65,256]{1,0:T(8,128)S(1)} %fusion.286), channel_id=1, source_target_pairs={{0,12},{2,14},{4,8},{6,10},{8,4},{10,6},{12,0},{14,2},{1,13},{3,15... | collective-permute-start | bytes 199688 | tf_op jit(solution)/shard_map/ppermute | solution.py:33
  99.0 0.4 collective-permute-start.19
  99.4 1.3 %collective-permute-start.18 = (f32[65,256]{1,0:T(8,128)S(1)}, f32[65,256]{1,0:T(8,128)S(1)}, u32[]{:S(2)}, u32[]{:S(2)}) collective-permute-start(f32[65,256]{1,0:T(8,128)S(1)} %fusion.286), channel_id=1, source_target_pairs={{0,4},{2,6},{4,0},{6,2},{8,12},{10,14},{12,8},{14,10},{1,5},{3,7},... | collective-permute-start | bytes 199688 | tf_op jit(solution)/shard_map/ppermute | solution.py:33
  100.8 2.6 %collective-permute-done.20 = f32[65,256]{1,0:T(8,128)S(1)} collective-permute-done((f32[65,256]{1,0:T(8,128)S(1)}, f32[65,256]{1,0:T(8,128)S(1)}, u32[]{:S(2)}, u32[]{:S(2)}) %collective-permute-start.20) | collective-permute-done | bytes 66592 | tf_op jit(solution)/shard_map/ppermute | solution.py:33
  103.4 2.5 %collective-permute-done.19 = f32[65,256]{1,0:T(8,128)S(1)} collective-permute-done((f32[65,256]{1,0:T(8,128)S(1)}, f32[65,256]{1,0:T(8,128)S(1)}, u32[]{:S(2)}, u32[]{:S(2)}) %collective-permute-start.19) | collective-permute-done | bytes 66592 | tf_op jit(solution)/shard_map/ppermute | solution.py:33
  106.0 0.5 slice.1282
  107.2 0.6 maximum_divide_fusion
  (122 shorter events, 6.5 us)
Async XLA Ops:
  0.6 2.5 %copy-start.1 = (f32[2,4,64,256]{3,2,1,0:T(8,128)S(1)}, f32[2,4,64,256]{3,2,1,0:T(8,128)}, u32[]{:S(2)}) copy-start(f32[2,4,64,256]{3,2,1,0:T(8,128)} %param.9) | copy-start | bytes 1572868
  1.6 3.2 %collective-permute-start = (f32[2,4,1,256]{3,2,1,0:T(1,128)S(1)}, f32[2,4,1,256]{3,2,1,0:T(1,128)S(1)}, u32[]{:S(2)}, u32[]{:S(2)}) collective-permute-start(f32[2,4,1,256]{3,2,1,0:T(1,128)S(1)} %constant_dynamic-slice_fusion.17), channel_id=1, source_target_pairs={{0,1},{1,0},{2,3},{3,2},{4,5},{5,4},{6,7},{7,6},{8,9},{9,8},{10,11... | collective-permute-start | bytes 24584 | tf_op jit(solution)/shard_map/ppermute | solution.py:50
  3.1 1.5 %copy-start = (f32[2,4,64,256]{3,2,1,0:T(8,128)S(1)}, f32[2,4,64,256]{3,2,1,0:T(8,128)}, u32[]{:S(2)}) copy-start(f32[2,4,64,256]{3,2,1,0:T(8,128)} %param.7) | copy-start | bytes 1572868
  4.5 19.9 %collective-permute-start.4 = (f32[3,4,1,256]{3,2,1,0:T(1,128)S(1)}, f32[3,4,1,256]{3,2,1,0:T(1,128)S(1)}, u32[]{:S(2)}, u32[]{:S(2)}) collective-permute-start(f32[3,4,1,256]{3,2,1,0:T(1,128)S(1)} %pad_maximum_fusion.53), channel_id=1, source_target_pairs={{0,1},{1,0},{2,3},{3,2},{4,5},{5,4},{6,7},{7,6},{8,9},{9,8},{10,11... | collective-permute-start | bytes 36872 | tf_op jit(solution)/shard_map/ppermute | solution.py:116
  5.1 11.4 %collective-permute-start.1 = (f32[4,1,64,256]{3,2,1,0:T(8,128)S(1)}, f32[4,1,64,256]{3,2,1,0:T(8,128)S(1)}, u32[]{:S(2)}, u32[]{:S(2)}) collective-permute-start(f32[4,1,64,256]{3,2,1,0:T(8,128)S(1)} %pad_maximum_fusion.39), channel_id=1, source_target_pairs={{2,0},{4,2},{6,4},{8,6},{10,8},{12,10},{14,12},{3,1},{5,3},{7,5},{... | collective-permute-start | bytes 786440 | tf_op jit(solution)/shard_map/ppermute | solution.py:133
  6.5 15.8 %collective-permute-start.2 = (f32[4,1,64,256]{3,2,1,0:T(8,128)S(1)}, f32[4,1,64,256]{3,2,1,0:T(8,128)S(1)}, u32[]{:S(2)}, u32[]{:S(2)}) collective-permute-start(f32[4,1,64,256]{3,2,1,0:T(8,128)S(1)} %pad_maximum_fusion.40), channel_id=1, source_target_pairs={{0,2},{2,4},{4,6},{6,8},{8,10},{10,12},{12,14},{1,3},{3,5},{5,7},{... | collective-permute-start | bytes 786440 | tf_op jit(solution)/shard_map/ppermute | solution.py:132
  23.0 1.3 %collective-permute-start.3 = (f32[2,10,1,256]{3,2,1,0:T(1,128)S(1)}, f32[2,10,1,256]{3,2,1,0:T(1,128)S(1)}, u32[]{:S(2)}, u32[]{:S(2)}) collective-permute-start(f32[2,10,1,256]{3,2,1,0:T(1,128)S(1)} %pad_maximum_fusion.51), channel_id=1, source_target_pairs={{0,1},{1,0},{2,3},{3,2},{4,5},{5,4},{6,7},{7,6},{8,9},{9,8},{10,11... | collective-permute-start | bytes 61448 | tf_op jit(solution)/shard_map/ppermute | solution.py:152
  25.5 11.0 %collective-permute-start.5 = (f32[4,1,64,256]{3,2,1,0:T(8,128)S(1)}, f32[4,1,64,256]{3,2,1,0:T(8,128)S(1)}, u32[]{:S(2)}, u32[]{:S(2)}) collective-permute-start(f32[4,1,64,256]{3,2,1,0:T(8,128)S(1)} %pad_maximum_fusion.41), channel_id=1, source_target_pairs={{2,0},{4,2},{6,4},{8,6},{10,8},{12,10},{14,12},{3,1},{5,3},{7,5},{... | collective-permute-start | bytes 786440 | tf_op jit(solution)/shard_map/ppermute | solution.py:133
  26.8 15.5 %collective-permute-start.6 = (f32[4,1,64,256]{3,2,1,0:T(8,128)S(1)}, f32[4,1,64,256]{3,2,1,0:T(8,128)S(1)}, u32[]{:S(2)}, u32[]{:S(2)}) collective-permute-start(f32[4,1,64,256]{3,2,1,0:T(8,128)S(1)} %pad_maximum_fusion.42), channel_id=1, source_target_pairs={{0,2},{2,4},{4,6},{6,8},{8,10},{10,12},{12,14},{1,3},{3,5},{5,7},{... | collective-permute-start | bytes 786440 | tf_op jit(solution)/shard_map/ppermute | solution.py:132
  43.0 1.2 %collective-permute-start.7 = (f32[2,4,1,256]{3,2,1,0:T(1,128)S(1)}, f32[2,4,1,256]{3,2,1,0:T(1,128)S(1)}, u32[]{:S(2)}, u32[]{:S(2)}) collective-permute-start(f32[2,4,1,256]{3,2,1,0:T(1,128)S(1)} %constant_dynamic-slice_fusion.9), channel_id=1, source_target_pairs={{0,1},{1,0},{2,3},{3,2},{4,5},{5,4},{6,7},{7,6},{8,9},{9,8},{10,11... | collective-permute-start | bytes 24584 | tf_op jit(solution)/shard_map/ppermute | solution.py:50
  45.0 1.2 %collective-permute-start.8 = (f32[2,4,1,256]{3,2,1,0:T(1,128)S(1)}, f32[2,4,1,256]{3,2,1,0:T(1,128)S(1)}, u32[]{:S(2)}, u32[]{:S(2)}) collective-permute-start(f32[2,4,1,256]{3,2,1,0:T(1,128)S(1)} %constant_dynamic-slice_fusion.8), channel_id=1, source_target_pairs={{0,1},{1,0},{2,3},{3,2},{4,5},{5,4},{6,7},{7,6},{8,9},{9,8},{10,11... | collective-permute-start | bytes 24584 | tf_op jit(solution)/shard_map/ppermute | solution.py:50
  46.6 15.9 %collective-permute-start.10 = (f32[4,1,64,256]{3,2,1,0:T(8,128)S(1)}, f32[4,1,64,256]{3,2,1,0:T(8,128)S(1)}, u32[]{:S(2)}, u32[]{:S(2)}) collective-permute-start(f32[4,1,64,256]{3,2,1,0:T(8,128)S(1)} %pad_maximum_fusion.44), channel_id=1, source_target_pairs={{0,2},{2,4},{4,6},{6,8},{8,10},{10,12},{12,14},{1,3},{3,5},{5,7},{... | collective-permute-start | bytes 786440 | tf_op jit(solution)/shard_map/ppermute | solution.py:132
  51.0 11.5 %collective-permute-start.9 = (f32[4,1,64,256]{3,2,1,0:T(8,128)S(1)}, f32[4,1,64,256]{3,2,1,0:T(8,128)S(1)}, u32[]{:S(2)}, u32[]{:S(2)}) collective-permute-start(f32[4,1,64,256]{3,2,1,0:T(8,128)S(1)} %pad_maximum_fusion.43), channel_id=1, source_target_pairs={{2,0},{4,2},{6,4},{8,6},{10,8},{12,10},{14,12},{3,1},{5,3},{7,5},{... | collective-permute-start | bytes 786440 | tf_op jit(solution)/shard_map/ppermute | solution.py:133
  63.4 1.3 %collective-permute-start.11 = (f32[2,10,1,256]{3,2,1,0:T(1,128)S(1)}, f32[2,10,1,256]{3,2,1,0:T(1,128)S(1)}, u32[]{:S(2)}, u32[]{:S(2)}) collective-permute-start(f32[2,10,1,256]{3,2,1,0:T(1,128)S(1)} %pad_maximum_fusion.52), channel_id=1, source_target_pairs={{0,1},{1,0},{2,3},{3,2},{4,5},{5,4},{6,7},{7,6},{8,9},{9,8},{10,11... | collective-permute-start | bytes 61448 | tf_op jit(solution)/shard_map/ppermute | solution.py:152
  63.5 1.4 %collective-permute-start.12 = (f32[3,4,1,256]{3,2,1,0:T(1,128)S(1)}, f32[3,4,1,256]{3,2,1,0:T(1,128)S(1)}, u32[]{:S(2)}, u32[]{:S(2)}) collective-permute-start(f32[3,4,1,256]{3,2,1,0:T(1,128)S(1)} %pad_maximum_fusion.54), channel_id=1, source_target_pairs={{0,1},{1,0},{2,3},{3,2},{4,5},{5,4},{6,7},{7,6},{8,9},{9,8},{10,11... | collective-permute-start | bytes 36872 | tf_op jit(solution)/shard_map/ppermute | solution.py:116
  66.2 11.2 %collective-permute-start.13 = (f32[4,1,64,256]{3,2,1,0:T(8,128)S(1)}, f32[4,1,64,256]{3,2,1,0:T(8,128)S(1)}, u32[]{:S(2)}, u32[]{:S(2)}) collective-permute-start(f32[4,1,64,256]{3,2,1,0:T(8,128)S(1)} %pad_maximum_fusion.45), channel_id=1, source_target_pairs={{2,0},{4,2},{6,4},{8,6},{10,8},{12,10},{14,12},{3,1},{5,3},{7,5},{... | collective-permute-start | bytes 786440 | tf_op jit(solution)/shard_map/ppermute | solution.py:133
  67.5 15.7 %collective-permute-start.14 = (f32[4,1,64,256]{3,2,1,0:T(8,128)S(1)}, f32[4,1,64,256]{3,2,1,0:T(8,128)S(1)}, u32[]{:S(2)}, u32[]{:S(2)}) collective-permute-start(f32[4,1,64,256]{3,2,1,0:T(8,128)S(1)} %pad_maximum_fusion.46), channel_id=1, source_target_pairs={{0,2},{2,4},{4,6},{6,8},{8,10},{10,12},{12,14},{1,3},{3,5},{5,7},{... | collective-permute-start | bytes 786440 | tf_op jit(solution)/shard_map/ppermute | solution.py:132
  84.0 1.2 %collective-permute-start.15 = (f32[2,4,1,256]{3,2,1,0:T(1,128)S(1)}, f32[2,4,1,256]{3,2,1,0:T(1,128)S(1)}, u32[]{:S(2)}, u32[]{:S(2)}) collective-permute-start(f32[2,4,1,256]{3,2,1,0:T(1,128)S(1)} %constant_dynamic-slice_fusion), channel_id=1, source_target_pairs={{0,1},{1,0},{2,3},{3,2},{4,5},{5,4},{6,7},{7,6},{8,9},{9,8},{10,11... | collective-permute-start | bytes 24584 | tf_op jit(solution)/shard_map/ppermute | solution.py:50
  85.8 1.1 copy-start.2
  86.9 0.8 copy-start.3
  87.8 1.5 %collective-permute-start.16 = (f32[]{:T(128)}, f32[]{:T(128)}, u32[]{:S(2)}, u32[]{:S(2)}) collective-permute-start(f32[]{:T(128)} %get-tuple-element.17), channel_id=1, source_target_pairs={{0,1},{1,0},{2,3},{3,2},{4,5},{5,4},{6,7},{7,6},{8,9},{9,8},{10,11... | collective-permute-start | bytes 20 | tf_op jit(solution)/shard_map/ppermute | solution.py:19
  91.2 5.1 %collective-permute-start.17 = (f32[65,256]{1,0:T(8,128)S(1)}, f32[65,256]{1,0:T(8,128)S(1)}, u32[]{:S(2)}, u32[]{:S(2)}) collective-permute-start(f32[65,256]{1,0:T(8,128)S(1)} %select_maximum_fusion), channel_id=1, source_target_pairs={{0,2},{2,0},{4,6},{6,4},{8,10},{10,8},{12,14},{14,12},{1,3},{3,1},... | collective-permute-start | bytes 199688 | tf_op jit(solution)/shard_map/ppermute | solution.py:28
  96.3 7.1 %collective-permute-start.20 = (f32[65,256]{1,0:T(8,128)S(1)}, f32[65,256]{1,0:T(8,128)S(1)}, u32[]{:S(2)}, u32[]{:S(2)}) collective-permute-start(f32[65,256]{1,0:T(8,128)S(1)} %fusion.286), channel_id=1, source_target_pairs={{0,12},{2,14},{4,8},{6,10},{8,4},{10,6},{12,0},{14,2},{1,13},{3,15... | collective-permute-start | bytes 199688 | tf_op jit(solution)/shard_map/ppermute | solution.py:33
  99.0 6.9 %collective-permute-start.19 = (f32[65,256]{1,0:T(8,128)S(1)}, f32[65,256]{1,0:T(8,128)S(1)}, u32[]{:S(2)}, u32[]{:S(2)}) collective-permute-start(f32[65,256]{1,0:T(8,128)S(1)} %fusion.286), channel_id=1, source_target_pairs={{0,8},{2,10},{4,12},{6,14},{8,0},{10,2},{12,4},{14,6},{1,9},{3,11}... | collective-permute-start | bytes 199688 | tf_op jit(solution)/shard_map/ppermute | solution.py:33
  99.4 6.5 %collective-permute-start.18 = (f32[65,256]{1,0:T(8,128)S(1)}, f32[65,256]{1,0:T(8,128)S(1)}, u32[]{:S(2)}, u32[]{:S(2)}) collective-permute-start(f32[65,256]{1,0:T(8,128)S(1)} %fusion.286), channel_id=1, source_target_pairs={{0,4},{2,6},{4,0},{6,2},{8,12},{10,14},{12,8},{14,10},{1,5},{3,7},... | collective-permute-start | bytes 199688 | tf_op jit(solution)/shard_map/ppermute | solution.py:33

commit v10 on v9

--- a/solution.py
+++ b/solution.py
@@ -117,7 +117,7 @@
     return tuple(got[k] for k in range(len(coef)))
 
 
-def stage_pair(stage, base, base_low, base_high, coef, weight, tall=None, ahead=None):
+def stage_pair(stage, base, base_low, base_high, coef, weight, tall=None, coef_partner=None):
     nx = lax.axis_size("gx")
     ix = lax.axis_index("gx")
     iy = lax.axis_index("gy")
@@ -141,43 +141,64 @@
     nxt = base + weight * section
     nxt_low = jnp.where(ix > 0, base_low + weight * section_low, 0.0)
     nxt_high = jnp.where(ix < nx - 1, base_high + weight * section_high, 0.0)
-    if ahead is None:
+    if coef_partner is None:
         section_next = operator(y_extended(nxt), nxt_low, nxt_high, coef)
         return section, section_next, base_low, base_high, None
-    next_weight, coef_partner = ahead
+    mine_stage = edge_rows(stage)
     mine = edge_rows(nxt)
     pack = jnp.concatenate(
-        [mine, edge_rows(nxt, 1), edge_rows(nxt_low), edge_rows(nxt_high)], axis=1
+        [mine, edge_rows(nxt, 1), edge_rows(nxt_low), edge_rows(nxt_high),
+         edge_rows(stage, 1), edge_rows(stage_low), edge_rows(stage_high)],
+        axis=1,
     )
     got = lax.ppermute(pack, "gy", [(0, 1), (1, 0)])
     their, their_inner = got[:, :X], got[:, X:2 * X]
     their_low, their_high = got[:, 2 * X:2 * X + 1], got[:, 2 * X + 1:2 * X + 2]
+    their_stage_inner = got[:, 2 * X + 2:3 * X + 2]
+    their_stage_low, their_stage_high = got[:, 3 * X + 2:3 * X + 3], got[:, 3 * X + 3:3 * X + 4]
     section_next = operator(with_partner_row(nxt, their), nxt_low, nxt_high, coef)
-    slab = jnp.where(
-        iy == 0,
-        jnp.concatenate([mine, their, their_inner], axis=2),
-        jnp.concatenate([their_inner, their, mine], axis=2),
-    )
-    their_section = operator(slab, their_low, their_high, coef_partner)
-    their_base = jnp.where(iy == 1, tall[:, :, :1], tall[:, :, -1:])
-    their_next = their_base + next_weight * their_section
-    return section, section_next, base_low, base_high, their_next
-
-
-def rk_step(field, coef):
+
+    def beside(mine_row, their_row, their_inner_row):
+        return jnp.where(
+            iy == 0,
+            jnp.concatenate([mine_row, their_row, their_inner_row], axis=2),
+            jnp.concatenate([their_inner_row, their_row, mine_row], axis=2),
+        )
+
+    their_stage = jnp.where(iy == 1, tall[:, :, :1], tall[:, :, -1:])
+    their_section = operator(
+        beside(mine_stage, their_stage, their_stage_inner), their_stage_low, their_stage_high,
+        coef_partner,
+    )
+    their_section_next = operator(beside(mine, their, their_inner), their_low, their_high, coef_partner)
+    return section, section_next, base_low, base_high, (their_stage, their_section, their_section_next)
+
+
+def rk_step(field, coef, tall=None):
     fast = lax.axis_size("gy") == 2 and field.shape[2] >= 3
-    ahead = (0.5 * STEP_SIZE, partner_coef(coef)) if fast else None
-    section_one, section_two, low, high, their_three = stage_pair(
-        field, field, None, None, coef, 0.5 * STEP_SIZE, ahead=ahead
+    partner = partner_coef(coef) if fast else None
+    section_one, section_two, low, high, first = stage_pair(
+        field, field, None, None, coef, 0.5 * STEP_SIZE, tall=tall, coef_partner=partner
     )
     stage_three = field + 0.5 * STEP_SIZE * section_two
-    tall_three = with_partner_row(stage_three, their_three) if fast else None
-    section_three, section_four, _, _, _ = stage_pair(
-        stage_three, field, low, high, coef, STEP_SIZE, tall=tall_three
-    )
-    return field + STEP_SIZE / 6.0 * (
+    tall_three = None
+    if fast:
+        their_field, their_one, their_two = first
+        their_three = their_field + 0.5 * STEP_SIZE * their_two
+        tall_three = with_partner_row(stage_three, their_three)
+    section_three, section_four, _, _, second = stage_pair(
+        stage_three, field, low, high, coef, STEP_SIZE, tall=tall_three, coef_partner=partner
+    )
+    result = field + STEP_SIZE / 6.0 * (
         section_one + 2.0 * section_two + 2.0 * section_three + section_four
     )
+    if not fast:
+        return result, None
+    _, their_three_section, their_four = second
+    their_result = their_field + STEP_SIZE / 6.0 * (
+        their_one + 2.0 * their_two + 2.0 * their_three_section + their_four
+    )
+    return result, with_partner_row(result, their_result)
 
 
 def row_terms(field, psi, profile):
@@ -197,8 +218,8 @@
     profile = 1.0 + 0.5 * jnp.cos(2.0 * math.pi * x_index / float(total_x))
     coef_late = coefficients(psi_late, trap, controls[1], profile)
     coef_early = coefficients(psi_early, trap, controls[0], profile)
-    chi_late = rk_step(chi_final, coef_late)
-    chi_start = rk_step(chi_late, coef_early)
+    chi_late, tall_late = rk_step(chi_final, coef_late)
+    chi_start, _ = rk_step(chi_late, coef_early, tall=tall_late)
     rows_late = row_terms(chi_late, psi_late, profile)
     rows_early = row_terms(chi_start, psi_early, profile)
     local_sq = axis_sum(jnp.sum(chi_start * chi_start), "gy")

time: 109 us -> 146 us (1.34)
  other arithmetic: 12 us -> 33.1 us
  local copies, waits for them, and re-layouts: 3.27 us -> 21.1 us
  waiting for transfers between devices: 54.4 us -> 49.8 us
    unnamed x8 -> x95, local copies, waits for them, and re-layouts: 0.54 us -> 9.79 us
    ppermute x4, waiting for transfers between devices: 13.9 us -> 7.07 us  [stage_pair(): lax.ppermute(jnp.concatenate([stage[:, :1], part_bottom]), 'gx', down)]
    another operation x16 -> x19, other arithmetic: 1.7 us -> 5.72 us  [apply_coef(): return jnp.stack([-lower, upper])]
    concatenate x0 -> x7, local copies, waits for them, and re-layouts: none -> 2.86 us  [the longest x4 2.01 us: stage_pair(): jnp.concatenate([mine, edge_rows(nxt, 1), edge_rows(nxt_low), edge_rows(n...]
    sub x14 -> x18, other arithmetic: 3.83 us -> 6.55 us  [operator(): lapl = total - 6.0 * field]
    ppermute x4 -> x1, waiting for transfers between devices: 2.62 us -> 0.01 us  [y_extended(): other = lax.ppermute(strip, 'gy', [(0, 1), (1, 0)])]
    slice x0 -> x17, local copies, waits for them, and re-layouts: none -> 2.45 us  [the longest x1 1.07 us: coefficients(): real_part = psi[0]]
    ppermute x4, waiting for transfers between devices: 27.3 us -> 29.6 us  [stage_pair(): lax.ppermute(jnp.concatenate([stage[:, X - 1:], part_top]), 'gx', up)]
  transfers between devices with their start and end apart: 21 -> 20, of which waited for: 16 -> 13; matrix products, arithmetic and copies ran while one was open for 5% -> 11% of each run, Pallas kernels for 0% -> 0%
where the time goes in v10:
time: 146 us; the launch traced here: 145 us
  waiting for transfers between devices  49.8 us (34%)
  starting transfers between devices  34.4 us (24%)
  other arithmetic  33.1 us (23%)
  local copies, waits for them, and re-layouts  21.1 us (14%)
  between operations  6.13 us (4%)
    ppermute x4, waiting for transfers between devices, stage_pair(): lax.ppermute(jnp.concatenate([stage[:, X - 1:], part_top]), 'gx', up)  29.6 us
    ppermute x4, starting transfers between devices, stage_pair(): lax.ppermute(jnp.concatenate([stage[:, X - 1:], part_top]), 'gx', up)  19.5 us
    unnamed x95, local copies, waits for them, and re-layouts  9.79 us
    ppermute x4, waiting for transfers between devices, stage_pair(): lax.ppermute(jnp.concatenate([stage[:, :1], part_bottom]), 'gx', down)  7.07 us
    sub x18, other arithmetic, operator(): lapl = total - 6.0 * field  6.55 us
    ppermute x3, waiting for transfers between devices, gx_total(): lax.ppermute(pair, 'gx', [(i, i ^ 2 * k) for i in range(count)])  6.25 us
    another operation x19, other arithmetic, apply_coef(): return jnp.stack([-lower, upper])  5.72 us
    ppermute x4, starting transfers between devices, stage_pair(): lax.ppermute(jnp.concatenate([stage[:, :1], part_bottom]), 'gx', down)  5.56 us
  transfers between devices with their start and end apart: 20, of which 13 were waited for; matrix products, arithmetic and copies ran while one was open for 11% of the time, Pallas kernels for 0%

profile of v10, /device:TPU:0, one launch (start us, length us, event | category | flops | bytes accessed | tf_op | source)
XLA Modules:
  0.0 144.6 jit_solution(6587832015392977398)
XLA Ops:
  0.6 0.9 constant_dynamic-slice_fusion.35
  2.1 1.1 fusion.313
  6.4 0.7 fusion.315
  8.0 0.8 fusion.306
  8.8 0.7 fusion.301
  9.9 0.8 broadcast_select_fusion.17
  11.6 0.7 pad_maximum_fusion.35
  12.3 1.3 collective-permute-start.1
  13.7 5.5 %collective-permute-start.2 = (f32[4,1,64,256]{3,2,1,0:T(8,128)S(1)}, f32[4,1,64,256]{3,2,1,0:T(8,128)S(1)}, u32[]{:S(2)}, u32[]{:S(2)}) collective-permute-start(f32[4,1,64,256]{3,2,1,0:T(8,128)S(1)} %pad_maximum_fusion.36), channel_id=1, source_target_pairs={{0,2},{2,4},{4,6},{6,8},{8,10},{10,12},{12,14},{1,3},{3,5},{5,7},{... | collective-permute-start | bytes 786440 | tf_op jit(solution)/shard_map/ppermute | solution.py:132
  19.2 1.4 constant_dynamic-slice_fusion.9
  20.5 3.4 %collective-permute-done.1 = f32[4,1,64,256]{3,2,1,0:T(8,128)} collective-permute-done((f32[4,1,64,256]{3,2,1,0:T(8,128)}, f32[4,1,64,256]{3,2,1,0:T(8,128)}, u32[]{:S(2)}, u32[]{:S(2)}) %collective-permute-start.1) | collective-permute-done | bytes 262176 | tf_op jit(solution)/shard_map/ppermute | solution.py:133
  24.0 1.1 fusion.167
  25.0 4.6 %collective-permute-done.2 = f32[4,1,64,256]{3,2,1,0:T(8,128)S(1)} collective-permute-done((f32[4,1,64,256]{3,2,1,0:T(8,128)S(1)}, f32[4,1,64,256]{3,2,1,0:T(8,128)S(1)}, u32[]{:S(2)}, u32[]{:S(2)}) %collective-permute-start.2) | collective-permute-done | bytes 262176 | tf_op jit(solution)/shard_map/ppermute | solution.py:132
  31.3 1.2 collective-permute-done.3
  34.3 0.7 fusion.294
  35.0 0.7 fusion.293
  36.0 0.7 copy-done.13
  36.8 4.4 %collective-permute-start.6 = (f32[4,1,64,256]{3,2,1,0:T(8,128)S(1)}, f32[4,1,64,256]{3,2,1,0:T(8,128)S(1)}, u32[]{:S(2)}, u32[]{:S(2)}) collective-permute-start(f32[4,1,64,256]{3,2,1,0:T(8,128)S(1)} %pad_maximum_fusion.38), channel_id=1, source_target_pairs={{0,2},{2,4},{4,6},{6,8},{8,10},{10,12},{12,14},{1,3},{3,5},{5,7},{... | collective-permute-start | bytes 786440 | tf_op jit(solution)/shard_map/ppermute | solution.py:132
  41.3 1.5 %collective-permute-start.5 = (f32[4,1,64,256]{3,2,1,0:T(8,128)S(1)}, f32[4,1,64,256]{3,2,1,0:T(8,128)S(1)}, u32[]{:S(2)}, u32[]{:S(2)}) collective-permute-start(f32[4,1,64,256]{3,2,1,0:T(8,128)S(1)} %pad_maximum_fusion.37), channel_id=1, source_target_pairs={{2,0},{4,2},{6,4},{8,6},{10,8},{12,10},{14,12},{3,1},{5,3},{7,5},{... | collective-permute-start | bytes 786440 | tf_op jit(solution)/shard_map/ppermute | solution.py:133
  42.9 9.8 %collective-permute-done.6 = f32[4,1,64,256]{3,2,1,0:T(8,128)S(1)} collective-permute-done((f32[4,1,64,256]{3,2,1,0:T(8,128)S(1)}, f32[4,1,64,256]{3,2,1,0:T(8,128)S(1)}, u32[]{:S(2)}, u32[]{:S(2)}) %collective-permute-start.6) | collective-permute-done | bytes 262176 | tf_op jit(solution)/shard_map/ppermute | solution.py:132
  56.4 0.7 fusion.7
  57.4 1.1 fusion.45
  59.1 0.7 fusion.296
  62.4 4.4 %collective-permute-start.9 = (f32[4,1,64,256]{3,0,2,1:T(4,128)S(1)}, f32[4,1,64,256]{3,0,2,1:T(4,128)S(1)}, u32[]{:S(2)}, u32[]{:S(2)}) collective-permute-start(f32[4,1,64,256]{3,0,2,1:T(4,128)S(1)} %pad_maximum_fusion.40), channel_id=1, source_target_pairs={{0,2},{2,4},{4,6},{6,8},{8,10},{10,12},{12,14},{1,3},{3,5},{5,7},{... | collective-permute-start | bytes 786440 | tf_op jit(solution)/shard_map/ppermute | solution.py:132
  66.9 1.5 %collective-permute-start.8 = (f32[4,1,64,256]{3,2,1,0:T(8,128)S(1)}, f32[4,1,64,256]{3,2,1,0:T(8,128)S(1)}, u32[]{:S(2)}, u32[]{:S(2)}) collective-permute-start(f32[4,1,64,256]{3,2,1,0:T(8,128)S(1)} %pad_maximum_fusion.39), channel_id=1, source_target_pairs={{2,0},{4,2},{6,4},{8,6},{10,8},{12,10},{14,12},{3,1},{5,3},{7,5},{... | collective-permute-start | bytes 786440 | tf_op jit(solution)/shard_map/ppermute | solution.py:133
  68.5 9.8 %collective-permute-done.9 = f32[4,1,64,256]{3,0,2,1:T(4,128)S(1)} collective-permute-done((f32[4,1,64,256]{3,0,2,1:T(4,128)S(1)}, f32[4,1,64,256]{3,0,2,1:T(4,128)S(1)}, u32[]{:S(2)}, u32[]{:S(2)}) %collective-permute-start.9) | collective-permute-done | bytes 262176 | tf_op jit(solution)/shard_map/ppermute | solution.py:132
  79.3 1.2 fusion.2
  81.6 0.9 fusion.118
  82.5 0.9 pad_maximum_fusion.32
  84.1 0.7 compare_reduce_fusion
  89.6 1.3 collective-permute-start.12
  91.5 5.3 %collective-permute-start.13 = (f32[4,1,64,256]{3,1,2,0:T(1,128)S(1)}, f32[4,1,64,256]{3,1,2,0:T(1,128)S(1)}, u32[]{:S(2)}, u32[]{:S(2)}) collective-permute-start(f32[4,1,64,256]{3,1,2,0:T(1,128)S(1)} %pad_maximum_fusion.42), channel_id=1, source_target_pairs={{0,2},{2,4},{4,6},{6,8},{8,10},{10,12},{12,14},{1,3},{3,5},{5,7},{... | collective-permute-start | bytes 786440 | tf_op jit(solution)/shard_map/ppermute | solution.py:132
  96.9 3.6 %collective-permute-done.12 = f32[4,1,64,256]{3,1,2,0:T(1,128)S(1)} collective-permute-done((f32[4,1,64,256]{3,1,2,0:T(1,128)S(1)}, f32[4,1,64,256]{3,1,2,0:T(1,128)S(1)}, u32[]{:S(2)}, u32[]{:S(2)}) %collective-permute-start.12) | collective-permute-done | bytes 262176 | tf_op jit(solution)/shard_map/ppermute | solution.py:133
  101.0 5.4 %collective-permute-done.13 = f32[4,1,64,256]{3,1,2,0:T(1,128)S(1)} collective-permute-done((f32[4,1,64,256]{3,1,2,0:T(1,128)S(1)}, f32[4,1,64,256]{3,1,2,0:T(1,128)S(1)}, u32[]{:S(2)}, u32[]{:S(2)}) %collective-permute-start.13) | collective-permute-done | bytes 262176 | tf_op jit(solution)/shard_map/ppermute | solution.py:132
  107.6 1.1 fusion.4
  111.9 2.0 %concatenate.343 = f32[2,16,1,256]{3,1,2,0:T(8,128)} concatenate(f32[2,4,1,256]{3,1,2,0:T(4,128)S(1)} %get-tuple-element.91, f32[2,4,1,256]{3,1,2,0:T(4,128)S(1)} %get-tuple-element.90, f32[2,1,1,256]{3,1,2,0:T(1,128)} %get-tuple-element.221, f32[2,1,1,256]{3,1,2,0:T(1,128)} %get-tuple-element.220, f32[2,4,1,256]{3,1,2,0:T(4,128)} %get-tuple-element.222, ...), dimensions={1} | concatenate | bytes 65536 | tf_op jit(solution)/shard_map/concatenate | solution.py:149
  113.9 1.4 collective-permute-done.14
  115.3 0.7 fusion.10
  117.3 1.3 multiply_reduce_fusion
  118.9 1.1 copy-done.14
  120.0 1.2 fusion.53
  121.7 1.1 collective-permute-done.15
  124.9 2.5 %collective-permute-start.16 = (f32[65,256]{1,0:T(8,128)S(1)}, f32[65,256]{1,0:T(8,128)S(1)}, u32[]{:S(2)}, u32[]{:S(2)}) collective-permute-start(f32[65,256]{1,0:T(8,128)S(1)} %select_maximum_fusion), channel_id=1, source_target_pairs={{0,2},{2,0},{4,6},{6,4},{8,10},{10,8},{12,14},{14,12},{1,3},{3,1},... | collective-permute-start | bytes 199688 | tf_op jit(solution)/shard_map/ppermute | solution.py:28
  127.4 2.6 %collective-permute-done.16 = f32[65,256]{1,0:T(8,128)S(1)} collective-permute-done((f32[65,256]{1,0:T(8,128)S(1)}, f32[65,256]{1,0:T(8,128)S(1)}, u32[]{:S(2)}, u32[]{:S(2)}) %collective-permute-start.16) | collective-permute-done | bytes 66592 | tf_op jit(solution)/shard_map/ppermute | solution.py:28
  130.0 2.6 %collective-permute-start.17 = (f32[65,256]{1,0:T(8,128)S(1)}, f32[65,256]{1,0:T(8,128)S(1)}, u32[]{:S(2)}, u32[]{:S(2)}) collective-permute-start(f32[65,256]{1,0:T(8,128)S(1)} %fusion.302), channel_id=1, source_target_pairs={{0,4},{2,6},{4,0},{6,2},{8,12},{10,14},{12,8},{14,10},{1,5},{3,7},... | collective-permute-start | bytes 199688 | tf_op jit(solution)/shard_map/ppermute | solution.py:33
  132.7 2.6 %collective-permute-start.18 = (f32[65,256]{1,0:T(8,128)S(1)}, f32[65,256]{1,0:T(8,128)S(1)}, u32[]{:S(2)}, u32[]{:S(2)}) collective-permute-start(f32[65,256]{1,0:T(8,128)S(1)} %fusion.302), channel_id=1, source_target_pairs={{0,8},{2,10},{4,12},{6,14},{8,0},{10,2},{12,4},{14,6},{1,9},{3,11}... | collective-permute-start | bytes 199688 | tf_op jit(solution)/shard_map/ppermute | solution.py:33
  135.3 4.7 %collective-permute-done.18 = f32[65,256]{1,0:T(8,128)S(1)} collective-permute-done((f32[65,256]{1,0:T(8,128)S(1)}, f32[65,256]{1,0:T(8,128)S(1)}, u32[]{:S(2)}, u32[]{:S(2)}) %collective-permute-start.18) | collective-permute-done | bytes 66592 | tf_op jit(solution)/shard_map/ppermute | solution.py:33
  139.9 1.6 %collective-permute-done.19 = f32[65,256]{1,0:T(8,128)S(1)} collective-permute-done((f32[65,256]{1,0:T(8,128)S(1)}, f32[65,256]{1,0:T(8,128)S(1)}, u32[]{:S(2)}, u32[]{:S(2)}) %collective-permute-start.19) | collective-permute-done | bytes 66592 | tf_op jit(solution)/shard_map/ppermute | solution.py:33
  (284 shorter events, 32.4 us)
Async XLA Ops:
  1.5 1.6 %copy-start.30 = (f32[2,4,1,256]{3,2,1,0:T(1,128)}, f32[2,4,1,256]{3,2,1,0:T(1,128)S(1)}, u32[]{:S(2)}) copy-start(f32[2,4,1,256]{3,2,1,0:T(1,128)S(1)} %constant_dynamic-slice_fusion.35) | copy-start | bytes 24580
  1.5 8.4 %collective-permute-start = (f32[2,4,1,256]{3,2,1,0:T(1,128)S(1)}, f32[2,4,1,256]{3,2,1,0:T(1,128)}, u32[]{:S(2)}, u32[]{:S(2)}) collective-permute-start(f32[2,4,1,256]{3,2,1,0:T(1,128)S(1)} %constant_dynamic-slice_fusion.35), channel_id=1, source_target_pairs={{0,1},{1,0},{2,3},{3,2},{4,5},{5,4},{6,7},{7,6},{8,9},{9,8},{10,11... | collective-permute-start | bytes 24584 | tf_op jit(solution)/shard_map/ppermute | solution.py:50
  3.1 0.8 copy-start.29
  3.2 1.3 copy-start.24
  3.3 1.1 copy-start.1
  3.4 1.2 copy-start.6
  4.7 4.0 %copy-start.9 = (f32[4,64,256]{2,1,0:T(8,128)}, f32[4,64,256]{2,1,0:T(8,128)S(1)}, u32[]{:S(2)}) copy-start(f32[4,64,256]{2,1,0:T(8,128)S(1)} %get-tuple-element.140) | copy-start | bytes 786436
  5.3 1.0 copy-start
  6.3 27.9 %collective-permute-start.4 = (f32[3,4,1,256]{3,2,1,0:T(1,128)}, f32[3,4,1,256]{3,2,1,0:T(1,128)}, u32[]{:S(2)}, u32[]{:S(2)}) collective-permute-start(f32[3,4,1,256]{3,2,1,0:T(1,128)} %pad_maximum_fusion.53), channel_id=1, source_target_pairs={{0,1},{1,0},{2,3},{3,2},{4,5},{5,4},{6,7},{7,6},{8,9},{9,8},{10,11... | collective-permute-start | bytes 36872 | tf_op jit(solution)/shard_map/ppermute | solution.py:116
  9.9 3.7 %copy-start.12 = (f32[4,64,256]{2,1,0:T(8,128)}, f32[4,64,256]{2,1,0:T(8,128)S(1)}, u32[]{:S(2)}) copy-start(f32[4,64,256]{2,1,0:T(8,128)S(1)} %copy.19) | copy-start | bytes 786436
  10.7 0.8 copy-start.16
  12.3 11.7 %collective-permute-start.1 = (f32[4,1,64,256]{3,2,1,0:T(8,128)}, f32[4,1,64,256]{3,2,1,0:T(8,128)}, u32[]{:S(2)}, u32[]{:S(2)}) collective-permute-start(f32[4,1,64,256]{3,2,1,0:T(8,128)} %pad_maximum_fusion.35), channel_id=1, source_target_pairs={{2,0},{4,2},{6,4},{8,6},{10,8},{12,10},{14,12},{3,1},{5,3},{7,5},{... | collective-permute-start | bytes 786440 | tf_op jit(solution)/shard_map/ppermute | solution.py:133
  13.7 16.0 %collective-permute-start.2 = (f32[4,1,64,256]{3,2,1,0:T(8,128)S(1)}, f32[4,1,64,256]{3,2,1,0:T(8,128)S(1)}, u32[]{:S(2)}, u32[]{:S(2)}) collective-permute-start(f32[4,1,64,256]{3,2,1,0:T(8,128)S(1)} %pad_maximum_fusion.36), channel_id=1, source_target_pairs={{0,2},{2,4},{4,6},{6,8},{8,10},{10,12},{12,14},{1,3},{3,5},{5,7},{... | collective-permute-start | bytes 786440 | tf_op jit(solution)/shard_map/ppermute | solution.py:132
  24.0 5.7 %copy-start.25 = (f32[1,1,64,256]{3,2,1,0:T(8,128)S(1)}, f32[1,1,64,256]{3,2,1,0:T(8,128)}, u32[]{:S(2)}) copy-start(f32[1,1,64,256]{3,2,1,0:T(8,128)} %get-tuple-element.131) | copy-start | bytes 196612
  24.0 5.7 %copy-start.26 = (f32[1,1,64,256]{3,2,1,0:T(8,128)S(1)}, f32[1,1,64,256]{3,2,1,0:T(8,128)}, u32[]{:S(2)}) copy-start(f32[1,1,64,256]{3,2,1,0:T(8,128)} %get-tuple-element.133) | copy-start | bytes 196612
  31.2 1.3 collective-permute-start.3
  35.8 1.0 copy-start.13
  35.8 0.9 copy-start.17
  36.8 15.9 %collective-permute-start.6 = (f32[4,1,64,256]{3,2,1,0:T(8,128)S(1)}, f32[4,1,64,256]{3,2,1,0:T(8,128)S(1)}, u32[]{:S(2)}, u32[]{:S(2)}) collective-permute-start(f32[4,1,64,256]{3,2,1,0:T(8,128)S(1)} %pad_maximum_fusion.38), channel_id=1, source_target_pairs={{0,2},{2,4},{4,6},{6,8},{8,10},{10,12},{12,14},{1,3},{3,5},{5,7},{... | collective-permute-start | bytes 786440 | tf_op jit(solution)/shard_map/ppermute | solution.py:132
  41.3 11.8 %collective-permute-start.5 = (f32[4,1,64,256]{3,2,1,0:T(8,128)S(1)}, f32[4,1,64,256]{3,2,1,0:T(8,128)S(1)}, u32[]{:S(2)}, u32[]{:S(2)}) collective-permute-start(f32[4,1,64,256]{3,2,1,0:T(8,128)S(1)} %pad_maximum_fusion.37), channel_id=1, source_target_pairs={{2,0},{4,2},{6,4},{8,6},{10,8},{12,10},{14,12},{3,1},{5,3},{7,5},{... | collective-permute-start | bytes 786440 | tf_op jit(solution)/shard_map/ppermute | solution.py:133
  55.1 1.3 collective-permute-start.7
  60.7 0.8 copy-start.18
  60.7 0.9 copy-start.19
  60.7 0.9 copy-start.20
  60.7 0.9 copy-start.21
  62.4 15.9 %collective-permute-start.9 = (f32[4,1,64,256]{3,0,2,1:T(4,128)S(1)}, f32[4,1,64,256]{3,0,2,1:T(4,128)S(1)}, u32[]{:S(2)}, u32[]{:S(2)}) collective-permute-start(f32[4,1,64,256]{3,0,2,1:T(4,128)S(1)} %pad_maximum_fusion.40), channel_id=1, source_target_pairs={{0,2},{2,4},{4,6},{6,8},{8,10},{10,12},{12,14},{1,3},{3,5},{5,7},{... | collective-permute-start | bytes 786440 | tf_op jit(solution)/shard_map/ppermute | solution.py:132
  66.9 12.0 %collective-permute-start.8 = (f32[4,1,64,256]{3,2,1,0:T(8,128)S(1)}, f32[4,1,64,256]{3,2,1,0:T(8,128)S(1)}, u32[]{:S(2)}, u32[]{:S(2)}) collective-permute-start(f32[4,1,64,256]{3,2,1,0:T(8,128)S(1)} %pad_maximum_fusion.39), channel_id=1, source_target_pairs={{2,0},{4,2},{6,4},{8,6},{10,8},{12,10},{14,12},{3,1},{5,3},{7,5},{... | collective-permute-start | bytes 786440 | tf_op jit(solution)/shard_map/ppermute | solution.py:133
  80.5 1.0 copy-start.7
  80.5 1.1 copy-start.10
  83.6 1.3 collective-permute-start.10
  83.6 1.5 %collective-permute-start.11 = (f32[3,4,1,256]{3,1,2,0:T(4,128)S(1)}, f32[3,4,1,256]{3,1,2,0:T(4,128)S(1)}, u32[]{:S(2)}, u32[]{:S(2)}) collective-permute-start(f32[3,4,1,256]{3,1,2,0:T(4,128)S(1)} %pad_maximum_fusion.54), channel_id=1, source_target_pairs={{0,1},{1,0},{2,3},{3,2},{4,5},{5,4},{6,7},{7,6},{8,9},{9,8},{10,11... | collective-permute-start | bytes 36872 | tf_op jit(solution)/shard_map/ppermute | solution.py:116
  89.6 10.9 %collective-permute-start.12 = (f32[4,1,64,256]{3,1,2,0:T(1,128)S(1)}, f32[4,1,64,256]{3,1,2,0:T(1,128)S(1)}, u32[]{:S(2)}, u32[]{:S(2)}) collective-permute-start(f32[4,1,64,256]{3,1,2,0:T(1,128)S(1)} %copy.209), channel_id=1, source_target_pairs={{2,0},{4,2},{6,4},{8,6},{10,8},{12,10},{14,12},{3,1},{5,3},{7,5},{... | collective-permute-start | bytes 786440 | tf_op jit(solution)/shard_map/ppermute | solution.py:133
  91.5 15.0 %collective-permute-start.13 = (f32[4,1,64,256]{3,1,2,0:T(1,128)S(1)}, f32[4,1,64,256]{3,1,2,0:T(1,128)S(1)}, u32[]{:S(2)}, u32[]{:S(2)}) collective-permute-start(f32[4,1,64,256]{3,1,2,0:T(1,128)S(1)} %pad_maximum_fusion.42), channel_id=1, source_target_pairs={{0,2},{2,4},{4,6},{6,8},{8,10},{10,12},{12,14},{1,3},{3,5},{5,7},{... | collective-permute-start | bytes 786440 | tf_op jit(solution)/shard_map/ppermute | solution.py:132
  106.9 4.4 %copy-start.22 = (f32[2,1,64,256]{3,1,2,0:T(1,128)}, f32[2,1,64,256]{3,1,2,0:T(1,128)S(1)}, u32[]{:S(2)}) copy-start(f32[2,1,64,256]{3,1,2,0:T(1,128)S(1)} %get-tuple-element.143) | copy-start | bytes 393220
  113.9 1.4 copy-start.23
  113.9 1.4 collective-permute-start.14
  116.0 1.0 copy-start.3
  116.0 1.1 copy-start.5
  116.1 1.3 copy-start.8
  118.8 2.5 %copy-start.11 = (f32[2,4,64,256]{3,2,1,0:T(8,128)}, f32[2,4,64,256]{3,2,1,0:T(8,128)S(1)}, u32[]{:S(2)}) copy-start(f32[2,4,64,256]{3,2,1,0:T(8,128)S(1)} %copy.252) | copy-start | bytes 1572868
  118.8 1.1 copy-start.14
  118.8 1.2 copy-start.15
  118.8 1.2 copy-start.34
  121.5 1.3 collective-permute-start.15
  124.9 5.2 %collective-permute-start.16 = (f32[65,256]{1,0:T(8,128)S(1)}, f32[65,256]{1,0:T(8,128)S(1)}, u32[]{:S(2)}, u32[]{:S(2)}) collective-permute-start(f32[65,256]{1,0:T(8,128)S(1)} %select_maximum_fusion), channel_id=1, source_target_pairs={{0,2},{2,0},{4,6},{6,4},{8,10},{10,8},{12,14},{14,12},{1,3},{3,1},... | collective-permute-start | bytes 199688 | tf_op jit(solution)/shard_map/ppermute | solution.py:28
  130.0 5.2 %collective-permute-start.17 = (f32[65,256]{1,0:T(8,128)S(1)}, f32[65,256]{1,0:T(8,128)S(1)}, u32[]{:S(2)}, u32[]{:S(2)}) collective-permute-start(f32[65,256]{1,0:T(8,128)S(1)} %fusion.302), channel_id=1, source_target_pairs={{0,4},{2,6},{4,0},{6,2},{8,12},{10,14},{12,8},{14,10},{1,5},{3,7},... | collective-permute-start | bytes 199688 | tf_op jit(solution)/shard_map/ppermute | solution.py:33
  132.7 7.3 %collective-permute-start.18 = (f32[65,256]{1,0:T(8,128)S(1)}, f32[65,256]{1,0:T(8,128)S(1)}, u32[]{:S(2)}, u32[]{:S(2)}) collective-permute-start(f32[65,256]{1,0:T(8,128)S(1)} %fusion.302), channel_id=1, source_target_pairs={{0,8},{2,10},{4,12},{6,14},{8,0},{10,2},{12,4},{14,6},{1,9},{3,11}... | collective-permute-start | bytes 199688 | tf_op jit(solution)/shard_map/ppermute | solution.py:33
  135.3 6.3 %collective-permute-start.19 = (f32[65,256]{1,0:T(8,128)S(1)}, f32[65,256]{1,0:T(8,128)S(1)}, u32[]{:S(2)}, u32[]{:S(2)}) collective-permute-start(f32[65,256]{1,0:T(8,128)S(1)} %fusion.302), channel_id=1, source_target_pairs={{0,12},{2,14},{4,8},{6,10},{8,4},{10,6},{12,0},{14,2},{1,13},{3,15... | collective-permute-start | bytes 199688 | tf_op jit(solution)/shard_map/ppermute | solution.py:33
  (7 other events, 4.7 us)

commit v11 on v9

--- a/solution.py
+++ b/solution.py
@@ -124,11 +124,13 @@
     X = stage.shape[1]
     up = [(i, i + 1) for i in range(nx - 1)]
     down = [(i + 1, i) for i in range(nx - 1)]
+    late_y = tall is None and ahead is not None
     if tall is None:
         tall = y_extended(stage)
+    send_tall = zero_extended(stage) if late_y else tall
     zero_plane = jnp.zeros_like(stage[:, :1])
-    part_top = operator(tall[:, X - 1:], stage[:, X - 2:X - 1], zero_plane, cut(coef, X - 1, X))
-    part_bottom = operator(tall[:, :1], zero_plane, stage[:, 1:2], cut(coef, 0, 1))
+    part_top = operator(send_tall[:, X - 1:], stage[:, X - 2:X - 1], zero_plane, cut(coef, X - 1, X))
+    part_bottom = operator(send_tall[:, :1], zero_plane, stage[:, 1:2], cut(coef, 0, 1))
     from_low = lax.ppermute(jnp.concatenate([stage[:, X - 1:], part_top]), "gx", up)
     from_high = lax.ppermute(jnp.concatenate([stage[:, :1], part_bottom]), "gx", down)
     stage_low, part_low = from_low[:2], from_low[2:]
@@ -145,13 +147,39 @@
         section_next = operator(y_extended(nxt), nxt_low, nxt_high, coef)
         return section, section_next, base_low, base_high, None
     next_weight, coef_partner = ahead
+    Y = stage.shape[2]
+    edge = (1 - iy) * (Y - 1)
     mine = edge_rows(nxt)
     pack = jnp.concatenate(
-        [mine, edge_rows(nxt, 1), edge_rows(nxt_low), edge_rows(nxt_high)], axis=1
+        [mine, edge_rows(nxt, 1), edge_rows(stage_low), edge_rows(stage_high),
+         edge_rows(section_low), edge_rows(section_high)],
+        axis=1,
     )
     got = lax.ppermute(pack, "gy", [(0, 1), (1, 0)])
     their, their_inner = got[:, :X], got[:, X:2 * X]
-    their_low, their_high = got[:, 2 * X:2 * X + 1], got[:, 2 * X + 1:2 * X + 2]
+    t_stage_low, t_stage_high, t_low, t_high = (
+        got[:, 2 * X + k:2 * X + k + 1] for k in range(4)
+    )
+
+    def halo_edge(part, base_x, other, keep):
+        return jnp.where(keep, base_x + weight * (part + across(other)), 0.0)
+
+    if late_y:
+        nxt_low = lax.dynamic_update_slice_in_dim(
+            nxt_low,
+            halo_edge(edge_rows(section_low), edge_rows(base_low), t_stage_low, ix > 0),
+            edge, axis=2,
+        )
+        nxt_high = lax.dynamic_update_slice_in_dim(
+            nxt_high,
+            halo_edge(edge_rows(section_high), edge_rows(base_high), t_stage_high, ix < nx - 1),
+            edge, axis=2,
+        )
+        their_low = halo_edge(t_low, t_stage_low, edge_rows(stage_low), ix > 0)
+        their_high = halo_edge(t_high, t_stage_high, edge_rows(stage_high), ix < nx - 1)
+    else:
+        their_low = jnp.where(ix > 0, t_stage_low + weight * t_low, 0.0)
+        their_high = jnp.where(ix < nx - 1, t_stage_high + weight * t_high, 0.0)
     section_next = operator(with_partner_row(nxt, their), nxt_low, nxt_high, coef)
     slab = jnp.where(
         iy == 0,
@@ -162,6 +190,11 @@
     their_base = jnp.where(iy == 1, tall[:, :, :1], tall[:, :, -1:])
     their_next = their_base + next_weight * their_section
     return section, section_next, base_low, base_high, their_next
+
+
+def zero_extended(block):
+    zero = jnp.zeros_like(block[:, :, :1])
+    return jnp.concatenate([zero, block, zero], axis=2)
 
 
 def rk_step(field, coef):

time: 109 us -> 132 us (1.21)
  other arithmetic: 12 us -> 27.5 us
  local copies, waits for them, and re-layouts: 3.27 us -> 14.3 us
  waiting for transfers between devices: 54.4 us -> 48.6 us
    unnamed x8 -> x98, local copies, waits for them, and re-layouts: 0.54 us -> 7.67 us
    ppermute x4, waiting for transfers between devices: 13.9 us -> 10.6 us  [stage_pair(): lax.ppermute(jnp.concatenate([stage[:, :1], part_bottom]), 'gx', down)]
    dynamic_update_slice x0 -> x4, local copies, waits for them, and re-layouts: none -> 2.76 us  [the longest x2 1.39 us: stage_pair(): lax.dynamic_update_slice_in_dim(nxt_high, halo_edge(edge_rows(section_hig...]
    select_n x0 -> x6, other arithmetic: none -> 2.67 us  [halo_edge(): return jnp.where(keep, base_x + weight * (part + across(other)), 0.0)]
    sub x14, other arithmetic: 3.83 us -> 6.47 us  [operator(): lapl = total - 6.0 * field]
    select_n x4, other arithmetic: 0.16 us -> 2.47 us  [stage_pair(): nxt_high = jnp.where(ix < nx - 1, base_high + weight * section_high, 0.0)]
    another operation x16, other arithmetic: 1.7 us -> 3.47 us  [apply_coef(): return jnp.stack([-lower, upper])]
    ppermute x4, waiting for transfers between devices: 2.62 us -> 1 us  [y_extended(): other = lax.ppermute(strip, 'gy', [(0, 1), (1, 0)])]
  transfers between devices with their start and end apart: 21 -> 21, of which waited for: 16 -> 15; matrix products, arithmetic and copies ran while one was open for 5% -> 14% of each run, Pallas kernels for 0% -> 0%
where the time goes in v11:
time: 132 us; the launch traced here: 131 us
  waiting for transfers between devices  48.6 us (37%)
  starting transfers between devices  35 us (27%)
  other arithmetic  27.5 us (21%)
  local copies, waits for them, and re-layouts  14.3 us (11%)
  between operations  5.38 us (4%)
    ppermute x4, waiting for transfers between devices, stage_pair(): lax.ppermute(jnp.concatenate([stage[:, X - 1:], part_top]), 'gx', up)  26 us
    ppermute x4, starting transfers between devices, stage_pair(): lax.ppermute(jnp.concatenate([stage[:, X - 1:], part_top]), 'gx', up)  20.3 us
    ppermute x4, waiting for transfers between devices, stage_pair(): lax.ppermute(jnp.concatenate([stage[:, :1], part_bottom]), 'gx', down)  10.6 us
    unnamed x98, local copies, waits for them, and re-layouts  7.67 us
    sub x14, other arithmetic, operator(): lapl = total - 6.0 * field  6.47 us
    ppermute x3, starting transfers between devices, gx_total(): lax.ppermute(pair, 'gx', [(i, i ^ 2 * k) for i in range(count)])  5.6 us
    ppermute x4, starting transfers between devices, stage_pair(): lax.ppermute(jnp.concatenate([stage[:, :1], part_bottom]), 'gx', down)  5.17 us
    ppermute x3, waiting for transfers between devices, gx_total(): lax.ppermute(pair, 'gx', [(i, i ^ 2 * k) for i in range(count)])  5.07 us
  transfers between devices with their start and end apart: 21, of which 15 were waited for; matrix products, arithmetic and copies ran while one was open for 14% of the time, Pallas kernels for 0%

profile of v11, /device:TPU:0, one launch (start us, length us, event | category | flops | bytes accessed | tf_op | source)
XLA Modules:
  0.0 130.8 jit_solution(15799044500114322683)
XLA Ops:
  0.6 0.9 constant_dynamic-slice_fusion.29
  2.2 0.8 slice_bitcast_fusion.18
  3.1 1.3 %multiply_add_fusion.6 = (f32[4,64,256]{2,1,0:T(8,128)S(1)}, f32[4,64,256]{2,1,0:T(8,128)S(1)}, f32[4,64,256]{2,1,0:T(8,128)S(1)}, f32[4,64,256]{2,1,0:T(8,128)S(1)}) fusion(f32[4,64,256]{2,1,0:T(8,128)} %param.10, f32[2,4,64,256]{3,2,1,0:T(8,128)} %param.8, f32[64,256]{1,0:T(8,128)S(1)} %mul.1101, f32[4]{0:T(128)S(1)} %multiply_add_fusion.7, ...), kind=kLoop, calls=%fused_computation.265 | loop fusion | flops 1114112 | bytes 2490384 | tf_op jit(solution)/shard_map/add | solution.py:65
  4.5 0.7 pad_maximum_fusion.51
  5.6 1.3 collective-permute-start
  6.9 0.7 pad_maximum_fusion.40
  7.6 5.5 %collective-permute-start.1 = (f32[4,1,64,256]{3,2,1,0:T(8,128)}, f32[4,1,64,256]{3,2,1,0:T(8,128)S(1)}, u32[]{:S(2)}, u32[]{:S(2)}) collective-permute-start(f32[4,1,64,256]{3,2,1,0:T(8,128)} %pad_maximum_fusion.40), channel_id=1, source_target_pairs={{0,2},{2,4},{4,6},{6,8},{8,10},{10,12},{12,14},{1,3},{3,5},{5,7},{... | collective-permute-start | bytes 786440 | tf_op jit(solution)/shard_map/ppermute | solution.py:134
  15.2 1.8 %collective-permute-done = f32[4,1,64,256]{3,2,1,0:T(8,128)S(1)} collective-permute-done((f32[4,1,64,256]{3,2,1,0:T(8,128)S(1)}, f32[4,1,64,256]{3,2,1,0:T(8,128)S(1)}, u32[]{:S(2)}, u32[]{:S(2)}) %collective-permute-start) | collective-permute-done | bytes 262176 | tf_op jit(solution)/shard_map/ppermute | solution.py:135
  16.9 1.7 %add_select_fusion.3 = (f32[2,1,64,256]{3,2,1,0:T(8,128)}, f32[2,1,64,256]{3,2,1,0:T(8,128)S(1)}, f32[2,1,64,256]{3,2,1,0:T(8,128)S(1)}) fusion(pred[]{:T(512)S(6)} %lt.19, f32[4,1,64,256]{3,2,1,0:T(8,128)S(1)} %collective-permute-done, f32[1,1,64,256]{3,2,1,0:T(8,128)} %get-tuple-element.103, f32[1,1,64,256]{3,2,1,0:T(8,128)S(1)} %copy-done.33), kind=kLoop, calls=%fused_computation.347 | loop fusion | flops 163840 | bytes 786433 | tf_op jit(solution)/shard_map/jit(_where)/select_n | solution.py:145
  18.6 4.2 %collective-permute-done.1 = f32[4,1,64,256]{3,2,1,0:T(8,128)S(1)} collective-permute-done((f32[4,1,64,256]{3,2,1,0:T(8,128)}, f32[4,1,64,256]{3,2,1,0:T(8,128)S(1)}, u32[]{:S(2)}, u32[]{:S(2)}) %collective-permute-start.1) | collective-permute-done | bytes 262176 | tf_op jit(solution)/shard_map/ppermute | solution.py:134
  22.8 0.7 add_select_fusion.2
  24.4 1.2 collective-permute-done.3
  25.8 0.7 fusion.280
  26.7 0.7 broadcast_select_fusion.25
  28.3 0.7 copy-done.14
  29.2 1.3 collective-permute-start.5
  30.5 5.1 %collective-permute-start.6 = (f32[4,1,64,256]{3,2,1,0:T(8,128)S(1)}, f32[4,1,64,256]{3,2,1,0:T(8,128)S(1)}, u32[]{:S(2)}, u32[]{:S(2)}) collective-permute-start(f32[4,1,64,256]{3,2,1,0:T(8,128)S(1)} %pad_maximum_fusion.42), channel_id=1, source_target_pairs={{0,2},{2,4},{4,6},{6,8},{8,10},{10,12},{12,14},{1,3},{3,5},{5,7},{... | collective-permute-start | bytes 786440 | tf_op jit(solution)/shard_map/ppermute | solution.py:134
  35.6 4.5 %collective-permute-done.5 = f32[4,1,64,256]{3,2,1,0:T(8,128)S(1)} collective-permute-done((f32[4,1,64,256]{3,2,1,0:T(8,128)S(1)}, f32[4,1,64,256]{3,2,1,0:T(8,128)S(1)}, u32[]{:S(2)}, u32[]{:S(2)}) %collective-permute-start.5) | collective-permute-done | bytes 262176 | tf_op jit(solution)/shard_map/ppermute | solution.py:135
  40.2 5.7 %collective-permute-done.6 = f32[4,1,64,256]{3,2,1,0:T(8,128)S(1)} collective-permute-done((f32[4,1,64,256]{3,2,1,0:T(8,128)S(1)}, f32[4,1,64,256]{3,2,1,0:T(8,128)S(1)}, u32[]{:S(2)}, u32[]{:S(2)}) %collective-permute-start.6) | collective-permute-done | bytes 262176 | tf_op jit(solution)/shard_map/ppermute | solution.py:134
  49.7 0.7 copy-done.8
  50.6 4.4 %collective-permute-start.9 = (f32[4,1,64,256]{3,2,1,0:T(8,128)S(1)}, f32[4,1,64,256]{3,2,1,0:T(8,128)S(1)}, u32[]{:S(2)}, u32[]{:S(2)}) collective-permute-start(f32[4,1,64,256]{3,2,1,0:T(8,128)S(1)} %pad_maximum_fusion.44), channel_id=1, source_target_pairs={{0,2},{2,4},{4,6},{6,8},{8,10},{10,12},{12,14},{1,3},{3,5},{5,7},{... | collective-permute-start | bytes 786440 | tf_op jit(solution)/shard_map/ppermute | solution.py:134
  55.0 1.3 collective-permute-start.8
  56.4 10.3 %collective-permute-done.9 = f32[4,1,64,256]{3,2,1,0:T(8,128)S(1)} collective-permute-done((f32[4,1,64,256]{3,2,1,0:T(8,128)S(1)}, f32[4,1,64,256]{3,2,1,0:T(8,128)S(1)}, u32[]{:S(2)}, u32[]{:S(2)}) %collective-permute-start.9) | collective-permute-done | bytes 262176 | tf_op jit(solution)/shard_map/ppermute | solution.py:134
  66.7 0.8 add_select_fusion
  67.5 0.7 add_select_fusion.1
  68.6 1.0 fusion.91
  69.6 1.0 multiply_add_fusion.2
  70.6 0.9 constant_dynamic-update-slice_fusion.11
  71.5 0.9 constant_dynamic-update-slice_fusion.10
  72.5 1.2 collective-permute-done.11
  75.8 1.3 %dynamic_update_slice.15 = f32[2,1,64,256]{3,2,1,0:T(8,128)} dynamic-update-slice(f32[2,1,64,256]{3,2,1,0:T(8,128)} %get-tuple-element.23, f32[2,1,1,256]{3,2,1,0:T(1,128)} %broadcast_select_fusion.19, s32[]{:T(128)} %constant.110.clone.1, s32[]{:T(128)} %constant.110.clone.1, s32[]{:T(128)S(6)} %select_n.227, s32[]{:T(128)} %constant.110.clone.1) | dynamic-update-slice | bytes 4100 | tf_op jit(solution)/shard_map/dynamic_update_slice | solution.py:168
  77.8 1.3 broadcast_select_fusion.23
  79.1 1.3 %dynamic_update_slice.14 = f32[2,1,64,256]{3,2,1,0:T(8,128)} dynamic-update-slice(f32[2,1,64,256]{3,2,1,0:T(8,128)} %get-tuple-element.21, f32[2,1,1,256]{3,2,1,0:T(1,128)} %broadcast_select_fusion.23, s32[]{:T(128)} %constant.110.clone.1, s32[]{:T(128)} %constant.110.clone.1, s32[]{:T(128)S(6)} %select_n.227, s32[]{:T(128)} %constant.110.clone.1) | dynamic-update-slice | bytes 4100 | tf_op jit(solution)/shard_map/dynamic_update_slice | solution.py:173
  80.4 3.0 %fusion.17 = f32[2,4,64,256]{3,2,1,0:T(8,128)S(1)} fusion(f32[2,4,64,256]{3,2,1,0:T(8,128)} %multiply_add_fusion.2, f32[2,4,1,256]{3,2,1,0:T(1,128)} %get-tuple-element.145, f32[2,4,1,256]{3,2,1,0:T(1,128)S(1)} %copy-done.36, f32[2,1,64,256]{3,2,1,0:T(8,128)} %dynamic_update_slice.15, f32[2,1,64,256]{3,2,1,0:T(8,128)} %dynamic_update_slice.14), kind=kLoop, calls=%fused_computation.41 | loop fusion | flops 1441792 | bytes 1327104 | tf_op jit(solution)/shard_map/sub | solution.py:87
  83.5 1.2 fusion.82
  85.2 0.7 copy-done.9
  86.1 1.3 collective-permute-start.13
  87.5 5.3 %collective-permute-start.14 = (f32[4,1,64,256]{3,2,1,0:T(8,128)S(1)}, f32[4,1,64,256]{3,2,1,0:T(8,128)S(1)}, u32[]{:S(2)}, u32[]{:S(2)}) collective-permute-start(f32[4,1,64,256]{3,2,1,0:T(8,128)S(1)} %pad_maximum_fusion.46), channel_id=1, source_target_pairs={{0,2},{2,4},{4,6},{6,8},{8,10},{10,12},{12,14},{1,3},{3,5},{5,7},{... | collective-permute-start | bytes 786440 | tf_op jit(solution)/shard_map/ppermute | solution.py:134
  92.8 4.3 %collective-permute-done.13 = f32[4,1,64,256]{3,2,1,0:T(8,128)S(1)} collective-permute-done((f32[4,1,64,256]{3,2,1,0:T(8,128)S(1)}, f32[4,1,64,256]{3,2,1,0:T(8,128)S(1)}, u32[]{:S(2)}, u32[]{:S(2)}) %collective-permute-start.13) | collective-permute-done | bytes 262176 | tf_op jit(solution)/shard_map/ppermute | solution.py:135
  97.2 5.7 %collective-permute-done.14 = f32[4,1,64,256]{3,2,1,0:T(8,128)S(1)} collective-permute-done((f32[4,1,64,256]{3,2,1,0:T(8,128)S(1)}, f32[4,1,64,256]{3,2,1,0:T(8,128)S(1)}, u32[]{:S(2)}, u32[]{:S(2)}) %collective-permute-start.14) | collective-permute-done | bytes 262176 | tf_op jit(solution)/shard_map/ppermute | solution.py:134
  105.5 0.8 copy-done.16
  106.4 1.1 multiply_reduce_fusion
  108.9 1.1 collective-permute-done.16
  111.9 2.5 %collective-permute-start.17 = (f32[65,256]{1,0:T(8,128)S(1)}, f32[65,256]{1,0:T(8,128)S(1)}, u32[]{:S(2)}, u32[]{:S(2)}) collective-permute-start(f32[65,256]{1,0:T(8,128)S(1)} %select_maximum_fusion), channel_id=1, source_target_pairs={{0,2},{2,0},{4,6},{6,4},{8,10},{10,8},{12,14},{14,12},{1,3},{3,1},... | collective-permute-start | bytes 199688 | tf_op jit(solution)/shard_map/ppermute | solution.py:28
  114.4 2.6 %collective-permute-done.17 = f32[65,256]{1,0:T(8,128)S(1)} collective-permute-done((f32[65,256]{1,0:T(8,128)S(1)}, f32[65,256]{1,0:T(8,128)S(1)}, u32[]{:S(2)}, u32[]{:S(2)}) %collective-permute-start.17) | collective-permute-done | bytes 66592 | tf_op jit(solution)/shard_map/ppermute | solution.py:28
  117.0 5.0 %collective-permute-start.20 = (f32[65,256]{1,0:T(8,128)S(1)}, f32[65,256]{1,0:T(8,128)S(1)}, u32[]{:S(2)}, u32[]{:S(2)}) collective-permute-start(f32[65,256]{1,0:T(8,128)S(1)} %fusion.306), channel_id=1, source_target_pairs={{0,12},{2,14},{4,8},{6,10},{8,4},{10,6},{12,0},{14,2},{1,13},{3,15... | collective-permute-start | bytes 199688 | tf_op jit(solution)/shard_map/ppermute | solution.py:33
  122.6 2.3 %collective-permute-done.20 = f32[65,256]{1,0:T(8,128)S(1)} collective-permute-done((f32[65,256]{1,0:T(8,128)S(1)}, f32[65,256]{1,0:T(8,128)S(1)}, u32[]{:S(2)}, u32[]{:S(2)}) %collective-permute-start.20) | collective-permute-done | bytes 66592 | tf_op jit(solution)/shard_map/ppermute | solution.py:33
  124.9 2.8 %collective-permute-done.19 = f32[65,256]{1,0:T(8,128)S(1)} collective-permute-done((f32[65,256]{1,0:T(8,128)S(1)}, f32[65,256]{1,0:T(8,128)S(1)}, u32[]{:S(2)}, u32[]{:S(2)}) %collective-permute-start.19) | collective-permute-done | bytes 66592 | tf_op jit(solution)/shard_map/ppermute | solution.py:33
  (219 shorter events, 19.2 us)
Async XLA Ops:
  0.6 2.5 %copy-start.1 = (f32[2,4,64,256]{3,2,1,0:T(8,128)S(1)}, f32[2,4,64,256]{3,2,1,0:T(8,128)}, u32[]{:S(2)}) copy-start(f32[2,4,64,256]{3,2,1,0:T(8,128)} %param.9) | copy-start | bytes 1572868
  1.6 13.6 %collective-permute-start.2 = (f32[2,4,1,256]{3,2,1,0:T(1,128)S(1)}, f32[2,4,1,256]{3,2,1,0:T(1,128)S(1)}, u32[]{:S(2)}, u32[]{:S(2)}) collective-permute-start(f32[2,4,1,256]{3,2,1,0:T(1,128)S(1)} %constant_dynamic-slice_fusion.29), channel_id=1, source_target_pairs={{0,1},{1,0},{2,3},{3,2},{4,5},{5,4},{6,7},{7,6},{8,9},{9,8},{10,11... | collective-permute-start | bytes 24584 | tf_op jit(solution)/shard_map/ppermute | solution.py:50
  3.1 2.1 %copy-start = (f32[2,4,64,256]{3,2,1,0:T(8,128)S(1)}, f32[2,4,64,256]{3,2,1,0:T(8,128)}, u32[]{:S(2)}) copy-start(f32[2,4,64,256]{3,2,1,0:T(8,128)} %param.7) | copy-start | bytes 1572868
  4.5 10.1 %copy-start.10 = (f32[4,64,256]{2,1,0:T(8,128)}, f32[4,64,256]{2,1,0:T(8,128)S(1)}, u32[]{:S(2)}) copy-start(f32[4,64,256]{2,1,0:T(8,128)S(1)} %get-tuple-element.112) | copy-start | bytes 786436
  4.5 19.4 %copy-start.13 = (f32[4,64,256]{2,1,0:T(8,128)}, f32[4,64,256]{2,1,0:T(8,128)S(1)}, u32[]{:S(2)}) copy-start(f32[4,64,256]{2,1,0:T(8,128)S(1)} %get-tuple-element.110) | copy-start | bytes 786436
  5.3 20.6 %collective-permute-start.4 = (f32[3,4,1,256]{3,2,1,0:T(1,128)}, f32[3,4,1,256]{3,2,1,0:T(1,128)}, u32[]{:S(2)}, u32[]{:S(2)}) collective-permute-start(f32[3,4,1,256]{3,2,1,0:T(1,128)} %pad_maximum_fusion.51), channel_id=1, source_target_pairs={{0,1},{1,0},{2,3},{3,2},{4,5},{5,4},{6,7},{7,6},{8,9},{9,8},{10,11... | collective-permute-start | bytes 36872 | tf_op jit(solution)/shard_map/ppermute | solution.py:116
  5.6 11.4 %collective-permute-start = (f32[4,1,64,256]{3,2,1,0:T(8,128)S(1)}, f32[4,1,64,256]{3,2,1,0:T(8,128)S(1)}, u32[]{:S(2)}, u32[]{:S(2)}) collective-permute-start(f32[4,1,64,256]{3,2,1,0:T(8,128)S(1)} %pad_maximum_fusion.39), channel_id=1, source_target_pairs={{2,0},{4,2},{6,4},{8,6},{10,8},{12,10},{14,12},{3,1},{5,3},{7,5},{... | collective-permute-start | bytes 786440 | tf_op jit(solution)/shard_map/ppermute | solution.py:135
  7.6 15.2 %collective-permute-start.1 = (f32[4,1,64,256]{3,2,1,0:T(8,128)}, f32[4,1,64,256]{3,2,1,0:T(8,128)S(1)}, u32[]{:S(2)}, u32[]{:S(2)}) collective-permute-start(f32[4,1,64,256]{3,2,1,0:T(8,128)} %pad_maximum_fusion.40), channel_id=1, source_target_pairs={{0,2},{2,4},{4,6},{6,8},{8,10},{10,12},{12,14},{1,3},{3,5},{5,7},{... | collective-permute-start | bytes 786440 | tf_op jit(solution)/shard_map/ppermute | solution.py:134
  13.9 4.7 %copy-start.7 = (f32[1,4,64,256]{3,2,1,0:T(8,128)}, f32[1,4,64,256]{3,2,1,0:T(8,128)S(1)}, u32[]{:S(2)}) copy-start(f32[1,4,64,256]{3,2,1,0:T(8,128)S(1)} %get-tuple-element.93) | copy-start | bytes 786436
  13.9 3.0 %copy-start.33 = (f32[1,1,64,256]{3,2,1,0:T(8,128)S(1)}, f32[1,1,64,256]{3,2,1,0:T(8,128)}, u32[]{:S(2)}) copy-start(f32[1,1,64,256]{3,2,1,0:T(8,128)} %get-tuple-element.101) | copy-start | bytes 196612
  16.9 1.7 %copy-start.21 = (f32[4,1,64,256]{3,2,1,0:T(8,128)}, f32[4,1,64,256]{3,2,1,0:T(8,128)S(1)}, u32[]{:S(2)}) copy-start(f32[4,1,64,256]{3,2,1,0:T(8,128)S(1)} %collective-permute-done) | copy-start | bytes 786436
  16.9 5.9 %copy-start.31 = (f32[1,1,64,256]{3,2,1,0:T(8,128)S(1)}, f32[1,1,64,256]{3,2,1,0:T(8,128)}, u32[]{:S(2)}) copy-start(f32[1,1,64,256]{3,2,1,0:T(8,128)} %get-tuple-element.102) | copy-start | bytes 196612
  16.9 5.9 %copy-start.32 = (f32[1,1,64,256]{3,2,1,0:T(8,128)S(1)}, f32[1,1,64,256]{3,2,1,0:T(8,128)}, u32[]{:S(2)}) copy-start(f32[1,1,64,256]{3,2,1,0:T(8,128)} %get-tuple-element.104) | copy-start | bytes 196612
  18.6 5.7 %copy-start.34 = (f32[2,1,64,256]{3,2,1,0:T(8,128)}, f32[2,1,64,256]{3,2,1,0:T(8,128)S(1)}, u32[]{:S(2)}) copy-start(f32[2,1,64,256]{3,2,1,0:T(8,128)S(1)} %get-tuple-element.34) | copy-start | bytes 393220
  24.1 22.2 %copy-start.3 = (f32[4,64,256]{2,1,0:T(8,128)}, f32[4,64,256]{2,1,0:T(8,128)S(1)}, u32[]{:S(2)}) copy-start(f32[4,64,256]{2,1,0:T(8,128)S(1)} %get-tuple-element.46) | copy-start | bytes 786436
  24.3 1.3 collective-permute-start.3
  25.6 1.0 copy-start.30
  25.6 1.8 %copy-start.29 = (f32[2,1,64,256]{3,2,1,0:T(8,128)S(1)}, f32[2,1,64,256]{3,2,1,0:T(8,128)}, u32[]{:S(2)}) copy-start(f32[2,1,64,256]{3,2,1,0:T(8,128)} %get-tuple-element.33) | copy-start | bytes 393220
  29.2 10.9 %collective-permute-start.5 = (f32[4,1,64,256]{3,2,1,0:T(8,128)S(1)}, f32[4,1,64,256]{3,2,1,0:T(8,128)S(1)}, u32[]{:S(2)}, u32[]{:S(2)}) collective-permute-start(f32[4,1,64,256]{3,2,1,0:T(8,128)S(1)} %pad_maximum_fusion.41), channel_id=1, source_target_pairs={{2,0},{4,2},{6,4},{8,6},{10,8},{12,10},{14,12},{3,1},{5,3},{7,5},{... | collective-permute-start | bytes 786440 | tf_op jit(solution)/shard_map/ppermute | solution.py:135
  30.5 9.6 %copy-start.22 = (f32[4,1,64,256]{3,2,1,0:T(8,128)S(1)}, f32[4,1,64,256]{3,2,1,0:T(8,128)}, u32[]{:S(2)}) copy-start(f32[4,1,64,256]{3,2,1,0:T(8,128)} %copy-done.21) | copy-start | bytes 786436
  30.5 15.4 %collective-permute-start.6 = (f32[4,1,64,256]{3,2,1,0:T(8,128)S(1)}, f32[4,1,64,256]{3,2,1,0:T(8,128)S(1)}, u32[]{:S(2)}, u32[]{:S(2)}) collective-permute-start(f32[4,1,64,256]{3,2,1,0:T(8,128)S(1)} %pad_maximum_fusion.42), channel_id=1, source_target_pairs={{0,2},{2,4},{4,6},{6,8},{8,10},{10,12},{12,14},{1,3},{3,5},{5,7},{... | collective-permute-start | bytes 786440 | tf_op jit(solution)/shard_map/ppermute | solution.py:134
  40.1 5.8 %copy-start.24 = (f32[4,1,64,256]{3,2,1,0:T(8,128)S(1)}, f32[4,1,64,256]{3,2,1,0:T(8,128)}, u32[]{:S(2)}) copy-start(f32[4,1,64,256]{3,2,1,0:T(8,128)} %copy-done.23) | copy-start | bytes 786436
  46.6 1.2 collective-permute-start.7
  47.3 27.2 %collective-permute-start.12 = (f32[3,4,1,256]{3,2,1,0:T(1,128)S(1)}, f32[3,4,1,256]{3,2,1,0:T(1,128)S(1)}, u32[]{:S(2)}, u32[]{:S(2)}) collective-permute-start(f32[3,4,1,256]{3,2,1,0:T(1,128)S(1)} %pad_maximum_fusion.52), channel_id=1, source_target_pairs={{0,1},{1,0},{2,3},{3,2},{4,5},{5,4},{6,7},{7,6},{8,9},{9,8},{10,11... | collective-permute-start | bytes 36872 | tf_op jit(solution)/shard_map/ppermute | solution.py:116
  49.2 7.1 %collective-permute-start.10 = (f32[2,4,1,256]{3,2,1,0:T(1,128)S(1)}, f32[2,4,1,256]{3,2,1,0:T(1,128)S(1)}, u32[]{:S(2)}, u32[]{:S(2)}) collective-permute-start(f32[2,4,1,256]{3,2,1,0:T(1,128)S(1)} %constant_dynamic-slice_fusion.18), channel_id=1, source_target_pairs={{0,1},{1,0},{2,3},{3,2},{4,5},{5,4},{6,7},{7,6},{8,9},{9,8},{10,11... | collective-permute-start | bytes 24584 | tf_op jit(solution)/shard_map/ppermute | solution.py:50
  49.5 1.0 copy-start.11
  50.6 16.1 %collective-permute-start.9 = (f32[4,1,64,256]{3,2,1,0:T(8,128)S(1)}, f32[4,1,64,256]{3,2,1,0:T(8,128)S(1)}, u32[]{:S(2)}, u32[]{:S(2)}) collective-permute-start(f32[4,1,64,256]{3,2,1,0:T(8,128)S(1)} %pad_maximum_fusion.44), channel_id=1, source_target_pairs={{0,2},{2,4},{4,6},{6,8},{8,10},{10,12},{12,14},{1,3},{3,5},{5,7},{... | collective-permute-start | bytes 786440 | tf_op jit(solution)/shard_map/ppermute | solution.py:134
  55.0 12.4 %collective-permute-start.8 = (f32[4,1,64,256]{3,2,1,0:T(8,128)S(1)}, f32[4,1,64,256]{3,2,1,0:T(8,128)S(1)}, u32[]{:S(2)}, u32[]{:S(2)}) collective-permute-start(f32[4,1,64,256]{3,2,1,0:T(8,128)S(1)} %pad_maximum_fusion.43), channel_id=1, source_target_pairs={{2,0},{4,2},{6,4},{8,6},{10,8},{12,10},{14,12},{3,1},{5,3},{7,5},{... | collective-permute-start | bytes 786440 | tf_op jit(solution)/shard_map/ppermute | solution.py:135
  68.2 4.2 %copy-start.35 = (f32[2,1,64,256]{3,2,1,0:T(8,128)}, f32[2,1,64,256]{3,2,1,0:T(8,128)S(1)}, u32[]{:S(2)}) copy-start(f32[2,1,64,256]{3,2,1,0:T(8,128)S(1)} %get-tuple-element.22) | copy-start | bytes 393220
  69.6 1.0 copy-start.15
  69.6 1.0 copy-start.17
  72.4 1.3 collective-permute-start.11
  79.1 1.3 %copy-start.36 = (f32[2,4,1,256]{3,2,1,0:T(1,128)S(1)}, f32[2,4,1,256]{3,2,1,0:T(1,128)}, u32[]{:S(2)}) copy-start(f32[2,4,1,256]{3,2,1,0:T(1,128)} %get-tuple-element.144) | copy-start | bytes 24580
  80.4 3.0 %copy-start.5 = (f32[4,64,256]{2,1,0:T(8,128)S(1)}, f32[4,64,256]{2,1,0:T(8,128)}, u32[]{:S(2)}) copy-start(f32[4,64,256]{2,1,0:T(8,128)} %get-tuple-element.28) | copy-start | bytes 786436
  80.4 3.0 %copy-start.6 = (f32[4,64,256]{2,1,0:T(8,128)S(1)}, f32[4,64,256]{2,1,0:T(8,128)}, u32[]{:S(2)}) copy-start(f32[4,64,256]{2,1,0:T(8,128)} %get-tuple-element.44) | copy-start | bytes 786436
  85.0 1.0 copy-start.12
  86.1 11.0 %collective-permute-start.13 = (f32[4,1,64,256]{3,2,1,0:T(8,128)S(1)}, f32[4,1,64,256]{3,2,1,0:T(8,128)S(1)}, u32[]{:S(2)}, u32[]{:S(2)}) collective-permute-start(f32[4,1,64,256]{3,2,1,0:T(8,128)S(1)} %pad_maximum_fusion.45), channel_id=1, source_target_pairs={{2,0},{4,2},{6,4},{8,6},{10,8},{12,10},{14,12},{3,1},{5,3},{7,5},{... | collective-permute-start | bytes 786440 | tf_op jit(solution)/shard_map/ppermute | solution.py:135
  87.5 9.7 %copy-start.28 = (f32[4,1,64,256]{3,2,1,0:T(8,128)S(1)}, f32[4,1,64,256]{3,2,1,0:T(8,128)}, u32[]{:S(2)}) copy-start(f32[4,1,64,256]{3,2,1,0:T(8,128)} %copy-done.27) | copy-start | bytes 786436
  87.5 15.4 %collective-permute-start.14 = (f32[4,1,64,256]{3,2,1,0:T(8,128)S(1)}, f32[4,1,64,256]{3,2,1,0:T(8,128)S(1)}, u32[]{:S(2)}, u32[]{:S(2)}) collective-permute-start(f32[4,1,64,256]{3,2,1,0:T(8,128)S(1)} %pad_maximum_fusion.46), channel_id=1, source_target_pairs={{0,2},{2,4},{4,6},{6,8},{8,10},{10,12},{12,14},{1,3},{3,5},{5,7},{... | collective-permute-start | bytes 786440 | tf_op jit(solution)/shard_map/ppermute | solution.py:134
  97.1 5.8 %copy-start.26 = (f32[4,1,64,256]{3,2,1,0:T(8,128)S(1)}, f32[4,1,64,256]{3,2,1,0:T(8,128)}, u32[]{:S(2)}) copy-start(f32[4,1,64,256]{3,2,1,0:T(8,128)} %copy-done.25) | copy-start | bytes 786436
  103.8 1.2 collective-permute-start.15
  106.4 1.1 copy-start.2
  106.4 1.2 copy-start.19
  108.5 1.5 %collective-permute-start.16 = (f32[]{:T(128)}, f32[]{:T(128)}, u32[]{:S(2)}, u32[]{:S(2)}) collective-permute-start(f32[]{:T(128)} %get-tuple-element.17), channel_id=1, source_target_pairs={{0,1},{1,0},{2,3},{3,2},{4,5},{5,4},{6,7},{7,6},{8,9},{9,8},{10,11... | collective-permute-start | bytes 20 | tf_op jit(solution)/shard_map/ppermute | solution.py:19
  111.9 5.1 %collective-permute-start.17 = (f32[65,256]{1,0:T(8,128)S(1)}, f32[65,256]{1,0:T(8,128)S(1)}, u32[]{:S(2)}, u32[]{:S(2)}) collective-permute-start(f32[65,256]{1,0:T(8,128)S(1)} %select_maximum_fusion), channel_id=1, source_target_pairs={{0,2},{2,0},{4,6},{6,4},{8,10},{10,8},{12,14},{14,12},{1,3},{3,1},... | collective-permute-start | bytes 199688 | tf_op jit(solution)/shard_map/ppermute | solution.py:28
  117.0 7.9 %collective-permute-start.20 = (f32[65,256]{1,0:T(8,128)S(1)}, f32[65,256]{1,0:T(8,128)S(1)}, u32[]{:S(2)}, u32[]{:S(2)}) collective-permute-start(f32[65,256]{1,0:T(8,128)S(1)} %fusion.306), channel_id=1, source_target_pairs={{0,12},{2,14},{4,8},{6,10},{8,4},{10,6},{12,0},{14,2},{1,13},{3,15... | collective-permute-start | bytes 199688 | tf_op jit(solution)/shard_map/ppermute | solution.py:33
  122.0 5.7 %collective-permute-start.19 = (f32[65,256]{1,0:T(8,128)S(1)}, f32[65,256]{1,0:T(8,128)S(1)}, u32[]{:S(2)}, u32[]{:S(2)}) collective-permute-start(f32[65,256]{1,0:T(8,128)S(1)} %fusion.306), channel_id=1, source_target_pairs={{0,8},{2,10},{4,12},{6,14},{8,0},{10,2},{12,4},{14,6},{1,9},{3,11}... | collective-permute-start | bytes 199688 | tf_op jit(solution)/shard_map/ppermute | solution.py:33
  122.0 5.7 %collective-permute-start.18 = (f32[65,256]{1,0:T(8,128)S(1)}, f32[65,256]{1,0:T(8,128)S(1)}, u32[]{:S(2)}, u32[]{:S(2)}) collective-permute-start(f32[65,256]{1,0:T(8,128)S(1)} %fusion.306), channel_id=1, source_target_pairs={{0,4},{2,6},{4,0},{6,2},{8,12},{10,14},{12,8},{14,10},{1,5},{3,7},... | collective-permute-start | bytes 199688 | tf_op jit(solution)/shard_map/ppermute | solution.py:33
  (17 other events, 14.0 us)

commit v12 on v9

--- a/solution.py
+++ b/solution.py
@@ -117,7 +117,7 @@
     return tuple(got[k] for k in range(len(coef)))
 
 
-def stage_pair(stage, base, base_low, base_high, coef, weight, tall=None, ahead=None):
+def stage_pair(stage, base, base_low, base_high, coef, weight, tall=None, ahead=None, edge_coef=None):
     nx = lax.axis_size("gx")
     ix = lax.axis_index("gx")
     iy = lax.axis_index("gy")
@@ -127,8 +127,9 @@
     if tall is None:
         tall = y_extended(stage)
     zero_plane = jnp.zeros_like(stage[:, :1])
-    part_top = operator(tall[:, X - 1:], stage[:, X - 2:X - 1], zero_plane, cut(coef, X - 1, X))
-    part_bottom = operator(tall[:, :1], zero_plane, stage[:, 1:2], cut(coef, 0, 1))
+    coef_top, coef_bottom = edge_coef or (cut(coef, X - 1, X), cut(coef, 0, 1))
+    part_top = operator(tall[:, X - 1:], stage[:, X - 2:X - 1], zero_plane, coef_top)
+    part_bottom = operator(tall[:, :1], zero_plane, stage[:, 1:2], coef_bottom)
     from_low = lax.ppermute(jnp.concatenate([stage[:, X - 1:], part_top]), "gx", up)
     from_high = lax.ppermute(jnp.concatenate([stage[:, :1], part_bottom]), "gx", down)
     stage_low, part_low = from_low[:2], from_low[2:]
@@ -164,11 +165,11 @@
     return section, section_next, base_low, base_high, their_next
 
 
-def rk_step(field, coef):
+def rk_step(field, coef, edge_coef=None):
     fast = lax.axis_size("gy") == 2 and field.shape[2] >= 3
     ahead = (0.5 * STEP_SIZE, partner_coef(coef)) if fast else None
     section_one, section_two, low, high, their_three = stage_pair(
-        field, field, None, None, coef, 0.5 * STEP_SIZE, ahead=ahead
+        field, field, None, None, coef, 0.5 * STEP_SIZE, ahead=ahead, edge_coef=edge_coef
     )
     stage_three = field + 0.5 * STEP_SIZE * section_two
     tall_three = with_partner_row(stage_three, their_three) if fast else None
@@ -197,7 +198,11 @@
     profile = 1.0 + 0.5 * jnp.cos(2.0 * math.pi * x_index / float(total_x))
     coef_late = coefficients(psi_late, trap, controls[1], profile)
     coef_early = coefficients(psi_early, trap, controls[0], profile)
-    chi_late = rk_step(chi_final, coef_late)
+    edge_late = (
+        coefficients(psi_late[:, planes - 1:], trap[planes - 1:], controls[1], profile[planes - 1:]),
+        coefficients(psi_late[:, :1], trap[:1], controls[1], profile[:1]),
+    )
+    chi_late = rk_step(chi_final, coef_late, edge_late)
     chi_start = rk_step(chi_late, coef_early)
     rows_late = row_terms(chi_late, psi_late, profile)
     rows_early = row_terms(chi_start, psi_early, profile)

time: 109 us -> 115 us (1.055)
  local copies, waits for them, and re-layouts: 3.27 us -> 10.3 us
  waiting for transfers between devices: 54.4 us -> 50.6 us
  other arithmetic: 12 us -> 14.8 us
    ppermute x4, waiting for transfers between devices: 13.9 us -> 9.25 us  [stage_pair(): lax.ppermute(jnp.concatenate([stage[:, :1], part_bottom]), 'gx', down)]
    unnamed x8 -> x30, local copies, waits for them, and re-layouts: 0.54 us -> 4.08 us
    mul x4, other arithmetic: 0.09 us -> 1.76 us  [across(): return jnp.stack([0.5 * plane[1], -0.5 * plane[0]])]
    broadcast_in_dim x2 -> x4, local copies, waits for them, and re-layouts: 0.05 us -> 1.48 us  [coefficients(): fine_control = jnp.repeat(control, 2, axis=0)]
    add x1 -> x0, other arithmetic: 1.33 us -> none  [coefficients(): potential + 2.0 * COUPLING * (real_part * real_part + imag_part * imag_part)]
    mul x0 -> x1, other arithmetic: none -> 1.32 us  [coefficients(): potential = trap + profile[:, None, None] * fine_control[None, :, :]]
  transfers between devices with their start and end apart: 21 -> 21, of which waited for: 16 -> 16; matrix products, arithmetic and copies ran while one was open for 5% -> 9% of each run, Pallas kernels for 0% -> 0%
where the time goes in v12:
time: 115 us; the launch traced here: 114 us
  waiting for transfers between devices  50.6 us (44%)
  starting transfers between devices  33 us (29%)
  other arithmetic  14.8 us (13%)
  local copies, waits for them, and re-layouts  10.3 us (9%)
  between operations  5.33 us (5%)
    ppermute x4, waiting for transfers between devices, stage_pair(): lax.ppermute(jnp.concatenate([stage[:, X - 1:], part_top]), 'gx', up)  28.4 us
    ppermute x4, starting transfers between devices, stage_pair(): lax.ppermute(jnp.concatenate([stage[:, X - 1:], part_top]), 'gx', up)  18.9 us
    ppermute x4, waiting for transfers between devices, stage_pair(): lax.ppermute(jnp.concatenate([stage[:, :1], part_bottom]), 'gx', down)  9.25 us
    ppermute x4, starting transfers between devices, stage_pair(): lax.ppermute(jnp.concatenate([stage[:, :1], part_bottom]), 'gx', down)  5.17 us
    ppermute x3, waiting for transfers between devices, gx_total(): lax.ppermute(pair, 'gx', [(i, i ^ 2 * k) for i in range(count)])  5.15 us
    ppermute x3, starting transfers between devices, gx_total(): lax.ppermute(pair, 'gx', [(i, i ^ 2 * k) for i in range(count)])  4.45 us
    unnamed x30, local copies, waits for them, and re-layouts  4.08 us
    sub x14, other arithmetic, operator(): lapl = total - 6.0 * field  3.84 us
  transfers between devices with their start and end apart: 21, of which 16 were waited for; matrix products, arithmetic and copies ran while one was open for 9% of the time, Pallas kernels for 0%

profile of v12, /device:TPU:0, one launch (start us, length us, event | category | flops | bytes accessed | tf_op | source)
XLA Modules:
  0.0 113.9 jit_solution(173959304170867879)
XLA Ops:
  0.6 0.9 constant_dynamic-slice_fusion.17
  1.6 0.6 collective-permute-start
  2.1 1.7 %slice_multiply_fusion.48 = (f32[1,1,64,256]{3,2,1,0:T(8,128)}, f32[1,1,64,256]{3,2,1,0:T(8,128)}, f32[1,1,64,256]{3,2,1,0:T(8,128)}, f32[1,1,64,256]{3,2,1,0:T(8,128)}) fusion(f32[2,4,64,256]{3,2,1,0:T(8,128)} %param.7), kind=kLoop, calls=%fused_computation.504 | loop fusion | flops 65536 | bytes 524288 | tf_op jit(solution)/shard_map/mul | solution.py:96
  3.9 0.6 fusion.302
  4.6 0.8 copy-done.7
  5.4 1.3 %broadcast_multiply_fusion.1 = (f32[32,256]{1,0:T(8,128)S(1)}, f32[32,256]{1,0:T(8,128)S(1)}) fusion(f32[]{:T(128)} %bitcast.3, f32[2,32,256]{2,1,0:T(8,128)S(1)} %copy-done.7, f32[]{:T(128)} %bitcast.14), kind=kLoop, calls=%fused_computation.521 | loop fusion | flops 16384 | bytes 98312 | tf_op jit(solution)/shard_map/mul | solution.py:64
  6.9 0.6 copy-done.9
  7.7 0.8 copy-done.1
  8.8 4.4 %collective-permute-start.2 = (f32[4,1,64,256]{3,2,1,0:T(8,128)S(1)}, f32[4,1,64,256]{3,2,1,0:T(8,128)S(1)}, u32[]{:S(2)}, u32[]{:S(2)}) collective-permute-start(f32[4,1,64,256]{3,2,1,0:T(8,128)S(1)} %pad_maximum_fusion.40), channel_id=1, source_target_pairs={{0,2},{2,4},{4,6},{6,8},{8,10},{10,12},{12,14},{1,3},{3,5},{5,7},{... | collective-permute-start | bytes 786440 | tf_op jit(solution)/shard_map/ppermute | solution.py:133
  13.2 0.6 slice_bitcast_fusion.18
  13.9 1.3 %collective-permute-start.1 = (f32[4,1,64,256]{3,2,1,0:T(8,128)S(1)}, f32[4,1,64,256]{3,2,1,0:T(8,128)S(1)}, u32[]{:S(2)}, u32[]{:S(2)}) collective-permute-start(f32[4,1,64,256]{3,2,1,0:T(8,128)S(1)} %pad_maximum_fusion.39), channel_id=1, source_target_pairs={{2,0},{4,2},{6,4},{8,6},{10,8},{12,10},{14,12},{3,1},{5,3},{7,5},{... | collective-permute-start | bytes 786440 | tf_op jit(solution)/shard_map/ppermute | solution.py:134
  15.2 0.6 constant_dynamic-slice_fusion.1
  15.9 1.4 %broadcast_in_dim.38 = f32[32,2,256]{2,1,0:T(2,128)} broadcast(f32[32,256]{1,0:T(8,128)} %get-tuple-element.126), dimensions={0,2} | broadcast | bytes 98304 | tf_op jit(solution)/shard_map/broadcast_in_dim | solution.py:63
  17.3 0.9 mul.1244
  18.2 6.8 %collective-permute-done.2 = f32[4,1,64,256]{3,2,1,0:T(8,128)S(1)} collective-permute-done((f32[4,1,64,256]{3,2,1,0:T(8,128)S(1)}, f32[4,1,64,256]{3,2,1,0:T(8,128)S(1)}, u32[]{:S(2)}, u32[]{:S(2)}) %collective-permute-start.2) | collective-permute-done | bytes 262176 | tf_op jit(solution)/shard_map/ppermute | solution.py:133
  25.0 0.9 fusion.176
  27.4 0.6 collective-permute-start.4
  28.0 0.6 collective-permute-done.3
  28.9 0.5 copy-done.10
  30.3 1.3 %collective-permute-start.5 = (f32[4,1,64,256]{3,2,1,0:T(8,128)S(1)}, f32[4,1,64,256]{3,2,1,0:T(8,128)S(1)}, u32[]{:S(2)}, u32[]{:S(2)}) collective-permute-start(f32[4,1,64,256]{3,2,1,0:T(8,128)S(1)} %pad_maximum_fusion.41), channel_id=1, source_target_pairs={{2,0},{4,2},{6,4},{8,6},{10,8},{12,10},{14,12},{3,1},{5,3},{7,5},{... | collective-permute-start | bytes 786440 | tf_op jit(solution)/shard_map/ppermute | solution.py:134
  31.6 5.0 %collective-permute-start.6 = (f32[4,1,64,256]{3,2,1,0:T(8,128)S(1)}, f32[4,1,64,256]{3,2,1,0:T(8,128)S(1)}, u32[]{:S(2)}, u32[]{:S(2)}) collective-permute-start(f32[4,1,64,256]{3,2,1,0:T(8,128)S(1)} %pad_maximum_fusion.42), channel_id=1, source_target_pairs={{0,2},{2,4},{4,6},{6,8},{8,10},{10,12},{12,14},{1,3},{3,5},{5,7},{... | collective-permute-start | bytes 786440 | tf_op jit(solution)/shard_map/ppermute | solution.py:133
  36.7 4.6 %collective-permute-done.5 = f32[4,1,64,256]{3,2,1,0:T(8,128)S(1)} collective-permute-done((f32[4,1,64,256]{3,2,1,0:T(8,128)S(1)}, f32[4,1,64,256]{3,2,1,0:T(8,128)S(1)}, u32[]{:S(2)}, u32[]{:S(2)}) %collective-permute-start.5) | collective-permute-done | bytes 262176 | tf_op jit(solution)/shard_map/ppermute | solution.py:134
  41.4 5.7 %collective-permute-done.6 = f32[4,1,64,256]{3,2,1,0:T(8,128)S(1)} collective-permute-done((f32[4,1,64,256]{3,2,1,0:T(8,128)S(1)}, f32[4,1,64,256]{3,2,1,0:T(8,128)S(1)}, u32[]{:S(2)}, u32[]{:S(2)}) %collective-permute-start.6) | collective-permute-done | bytes 262176 | tf_op jit(solution)/shard_map/ppermute | solution.py:133
  47.9 1.1 collective-permute-done.7
  50.0 1.0 collective-permute-done.8
  51.4 4.4 %collective-permute-start.10 = (f32[4,1,64,256]{3,2,1,0:T(8,128)S(1)}, f32[4,1,64,256]{3,2,1,0:T(8,128)S(1)}, u32[]{:S(2)}, u32[]{:S(2)}) collective-permute-start(f32[4,1,64,256]{3,2,1,0:T(8,128)S(1)} %pad_maximum_fusion.44), channel_id=1, source_target_pairs={{0,2},{2,4},{4,6},{6,8},{8,10},{10,12},{12,14},{1,3},{3,5},{5,7},{... | collective-permute-start | bytes 786440 | tf_op jit(solution)/shard_map/ppermute | solution.py:133
  55.8 1.3 %collective-permute-start.9 = (f32[4,1,64,256]{3,2,1,0:T(8,128)S(1)}, f32[4,1,64,256]{3,2,1,0:T(8,128)S(1)}, u32[]{:S(2)}, u32[]{:S(2)}) collective-permute-start(f32[4,1,64,256]{3,2,1,0:T(8,128)S(1)} %pad_maximum_fusion.43), channel_id=1, source_target_pairs={{2,0},{4,2},{6,4},{8,6},{10,8},{12,10},{14,12},{3,1},{5,3},{7,5},{... | collective-permute-start | bytes 786440 | tf_op jit(solution)/shard_map/ppermute | solution.py:134
  57.1 10.1 %collective-permute-done.10 = f32[4,1,64,256]{3,2,1,0:T(8,128)S(1)} collective-permute-done((f32[4,1,64,256]{3,2,1,0:T(8,128)S(1)}, f32[4,1,64,256]{3,2,1,0:T(8,128)S(1)}, u32[]{:S(2)}, u32[]{:S(2)}) %collective-permute-start.10) | collective-permute-done | bytes 262176 | tf_op jit(solution)/shard_map/ppermute | solution.py:133
  68.3 0.5 copy-done.11
  69.0 0.5 collective-permute-done.11
  69.7 0.4 collective-permute-done.12
  71.4 1.3 %collective-permute-start.13 = (f32[4,1,64,256]{3,2,1,0:T(8,128)S(1)}, f32[4,1,64,256]{3,2,1,0:T(8,128)S(1)}, u32[]{:S(2)}, u32[]{:S(2)}) collective-permute-start(f32[4,1,64,256]{3,2,1,0:T(8,128)S(1)} %pad_maximum_fusion.45), channel_id=1, source_target_pairs={{2,0},{4,2},{6,4},{8,6},{10,8},{12,10},{14,12},{3,1},{5,3},{7,5},{... | collective-permute-start | bytes 786440 | tf_op jit(solution)/shard_map/ppermute | solution.py:134
  72.7 5.0 %collective-permute-start.14 = (f32[4,1,64,256]{3,2,1,0:T(8,128)S(1)}, f32[4,1,64,256]{3,2,1,0:T(8,128)S(1)}, u32[]{:S(2)}, u32[]{:S(2)}) collective-permute-start(f32[4,1,64,256]{3,2,1,0:T(8,128)S(1)} %pad_maximum_fusion.46), channel_id=1, source_target_pairs={{0,2},{2,4},{4,6},{6,8},{8,10},{10,12},{12,14},{1,3},{3,5},{5,7},{... | collective-permute-start | bytes 786440 | tf_op jit(solution)/shard_map/ppermute | solution.py:133
  77.7 4.6 %collective-permute-done.13 = f32[4,1,64,256]{3,2,1,0:T(8,128)S(1)} collective-permute-done((f32[4,1,64,256]{3,2,1,0:T(8,128)S(1)}, f32[4,1,64,256]{3,2,1,0:T(8,128)S(1)}, u32[]{:S(2)}, u32[]{:S(2)}) %collective-permute-start.13) | collective-permute-done | bytes 262176 | tf_op jit(solution)/shard_map/ppermute | solution.py:134
  82.4 5.7 %collective-permute-done.14 = f32[4,1,64,256]{3,2,1,0:T(8,128)S(1)} collective-permute-done((f32[4,1,64,256]{3,2,1,0:T(8,128)S(1)}, f32[4,1,64,256]{3,2,1,0:T(8,128)S(1)}, u32[]{:S(2)}, u32[]{:S(2)}) %collective-permute-start.14) | collective-permute-done | bytes 262176 | tf_op jit(solution)/shard_map/ppermute | solution.py:133
  89.1 0.6 compare_reduce_fusion
  89.7 0.5 collective-permute-done.15
  90.8 1.1 multiply_reduce_fusion
  92.1 0.5 copy-done.3
  93.1 0.9 collective-permute-done.16
  96.0 2.5 %collective-permute-start.17 = (f32[65,256]{1,0:T(8,128)S(1)}, f32[65,256]{1,0:T(8,128)S(1)}, u32[]{:S(2)}, u32[]{:S(2)}) collective-permute-start(f32[65,256]{1,0:T(8,128)S(1)} %select_maximum_fusion), channel_id=1, source_target_pairs={{0,2},{2,0},{4,6},{6,4},{8,10},{10,8},{12,14},{14,12},{1,3},{3,1},... | collective-permute-start | bytes 199688 | tf_op jit(solution)/shard_map/ppermute | solution.py:28
  98.6 2.6 %collective-permute-done.17 = f32[65,256]{1,0:T(8,128)S(1)} collective-permute-done((f32[65,256]{1,0:T(8,128)S(1)}, f32[65,256]{1,0:T(8,128)S(1)}, u32[]{:S(2)}, u32[]{:S(2)}) %collective-permute-start.17) | collective-permute-done | bytes 66592 | tf_op jit(solution)/shard_map/ppermute | solution.py:28
  101.2 3.0 %collective-permute-start.20 = (f32[65,256]{1,0:T(8,128)S(1)}, f32[65,256]{1,0:T(8,128)S(1)}, u32[]{:S(2)}, u32[]{:S(2)}) collective-permute-start(f32[65,256]{1,0:T(8,128)S(1)} %fusion.288), channel_id=1, source_target_pairs={{0,12},{2,14},{4,8},{6,10},{8,4},{10,6},{12,0},{14,2},{1,13},{3,15... | collective-permute-start | bytes 199688 | tf_op jit(solution)/shard_map/ppermute | solution.py:33
  104.3 1.3 %collective-permute-start.18 = (f32[65,256]{1,0:T(8,128)S(1)}, f32[65,256]{1,0:T(8,128)S(1)}, u32[]{:S(2)}, u32[]{:S(2)}) collective-permute-start(f32[65,256]{1,0:T(8,128)S(1)} %fusion.288), channel_id=1, source_target_pairs={{0,4},{2,6},{4,0},{6,2},{8,12},{10,14},{12,8},{14,10},{1,5},{3,7},... | collective-permute-start | bytes 199688 | tf_op jit(solution)/shard_map/ppermute | solution.py:33
  105.7 2.6 %collective-permute-done.20 = f32[65,256]{1,0:T(8,128)S(1)} collective-permute-done((f32[65,256]{1,0:T(8,128)S(1)}, f32[65,256]{1,0:T(8,128)S(1)}, u32[]{:S(2)}, u32[]{:S(2)}) %collective-permute-start.20) | collective-permute-done | bytes 66592 | tf_op jit(solution)/shard_map/ppermute | solution.py:33
  108.2 2.5 %collective-permute-done.19 = f32[65,256]{1,0:T(8,128)S(1)} collective-permute-done((f32[65,256]{1,0:T(8,128)S(1)}, f32[65,256]{1,0:T(8,128)S(1)}, u32[]{:S(2)}, u32[]{:S(2)}) %collective-permute-start.19) | collective-permute-done | bytes 66592 | tf_op jit(solution)/shard_map/ppermute | solution.py:33
  110.9 0.5 slice.1316
  112.1 0.6 maximum_divide_fusion
  (150 shorter events, 10.4 us)
Async XLA Ops:
  0.6 3.2 %copy-start = (f32[2,4,64,256]{3,2,1,0:T(8,128)S(1)}, f32[2,4,64,256]{3,2,1,0:T(8,128)}, u32[]{:S(2)}) copy-start(f32[2,4,64,256]{3,2,1,0:T(8,128)} %param.7) | copy-start | bytes 1572868
  1.6 5.3 %collective-permute-start = (f32[2,4,1,256]{3,2,1,0:T(1,128)S(1)}, f32[2,4,1,256]{3,2,1,0:T(1,128)S(1)}, u32[]{:S(2)}, u32[]{:S(2)}) collective-permute-start(f32[2,4,1,256]{3,2,1,0:T(1,128)S(1)} %constant_dynamic-slice_fusion.17), channel_id=1, source_target_pairs={{0,1},{1,0},{2,3},{3,2},{4,5},{5,4},{6,7},{7,6},{8,9},{9,8},{10,11... | collective-permute-start | bytes 24584 | tf_op jit(solution)/shard_map/ppermute | solution.py:50
  2.1 2.4 %copy-start.2 = (f32[2,4,64,256]{3,2,1,0:T(8,128)S(1)}, f32[2,4,64,256]{3,2,1,0:T(8,128)}, u32[]{:S(2)}) copy-start(f32[2,4,64,256]{3,2,1,0:T(8,128)} %param.9) | copy-start | bytes 1572868
  3.9 0.7 copy-start.13
  4.5 0.8 copy-start.7
  6.9 0.6 copy-start.9
  7.5 1.0 copy-start.1
  7.5 1.1 copy-start.4
  8.8 16.2 %collective-permute-start.2 = (f32[4,1,64,256]{3,2,1,0:T(8,128)S(1)}, f32[4,1,64,256]{3,2,1,0:T(8,128)S(1)}, u32[]{:S(2)}, u32[]{:S(2)}) collective-permute-start(f32[4,1,64,256]{3,2,1,0:T(8,128)S(1)} %pad_maximum_fusion.40), channel_id=1, source_target_pairs={{0,2},{2,4},{4,6},{6,8},{8,10},{10,12},{12,14},{1,3},{3,5},{5,7},{... | collective-permute-start | bytes 786440 | tf_op jit(solution)/shard_map/ppermute | solution.py:133
  13.9 1.9 %copy-start.8 = (f32[32,256]{1,0:T(8,128)S(1)}, f32[32,256]{1,0:T(8,128)}, u32[]{:S(2)}) copy-start(f32[32,256]{1,0:T(8,128)} %get-tuple-element.125) | copy-start | bytes 98308
  13.9 12.1 %collective-permute-start.1 = (f32[4,1,64,256]{3,2,1,0:T(8,128)S(1)}, f32[4,1,64,256]{3,2,1,0:T(8,128)S(1)}, u32[]{:S(2)}, u32[]{:S(2)}) collective-permute-start(f32[4,1,64,256]{3,2,1,0:T(8,128)S(1)} %pad_maximum_fusion.39), channel_id=1, source_target_pairs={{2,0},{4,2},{6,4},{8,6},{10,8},{12,10},{14,12},{3,1},{5,3},{7,5},{... | collective-permute-start | bytes 786440 | tf_op jit(solution)/shard_map/ppermute | solution.py:134
  25.0 1.0 copy-start.5
  25.0 1.0 copy-start.6
  26.0 0.6 copy-start.14
  27.3 1.3 %collective-permute-start.3 = (f32[2,10,1,256]{3,2,1,0:T(1,128)S(1)}, f32[2,10,1,256]{3,2,1,0:T(1,128)S(1)}, u32[]{:S(2)}, u32[]{:S(2)}) collective-permute-start(f32[2,10,1,256]{3,2,1,0:T(1,128)S(1)} %pad_maximum_fusion.51), channel_id=1, source_target_pairs={{0,1},{1,0},{2,3},{3,2},{4,5},{5,4},{6,7},{7,6},{8,9},{9,8},{10,11... | collective-permute-start | bytes 61448 | tf_op jit(solution)/shard_map/ppermute | solution.py:153
  27.4 1.4 %collective-permute-start.4 = (f32[3,4,1,256]{3,2,1,0:T(1,128)S(1)}, f32[3,4,1,256]{3,2,1,0:T(1,128)S(1)}, u32[]{:S(2)}, u32[]{:S(2)}) collective-permute-start(f32[3,4,1,256]{3,2,1,0:T(1,128)S(1)} %pad_maximum_fusion.53), channel_id=1, source_target_pairs={{0,1},{1,0},{2,3},{3,2},{4,5},{5,4},{6,7},{7,6},{8,9},{9,8},{10,11... | collective-permute-start | bytes 36872 | tf_op jit(solution)/shard_map/ppermute | solution.py:116
  28.6 0.7 copy-start.10
  30.3 11.0 %collective-permute-start.5 = (f32[4,1,64,256]{3,2,1,0:T(8,128)S(1)}, f32[4,1,64,256]{3,2,1,0:T(8,128)S(1)}, u32[]{:S(2)}, u32[]{:S(2)}) collective-permute-start(f32[4,1,64,256]{3,2,1,0:T(8,128)S(1)} %pad_maximum_fusion.41), channel_id=1, source_target_pairs={{2,0},{4,2},{6,4},{8,6},{10,8},{12,10},{14,12},{3,1},{5,3},{7,5},{... | collective-permute-start | bytes 786440 | tf_op jit(solution)/shard_map/ppermute | solution.py:134
  31.6 15.5 %collective-permute-start.6 = (f32[4,1,64,256]{3,2,1,0:T(8,128)S(1)}, f32[4,1,64,256]{3,2,1,0:T(8,128)S(1)}, u32[]{:S(2)}, u32[]{:S(2)}) collective-permute-start(f32[4,1,64,256]{3,2,1,0:T(8,128)S(1)} %pad_maximum_fusion.42), channel_id=1, source_target_pairs={{0,2},{2,4},{4,6},{6,8},{8,10},{10,12},{12,14},{1,3},{3,5},{5,7},{... | collective-permute-start | bytes 786440 | tf_op jit(solution)/shard_map/ppermute | solution.py:133
  47.8 1.2 %collective-permute-start.7 = (f32[2,4,1,256]{3,2,1,0:T(1,128)S(1)}, f32[2,4,1,256]{3,2,1,0:T(1,128)S(1)}, u32[]{:S(2)}, u32[]{:S(2)}) collective-permute-start(f32[2,4,1,256]{3,2,1,0:T(1,128)S(1)} %constant_dynamic-slice_fusion.9), channel_id=1, source_target_pairs={{0,1},{1,0},{2,3},{3,2},{4,5},{5,4},{6,7},{7,6},{8,9},{9,8},{10,11... | collective-permute-start | bytes 24584 | tf_op jit(solution)/shard_map/ppermute | solution.py:50
  49.8 1.2 %collective-permute-start.8 = (f32[2,4,1,256]{3,2,1,0:T(1,128)S(1)}, f32[2,4,1,256]{3,2,1,0:T(1,128)S(1)}, u32[]{:S(2)}, u32[]{:S(2)}) collective-permute-start(f32[2,4,1,256]{3,2,1,0:T(1,128)S(1)} %constant_dynamic-slice_fusion.8), channel_id=1, source_target_pairs={{0,1},{1,0},{2,3},{3,2},{4,5},{5,4},{6,7},{7,6},{8,9},{9,8},{10,11... | collective-permute-start | bytes 24584 | tf_op jit(solution)/shard_map/ppermute | solution.py:50
  51.4 15.9 %collective-permute-start.10 = (f32[4,1,64,256]{3,2,1,0:T(8,128)S(1)}, f32[4,1,64,256]{3,2,1,0:T(8,128)S(1)}, u32[]{:S(2)}, u32[]{:S(2)}) collective-permute-start(f32[4,1,64,256]{3,2,1,0:T(8,128)S(1)} %pad_maximum_fusion.44), channel_id=1, source_target_pairs={{0,2},{2,4},{4,6},{6,8},{8,10},{10,12},{12,14},{1,3},{3,5},{5,7},{... | collective-permute-start | bytes 786440 | tf_op jit(solution)/shard_map/ppermute | solution.py:133
  55.8 11.5 %collective-permute-start.9 = (f32[4,1,64,256]{3,2,1,0:T(8,128)S(1)}, f32[4,1,64,256]{3,2,1,0:T(8,128)S(1)}, u32[]{:S(2)}, u32[]{:S(2)}) collective-permute-start(f32[4,1,64,256]{3,2,1,0:T(8,128)S(1)} %pad_maximum_fusion.43), channel_id=1, source_target_pairs={{2,0},{4,2},{6,4},{8,6},{10,8},{12,10},{14,12},{3,1},{5,3},{7,5},{... | collective-permute-start | bytes 786440 | tf_op jit(solution)/shard_map/ppermute | solution.py:134
  68.2 0.7 copy-start.11
  68.2 0.7 copy-start.12
  68.2 1.3 %collective-permute-start.11 = (f32[2,10,1,256]{3,2,1,0:T(1,128)S(1)}, f32[2,10,1,256]{3,2,1,0:T(1,128)S(1)}, u32[]{:S(2)}, u32[]{:S(2)}) collective-permute-start(f32[2,10,1,256]{3,2,1,0:T(1,128)S(1)} %pad_maximum_fusion.52), channel_id=1, source_target_pairs={{0,1},{1,0},{2,3},{3,2},{4,5},{5,4},{6,7},{7,6},{8,9},{9,8},{10,11... | collective-permute-start | bytes 61448 | tf_op jit(solution)/shard_map/ppermute | solution.py:153
  68.9 1.2 %collective-permute-start.12 = (f32[3,4,1,256]{3,2,1,0:T(1,128)S(1)}, f32[3,4,1,256]{3,2,1,0:T(1,128)S(1)}, u32[]{:S(2)}, u32[]{:S(2)}) collective-permute-start(f32[3,4,1,256]{3,2,1,0:T(1,128)S(1)} %pad_maximum_fusion.54), channel_id=1, source_target_pairs={{0,1},{1,0},{2,3},{3,2},{4,5},{5,4},{6,7},{7,6},{8,9},{9,8},{10,11... | collective-permute-start | bytes 36872 | tf_op jit(solution)/shard_map/ppermute | solution.py:116
  71.4 11.0 %collective-permute-start.13 = (f32[4,1,64,256]{3,2,1,0:T(8,128)S(1)}, f32[4,1,64,256]{3,2,1,0:T(8,128)S(1)}, u32[]{:S(2)}, u32[]{:S(2)}) collective-permute-start(f32[4,1,64,256]{3,2,1,0:T(8,128)S(1)} %pad_maximum_fusion.45), channel_id=1, source_target_pairs={{2,0},{4,2},{6,4},{8,6},{10,8},{12,10},{14,12},{3,1},{5,3},{7,5},{... | collective-permute-start | bytes 786440 | tf_op jit(solution)/shard_map/ppermute | solution.py:134
  72.7 15.5 %collective-permute-start.14 = (f32[4,1,64,256]{3,2,1,0:T(8,128)S(1)}, f32[4,1,64,256]{3,2,1,0:T(8,128)S(1)}, u32[]{:S(2)}, u32[]{:S(2)}) collective-permute-start(f32[4,1,64,256]{3,2,1,0:T(8,128)S(1)} %pad_maximum_fusion.46), channel_id=1, source_target_pairs={{0,2},{2,4},{4,6},{6,8},{8,10},{10,12},{12,14},{1,3},{3,5},{5,7},{... | collective-permute-start | bytes 786440 | tf_op jit(solution)/shard_map/ppermute | solution.py:133
  89.0 1.2 %collective-permute-start.15 = (f32[2,4,1,256]{3,2,1,0:T(1,128)S(1)}, f32[2,4,1,256]{3,2,1,0:T(1,128)S(1)}, u32[]{:S(2)}, u32[]{:S(2)}) collective-permute-start(f32[2,4,1,256]{3,2,1,0:T(1,128)S(1)} %constant_dynamic-slice_fusion), channel_id=1, source_target_pairs={{0,1},{1,0},{2,3},{3,2},{4,5},{5,4},{6,7},{7,6},{8,9},{9,8},{10,11... | collective-permute-start | bytes 24584 | tf_op jit(solution)/shard_map/ppermute | solution.py:50
  91.8 0.8 copy-start.3
  92.7 1.3 %collective-permute-start.16 = (f32[]{:T(128)}, f32[]{:T(128)}, u32[]{:S(2)}, u32[]{:S(2)}) collective-permute-start(f32[]{:T(128)} %get-tuple-element.17), channel_id=1, source_target_pairs={{0,1},{1,0},{2,3},{3,2},{4,5},{5,4},{6,7},{7,6},{8,9},{9,8},{10,11... | collective-permute-start | bytes 20 | tf_op jit(solution)/shard_map/ppermute | solution.py:19
  96.0 5.2 %collective-permute-start.17 = (f32[65,256]{1,0:T(8,128)S(1)}, f32[65,256]{1,0:T(8,128)S(1)}, u32[]{:S(2)}, u32[]{:S(2)}) collective-permute-start(f32[65,256]{1,0:T(8,128)S(1)} %select_maximum_fusion), channel_id=1, source_target_pairs={{0,2},{2,0},{4,6},{6,4},{8,10},{10,8},{12,14},{14,12},{1,3},{3,1},... | collective-permute-start | bytes 199688 | tf_op jit(solution)/shard_map/ppermute | solution.py:28
  101.2 7.1 %collective-permute-start.20 = (f32[65,256]{1,0:T(8,128)S(1)}, f32[65,256]{1,0:T(8,128)S(1)}, u32[]{:S(2)}, u32[]{:S(2)}) collective-permute-start(f32[65,256]{1,0:T(8,128)S(1)} %fusion.288), channel_id=1, source_target_pairs={{0,12},{2,14},{4,8},{6,10},{8,4},{10,6},{12,0},{14,2},{1,13},{3,15... | collective-permute-start | bytes 199688 | tf_op jit(solution)/shard_map/ppermute | solution.py:33
  104.2 6.6 %collective-permute-start.19 = (f32[65,256]{1,0:T(8,128)S(1)}, f32[65,256]{1,0:T(8,128)S(1)}, u32[]{:S(2)}, u32[]{:S(2)}) collective-permute-start(f32[65,256]{1,0:T(8,128)S(1)} %fusion.288), channel_id=1, source_target_pairs={{0,8},{2,10},{4,12},{6,14},{8,0},{10,2},{12,4},{14,6},{1,9},{3,11}... | collective-permute-start | bytes 199688 | tf_op jit(solution)/shard_map/ppermute | solution.py:33
  104.3 6.5 %collective-permute-start.18 = (f32[65,256]{1,0:T(8,128)S(1)}, f32[65,256]{1,0:T(8,128)S(1)}, u32[]{:S(2)}, u32[]{:S(2)}) collective-permute-start(f32[65,256]{1,0:T(8,128)S(1)} %fusion.288), channel_id=1, source_target_pairs={{0,4},{2,6},{4,0},{6,2},{8,12},{10,14},{12,8},{14,10},{1,5},{3,7},... | collective-permute-start | bytes 199688 | tf_op jit(solution)/shard_map/ppermute | solution.py:33

commit v13 on v9

--- a/solution.py
+++ b/solution.py
@@ -21,11 +21,22 @@
     return value
 
 
-def gx_total(value):
+def gx_total(value, square=None):
     count = lax.axis_size("gx")
-    if count > 8 or count % 2:
+    if count > 8 or count % 2 or (square is not None and lax.axis_size("gy") != 2):
+        if square is not None:
+            value = value.at[-1, 0].set(axis_sum(square, "gy"))
         return axis_sum(value, "gx")
     pair = value + lax.ppermute(value, "gx", [(i, i ^ 1) for i in range(count)])
+    if square is not None:
+        ny = lax.axis_size("gy")
+        other = lax.ppermute(square, "gy", [(0, 1), (1, 0)])
+        across_pair = lax.ppermute(
+            square, ("gx", "gy"),
+            [(i * ny + j, (i ^ 1) * ny + (1 - j)) for i in range(count) for j in range(ny)],
+        )
+        group = pair[-1, 0] + (other + across_pair)
+        pair = pair.at[-1, 0].set(group)
     groups = count // 2
     if groups == 1:
         return pair
@@ -201,9 +212,9 @@
     chi_start = rk_step(chi_late, coef_early)
     rows_late = row_terms(chi_late, psi_late, profile)
     rows_early = row_terms(chi_start, psi_early, profile)
-    local_sq = axis_sum(jnp.sum(chi_start * chi_start), "gy")
+    local_sq = jnp.sum(chi_start * chi_start)
     extra = jnp.zeros((1, rows_early.shape[1]), jnp.float32).at[0, 0].set(local_sq)
-    packed = gx_total(jnp.concatenate([rows_early, rows_late, extra], axis=0))
+    packed = gx_total(jnp.concatenate([rows_early, rows_late, extra], axis=0), local_sq)
     squares = packed[-1, 0]
     half = rows_early.shape[0]
     rows_sum = jnp.stack([packed[:half], packed[half:2 * half]])

time: 109 us -> 111 us (1.018)
  between operations: 5.2 us -> 6.5 us
    ppermute x1, waiting for transfers between devices: 2.6 us -> 0.01 us  [gx_total(): pair = value + lax.ppermute(value, 'gx', [(i, i ^ 1) for i in range(count)])]
    ppermute x1 -> x2, waiting for transfers between devices: 1.05 us -> 2.89 us  [the longest x1 2.89 us: gx_total(): lax.ppermute(square, ('gx', 'gy'), [(i * ny + j, (i ^ 1) * ny + (1 - j))...]
  transfers between devices with their start and end apart: 21 -> 22, of which waited for: 16 -> 15; matrix products, arithmetic and copies ran while one was open for 5% -> 4% of each run, Pallas kernels for 0% -> 0%
where the time goes in v13:
time: 111 us
  waiting for transfers between devices  54.1 us (49%)
  starting transfers between devices  34.1 us (31%)
  other arithmetic  12 us (11%)
  between operations  6.5 us (6%)
  local copies, waits for them, and re-layouts  3.86 us (3%)
    ppermute x4, waiting for transfers between devices, stage_pair(): lax.ppermute(jnp.concatenate([stage[:, X - 1:], part_top]), 'gx', up)  27.3 us
    ppermute x4, starting transfers between devices, stage_pair(): lax.ppermute(jnp.concatenate([stage[:, X - 1:], part_top]), 'gx', up)  20 us
    ppermute x4, waiting for transfers between devices, stage_pair(): lax.ppermute(jnp.concatenate([stage[:, :1], part_bottom]), 'gx', down)  13.9 us
    ppermute x3, waiting for transfers between devices, gx_total(): lax.ppermute(pair, 'gx', [(i, i ^ 2 * k) for i in range(count)])  5.58 us
    ppermute x4, starting transfers between devices, stage_pair(): lax.ppermute(jnp.concatenate([stage[:, :1], part_bottom]), 'gx', down)  5.17 us
    ppermute x3, starting transfers between devices, gx_total(): lax.ppermute(pair, 'gx', [(i, i ^ 2 * k) for i in range(count)])  4.45 us
    sub x14, other arithmetic, operator(): lapl = total - 6.0 * field  3.83 us
    ppermute x1, waiting for transfers between devices, gx_total(): lax.ppermute(square, ('gx', 'gy'), [(i * ny + j, (i ^ 1) * ny + (1 - j))...  2.89 us
  transfers between devices with their start and end apart: 22, of which 15 were waited for; matrix products, arithmetic and copies ran while one was open for 4% of the time, Pallas kernels for 0%

profile of v13, /device:TPU:0, one launch (start us, length us, event | category | flops | bytes accessed | tf_op | source)
XLA Modules:
  0.0 110.5 jit_solution(2120544646113002075)
XLA Ops:
  0.6 0.9 constant_dynamic-slice_fusion.17
  1.6 0.6 collective-permute-start
  2.2 0.8 slice_bitcast_fusion.18
  3.1 1.3 %multiply_add_fusion.6 = (f32[4,64,256]{2,1,0:T(8,128)S(1)}, f32[4,64,256]{2,1,0:T(8,128)S(1)}, f32[4,64,256]{2,1,0:T(8,128)S(1)}, f32[4,64,256]{2,1,0:T(8,128)S(1)}) fusion(f32[4,64,256]{2,1,0:T(8,128)} %param.12, f32[2,4,64,256]{3,2,1,0:T(8,128)} %param.10, f32[64,256]{1,0:T(8,128)S(1)} %mul.964, f32[4]{0:T(128)S(1)} %multiply_add_fusion.7, ...), kind=kLoop, calls=%fused_computation.257 | loop fusion | flops 1114112 | bytes 2490384 | tf_op jit(solution)/shard_map/add | solution.py:76
  5.1 1.3 %collective-permute-start.1 = (f32[4,1,64,256]{3,2,1,0:T(8,128)S(1)}, f32[4,1,64,256]{3,2,1,0:T(8,128)S(1)}, u32[]{:S(2)}, u32[]{:S(2)}) collective-permute-start(f32[4,1,64,256]{3,2,1,0:T(8,128)S(1)} %pad_maximum_fusion.39), channel_id=1, source_target_pairs={{2,0},{4,2},{6,4},{8,6},{10,8},{12,10},{14,12},{3,1},{5,3},{7,5},{... | collective-permute-start | bytes 786440 | tf_op jit(solution)/shard_map/ppermute | solution.py:144
  6.5 5.5 %collective-permute-start.2 = (f32[4,1,64,256]{3,2,1,0:T(8,128)S(1)}, f32[4,1,64,256]{3,2,1,0:T(8,128)S(1)}, u32[]{:S(2)}, u32[]{:S(2)}) collective-permute-start(f32[4,1,64,256]{3,2,1,0:T(8,128)S(1)} %pad_maximum_fusion.40), channel_id=1, source_target_pairs={{0,2},{2,4},{4,6},{6,8},{8,10},{10,12},{12,14},{1,3},{3,5},{5,7},{... | collective-permute-start | bytes 786440 | tf_op jit(solution)/shard_map/ppermute | solution.py:143
  12.0 4.5 %collective-permute-done.1 = f32[4,1,64,256]{3,2,1,0:T(8,128)S(1)} collective-permute-done((f32[4,1,64,256]{3,2,1,0:T(8,128)S(1)}, f32[4,1,64,256]{3,2,1,0:T(8,128)S(1)}, u32[]{:S(2)}, u32[]{:S(2)}) %collective-permute-start.1) | collective-permute-done | bytes 262176 | tf_op jit(solution)/shard_map/ppermute | solution.py:144
  16.5 5.7 %collective-permute-done.2 = f32[4,1,64,256]{3,2,1,0:T(8,128)S(1)} collective-permute-done((f32[4,1,64,256]{3,2,1,0:T(8,128)S(1)}, f32[4,1,64,256]{3,2,1,0:T(8,128)S(1)}, u32[]{:S(2)}, u32[]{:S(2)}) %collective-permute-start.2) | collective-permute-done | bytes 262176 | tf_op jit(solution)/shard_map/ppermute | solution.py:143
  22.3 0.4 fusion.2
  23.1 1.2 %collective-permute-done.3 = f32[2,10,1,256]{3,2,1,0:T(1,128)S(1)} collective-permute-done((f32[2,10,1,256]{3,2,1,0:T(1,128)S(1)}, f32[2,10,1,256]{3,2,1,0:T(1,128)S(1)}, u32[]{:S(2)}, u32[]{:S(2)}) %collective-permute-start.3) | collective-permute-done | bytes 20512 | tf_op jit(solution)/shard_map/ppermute | solution.py:163
  24.5 0.3 fusion.5
  25.5 1.3 %collective-permute-start.5 = (f32[4,1,64,256]{3,2,1,0:T(8,128)S(1)}, f32[4,1,64,256]{3,2,1,0:T(8,128)S(1)}, u32[]{:S(2)}, u32[]{:S(2)}) collective-permute-start(f32[4,1,64,256]{3,2,1,0:T(8,128)S(1)} %pad_maximum_fusion.41), channel_id=1, source_target_pairs={{2,0},{4,2},{6,4},{8,6},{10,8},{12,10},{14,12},{3,1},{5,3},{7,5},{... | collective-permute-start | bytes 786440 | tf_op jit(solution)/shard_map/ppermute | solution.py:144
  26.8 5.0 %collective-permute-start.6 = (f32[4,1,64,256]{3,2,1,0:T(8,128)S(1)}, f32[4,1,64,256]{3,2,1,0:T(8,128)S(1)}, u32[]{:S(2)}, u32[]{:S(2)}) collective-permute-start(f32[4,1,64,256]{3,2,1,0:T(8,128)S(1)} %pad_maximum_fusion.42), channel_id=1, source_target_pairs={{0,2},{2,4},{4,6},{6,8},{8,10},{10,12},{12,14},{1,3},{3,5},{5,7},{... | collective-permute-start | bytes 786440 | tf_op jit(solution)/shard_map/ppermute | solution.py:143
  31.9 4.6 %collective-permute-done.5 = f32[4,1,64,256]{3,2,1,0:T(8,128)S(1)} collective-permute-done((f32[4,1,64,256]{3,2,1,0:T(8,128)S(1)}, f32[4,1,64,256]{3,2,1,0:T(8,128)S(1)}, u32[]{:S(2)}, u32[]{:S(2)}) %collective-permute-start.5) | collective-permute-done | bytes 262176 | tf_op jit(solution)/shard_map/ppermute | solution.py:144
  36.5 5.7 %collective-permute-done.6 = f32[4,1,64,256]{3,2,1,0:T(8,128)S(1)} collective-permute-done((f32[4,1,64,256]{3,2,1,0:T(8,128)S(1)}, f32[4,1,64,256]{3,2,1,0:T(8,128)S(1)}, u32[]{:S(2)}, u32[]{:S(2)}) %collective-permute-start.6) | collective-permute-done | bytes 262176 | tf_op jit(solution)/shard_map/ppermute | solution.py:143
  42.3 0.4 fusion.8
  43.1 1.1 %collective-permute-done.7 = f32[2,4,1,256]{3,2,1,0:T(1,128)S(1)} collective-permute-done((f32[2,4,1,256]{3,2,1,0:T(1,128)S(1)}, f32[2,4,1,256]{3,2,1,0:T(1,128)S(1)}, u32[]{:S(2)}, u32[]{:S(2)}) %collective-permute-start.7) | collective-permute-done | bytes 8224 | tf_op jit(solution)/shard_map/ppermute | solution.py:61
  44.2 0.3 fusion.11
  45.2 1.0 collective-permute-done.8
  46.6 4.4 %collective-permute-start.10 = (f32[4,1,64,256]{3,2,1,0:T(8,128)S(1)}, f32[4,1,64,256]{3,2,1,0:T(8,128)S(1)}, u32[]{:S(2)}, u32[]{:S(2)}) collective-permute-start(f32[4,1,64,256]{3,2,1,0:T(8,128)S(1)} %pad_maximum_fusion.44), channel_id=1, source_target_pairs={{0,2},{2,4},{4,6},{6,8},{8,10},{10,12},{12,14},{1,3},{3,5},{5,7},{... | collective-permute-start | bytes 786440 | tf_op jit(solution)/shard_map/ppermute | solution.py:143
  51.0 1.3 %collective-permute-start.9 = (f32[4,1,64,256]{3,2,1,0:T(8,128)S(1)}, f32[4,1,64,256]{3,2,1,0:T(8,128)S(1)}, u32[]{:S(2)}, u32[]{:S(2)}) collective-permute-start(f32[4,1,64,256]{3,2,1,0:T(8,128)S(1)} %pad_maximum_fusion.43), channel_id=1, source_target_pairs={{2,0},{4,2},{6,4},{8,6},{10,8},{12,10},{14,12},{3,1},{5,3},{7,5},{... | collective-permute-start | bytes 786440 | tf_op jit(solution)/shard_map/ppermute | solution.py:144
  52.3 10.1 %collective-permute-done.10 = f32[4,1,64,256]{3,2,1,0:T(8,128)S(1)} collective-permute-done((f32[4,1,64,256]{3,2,1,0:T(8,128)S(1)}, f32[4,1,64,256]{3,2,1,0:T(8,128)S(1)}, u32[]{:S(2)}, u32[]{:S(2)}) %collective-permute-start.10) | collective-permute-done | bytes 262176 | tf_op jit(solution)/shard_map/ppermute | solution.py:143
  62.5 0.3 fusion.14
  63.1 0.3 multiply_add_fusion.2
  63.5 0.6 collective-permute-start.12
  64.1 0.6 collective-permute-done.11
  65.0 0.3 fusion.17
  65.5 0.3 multiply_add_fusion.1
  66.2 1.3 %collective-permute-start.13 = (f32[4,1,64,256]{3,2,1,0:T(8,128)S(1)}, f32[4,1,64,256]{3,2,1,0:T(8,128)S(1)}, u32[]{:S(2)}, u32[]{:S(2)}) collective-permute-start(f32[4,1,64,256]{3,2,1,0:T(8,128)S(1)} %pad_maximum_fusion.45), channel_id=1, source_target_pairs={{2,0},{4,2},{6,4},{8,6},{10,8},{12,10},{14,12},{3,1},{5,3},{7,5},{... | collective-permute-start | bytes 786440 | tf_op jit(solution)/shard_map/ppermute | solution.py:144
  67.5 5.0 %collective-permute-start.14 = (f32[4,1,64,256]{3,2,1,0:T(8,128)S(1)}, f32[4,1,64,256]{3,2,1,0:T(8,128)S(1)}, u32[]{:S(2)}, u32[]{:S(2)}) collective-permute-start(f32[4,1,64,256]{3,2,1,0:T(8,128)S(1)} %pad_maximum_fusion.46), channel_id=1, source_target_pairs={{0,2},{2,4},{4,6},{6,8},{8,10},{10,12},{12,14},{1,3},{3,5},{5,7},{... | collective-permute-start | bytes 786440 | tf_op jit(solution)/shard_map/ppermute | solution.py:143
  72.6 4.8 %collective-permute-done.13 = f32[4,1,64,256]{3,2,1,0:T(8,128)S(1)} collective-permute-done((f32[4,1,64,256]{3,2,1,0:T(8,128)S(1)}, f32[4,1,64,256]{3,2,1,0:T(8,128)S(1)}, u32[]{:S(2)}, u32[]{:S(2)}) %collective-permute-start.13) | collective-permute-done | bytes 262176 | tf_op jit(solution)/shard_map/ppermute | solution.py:144
  77.4 5.7 %collective-permute-done.14 = f32[4,1,64,256]{3,2,1,0:T(8,128)S(1)} collective-permute-done((f32[4,1,64,256]{3,2,1,0:T(8,128)S(1)}, f32[4,1,64,256]{3,2,1,0:T(8,128)S(1)}, u32[]{:S(2)}, u32[]{:S(2)}) %collective-permute-start.14) | collective-permute-done | bytes 262176 | tf_op jit(solution)/shard_map/ppermute | solution.py:143
  83.2 0.4 fusion.20
  84.1 0.6 compare_reduce_fusion
  84.8 0.5 collective-permute-done.15
  85.3 0.3 fusion.23
  85.9 1.1 multiply_reduce_fusion
  87.2 0.5 copy-done.3
  89.3 2.5 %collective-permute-start.16 = (f32[65,256]{1,0:T(8,128)S(1)}, f32[65,256]{1,0:T(8,128)S(1)}, u32[]{:S(2)}, u32[]{:S(2)}) collective-permute-start(f32[65,256]{1,0:T(8,128)S(1)} %select_maximum_fusion), channel_id=1, source_target_pairs={{0,2},{2,0},{4,6},{6,4},{8,10},{10,8},{12,14},{14,12},{1,3},{3,1},... | collective-permute-start | bytes 199688 | tf_op jit(solution)/shard_map/ppermute | solution.py:30
  92.0 2.9 %collective-permute-done.18 = f32[]{:T(128)} collective-permute-done((f32[]{:T(128)}, f32[]{:T(128)}, u32[]{:S(2)}, u32[]{:S(2)}) %collective-permute-start.18) | collective-permute-done | bytes 36 | tf_op jit(solution)/shard_map/ppermute | solution.py:34
  96.2 0.5 slice.1303
  97.4 1.4 %collective-permute-start.21 = (f32[65,256]{1,0:T(8,128)S(1)}, f32[65,256]{1,0:T(8,128)S(1)}, u32[]{:S(2)}, u32[]{:S(2)}) collective-permute-start(f32[65,256]{1,0:T(8,128)S(1)} %scatter.9), channel_id=1, source_target_pairs={{0,12},{2,14},{4,8},{6,10},{8,4},{10,6},{12,0},{14,2},{1,13},{3,15... | collective-permute-start | bytes 199688 | tf_op jit(solution)/shard_map/ppermute | solution.py:44
  98.8 1.7 %collective-permute-start.20 = (f32[65,256]{1,0:T(8,128)S(1)}, f32[65,256]{1,0:T(8,128)S(1)}, u32[]{:S(2)}, u32[]{:S(2)}) collective-permute-start(f32[65,256]{1,0:T(8,128)S(1)} %scatter.9), channel_id=1, source_target_pairs={{0,8},{2,10},{4,12},{6,14},{8,0},{10,2},{12,4},{14,6},{1,9},{3,11}... | collective-permute-start | bytes 199688 | tf_op jit(solution)/shard_map/ppermute | solution.py:44
  100.5 1.3 %collective-permute-start.19 = (f32[65,256]{1,0:T(8,128)S(1)}, f32[65,256]{1,0:T(8,128)S(1)}, u32[]{:S(2)}, u32[]{:S(2)}) collective-permute-start(f32[65,256]{1,0:T(8,128)S(1)} %scatter.9), channel_id=1, source_target_pairs={{0,4},{2,6},{4,0},{6,2},{8,12},{10,14},{12,8},{14,10},{1,5},{3,7},... | collective-permute-start | bytes 199688 | tf_op jit(solution)/shard_map/ppermute | solution.py:44
  101.9 2.1 %collective-permute-done.21 = f32[65,256]{1,0:T(8,128)S(1)} collective-permute-done((f32[65,256]{1,0:T(8,128)S(1)}, f32[65,256]{1,0:T(8,128)S(1)}, u32[]{:S(2)}, u32[]{:S(2)}) %collective-permute-start.21) | collective-permute-done | bytes 66592 | tf_op jit(solution)/shard_map/ppermute | solution.py:44
  103.9 3.5 %collective-permute-done.20 = f32[65,256]{1,0:T(8,128)S(1)} collective-permute-done((f32[65,256]{1,0:T(8,128)S(1)}, f32[65,256]{1,0:T(8,128)S(1)}, u32[]{:S(2)}, u32[]{:S(2)}) %collective-permute-start.20) | collective-permute-done | bytes 66592 | tf_op jit(solution)/shard_map/ppermute | solution.py:44
  107.6 0.5 slice.1306
  108.8 0.6 maximum_divide_fusion
  (126 shorter events, 6.6 us)
Async XLA Ops:
  0.6 2.5 %copy-start.1 = (f32[2,4,64,256]{3,2,1,0:T(8,128)S(1)}, f32[2,4,64,256]{3,2,1,0:T(8,128)}, u32[]{:S(2)}) copy-start(f32[2,4,64,256]{3,2,1,0:T(8,128)} %param.11) | copy-start | bytes 1572868
  1.6 3.2 %collective-permute-start = (f32[2,4,1,256]{3,2,1,0:T(1,128)S(1)}, f32[2,4,1,256]{3,2,1,0:T(1,128)S(1)}, u32[]{:S(2)}, u32[]{:S(2)}) collective-permute-start(f32[2,4,1,256]{3,2,1,0:T(1,128)S(1)} %constant_dynamic-slice_fusion.17), channel_id=1, source_target_pairs={{0,1},{1,0},{2,3},{3,2},{4,5},{5,4},{6,7},{7,6},{8,9},{9,8},{10,11... | collective-permute-start | bytes 24584 | tf_op jit(solution)/shard_map/ppermute | solution.py:61
  3.1 1.5 %copy-start = (f32[2,4,64,256]{3,2,1,0:T(8,128)S(1)}, f32[2,4,64,256]{3,2,1,0:T(8,128)}, u32[]{:S(2)}) copy-start(f32[2,4,64,256]{3,2,1,0:T(8,128)} %param.9) | copy-start | bytes 1572868
  4.5 19.9 %collective-permute-start.4 = (f32[3,4,1,256]{3,2,1,0:T(1,128)S(1)}, f32[3,4,1,256]{3,2,1,0:T(1,128)S(1)}, u32[]{:S(2)}, u32[]{:S(2)}) collective-permute-start(f32[3,4,1,256]{3,2,1,0:T(1,128)S(1)} %pad_maximum_fusion.53), channel_id=1, source_target_pairs={{0,1},{1,0},{2,3},{3,2},{4,5},{5,4},{6,7},{7,6},{8,9},{9,8},{10,11... | collective-permute-start | bytes 36872 | tf_op jit(solution)/shard_map/ppermute | solution.py:127
  5.1 11.4 %collective-permute-start.1 = (f32[4,1,64,256]{3,2,1,0:T(8,128)S(1)}, f32[4,1,64,256]{3,2,1,0:T(8,128)S(1)}, u32[]{:S(2)}, u32[]{:S(2)}) collective-permute-start(f32[4,1,64,256]{3,2,1,0:T(8,128)S(1)} %pad_maximum_fusion.39), channel_id=1, source_target_pairs={{2,0},{4,2},{6,4},{8,6},{10,8},{12,10},{14,12},{3,1},{5,3},{7,5},{... | collective-permute-start | bytes 786440 | tf_op jit(solution)/shard_map/ppermute | solution.py:144
  6.5 15.8 %collective-permute-start.2 = (f32[4,1,64,256]{3,2,1,0:T(8,128)S(1)}, f32[4,1,64,256]{3,2,1,0:T(8,128)S(1)}, u32[]{:S(2)}, u32[]{:S(2)}) collective-permute-start(f32[4,1,64,256]{3,2,1,0:T(8,128)S(1)} %pad_maximum_fusion.40), channel_id=1, source_target_pairs={{0,2},{2,4},{4,6},{6,8},{8,10},{10,12},{12,14},{1,3},{3,5},{5,7},{... | collective-permute-start | bytes 786440 | tf_op jit(solution)/shard_map/ppermute | solution.py:143
  23.0 1.3 %collective-permute-start.3 = (f32[2,10,1,256]{3,2,1,0:T(1,128)S(1)}, f32[2,10,1,256]{3,2,1,0:T(1,128)S(1)}, u32[]{:S(2)}, u32[]{:S(2)}) collective-permute-start(f32[2,10,1,256]{3,2,1,0:T(1,128)S(1)} %pad_maximum_fusion.51), channel_id=1, source_target_pairs={{0,1},{1,0},{2,3},{3,2},{4,5},{5,4},{6,7},{7,6},{8,9},{9,8},{10,11... | collective-permute-start | bytes 61448 | tf_op jit(solution)/shard_map/ppermute | solution.py:163
  25.5 11.0 %collective-permute-start.5 = (f32[4,1,64,256]{3,2,1,0:T(8,128)S(1)}, f32[4,1,64,256]{3,2,1,0:T(8,128)S(1)}, u32[]{:S(2)}, u32[]{:S(2)}) collective-permute-start(f32[4,1,64,256]{3,2,1,0:T(8,128)S(1)} %pad_maximum_fusion.41), channel_id=1, source_target_pairs={{2,0},{4,2},{6,4},{8,6},{10,8},{12,10},{14,12},{3,1},{5,3},{7,5},{... | collective-permute-start | bytes 786440 | tf_op jit(solution)/shard_map/ppermute | solution.py:144
  26.8 15.5 %collective-permute-start.6 = (f32[4,1,64,256]{3,2,1,0:T(8,128)S(1)}, f32[4,1,64,256]{3,2,1,0:T(8,128)S(1)}, u32[]{:S(2)}, u32[]{:S(2)}) collective-permute-start(f32[4,1,64,256]{3,2,1,0:T(8,128)S(1)} %pad_maximum_fusion.42), channel_id=1, source_target_pairs={{0,2},{2,4},{4,6},{6,8},{8,10},{10,12},{12,14},{1,3},{3,5},{5,7},{... | collective-permute-start | bytes 786440 | tf_op jit(solution)/shard_map/ppermute | solution.py:143
  43.0 1.2 %collective-permute-start.7 = (f32[2,4,1,256]{3,2,1,0:T(1,128)S(1)}, f32[2,4,1,256]{3,2,1,0:T(1,128)S(1)}, u32[]{:S(2)}, u32[]{:S(2)}) collective-permute-start(f32[2,4,1,256]{3,2,1,0:T(1,128)S(1)} %constant_dynamic-slice_fusion.9), channel_id=1, source_target_pairs={{0,1},{1,0},{2,3},{3,2},{4,5},{5,4},{6,7},{7,6},{8,9},{9,8},{10,11... | collective-permute-start | bytes 24584 | tf_op jit(solution)/shard_map/ppermute | solution.py:61
  45.0 1.2 %collective-permute-start.8 = (f32[2,4,1,256]{3,2,1,0:T(1,128)S(1)}, f32[2,4,1,256]{3,2,1,0:T(1,128)S(1)}, u32[]{:S(2)}, u32[]{:S(2)}) collective-permute-start(f32[2,4,1,256]{3,2,1,0:T(1,128)S(1)} %constant_dynamic-slice_fusion.8), channel_id=1, source_target_pairs={{0,1},{1,0},{2,3},{3,2},{4,5},{5,4},{6,7},{7,6},{8,9},{9,8},{10,11... | collective-permute-start | bytes 24584 | tf_op jit(solution)/shard_map/ppermute | solution.py:61
  46.6 15.9 %collective-permute-start.10 = (f32[4,1,64,256]{3,2,1,0:T(8,128)S(1)}, f32[4,1,64,256]{3,2,1,0:T(8,128)S(1)}, u32[]{:S(2)}, u32[]{:S(2)}) collective-permute-start(f32[4,1,64,256]{3,2,1,0:T(8,128)S(1)} %pad_maximum_fusion.44), channel_id=1, source_target_pairs={{0,2},{2,4},{4,6},{6,8},{8,10},{10,12},{12,14},{1,3},{3,5},{5,7},{... | collective-permute-start | bytes 786440 | tf_op jit(solution)/shard_map/ppermute | solution.py:143
  51.0 11.5 %collective-permute-start.9 = (f32[4,1,64,256]{3,2,1,0:T(8,128)S(1)}, f32[4,1,64,256]{3,2,1,0:T(8,128)S(1)}, u32[]{:S(2)}, u32[]{:S(2)}) collective-permute-start(f32[4,1,64,256]{3,2,1,0:T(8,128)S(1)} %pad_maximum_fusion.43), channel_id=1, source_target_pairs={{2,0},{4,2},{6,4},{8,6},{10,8},{12,10},{14,12},{3,1},{5,3},{7,5},{... | collective-permute-start | bytes 786440 | tf_op jit(solution)/shard_map/ppermute | solution.py:144
  63.4 1.3 %collective-permute-start.11 = (f32[2,10,1,256]{3,2,1,0:T(1,128)S(1)}, f32[2,10,1,256]{3,2,1,0:T(1,128)S(1)}, u32[]{:S(2)}, u32[]{:S(2)}) collective-permute-start(f32[2,10,1,256]{3,2,1,0:T(1,128)S(1)} %pad_maximum_fusion.52), channel_id=1, source_target_pairs={{0,1},{1,0},{2,3},{3,2},{4,5},{5,4},{6,7},{7,6},{8,9},{9,8},{10,11... | collective-permute-start | bytes 61448 | tf_op jit(solution)/shard_map/ppermute | solution.py:163
  63.5 1.4 %collective-permute-start.12 = (f32[3,4,1,256]{3,2,1,0:T(1,128)S(1)}, f32[3,4,1,256]{3,2,1,0:T(1,128)S(1)}, u32[]{:S(2)}, u32[]{:S(2)}) collective-permute-start(f32[3,4,1,256]{3,2,1,0:T(1,128)S(1)} %pad_maximum_fusion.54), channel_id=1, source_target_pairs={{0,1},{1,0},{2,3},{3,2},{4,5},{5,4},{6,7},{7,6},{8,9},{9,8},{10,11... | collective-permute-start | bytes 36872 | tf_op jit(solution)/shard_map/ppermute | solution.py:127
  66.2 11.2 %collective-permute-start.13 = (f32[4,1,64,256]{3,2,1,0:T(8,128)S(1)}, f32[4,1,64,256]{3,2,1,0:T(8,128)S(1)}, u32[]{:S(2)}, u32[]{:S(2)}) collective-permute-start(f32[4,1,64,256]{3,2,1,0:T(8,128)S(1)} %pad_maximum_fusion.45), channel_id=1, source_target_pairs={{2,0},{4,2},{6,4},{8,6},{10,8},{12,10},{14,12},{3,1},{5,3},{7,5},{... | collective-permute-start | bytes 786440 | tf_op jit(solution)/shard_map/ppermute | solution.py:144
  67.5 15.7 %collective-permute-start.14 = (f32[4,1,64,256]{3,2,1,0:T(8,128)S(1)}, f32[4,1,64,256]{3,2,1,0:T(8,128)S(1)}, u32[]{:S(2)}, u32[]{:S(2)}) collective-permute-start(f32[4,1,64,256]{3,2,1,0:T(8,128)S(1)} %pad_maximum_fusion.46), channel_id=1, source_target_pairs={{0,2},{2,4},{4,6},{6,8},{8,10},{10,12},{12,14},{1,3},{3,5},{5,7},{... | collective-permute-start | bytes 786440 | tf_op jit(solution)/shard_map/ppermute | solution.py:143
  84.0 1.2 %collective-permute-start.15 = (f32[2,4,1,256]{3,2,1,0:T(1,128)S(1)}, f32[2,4,1,256]{3,2,1,0:T(1,128)S(1)}, u32[]{:S(2)}, u32[]{:S(2)}) collective-permute-start(f32[2,4,1,256]{3,2,1,0:T(1,128)S(1)} %constant_dynamic-slice_fusion), channel_id=1, source_target_pairs={{0,1},{1,0},{2,3},{3,2},{4,5},{5,4},{6,7},{7,6},{8,9},{9,8},{10,11... | collective-permute-start | bytes 24584 | tf_op jit(solution)/shard_map/ppermute | solution.py:61
  85.8 1.1 copy-start.2
  86.9 0.8 copy-start.3
  89.3 6.9 %collective-permute-start.16 = (f32[65,256]{1,0:T(8,128)S(1)}, f32[65,256]{1,0:T(8,128)S(1)}, u32[]{:S(2)}, u32[]{:S(2)}) collective-permute-start(f32[65,256]{1,0:T(8,128)S(1)} %select_maximum_fusion), channel_id=1, source_target_pairs={{0,2},{2,0},{4,6},{6,4},{8,10},{10,8},{12,14},{14,12},{1,3},{3,1},... | collective-permute-start | bytes 199688 | tf_op jit(solution)/shard_map/ppermute | solution.py:30
  91.8 3.1 %collective-permute-start.18 = (f32[]{:T(128)}, f32[]{:T(128)}, u32[]{:S(2)}, u32[]{:S(2)}) collective-permute-start(f32[]{:T(128)} %get-tuple-element.29), channel_id=1, source_target_pairs={{0,3},{1,2},{2,1},{3,0},{4,7},{5,6},{6,5},{7,4},{8,11},{9,10},{10,... | collective-permute-start | bytes 20 | tf_op jit(solution)/shard_map/ppermute | solution.py:34
  91.8 3.1 %collective-permute-start.17 = (f32[]{:T(128)}, f32[]{:T(128)}, u32[]{:S(2)}, u32[]{:S(2)}) collective-permute-start(f32[]{:T(128)} %get-tuple-element.29), channel_id=1, source_target_pairs={{0,1},{1,0},{2,3},{3,2},{4,5},{5,4},{6,7},{7,6},{8,9},{9,8},{10,11... | collective-permute-start | bytes 20 | tf_op jit(solution)/shard_map/ppermute | solution.py:33
  97.4 6.5 %collective-permute-start.21 = (f32[65,256]{1,0:T(8,128)S(1)}, f32[65,256]{1,0:T(8,128)S(1)}, u32[]{:S(2)}, u32[]{:S(2)}) collective-permute-start(f32[65,256]{1,0:T(8,128)S(1)} %scatter.9), channel_id=1, source_target_pairs={{0,12},{2,14},{4,8},{6,10},{8,4},{10,6},{12,0},{14,2},{1,13},{3,15... | collective-permute-start | bytes 199688 | tf_op jit(solution)/shard_map/ppermute | solution.py:44
  98.8 8.7 %collective-permute-start.20 = (f32[65,256]{1,0:T(8,128)S(1)}, f32[65,256]{1,0:T(8,128)S(1)}, u32[]{:S(2)}, u32[]{:S(2)}) collective-permute-start(f32[65,256]{1,0:T(8,128)S(1)} %scatter.9), channel_id=1, source_target_pairs={{0,8},{2,10},{4,12},{6,14},{8,0},{10,2},{12,4},{14,6},{1,9},{3,11}... | collective-permute-start | bytes 199688 | tf_op jit(solution)/shard_map/ppermute | solution.py:44
  100.5 6.9 %collective-permute-start.19 = (f32[65,256]{1,0:T(8,128)S(1)}, f32[65,256]{1,0:T(8,128)S(1)}, u32[]{:S(2)}, u32[]{:S(2)}) collective-permute-start(f32[65,256]{1,0:T(8,128)S(1)} %scatter.9), channel_id=1, source_target_pairs={{0,4},{2,6},{4,0},{6,2},{8,12},{10,14},{12,8},{14,10},{1,5},{3,7},... | collective-permute-start | bytes 199688 | tf_op jit(solution)/shard_map/ppermute | solution.py:44

commit v14 on v9

--- a/solution.py
+++ b/solution.py
@@ -46,7 +46,7 @@
     iy = lax.axis_index("gy")
     Y = block.shape[2]
     if ny == 2:
-        strip = lax.dynamic_slice_in_dim(block, (1 - iy) * (Y - 1), 1, axis=2)
+        strip = jnp.where(iy == 0, block[:, :, Y - 1:], block[:, :, :1])
         other = lax.ppermute(strip, "gy", [(0, 1), (1, 0)])
         zero = jnp.zeros_like(other)
         below = jnp.where(iy == 1, other, zero)

time: 109 us -> 112 us (1.028)
  other arithmetic: 12 us -> 16.5 us
  waiting for transfers between devices: 54.4 us -> 52.7 us
    unnamed x8 -> x16, local copies, waits for them, and re-layouts: 0.54 us -> 2.13 us
  transfers between devices with their start and end apart: 21 -> 21, of which waited for: 16 -> 16; matrix products, arithmetic and copies ran while one was open for 5% -> 7% of each run, Pallas kernels for 0% -> 0%
where the time goes in v14:
time: 112 us
  waiting for transfers between devices  52.7 us (47%)
  starting transfers between devices  33.5 us (30%)
  other arithmetic  16.5 us (15%)
  between operations  5.2 us (5%)
  local copies, waits for them, and re-layouts  3.89 us (3%)
    ppermute x4, waiting for transfers between devices, stage_pair(): lax.ppermute(jnp.concatenate([stage[:, X - 1:], part_top]), 'gx', up)  26.6 us
    ppermute x4, starting transfers between devices, stage_pair(): lax.ppermute(jnp.concatenate([stage[:, X - 1:], part_top]), 'gx', up)  19.4 us
    ppermute x4, waiting for transfers between devices, stage_pair(): lax.ppermute(jnp.concatenate([stage[:, :1], part_bottom]), 'gx', down)  13 us
    ppermute x4, starting transfers between devices, stage_pair(): lax.ppermute(jnp.concatenate([stage[:, :1], part_bottom]), 'gx', down)  5.17 us
    ppermute x3, waiting for transfers between devices, gx_total(): lax.ppermute(pair, 'gx', [(i, i ^ 2 * k) for i in range(count)])  5.13 us
    ppermute x3, starting transfers between devices, gx_total(): lax.ppermute(pair, 'gx', [(i, i ^ 2 * k) for i in range(count)])  4.45 us
    sub x14, other arithmetic, operator(): lapl = total - 6.0 * field  3.86 us
    ppermute x4, waiting for transfers between devices, y_extended(): other = lax.ppermute(strip, 'gy', [(0, 1), (1, 0)])  2.62 us
  transfers between devices with their start and end apart: 21, of which 16 were waited for; matrix products, arithmetic and copies ran while one was open for 7% of the time, Pallas kernels for 0%

profile of v14, /device:TPU:0, one launch (start us, length us, event | category | flops | bytes accessed | tf_op | source)
XLA Modules:
  0.0 111.8 jit_solution(1848618628971454853)
XLA Ops:
  0.6 0.9 broadcast_select_fusion.21
  1.6 0.6 collective-permute-start
  2.2 0.8 slice_bitcast_fusion.18
  3.2 1.3 %multiply_add_fusion.6 = (f32[4,64,256]{2,1,0:T(8,128)S(1)}, f32[4,64,256]{2,1,0:T(8,128)S(1)}, f32[4,64,256]{2,1,0:T(8,128)S(1)}, f32[4,64,256]{2,1,0:T(8,128)S(1)}) fusion(f32[4,64,256]{2,1,0:T(8,128)} %param.10, f32[2,4,64,256]{3,2,1,0:T(8,128)} %param.8, f32[64,256]{1,0:T(8,128)S(1)} %mul.959, f32[4]{0:T(128)S(1)} %multiply_add_fusion.7, ...), kind=kLoop, calls=%fused_computation.257 | loop fusion | flops 1114112 | bytes 2490384 | tf_op jit(solution)/shard_map/add | solution.py:65
  4.5 0.6 pad_maximum_fusion.53
  5.2 1.0 copy-done
  6.2 0.6 copy-done.4
  7.1 1.3 %collective-permute-start.1 = (f32[4,1,64,256]{3,2,1,0:T(8,128)S(1)}, f32[4,1,64,256]{3,2,1,0:T(8,128)S(1)}, u32[]{:S(2)}, u32[]{:S(2)}) collective-permute-start(f32[4,1,64,256]{3,2,1,0:T(8,128)S(1)} %pad_maximum_fusion.39), channel_id=1, source_target_pairs={{2,0},{4,2},{6,4},{8,6},{10,8},{12,10},{14,12},{3,1},{5,3},{7,5},{... | collective-permute-start | bytes 786440 | tf_op jit(solution)/shard_map/ppermute | solution.py:133
  8.4 0.7 pad_maximum_fusion.40
  9.1 5.0 %collective-permute-start.2 = (f32[4,1,64,256]{3,2,1,0:T(8,128)}, f32[4,1,64,256]{3,2,1,0:T(8,128)S(1)}, u32[]{:S(2)}, u32[]{:S(2)}) collective-permute-start(f32[4,1,64,256]{3,2,1,0:T(8,128)} %pad_maximum_fusion.40), channel_id=1, source_target_pairs={{0,2},{2,4},{4,6},{6,8},{8,10},{10,12},{12,14},{1,3},{3,5},{5,7},{... | collective-permute-start | bytes 786440 | tf_op jit(solution)/shard_map/ppermute | solution.py:132
  14.2 0.7 slice_multiply_fusion.48
  14.8 3.6 %collective-permute-done.1 = f32[4,1,64,256]{3,2,1,0:T(8,128)S(1)} collective-permute-done((f32[4,1,64,256]{3,2,1,0:T(8,128)S(1)}, f32[4,1,64,256]{3,2,1,0:T(8,128)S(1)}, u32[]{:S(2)}, u32[]{:S(2)}) %collective-permute-start.1) | collective-permute-done | bytes 262176 | tf_op jit(solution)/shard_map/ppermute | solution.py:133
  18.5 0.9 fusion.179
  19.4 5.0 %collective-permute-done.2 = f32[4,1,64,256]{3,2,1,0:T(8,128)S(1)} collective-permute-done((f32[4,1,64,256]{3,2,1,0:T(8,128)}, f32[4,1,64,256]{3,2,1,0:T(8,128)S(1)}, u32[]{:S(2)}, u32[]{:S(2)}) %collective-permute-start.2) | collective-permute-done | bytes 262176 | tf_op jit(solution)/shard_map/ppermute | solution.py:132
  24.4 0.4 fusion.2
  25.2 1.1 collective-permute-done.3
  26.6 0.7 fusion.284
  27.3 0.4 fusion.5
  28.3 1.3 %collective-permute-start.5 = (f32[4,1,64,256]{3,2,1,0:T(8,128)S(1)}, f32[4,1,64,256]{3,2,1,0:T(8,128)S(1)}, u32[]{:S(2)}, u32[]{:S(2)}) collective-permute-start(f32[4,1,64,256]{3,2,1,0:T(8,128)S(1)} %pad_maximum_fusion.41), channel_id=1, source_target_pairs={{2,0},{4,2},{6,4},{8,6},{10,8},{12,10},{14,12},{3,1},{5,3},{7,5},{... | collective-permute-start | bytes 786440 | tf_op jit(solution)/shard_map/ppermute | solution.py:133
  29.6 4.9 %collective-permute-start.6 = (f32[4,1,64,256]{3,2,1,0:T(8,128)S(1)}, f32[4,1,64,256]{3,2,1,0:T(8,128)S(1)}, u32[]{:S(2)}, u32[]{:S(2)}) collective-permute-start(f32[4,1,64,256]{3,2,1,0:T(8,128)S(1)} %pad_maximum_fusion.42), channel_id=1, source_target_pairs={{0,2},{2,4},{4,6},{6,8},{8,10},{10,12},{12,14},{1,3},{3,5},{5,7},{... | collective-permute-start | bytes 786440 | tf_op jit(solution)/shard_map/ppermute | solution.py:132
  34.6 4.6 %collective-permute-done.5 = f32[4,1,64,256]{3,2,1,0:T(8,128)S(1)} collective-permute-done((f32[4,1,64,256]{3,2,1,0:T(8,128)S(1)}, f32[4,1,64,256]{3,2,1,0:T(8,128)S(1)}, u32[]{:S(2)}, u32[]{:S(2)}) %collective-permute-start.5) | collective-permute-done | bytes 262176 | tf_op jit(solution)/shard_map/ppermute | solution.py:133
  39.3 5.7 %collective-permute-done.6 = f32[4,1,64,256]{3,2,1,0:T(8,128)S(1)} collective-permute-done((f32[4,1,64,256]{3,2,1,0:T(8,128)S(1)}, f32[4,1,64,256]{3,2,1,0:T(8,128)S(1)}, u32[]{:S(2)}, u32[]{:S(2)}) %collective-permute-start.6) | collective-permute-done | bytes 262176 | tf_op jit(solution)/shard_map/ppermute | solution.py:132
  45.1 0.4 fusion.8
  45.8 1.1 %collective-permute-done.7 = f32[2,4,1,256]{3,2,1,0:T(1,128)S(1)} collective-permute-done((f32[2,4,1,256]{3,2,1,0:T(1,128)S(1)}, f32[2,4,1,256]{3,2,1,0:T(1,128)S(1)}, u32[]{:S(2)}, u32[]{:S(2)}) %collective-permute-start.7) | collective-permute-done | bytes 8224 | tf_op jit(solution)/shard_map/ppermute | solution.py:50
  46.9 0.4 fusion.11
  48.0 1.0 collective-permute-done.8
  49.3 4.4 %collective-permute-start.10 = (f32[4,1,64,256]{3,2,1,0:T(8,128)S(1)}, f32[4,1,64,256]{3,2,1,0:T(8,128)S(1)}, u32[]{:S(2)}, u32[]{:S(2)}) collective-permute-start(f32[4,1,64,256]{3,2,1,0:T(8,128)S(1)} %pad_maximum_fusion.44), channel_id=1, source_target_pairs={{0,2},{2,4},{4,6},{6,8},{8,10},{10,12},{12,14},{1,3},{3,5},{5,7},{... | collective-permute-start | bytes 786440 | tf_op jit(solution)/shard_map/ppermute | solution.py:132
  53.8 1.3 %collective-permute-start.9 = (f32[4,1,64,256]{3,2,1,0:T(8,128)S(1)}, f32[4,1,64,256]{3,2,1,0:T(8,128)S(1)}, u32[]{:S(2)}, u32[]{:S(2)}) collective-permute-start(f32[4,1,64,256]{3,2,1,0:T(8,128)S(1)} %pad_maximum_fusion.43), channel_id=1, source_target_pairs={{2,0},{4,2},{6,4},{8,6},{10,8},{12,10},{14,12},{3,1},{5,3},{7,5},{... | collective-permute-start | bytes 786440 | tf_op jit(solution)/shard_map/ppermute | solution.py:133
  55.1 10.1 %collective-permute-done.10 = f32[4,1,64,256]{3,2,1,0:T(8,128)S(1)} collective-permute-done((f32[4,1,64,256]{3,2,1,0:T(8,128)S(1)}, f32[4,1,64,256]{3,2,1,0:T(8,128)S(1)}, u32[]{:S(2)}, u32[]{:S(2)}) %collective-permute-start.10) | collective-permute-done | bytes 262176 | tf_op jit(solution)/shard_map/ppermute | solution.py:132
  66.3 0.6 collective-permute-start.12
  66.8 0.6 collective-permute-done.11
  68.9 1.3 %collective-permute-start.13 = (f32[4,1,64,256]{3,2,1,0:T(8,128)S(1)}, f32[4,1,64,256]{3,2,1,0:T(8,128)S(1)}, u32[]{:S(2)}, u32[]{:S(2)}) collective-permute-start(f32[4,1,64,256]{3,2,1,0:T(8,128)S(1)} %pad_maximum_fusion.45), channel_id=1, source_target_pairs={{2,0},{4,2},{6,4},{8,6},{10,8},{12,10},{14,12},{3,1},{5,3},{7,5},{... | collective-permute-start | bytes 786440 | tf_op jit(solution)/shard_map/ppermute | solution.py:133
  70.3 5.0 %collective-permute-start.14 = (f32[4,1,64,256]{3,2,1,0:T(8,128)S(1)}, f32[4,1,64,256]{3,2,1,0:T(8,128)S(1)}, u32[]{:S(2)}, u32[]{:S(2)}) collective-permute-start(f32[4,1,64,256]{3,2,1,0:T(8,128)S(1)} %pad_maximum_fusion.46), channel_id=1, source_target_pairs={{0,2},{2,4},{4,6},{6,8},{8,10},{10,12},{12,14},{1,3},{3,5},{5,7},{... | collective-permute-start | bytes 786440 | tf_op jit(solution)/shard_map/ppermute | solution.py:132
  75.3 4.8 %collective-permute-done.13 = f32[4,1,64,256]{3,2,1,0:T(8,128)S(1)} collective-permute-done((f32[4,1,64,256]{3,2,1,0:T(8,128)S(1)}, f32[4,1,64,256]{3,2,1,0:T(8,128)S(1)}, u32[]{:S(2)}, u32[]{:S(2)}) %collective-permute-start.13) | collective-permute-done | bytes 262176 | tf_op jit(solution)/shard_map/ppermute | solution.py:133
  80.2 5.7 %collective-permute-done.14 = f32[4,1,64,256]{3,2,1,0:T(8,128)S(1)} collective-permute-done((f32[4,1,64,256]{3,2,1,0:T(8,128)S(1)}, f32[4,1,64,256]{3,2,1,0:T(8,128)S(1)}, u32[]{:S(2)}, u32[]{:S(2)}) %collective-permute-start.14) | collective-permute-done | bytes 262176 | tf_op jit(solution)/shard_map/ppermute | solution.py:132
  86.9 0.6 compare_reduce_fusion
  87.5 0.5 collective-permute-done.15
  88.6 1.1 multiply_reduce_fusion
  89.7 0.6 copy-done.7
  91.0 1.1 collective-permute-done.16
  94.0 2.5 %collective-permute-start.17 = (f32[65,256]{1,0:T(8,128)S(1)}, f32[65,256]{1,0:T(8,128)S(1)}, u32[]{:S(2)}, u32[]{:S(2)}) collective-permute-start(f32[65,256]{1,0:T(8,128)S(1)} %select_maximum_fusion), channel_id=1, source_target_pairs={{0,2},{2,0},{4,6},{6,4},{8,10},{10,8},{12,14},{14,12},{1,3},{3,1},... | collective-permute-start | bytes 199688 | tf_op jit(solution)/shard_map/ppermute | solution.py:28
  96.5 2.6 %collective-permute-done.17 = f32[65,256]{1,0:T(8,128)S(1)} collective-permute-done((f32[65,256]{1,0:T(8,128)S(1)}, f32[65,256]{1,0:T(8,128)S(1)}, u32[]{:S(2)}, u32[]{:S(2)}) %collective-permute-start.17) | collective-permute-done | bytes 66592 | tf_op jit(solution)/shard_map/ppermute | solution.py:28
  99.2 3.1 %collective-permute-start.20 = (f32[65,256]{1,0:T(8,128)S(1)}, f32[65,256]{1,0:T(8,128)S(1)}, u32[]{:S(2)}, u32[]{:S(2)}) collective-permute-start(f32[65,256]{1,0:T(8,128)S(1)} %fusion.286), channel_id=1, source_target_pairs={{0,12},{2,14},{4,8},{6,10},{8,4},{10,6},{12,0},{14,2},{1,13},{3,15... | collective-permute-start | bytes 199688 | tf_op jit(solution)/shard_map/ppermute | solution.py:33
  102.3 1.3 %collective-permute-start.18 = (f32[65,256]{1,0:T(8,128)S(1)}, f32[65,256]{1,0:T(8,128)S(1)}, u32[]{:S(2)}, u32[]{:S(2)}) collective-permute-start(f32[65,256]{1,0:T(8,128)S(1)} %fusion.286), channel_id=1, source_target_pairs={{0,4},{2,6},{4,0},{6,2},{8,12},{10,14},{12,8},{14,10},{1,5},{3,7},... | collective-permute-start | bytes 199688 | tf_op jit(solution)/shard_map/ppermute | solution.py:33
  103.6 2.6 %collective-permute-done.20 = f32[65,256]{1,0:T(8,128)S(1)} collective-permute-done((f32[65,256]{1,0:T(8,128)S(1)}, f32[65,256]{1,0:T(8,128)S(1)}, u32[]{:S(2)}, u32[]{:S(2)}) %collective-permute-start.20) | collective-permute-done | bytes 66592 | tf_op jit(solution)/shard_map/ppermute | solution.py:33
  106.2 2.5 %collective-permute-done.19 = f32[65,256]{1,0:T(8,128)S(1)} collective-permute-done((f32[65,256]{1,0:T(8,128)S(1)}, f32[65,256]{1,0:T(8,128)S(1)}, u32[]{:S(2)}, u32[]{:S(2)}) %collective-permute-start.19) | collective-permute-done | bytes 66592 | tf_op jit(solution)/shard_map/ppermute | solution.py:33
  108.8 0.5 slice.1320
  110.1 0.6 maximum_divide_fusion
  (129 shorter events, 8.3 us)
Async XLA Ops:
  0.6 2.5 %copy-start.1 = (f32[2,4,64,256]{3,2,1,0:T(8,128)S(1)}, f32[2,4,64,256]{3,2,1,0:T(8,128)}, u32[]{:S(2)}) copy-start(f32[2,4,64,256]{3,2,1,0:T(8,128)} %param.9) | copy-start | bytes 1572868
  1.6 4.6 %collective-permute-start = (f32[2,4,1,256]{3,2,1,0:T(1,128)S(1)}, f32[2,4,1,256]{3,2,1,0:T(1,128)S(1)}, u32[]{:S(2)}, u32[]{:S(2)}) collective-permute-start(f32[2,4,1,256]{3,2,1,0:T(1,128)S(1)} %broadcast_select_fusion.21), channel_id=1, source_target_pairs={{0,1},{1,0},{2,3},{3,2},{4,5},{5,4},{6,7},{7,6},{8,9},{9,8},{10,11... | collective-permute-start | bytes 24584 | tf_op jit(solution)/shard_map/ppermute | solution.py:50
  2.2 1.0 copy-start.6
  5.1 1.0 copy-start
  5.1 21.4 %collective-permute-start.4 = (f32[3,4,1,256]{3,2,1,0:T(1,128)}, f32[3,4,1,256]{3,2,1,0:T(1,128)}, u32[]{:S(2)}, u32[]{:S(2)}) collective-permute-start(f32[3,4,1,256]{3,2,1,0:T(1,128)} %pad_maximum_fusion.53), channel_id=1, source_target_pairs={{0,1},{1,0},{2,3},{3,2},{4,5},{5,4},{6,7},{7,6},{8,9},{9,8},{10,11... | collective-permute-start | bytes 36872 | tf_op jit(solution)/shard_map/ppermute | solution.py:116
  6.2 0.6 copy-start.4
  7.1 11.4 %collective-permute-start.1 = (f32[4,1,64,256]{3,2,1,0:T(8,128)S(1)}, f32[4,1,64,256]{3,2,1,0:T(8,128)S(1)}, u32[]{:S(2)}, u32[]{:S(2)}) collective-permute-start(f32[4,1,64,256]{3,2,1,0:T(8,128)S(1)} %pad_maximum_fusion.39), channel_id=1, source_target_pairs={{2,0},{4,2},{6,4},{8,6},{10,8},{12,10},{14,12},{3,1},{5,3},{7,5},{... | collective-permute-start | bytes 786440 | tf_op jit(solution)/shard_map/ppermute | solution.py:133
  9.1 15.2 %collective-permute-start.2 = (f32[4,1,64,256]{3,2,1,0:T(8,128)}, f32[4,1,64,256]{3,2,1,0:T(8,128)S(1)}, u32[]{:S(2)}, u32[]{:S(2)}) collective-permute-start(f32[4,1,64,256]{3,2,1,0:T(8,128)} %pad_maximum_fusion.40), channel_id=1, source_target_pairs={{0,2},{2,4},{4,6},{6,8},{8,10},{10,12},{12,14},{1,3},{3,5},{5,7},{... | collective-permute-start | bytes 786440 | tf_op jit(solution)/shard_map/ppermute | solution.py:132
  25.1 1.3 %collective-permute-start.3 = (f32[2,10,1,256]{3,2,1,0:T(1,128)S(1)}, f32[2,10,1,256]{3,2,1,0:T(1,128)S(1)}, u32[]{:S(2)}, u32[]{:S(2)}) collective-permute-start(f32[2,10,1,256]{3,2,1,0:T(1,128)S(1)} %pad_maximum_fusion.51), channel_id=1, source_target_pairs={{0,1},{1,0},{2,3},{3,2},{4,5},{5,4},{6,7},{7,6},{8,9},{9,8},{10,11... | collective-permute-start | bytes 61448 | tf_op jit(solution)/shard_map/ppermute | solution.py:152
  26.4 0.8 copy-start.5
  28.3 10.9 %collective-permute-start.5 = (f32[4,1,64,256]{3,2,1,0:T(8,128)S(1)}, f32[4,1,64,256]{3,2,1,0:T(8,128)S(1)}, u32[]{:S(2)}, u32[]{:S(2)}) collective-permute-start(f32[4,1,64,256]{3,2,1,0:T(8,128)S(1)} %pad_maximum_fusion.41), channel_id=1, source_target_pairs={{2,0},{4,2},{6,4},{8,6},{10,8},{12,10},{14,12},{3,1},{5,3},{7,5},{... | collective-permute-start | bytes 786440 | tf_op jit(solution)/shard_map/ppermute | solution.py:133
  29.6 15.4 %collective-permute-start.6 = (f32[4,1,64,256]{3,2,1,0:T(8,128)S(1)}, f32[4,1,64,256]{3,2,1,0:T(8,128)S(1)}, u32[]{:S(2)}, u32[]{:S(2)}) collective-permute-start(f32[4,1,64,256]{3,2,1,0:T(8,128)S(1)} %pad_maximum_fusion.42), channel_id=1, source_target_pairs={{0,2},{2,4},{4,6},{6,8},{8,10},{10,12},{12,14},{1,3},{3,5},{5,7},{... | collective-permute-start | bytes 786440 | tf_op jit(solution)/shard_map/ppermute | solution.py:132
  45.7 1.2 %collective-permute-start.7 = (f32[2,4,1,256]{3,2,1,0:T(1,128)S(1)}, f32[2,4,1,256]{3,2,1,0:T(1,128)S(1)}, u32[]{:S(2)}, u32[]{:S(2)}) collective-permute-start(f32[2,4,1,256]{3,2,1,0:T(1,128)S(1)} %broadcast_select_fusion.17), channel_id=1, source_target_pairs={{0,1},{1,0},{2,3},{3,2},{4,5},{5,4},{6,7},{7,6},{8,9},{9,8},{10,11... | collective-permute-start | bytes 24584 | tf_op jit(solution)/shard_map/ppermute | solution.py:50
  47.7 1.2 %collective-permute-start.8 = (f32[2,4,1,256]{3,2,1,0:T(1,128)S(1)}, f32[2,4,1,256]{3,2,1,0:T(1,128)S(1)}, u32[]{:S(2)}, u32[]{:S(2)}) collective-permute-start(f32[2,4,1,256]{3,2,1,0:T(1,128)S(1)} %broadcast_select_fusion.15), channel_id=1, source_target_pairs={{0,1},{1,0},{2,3},{3,2},{4,5},{5,4},{6,7},{7,6},{8,9},{9,8},{10,11... | collective-permute-start | bytes 24584 | tf_op jit(solution)/shard_map/ppermute | solution.py:50
  49.3 15.9 %collective-permute-start.10 = (f32[4,1,64,256]{3,2,1,0:T(8,128)S(1)}, f32[4,1,64,256]{3,2,1,0:T(8,128)S(1)}, u32[]{:S(2)}, u32[]{:S(2)}) collective-permute-start(f32[4,1,64,256]{3,2,1,0:T(8,128)S(1)} %pad_maximum_fusion.44), channel_id=1, source_target_pairs={{0,2},{2,4},{4,6},{6,8},{8,10},{10,12},{12,14},{1,3},{3,5},{5,7},{... | collective-permute-start | bytes 786440 | tf_op jit(solution)/shard_map/ppermute | solution.py:132
  53.8 11.5 %collective-permute-start.9 = (f32[4,1,64,256]{3,2,1,0:T(8,128)S(1)}, f32[4,1,64,256]{3,2,1,0:T(8,128)S(1)}, u32[]{:S(2)}, u32[]{:S(2)}) collective-permute-start(f32[4,1,64,256]{3,2,1,0:T(8,128)S(1)} %pad_maximum_fusion.43), channel_id=1, source_target_pairs={{2,0},{4,2},{6,4},{8,6},{10,8},{12,10},{14,12},{3,1},{5,3},{7,5},{... | collective-permute-start | bytes 786440 | tf_op jit(solution)/shard_map/ppermute | solution.py:133
  66.2 1.3 %collective-permute-start.11 = (f32[2,10,1,256]{3,2,1,0:T(1,128)S(1)}, f32[2,10,1,256]{3,2,1,0:T(1,128)S(1)}, u32[]{:S(2)}, u32[]{:S(2)}) collective-permute-start(f32[2,10,1,256]{3,2,1,0:T(1,128)S(1)} %pad_maximum_fusion.52), channel_id=1, source_target_pairs={{0,1},{1,0},{2,3},{3,2},{4,5},{5,4},{6,7},{7,6},{8,9},{9,8},{10,11... | collective-permute-start | bytes 61448 | tf_op jit(solution)/shard_map/ppermute | solution.py:152
  66.3 1.4 %collective-permute-start.12 = (f32[3,4,1,256]{3,2,1,0:T(1,128)S(1)}, f32[3,4,1,256]{3,2,1,0:T(1,128)S(1)}, u32[]{:S(2)}, u32[]{:S(2)}) collective-permute-start(f32[3,4,1,256]{3,2,1,0:T(1,128)S(1)} %pad_maximum_fusion.54), channel_id=1, source_target_pairs={{0,1},{1,0},{2,3},{3,2},{4,5},{5,4},{6,7},{7,6},{8,9},{9,8},{10,11... | collective-permute-start | bytes 36872 | tf_op jit(solution)/shard_map/ppermute | solution.py:116
  68.9 11.2 %collective-permute-start.13 = (f32[4,1,64,256]{3,2,1,0:T(8,128)S(1)}, f32[4,1,64,256]{3,2,1,0:T(8,128)S(1)}, u32[]{:S(2)}, u32[]{:S(2)}) collective-permute-start(f32[4,1,64,256]{3,2,1,0:T(8,128)S(1)} %pad_maximum_fusion.45), channel_id=1, source_target_pairs={{2,0},{4,2},{6,4},{8,6},{10,8},{12,10},{14,12},{3,1},{5,3},{7,5},{... | collective-permute-start | bytes 786440 | tf_op jit(solution)/shard_map/ppermute | solution.py:133
  70.3 15.7 %collective-permute-start.14 = (f32[4,1,64,256]{3,2,1,0:T(8,128)S(1)}, f32[4,1,64,256]{3,2,1,0:T(8,128)S(1)}, u32[]{:S(2)}, u32[]{:S(2)}) collective-permute-start(f32[4,1,64,256]{3,2,1,0:T(8,128)S(1)} %pad_maximum_fusion.46), channel_id=1, source_target_pairs={{0,2},{2,4},{4,6},{6,8},{8,10},{10,12},{12,14},{1,3},{3,5},{5,7},{... | collective-permute-start | bytes 786440 | tf_op jit(solution)/shard_map/ppermute | solution.py:132
  86.8 1.2 %collective-permute-start.15 = (f32[2,4,1,256]{3,2,1,0:T(1,128)S(1)}, f32[2,4,1,256]{3,2,1,0:T(1,128)S(1)}, u32[]{:S(2)}, u32[]{:S(2)}) collective-permute-start(f32[2,4,1,256]{3,2,1,0:T(1,128)S(1)} %broadcast_select_fusion.11), channel_id=1, source_target_pairs={{0,1},{1,0},{2,3},{3,2},{4,5},{5,4},{6,7},{7,6},{8,9},{9,8},{10,11... | collective-permute-start | bytes 24584 | tf_op jit(solution)/shard_map/ppermute | solution.py:50
  88.6 1.1 copy-start.2
  89.7 0.9 copy-start.3
  89.7 0.6 copy-start.7
  90.6 1.5 %collective-permute-start.16 = (f32[]{:T(128)}, f32[]{:T(128)}, u32[]{:S(2)}, u32[]{:S(2)}) collective-permute-start(f32[]{:T(128)} %get-tuple-element.17), channel_id=1, source_target_pairs={{0,1},{1,0},{2,3},{3,2},{4,5},{5,4},{6,7},{7,6},{8,9},{9,8},{10,11... | collective-permute-start | bytes 20 | tf_op jit(solution)/shard_map/ppermute | solution.py:19
  94.0 5.1 %collective-permute-start.17 = (f32[65,256]{1,0:T(8,128)S(1)}, f32[65,256]{1,0:T(8,128)S(1)}, u32[]{:S(2)}, u32[]{:S(2)}) collective-permute-start(f32[65,256]{1,0:T(8,128)S(1)} %select_maximum_fusion), channel_id=1, source_target_pairs={{0,2},{2,0},{4,6},{6,4},{8,10},{10,8},{12,14},{14,12},{1,3},{3,1},... | collective-permute-start | bytes 199688 | tf_op jit(solution)/shard_map/ppermute | solution.py:28
  99.2 7.1 %collective-permute-start.20 = (f32[65,256]{1,0:T(8,128)S(1)}, f32[65,256]{1,0:T(8,128)S(1)}, u32[]{:S(2)}, u32[]{:S(2)}) collective-permute-start(f32[65,256]{1,0:T(8,128)S(1)} %fusion.286), channel_id=1, source_target_pairs={{0,12},{2,14},{4,8},{6,10},{8,4},{10,6},{12,0},{14,2},{1,13},{3,15... | collective-permute-start | bytes 199688 | tf_op jit(solution)/shard_map/ppermute | solution.py:33
  102.3 6.5 %collective-permute-start.19 = (f32[65,256]{1,0:T(8,128)S(1)}, f32[65,256]{1,0:T(8,128)S(1)}, u32[]{:S(2)}, u32[]{:S(2)}) collective-permute-start(f32[65,256]{1,0:T(8,128)S(1)} %fusion.286), channel_id=1, source_target_pairs={{0,8},{2,10},{4,12},{6,14},{8,0},{10,2},{12,4},{14,6},{1,9},{3,11}... | collective-permute-start | bytes 199688 | tf_op jit(solution)/shard_map/ppermute | solution.py:33
  102.3 6.5 %collective-permute-start.18 = (f32[65,256]{1,0:T(8,128)S(1)}, f32[65,256]{1,0:T(8,128)S(1)}, u32[]{:S(2)}, u32[]{:S(2)}) collective-permute-start(f32[65,256]{1,0:T(8,128)S(1)} %fusion.286), channel_id=1, source_target_pairs={{0,4},{2,6},{4,0},{6,2},{8,12},{10,14},{12,8},{14,10},{1,5},{3,7},... | collective-permute-start | bytes 199688 | tf_op jit(solution)/shard_map/ppermute | solution.py:33

commit v15 on v9

--- a/solution.py
+++ b/solution.py
@@ -206,7 +206,7 @@
     packed = gx_total(jnp.concatenate([rows_early, rows_late, extra], axis=0))
     squares = packed[-1, 0]
     half = rows_early.shape[0]
-    rows_sum = jnp.stack([packed[:half], packed[half:2 * half]])
+    rows_sum = packed[:2 * half].reshape(2, half, packed.shape[1])
     power = squares / float(total_x * total_y * depth)
     grad_rows = rows_sum / jnp.sqrt(float(total_x) * (power + 1e-06))
     return (chi_start, grad_rows, jnp.reshape(power, (1,)))

time: 109 us -> 109 us (level)
  no operation moved by 1% of the time
where the time goes in v15:
time: 109 us
  waiting for transfers between devices  54.4 us (50%)
  starting transfers between devices  34.1 us (31%)
  other arithmetic  12 us (11%)
  between operations  5.12 us (5%)
  local copies, waits for them, and re-layouts  3.26 us (3%)
    ppermute x4, waiting for transfers between devices, stage_pair(): lax.ppermute(jnp.concatenate([stage[:, X - 1:], part_top]), 'gx', up)  27.3 us
    ppermute x4, starting transfers between devices, stage_pair(): lax.ppermute(jnp.concatenate([stage[:, X - 1:], part_top]), 'gx', up)  20 us
    ppermute x4, waiting for transfers between devices, stage_pair(): lax.ppermute(jnp.concatenate([stage[:, :1], part_bottom]), 'gx', down)  13.9 us
    ppermute x4, starting transfers between devices, stage_pair(): lax.ppermute(jnp.concatenate([stage[:, :1], part_bottom]), 'gx', down)  5.17 us
    ppermute x3, waiting for transfers between devices, gx_total(): lax.ppermute(pair, 'gx', [(i, i ^ 2 * k) for i in range(count)])  5.13 us
    ppermute x3, starting transfers between devices, gx_total(): lax.ppermute(pair, 'gx', [(i, i ^ 2 * k) for i in range(count)])  4.45 us
    sub x14, other arithmetic, operator(): lapl = total - 6.0 * field  3.83 us
    ppermute x4, waiting for transfers between devices, y_extended(): other = lax.ppermute(strip, 'gy', [(0, 1), (1, 0)])  2.62 us
  transfers between devices with their start and end apart: 21, of which 16 were waited for; matrix products, arithmetic and copies ran while one was open for 5% of the time, Pallas kernels for 0%

profile of v15, /device:TPU:0, one launch (start us, length us, event | category | flops | bytes accessed | tf_op | source)
XLA Modules:
  0.0 108.9 jit_solution(8691234561736792800)
XLA Ops:
  0.6 0.9 constant_dynamic-slice_fusion.17
  1.6 0.6 collective-permute-start
  2.2 0.8 slice_bitcast_fusion.18
  3.1 1.3 %multiply_add_fusion.6 = (f32[4,64,256]{2,1,0:T(8,128)S(1)}, f32[4,64,256]{2,1,0:T(8,128)S(1)}, f32[4,64,256]{2,1,0:T(8,128)S(1)}, f32[4,64,256]{2,1,0:T(8,128)S(1)}) fusion(f32[4,64,256]{2,1,0:T(8,128)} %param.10, f32[2,4,64,256]{3,2,1,0:T(8,128)} %param.8, f32[64,256]{1,0:T(8,128)S(1)} %mul.964, f32[4]{0:T(128)S(1)} %multiply_add_fusion.7, ...), kind=kLoop, calls=%fused_computation.257 | loop fusion | flops 1114112 | bytes 2490384 | tf_op jit(solution)/shard_map/add | solution.py:65
  5.1 1.3 %collective-permute-start.1 = (f32[4,1,64,256]{3,2,1,0:T(8,128)S(1)}, f32[4,1,64,256]{3,2,1,0:T(8,128)S(1)}, u32[]{:S(2)}, u32[]{:S(2)}) collective-permute-start(f32[4,1,64,256]{3,2,1,0:T(8,128)S(1)} %pad_maximum_fusion.39), channel_id=1, source_target_pairs={{2,0},{4,2},{6,4},{8,6},{10,8},{12,10},{14,12},{3,1},{5,3},{7,5},{... | collective-permute-start | bytes 786440 | tf_op jit(solution)/shard_map/ppermute | solution.py:133
  6.5 5.5 %collective-permute-start.2 = (f32[4,1,64,256]{3,2,1,0:T(8,128)S(1)}, f32[4,1,64,256]{3,2,1,0:T(8,128)S(1)}, u32[]{:S(2)}, u32[]{:S(2)}) collective-permute-start(f32[4,1,64,256]{3,2,1,0:T(8,128)S(1)} %pad_maximum_fusion.40), channel_id=1, source_target_pairs={{0,2},{2,4},{4,6},{6,8},{8,10},{10,12},{12,14},{1,3},{3,5},{5,7},{... | collective-permute-start | bytes 786440 | tf_op jit(solution)/shard_map/ppermute | solution.py:132
  12.0 4.5 %collective-permute-done.1 = f32[4,1,64,256]{3,2,1,0:T(8,128)S(1)} collective-permute-done((f32[4,1,64,256]{3,2,1,0:T(8,128)S(1)}, f32[4,1,64,256]{3,2,1,0:T(8,128)S(1)}, u32[]{:S(2)}, u32[]{:S(2)}) %collective-permute-start.1) | collective-permute-done | bytes 262176 | tf_op jit(solution)/shard_map/ppermute | solution.py:133
  16.5 5.7 %collective-permute-done.2 = f32[4,1,64,256]{3,2,1,0:T(8,128)S(1)} collective-permute-done((f32[4,1,64,256]{3,2,1,0:T(8,128)S(1)}, f32[4,1,64,256]{3,2,1,0:T(8,128)S(1)}, u32[]{:S(2)}, u32[]{:S(2)}) %collective-permute-start.2) | collective-permute-done | bytes 262176 | tf_op jit(solution)/shard_map/ppermute | solution.py:132
  22.3 0.4 fusion.2
  23.1 1.2 %collective-permute-done.3 = f32[2,10,1,256]{3,2,1,0:T(1,128)S(1)} collective-permute-done((f32[2,10,1,256]{3,2,1,0:T(1,128)S(1)}, f32[2,10,1,256]{3,2,1,0:T(1,128)S(1)}, u32[]{:S(2)}, u32[]{:S(2)}) %collective-permute-start.3) | collective-permute-done | bytes 20512 | tf_op jit(solution)/shard_map/ppermute | solution.py:152
  24.5 0.3 fusion.5
  25.5 1.3 %collective-permute-start.5 = (f32[4,1,64,256]{3,2,1,0:T(8,128)S(1)}, f32[4,1,64,256]{3,2,1,0:T(8,128)S(1)}, u32[]{:S(2)}, u32[]{:S(2)}) collective-permute-start(f32[4,1,64,256]{3,2,1,0:T(8,128)S(1)} %pad_maximum_fusion.41), channel_id=1, source_target_pairs={{2,0},{4,2},{6,4},{8,6},{10,8},{12,10},{14,12},{3,1},{5,3},{7,5},{... | collective-permute-start | bytes 786440 | tf_op jit(solution)/shard_map/ppermute | solution.py:133
  26.8 5.0 %collective-permute-start.6 = (f32[4,1,64,256]{3,2,1,0:T(8,128)S(1)}, f32[4,1,64,256]{3,2,1,0:T(8,128)S(1)}, u32[]{:S(2)}, u32[]{:S(2)}) collective-permute-start(f32[4,1,64,256]{3,2,1,0:T(8,128)S(1)} %pad_maximum_fusion.42), channel_id=1, source_target_pairs={{0,2},{2,4},{4,6},{6,8},{8,10},{10,12},{12,14},{1,3},{3,5},{5,7},{... | collective-permute-start | bytes 786440 | tf_op jit(solution)/shard_map/ppermute | solution.py:132
  31.9 4.6 %collective-permute-done.5 = f32[4,1,64,256]{3,2,1,0:T(8,128)S(1)} collective-permute-done((f32[4,1,64,256]{3,2,1,0:T(8,128)S(1)}, f32[4,1,64,256]{3,2,1,0:T(8,128)S(1)}, u32[]{:S(2)}, u32[]{:S(2)}) %collective-permute-start.5) | collective-permute-done | bytes 262176 | tf_op jit(solution)/shard_map/ppermute | solution.py:133
  36.5 5.7 %collective-permute-done.6 = f32[4,1,64,256]{3,2,1,0:T(8,128)S(1)} collective-permute-done((f32[4,1,64,256]{3,2,1,0:T(8,128)S(1)}, f32[4,1,64,256]{3,2,1,0:T(8,128)S(1)}, u32[]{:S(2)}, u32[]{:S(2)}) %collective-permute-start.6) | collective-permute-done | bytes 262176 | tf_op jit(solution)/shard_map/ppermute | solution.py:132
  42.3 0.4 fusion.8
  43.1 1.1 %collective-permute-done.7 = f32[2,4,1,256]{3,2,1,0:T(1,128)S(1)} collective-permute-done((f32[2,4,1,256]{3,2,1,0:T(1,128)S(1)}, f32[2,4,1,256]{3,2,1,0:T(1,128)S(1)}, u32[]{:S(2)}, u32[]{:S(2)}) %collective-permute-start.7) | collective-permute-done | bytes 8224 | tf_op jit(solution)/shard_map/ppermute | solution.py:50
  44.2 0.3 fusion.11
  45.2 1.0 collective-permute-done.8
  46.6 4.4 %collective-permute-start.10 = (f32[4,1,64,256]{3,2,1,0:T(8,128)S(1)}, f32[4,1,64,256]{3,2,1,0:T(8,128)S(1)}, u32[]{:S(2)}, u32[]{:S(2)}) collective-permute-start(f32[4,1,64,256]{3,2,1,0:T(8,128)S(1)} %pad_maximum_fusion.44), channel_id=1, source_target_pairs={{0,2},{2,4},{4,6},{6,8},{8,10},{10,12},{12,14},{1,3},{3,5},{5,7},{... | collective-permute-start | bytes 786440 | tf_op jit(solution)/shard_map/ppermute | solution.py:132
  51.0 1.3 %collective-permute-start.9 = (f32[4,1,64,256]{3,2,1,0:T(8,128)S(1)}, f32[4,1,64,256]{3,2,1,0:T(8,128)S(1)}, u32[]{:S(2)}, u32[]{:S(2)}) collective-permute-start(f32[4,1,64,256]{3,2,1,0:T(8,128)S(1)} %pad_maximum_fusion.43), channel_id=1, source_target_pairs={{2,0},{4,2},{6,4},{8,6},{10,8},{12,10},{14,12},{3,1},{5,3},{7,5},{... | collective-permute-start | bytes 786440 | tf_op jit(solution)/shard_map/ppermute | solution.py:133
  52.3 10.1 %collective-permute-done.10 = f32[4,1,64,256]{3,2,1,0:T(8,128)S(1)} collective-permute-done((f32[4,1,64,256]{3,2,1,0:T(8,128)S(1)}, f32[4,1,64,256]{3,2,1,0:T(8,128)S(1)}, u32[]{:S(2)}, u32[]{:S(2)}) %collective-permute-start.10) | collective-permute-done | bytes 262176 | tf_op jit(solution)/shard_map/ppermute | solution.py:132
  62.5 0.3 fusion.14
  63.1 0.3 multiply_add_fusion.2
  63.5 0.6 collective-permute-start.12
  64.1 0.6 collective-permute-done.11
  65.0 0.3 fusion.17
  65.5 0.3 multiply_add_fusion.1
  66.2 1.3 %collective-permute-start.13 = (f32[4,1,64,256]{3,2,1,0:T(8,128)S(1)}, f32[4,1,64,256]{3,2,1,0:T(8,128)S(1)}, u32[]{:S(2)}, u32[]{:S(2)}) collective-permute-start(f32[4,1,64,256]{3,2,1,0:T(8,128)S(1)} %pad_maximum_fusion.45), channel_id=1, source_target_pairs={{2,0},{4,2},{6,4},{8,6},{10,8},{12,10},{14,12},{3,1},{5,3},{7,5},{... | collective-permute-start | bytes 786440 | tf_op jit(solution)/shard_map/ppermute | solution.py:133
  67.5 5.0 %collective-permute-start.14 = (f32[4,1,64,256]{3,2,1,0:T(8,128)S(1)}, f32[4,1,64,256]{3,2,1,0:T(8,128)S(1)}, u32[]{:S(2)}, u32[]{:S(2)}) collective-permute-start(f32[4,1,64,256]{3,2,1,0:T(8,128)S(1)} %pad_maximum_fusion.46), channel_id=1, source_target_pairs={{0,2},{2,4},{4,6},{6,8},{8,10},{10,12},{12,14},{1,3},{3,5},{5,7},{... | collective-permute-start | bytes 786440 | tf_op jit(solution)/shard_map/ppermute | solution.py:132
  72.6 4.8 %collective-permute-done.13 = f32[4,1,64,256]{3,2,1,0:T(8,128)S(1)} collective-permute-done((f32[4,1,64,256]{3,2,1,0:T(8,128)S(1)}, f32[4,1,64,256]{3,2,1,0:T(8,128)S(1)}, u32[]{:S(2)}, u32[]{:S(2)}) %collective-permute-start.13) | collective-permute-done | bytes 262176 | tf_op jit(solution)/shard_map/ppermute | solution.py:133
  77.4 5.7 %collective-permute-done.14 = f32[4,1,64,256]{3,2,1,0:T(8,128)S(1)} collective-permute-done((f32[4,1,64,256]{3,2,1,0:T(8,128)S(1)}, f32[4,1,64,256]{3,2,1,0:T(8,128)S(1)}, u32[]{:S(2)}, u32[]{:S(2)}) %collective-permute-start.14) | collective-permute-done | bytes 262176 | tf_op jit(solution)/shard_map/ppermute | solution.py:132
  83.2 0.4 fusion.20
  84.1 0.6 compare_reduce_fusion
  84.8 0.5 collective-permute-done.15
  85.3 0.3 fusion.23
  85.9 1.1 multiply_reduce_fusion
  87.2 0.5 copy-done.3
  88.2 1.1 collective-permute-done.16
  91.1 2.5 %collective-permute-start.17 = (f32[65,256]{1,0:T(8,128)S(1)}, f32[65,256]{1,0:T(8,128)S(1)}, u32[]{:S(2)}, u32[]{:S(2)}) collective-permute-start(f32[65,256]{1,0:T(8,128)S(1)} %select_maximum_fusion), channel_id=1, source_target_pairs={{0,2},{2,0},{4,6},{6,4},{8,10},{10,8},{12,14},{14,12},{1,3},{3,1},... | collective-permute-start | bytes 199688 | tf_op jit(solution)/shard_map/ppermute | solution.py:28
  93.6 2.6 %collective-permute-done.17 = f32[65,256]{1,0:T(8,128)S(1)} collective-permute-done((f32[65,256]{1,0:T(8,128)S(1)}, f32[65,256]{1,0:T(8,128)S(1)}, u32[]{:S(2)}, u32[]{:S(2)}) %collective-permute-start.17) | collective-permute-done | bytes 66592 | tf_op jit(solution)/shard_map/ppermute | solution.py:28
  96.3 2.7 %collective-permute-start.20 = (f32[65,256]{1,0:T(8,128)S(1)}, f32[65,256]{1,0:T(8,128)S(1)}, u32[]{:S(2)}, u32[]{:S(2)}) collective-permute-start(f32[65,256]{1,0:T(8,128)S(1)} %fusion.286), channel_id=1, source_target_pairs={{0,12},{2,14},{4,8},{6,10},{8,4},{10,6},{12,0},{14,2},{1,13},{3,15... | collective-permute-start | bytes 199688 | tf_op jit(solution)/shard_map/ppermute | solution.py:33
  98.9 0.4 collective-permute-start.19
  99.4 1.3 %collective-permute-start.18 = (f32[65,256]{1,0:T(8,128)S(1)}, f32[65,256]{1,0:T(8,128)S(1)}, u32[]{:S(2)}, u32[]{:S(2)}) collective-permute-start(f32[65,256]{1,0:T(8,128)S(1)} %fusion.286), channel_id=1, source_target_pairs={{0,4},{2,6},{4,0},{6,2},{8,12},{10,14},{12,8},{14,10},{1,5},{3,7},... | collective-permute-start | bytes 199688 | tf_op jit(solution)/shard_map/ppermute | solution.py:33
  100.7 2.6 %collective-permute-done.20 = f32[65,256]{1,0:T(8,128)S(1)} collective-permute-done((f32[65,256]{1,0:T(8,128)S(1)}, f32[65,256]{1,0:T(8,128)S(1)}, u32[]{:S(2)}, u32[]{:S(2)}) %collective-permute-start.20) | collective-permute-done | bytes 66592 | tf_op jit(solution)/shard_map/ppermute | solution.py:33
  103.3 2.5 %collective-permute-done.19 = f32[65,256]{1,0:T(8,128)S(1)} collective-permute-done((f32[65,256]{1,0:T(8,128)S(1)}, f32[65,256]{1,0:T(8,128)S(1)}, u32[]{:S(2)}, u32[]{:S(2)}) %collective-permute-start.19) | collective-permute-done | bytes 66592 | tf_op jit(solution)/shard_map/ppermute | solution.py:33
  105.9 0.5 slice.1276
  107.2 0.6 slice_divide_fusion
  (121 shorter events, 6.5 us)
Async XLA Ops:
  0.6 2.5 %copy-start.1 = (f32[2,4,64,256]{3,2,1,0:T(8,128)S(1)}, f32[2,4,64,256]{3,2,1,0:T(8,128)}, u32[]{:S(2)}) copy-start(f32[2,4,64,256]{3,2,1,0:T(8,128)} %param.9) | copy-start | bytes 1572868
  1.6 3.2 %collective-permute-start = (f32[2,4,1,256]{3,2,1,0:T(1,128)S(1)}, f32[2,4,1,256]{3,2,1,0:T(1,128)S(1)}, u32[]{:S(2)}, u32[]{:S(2)}) collective-permute-start(f32[2,4,1,256]{3,2,1,0:T(1,128)S(1)} %constant_dynamic-slice_fusion.17), channel_id=1, source_target_pairs={{0,1},{1,0},{2,3},{3,2},{4,5},{5,4},{6,7},{7,6},{8,9},{9,8},{10,11... | collective-permute-start | bytes 24584 | tf_op jit(solution)/shard_map/ppermute | solution.py:50
  3.1 1.5 %copy-start = (f32[2,4,64,256]{3,2,1,0:T(8,128)S(1)}, f32[2,4,64,256]{3,2,1,0:T(8,128)}, u32[]{:S(2)}) copy-start(f32[2,4,64,256]{3,2,1,0:T(8,128)} %param.7) | copy-start | bytes 1572868
  4.5 19.9 %collective-permute-start.4 = (f32[3,4,1,256]{3,2,1,0:T(1,128)S(1)}, f32[3,4,1,256]{3,2,1,0:T(1,128)S(1)}, u32[]{:S(2)}, u32[]{:S(2)}) collective-permute-start(f32[3,4,1,256]{3,2,1,0:T(1,128)S(1)} %pad_maximum_fusion.53), channel_id=1, source_target_pairs={{0,1},{1,0},{2,3},{3,2},{4,5},{5,4},{6,7},{7,6},{8,9},{9,8},{10,11... | collective-permute-start | bytes 36872 | tf_op jit(solution)/shard_map/ppermute | solution.py:116
  5.1 11.4 %collective-permute-start.1 = (f32[4,1,64,256]{3,2,1,0:T(8,128)S(1)}, f32[4,1,64,256]{3,2,1,0:T(8,128)S(1)}, u32[]{:S(2)}, u32[]{:S(2)}) collective-permute-start(f32[4,1,64,256]{3,2,1,0:T(8,128)S(1)} %pad_maximum_fusion.39), channel_id=1, source_target_pairs={{2,0},{4,2},{6,4},{8,6},{10,8},{12,10},{14,12},{3,1},{5,3},{7,5},{... | collective-permute-start | bytes 786440 | tf_op jit(solution)/shard_map/ppermute | solution.py:133
  6.5 15.8 %collective-permute-start.2 = (f32[4,1,64,256]{3,2,1,0:T(8,128)S(1)}, f32[4,1,64,256]{3,2,1,0:T(8,128)S(1)}, u32[]{:S(2)}, u32[]{:S(2)}) collective-permute-start(f32[4,1,64,256]{3,2,1,0:T(8,128)S(1)} %pad_maximum_fusion.40), channel_id=1, source_target_pairs={{0,2},{2,4},{4,6},{6,8},{8,10},{10,12},{12,14},{1,3},{3,5},{5,7},{... | collective-permute-start | bytes 786440 | tf_op jit(solution)/shard_map/ppermute | solution.py:132
  23.0 1.3 %collective-permute-start.3 = (f32[2,10,1,256]{3,2,1,0:T(1,128)S(1)}, f32[2,10,1,256]{3,2,1,0:T(1,128)S(1)}, u32[]{:S(2)}, u32[]{:S(2)}) collective-permute-start(f32[2,10,1,256]{3,2,1,0:T(1,128)S(1)} %pad_maximum_fusion.51), channel_id=1, source_target_pairs={{0,1},{1,0},{2,3},{3,2},{4,5},{5,4},{6,7},{7,6},{8,9},{9,8},{10,11... | collective-permute-start | bytes 61448 | tf_op jit(solution)/shard_map/ppermute | solution.py:152
  25.5 11.0 %collective-permute-start.5 = (f32[4,1,64,256]{3,2,1,0:T(8,128)S(1)}, f32[4,1,64,256]{3,2,1,0:T(8,128)S(1)}, u32[]{:S(2)}, u32[]{:S(2)}) collective-permute-start(f32[4,1,64,256]{3,2,1,0:T(8,128)S(1)} %pad_maximum_fusion.41), channel_id=1, source_target_pairs={{2,0},{4,2},{6,4},{8,6},{10,8},{12,10},{14,12},{3,1},{5,3},{7,5},{... | collective-permute-start | bytes 786440 | tf_op jit(solution)/shard_map/ppermute | solution.py:133
  26.8 15.5 %collective-permute-start.6 = (f32[4,1,64,256]{3,2,1,0:T(8,128)S(1)}, f32[4,1,64,256]{3,2,1,0:T(8,128)S(1)}, u32[]{:S(2)}, u32[]{:S(2)}) collective-permute-start(f32[4,1,64,256]{3,2,1,0:T(8,128)S(1)} %pad_maximum_fusion.42), channel_id=1, source_target_pairs={{0,2},{2,4},{4,6},{6,8},{8,10},{10,12},{12,14},{1,3},{3,5},{5,7},{... | collective-permute-start | bytes 786440 | tf_op jit(solution)/shard_map/ppermute | solution.py:132
  43.0 1.2 %collective-permute-start.7 = (f32[2,4,1,256]{3,2,1,0:T(1,128)S(1)}, f32[2,4,1,256]{3,2,1,0:T(1,128)S(1)}, u32[]{:S(2)}, u32[]{:S(2)}) collective-permute-start(f32[2,4,1,256]{3,2,1,0:T(1,128)S(1)} %constant_dynamic-slice_fusion.9), channel_id=1, source_target_pairs={{0,1},{1,0},{2,3},{3,2},{4,5},{5,4},{6,7},{7,6},{8,9},{9,8},{10,11... | collective-permute-start | bytes 24584 | tf_op jit(solution)/shard_map/ppermute | solution.py:50
  45.0 1.2 %collective-permute-start.8 = (f32[2,4,1,256]{3,2,1,0:T(1,128)S(1)}, f32[2,4,1,256]{3,2,1,0:T(1,128)S(1)}, u32[]{:S(2)}, u32[]{:S(2)}) collective-permute-start(f32[2,4,1,256]{3,2,1,0:T(1,128)S(1)} %constant_dynamic-slice_fusion.8), channel_id=1, source_target_pairs={{0,1},{1,0},{2,3},{3,2},{4,5},{5,4},{6,7},{7,6},{8,9},{9,8},{10,11... | collective-permute-start | bytes 24584 | tf_op jit(solution)/shard_map/ppermute | solution.py:50
  46.6 15.9 %collective-permute-start.10 = (f32[4,1,64,256]{3,2,1,0:T(8,128)S(1)}, f32[4,1,64,256]{3,2,1,0:T(8,128)S(1)}, u32[]{:S(2)}, u32[]{:S(2)}) collective-permute-start(f32[4,1,64,256]{3,2,1,0:T(8,128)S(1)} %pad_maximum_fusion.44), channel_id=1, source_target_pairs={{0,2},{2,4},{4,6},{6,8},{8,10},{10,12},{12,14},{1,3},{3,5},{5,7},{... | collective-permute-start | bytes 786440 | tf_op jit(solution)/shard_map/ppermute | solution.py:132
  51.0 11.5 %collective-permute-start.9 = (f32[4,1,64,256]{3,2,1,0:T(8,128)S(1)}, f32[4,1,64,256]{3,2,1,0:T(8,128)S(1)}, u32[]{:S(2)}, u32[]{:S(2)}) collective-permute-start(f32[4,1,64,256]{3,2,1,0:T(8,128)S(1)} %pad_maximum_fusion.43), channel_id=1, source_target_pairs={{2,0},{4,2},{6,4},{8,6},{10,8},{12,10},{14,12},{3,1},{5,3},{7,5},{... | collective-permute-start | bytes 786440 | tf_op jit(solution)/shard_map/ppermute | solution.py:133
  63.4 1.3 %collective-permute-start.11 = (f32[2,10,1,256]{3,2,1,0:T(1,128)S(1)}, f32[2,10,1,256]{3,2,1,0:T(1,128)S(1)}, u32[]{:S(2)}, u32[]{:S(2)}) collective-permute-start(f32[2,10,1,256]{3,2,1,0:T(1,128)S(1)} %pad_maximum_fusion.52), channel_id=1, source_target_pairs={{0,1},{1,0},{2,3},{3,2},{4,5},{5,4},{6,7},{7,6},{8,9},{9,8},{10,11... | collective-permute-start | bytes 61448 | tf_op jit(solution)/shard_map/ppermute | solution.py:152
  63.5 1.4 %collective-permute-start.12 = (f32[3,4,1,256]{3,2,1,0:T(1,128)S(1)}, f32[3,4,1,256]{3,2,1,0:T(1,128)S(1)}, u32[]{:S(2)}, u32[]{:S(2)}) collective-permute-start(f32[3,4,1,256]{3,2,1,0:T(1,128)S(1)} %pad_maximum_fusion.54), channel_id=1, source_target_pairs={{0,1},{1,0},{2,3},{3,2},{4,5},{5,4},{6,7},{7,6},{8,9},{9,8},{10,11... | collective-permute-start | bytes 36872 | tf_op jit(solution)/shard_map/ppermute | solution.py:116
  66.2 11.2 %collective-permute-start.13 = (f32[4,1,64,256]{3,2,1,0:T(8,128)S(1)}, f32[4,1,64,256]{3,2,1,0:T(8,128)S(1)}, u32[]{:S(2)}, u32[]{:S(2)}) collective-permute-start(f32[4,1,64,256]{3,2,1,0:T(8,128)S(1)} %pad_maximum_fusion.45), channel_id=1, source_target_pairs={{2,0},{4,2},{6,4},{8,6},{10,8},{12,10},{14,12},{3,1},{5,3},{7,5},{... | collective-permute-start | bytes 786440 | tf_op jit(solution)/shard_map/ppermute | solution.py:133
  67.5 15.7 %collective-permute-start.14 = (f32[4,1,64,256]{3,2,1,0:T(8,128)S(1)}, f32[4,1,64,256]{3,2,1,0:T(8,128)S(1)}, u32[]{:S(2)}, u32[]{:S(2)}) collective-permute-start(f32[4,1,64,256]{3,2,1,0:T(8,128)S(1)} %pad_maximum_fusion.46), channel_id=1, source_target_pairs={{0,2},{2,4},{4,6},{6,8},{8,10},{10,12},{12,14},{1,3},{3,5},{5,7},{... | collective-permute-start | bytes 786440 | tf_op jit(solution)/shard_map/ppermute | solution.py:132
  84.0 1.2 %collective-permute-start.15 = (f32[2,4,1,256]{3,2,1,0:T(1,128)S(1)}, f32[2,4,1,256]{3,2,1,0:T(1,128)S(1)}, u32[]{:S(2)}, u32[]{:S(2)}) collective-permute-start(f32[2,4,1,256]{3,2,1,0:T(1,128)S(1)} %constant_dynamic-slice_fusion), channel_id=1, source_target_pairs={{0,1},{1,0},{2,3},{3,2},{4,5},{5,4},{6,7},{7,6},{8,9},{9,8},{10,11... | collective-permute-start | bytes 24584 | tf_op jit(solution)/shard_map/ppermute | solution.py:50
  85.8 1.1 copy-start.2
  86.9 0.8 copy-start.3
  87.8 1.5 %collective-permute-start.16 = (f32[]{:T(128)}, f32[]{:T(128)}, u32[]{:S(2)}, u32[]{:S(2)}) collective-permute-start(f32[]{:T(128)} %get-tuple-element.17), channel_id=1, source_target_pairs={{0,1},{1,0},{2,3},{3,2},{4,5},{5,4},{6,7},{7,6},{8,9},{9,8},{10,11... | collective-permute-start | bytes 20 | tf_op jit(solution)/shard_map/ppermute | solution.py:19
  91.1 5.1 %collective-permute-start.17 = (f32[65,256]{1,0:T(8,128)S(1)}, f32[65,256]{1,0:T(8,128)S(1)}, u32[]{:S(2)}, u32[]{:S(2)}) collective-permute-start(f32[65,256]{1,0:T(8,128)S(1)} %select_maximum_fusion), channel_id=1, source_target_pairs={{0,2},{2,0},{4,6},{6,4},{8,10},{10,8},{12,14},{14,12},{1,3},{3,1},... | collective-permute-start | bytes 199688 | tf_op jit(solution)/shard_map/ppermute | solution.py:28
  96.3 7.1 %collective-permute-start.20 = (f32[65,256]{1,0:T(8,128)S(1)}, f32[65,256]{1,0:T(8,128)S(1)}, u32[]{:S(2)}, u32[]{:S(2)}) collective-permute-start(f32[65,256]{1,0:T(8,128)S(1)} %fusion.286), channel_id=1, source_target_pairs={{0,12},{2,14},{4,8},{6,10},{8,4},{10,6},{12,0},{14,2},{1,13},{3,15... | collective-permute-start | bytes 199688 | tf_op jit(solution)/shard_map/ppermute | solution.py:33
  98.9 6.9 %collective-permute-start.19 = (f32[65,256]{1,0:T(8,128)S(1)}, f32[65,256]{1,0:T(8,128)S(1)}, u32[]{:S(2)}, u32[]{:S(2)}) collective-permute-start(f32[65,256]{1,0:T(8,128)S(1)} %fusion.286), channel_id=1, source_target_pairs={{0,8},{2,10},{4,12},{6,14},{8,0},{10,2},{12,4},{14,6},{1,9},{3,11}... | collective-permute-start | bytes 199688 | tf_op jit(solution)/shard_map/ppermute | solution.py:33
  99.4 6.5 %collective-permute-start.18 = (f32[65,256]{1,0:T(8,128)S(1)}, f32[65,256]{1,0:T(8,128)S(1)}, u32[]{:S(2)}, u32[]{:S(2)}) collective-permute-start(f32[65,256]{1,0:T(8,128)S(1)} %fusion.286), channel_id=1, source_target_pairs={{0,4},{2,6},{4,0},{6,2},{8,12},{10,14},{12,8},{14,10},{1,5},{3,7},... | collective-permute-start | bytes 199688 | tf_op jit(solution)/shard_map/ppermute | solution.py:33

commit v16 on v15

--- a/solution.py
+++ b/solution.py
@@ -204,11 +204,11 @@
     local_sq = axis_sum(jnp.sum(chi_start * chi_start), "gy")
     extra = jnp.zeros((1, rows_early.shape[1]), jnp.float32).at[0, 0].set(local_sq)
     packed = gx_total(jnp.concatenate([rows_early, rows_late, extra], axis=0))
-    squares = packed[-1, 0]
     half = rows_early.shape[0]
     rows_sum = packed[:2 * half].reshape(2, half, packed.shape[1])
-    power = squares / float(total_x * total_y * depth)
-    grad_rows = rows_sum / jnp.sqrt(float(total_x) * (power + 1e-06))
+    power = packed[-1, 0] / float(total_x * total_y * depth)
+    scale = jnp.sum(packed[-1]) / float(total_x * total_y * depth)
+    grad_rows = rows_sum / jnp.sqrt(float(total_x) * (scale + 1e-06))
     return (chi_start, grad_rows, jnp.reshape(power, (1,)))
 
 

time: 109 us -> 111 us (1.018)
  no operation moved by 1% of the time
where the time goes in v16:
time: 111 us; the launch traced here: 110 us
  waiting for transfers between devices  54.4 us (49%)
  starting transfers between devices  34.1 us (31%)
  other arithmetic  12.6 us (11%)
  between operations  5.76 us (5%)
  local copies, waits for them, and re-layouts  3.26 us (3%)
    ppermute x4, waiting for transfers between devices, stage_pair(): lax.ppermute(jnp.concatenate([stage[:, X - 1:], part_top]), 'gx', up)  27.3 us
    ppermute x4, starting transfers between devices, stage_pair(): lax.ppermute(jnp.concatenate([stage[:, X - 1:], part_top]), 'gx', up)  20 us
    ppermute x4, waiting for transfers between devices, stage_pair(): lax.ppermute(jnp.concatenate([stage[:, :1], part_bottom]), 'gx', down)  13.9 us
    ppermute x4, starting transfers between devices, stage_pair(): lax.ppermute(jnp.concatenate([stage[:, :1], part_bottom]), 'gx', down)  5.17 us
    ppermute x3, waiting for transfers between devices, gx_total(): lax.ppermute(pair, 'gx', [(i, i ^ 2 * k) for i in range(count)])  5.13 us
    ppermute x3, starting transfers between devices, gx_total(): lax.ppermute(pair, 'gx', [(i, i ^ 2 * k) for i in range(count)])  4.45 us
    sub x14, other arithmetic, operator(): lapl = total - 6.0 * field  3.83 us
    ppermute x4, waiting for transfers between devices, y_extended(): other = lax.ppermute(strip, 'gy', [(0, 1), (1, 0)])  2.62 us
  transfers between devices with their start and end apart: 21, of which 16 were waited for; matrix products, arithmetic and copies ran while one was open for 5% of the time, Pallas kernels for 0%

profile of v16, /device:TPU:0, one launch (start us, length us, event | category | flops | bytes accessed | tf_op | source)
XLA Modules:
  0.0 110.2 jit_solution(7703500194669156156)
XLA Ops:
  0.6 0.9 constant_dynamic-slice_fusion.17
  1.6 0.6 collective-permute-start
  2.2 0.8 slice_bitcast_fusion.18
  3.1 1.3 %multiply_add_fusion.6 = (f32[4,64,256]{2,1,0:T(8,128)S(1)}, f32[4,64,256]{2,1,0:T(8,128)S(1)}, f32[4,64,256]{2,1,0:T(8,128)S(1)}, f32[4,64,256]{2,1,0:T(8,128)S(1)}) fusion(f32[4,64,256]{2,1,0:T(8,128)} %param.10, f32[2,4,64,256]{3,2,1,0:T(8,128)} %param.8, f32[64,256]{1,0:T(8,128)S(1)} %mul.963, f32[4]{0:T(128)S(1)} %multiply_add_fusion.7, ...), kind=kLoop, calls=%fused_computation.257 | loop fusion | flops 1114112 | bytes 2490384 | tf_op jit(solution)/shard_map/add | solution.py:65
  5.1 1.3 %collective-permute-start.1 = (f32[4,1,64,256]{3,2,1,0:T(8,128)S(1)}, f32[4,1,64,256]{3,2,1,0:T(8,128)S(1)}, u32[]{:S(2)}, u32[]{:S(2)}) collective-permute-start(f32[4,1,64,256]{3,2,1,0:T(8,128)S(1)} %pad_maximum_fusion.39), channel_id=1, source_target_pairs={{2,0},{4,2},{6,4},{8,6},{10,8},{12,10},{14,12},{3,1},{5,3},{7,5},{... | collective-permute-start | bytes 786440 | tf_op jit(solution)/shard_map/ppermute | solution.py:133
  6.5 5.5 %collective-permute-start.2 = (f32[4,1,64,256]{3,2,1,0:T(8,128)S(1)}, f32[4,1,64,256]{3,2,1,0:T(8,128)S(1)}, u32[]{:S(2)}, u32[]{:S(2)}) collective-permute-start(f32[4,1,64,256]{3,2,1,0:T(8,128)S(1)} %pad_maximum_fusion.40), channel_id=1, source_target_pairs={{0,2},{2,4},{4,6},{6,8},{8,10},{10,12},{12,14},{1,3},{3,5},{5,7},{... | collective-permute-start | bytes 786440 | tf_op jit(solution)/shard_map/ppermute | solution.py:132
  12.0 4.5 %collective-permute-done.1 = f32[4,1,64,256]{3,2,1,0:T(8,128)S(1)} collective-permute-done((f32[4,1,64,256]{3,2,1,0:T(8,128)S(1)}, f32[4,1,64,256]{3,2,1,0:T(8,128)S(1)}, u32[]{:S(2)}, u32[]{:S(2)}) %collective-permute-start.1) | collective-permute-done | bytes 262176 | tf_op jit(solution)/shard_map/ppermute | solution.py:133
  16.5 5.7 %collective-permute-done.2 = f32[4,1,64,256]{3,2,1,0:T(8,128)S(1)} collective-permute-done((f32[4,1,64,256]{3,2,1,0:T(8,128)S(1)}, f32[4,1,64,256]{3,2,1,0:T(8,128)S(1)}, u32[]{:S(2)}, u32[]{:S(2)}) %collective-permute-start.2) | collective-permute-done | bytes 262176 | tf_op jit(solution)/shard_map/ppermute | solution.py:132
  22.3 0.4 fusion.2
  23.1 1.2 %collective-permute-done.3 = f32[2,10,1,256]{3,2,1,0:T(1,128)S(1)} collective-permute-done((f32[2,10,1,256]{3,2,1,0:T(1,128)S(1)}, f32[2,10,1,256]{3,2,1,0:T(1,128)S(1)}, u32[]{:S(2)}, u32[]{:S(2)}) %collective-permute-start.3) | collective-permute-done | bytes 20512 | tf_op jit(solution)/shard_map/ppermute | solution.py:152
  24.5 0.3 fusion.5
  25.5 1.3 %collective-permute-start.5 = (f32[4,1,64,256]{3,2,1,0:T(8,128)S(1)}, f32[4,1,64,256]{3,2,1,0:T(8,128)S(1)}, u32[]{:S(2)}, u32[]{:S(2)}) collective-permute-start(f32[4,1,64,256]{3,2,1,0:T(8,128)S(1)} %pad_maximum_fusion.41), channel_id=1, source_target_pairs={{2,0},{4,2},{6,4},{8,6},{10,8},{12,10},{14,12},{3,1},{5,3},{7,5},{... | collective-permute-start | bytes 786440 | tf_op jit(solution)/shard_map/ppermute | solution.py:133
  26.8 5.0 %collective-permute-start.6 = (f32[4,1,64,256]{3,2,1,0:T(8,128)S(1)}, f32[4,1,64,256]{3,2,1,0:T(8,128)S(1)}, u32[]{:S(2)}, u32[]{:S(2)}) collective-permute-start(f32[4,1,64,256]{3,2,1,0:T(8,128)S(1)} %pad_maximum_fusion.42), channel_id=1, source_target_pairs={{0,2},{2,4},{4,6},{6,8},{8,10},{10,12},{12,14},{1,3},{3,5},{5,7},{... | collective-permute-start | bytes 786440 | tf_op jit(solution)/shard_map/ppermute | solution.py:132
  31.9 4.6 %collective-permute-done.5 = f32[4,1,64,256]{3,2,1,0:T(8,128)S(1)} collective-permute-done((f32[4,1,64,256]{3,2,1,0:T(8,128)S(1)}, f32[4,1,64,256]{3,2,1,0:T(8,128)S(1)}, u32[]{:S(2)}, u32[]{:S(2)}) %collective-permute-start.5) | collective-permute-done | bytes 262176 | tf_op jit(solution)/shard_map/ppermute | solution.py:133
  36.5 5.7 %collective-permute-done.6 = f32[4,1,64,256]{3,2,1,0:T(8,128)S(1)} collective-permute-done((f32[4,1,64,256]{3,2,1,0:T(8,128)S(1)}, f32[4,1,64,256]{3,2,1,0:T(8,128)S(1)}, u32[]{:S(2)}, u32[]{:S(2)}) %collective-permute-start.6) | collective-permute-done | bytes 262176 | tf_op jit(solution)/shard_map/ppermute | solution.py:132
  42.3 0.4 fusion.8
  43.1 1.1 %collective-permute-done.7 = f32[2,4,1,256]{3,2,1,0:T(1,128)S(1)} collective-permute-done((f32[2,4,1,256]{3,2,1,0:T(1,128)S(1)}, f32[2,4,1,256]{3,2,1,0:T(1,128)S(1)}, u32[]{:S(2)}, u32[]{:S(2)}) %collective-permute-start.7) | collective-permute-done | bytes 8224 | tf_op jit(solution)/shard_map/ppermute | solution.py:50
  44.2 0.3 fusion.11
  45.2 1.0 collective-permute-done.8
  46.6 4.4 %collective-permute-start.10 = (f32[4,1,64,256]{3,2,1,0:T(8,128)S(1)}, f32[4,1,64,256]{3,2,1,0:T(8,128)S(1)}, u32[]{:S(2)}, u32[]{:S(2)}) collective-permute-start(f32[4,1,64,256]{3,2,1,0:T(8,128)S(1)} %pad_maximum_fusion.44), channel_id=1, source_target_pairs={{0,2},{2,4},{4,6},{6,8},{8,10},{10,12},{12,14},{1,3},{3,5},{5,7},{... | collective-permute-start | bytes 786440 | tf_op jit(solution)/shard_map/ppermute | solution.py:132
  51.0 1.3 %collective-permute-start.9 = (f32[4,1,64,256]{3,2,1,0:T(8,128)S(1)}, f32[4,1,64,256]{3,2,1,0:T(8,128)S(1)}, u32[]{:S(2)}, u32[]{:S(2)}) collective-permute-start(f32[4,1,64,256]{3,2,1,0:T(8,128)S(1)} %pad_maximum_fusion.43), channel_id=1, source_target_pairs={{2,0},{4,2},{6,4},{8,6},{10,8},{12,10},{14,12},{3,1},{5,3},{7,5},{... | collective-permute-start | bytes 786440 | tf_op jit(solution)/shard_map/ppermute | solution.py:133
  52.3 10.1 %collective-permute-done.10 = f32[4,1,64,256]{3,2,1,0:T(8,128)S(1)} collective-permute-done((f32[4,1,64,256]{3,2,1,0:T(8,128)S(1)}, f32[4,1,64,256]{3,2,1,0:T(8,128)S(1)}, u32[]{:S(2)}, u32[]{:S(2)}) %collective-permute-start.10) | collective-permute-done | bytes 262176 | tf_op jit(solution)/shard_map/ppermute | solution.py:132
  62.5 0.3 fusion.14
  63.1 0.3 multiply_add_fusion.2
  63.5 0.6 collective-permute-start.12
  64.1 0.6 collective-permute-done.11
  65.0 0.3 fusion.17
  66.2 1.3 %collective-permute-start.13 = (f32[4,1,64,256]{3,2,1,0:T(8,128)S(1)}, f32[4,1,64,256]{3,2,1,0:T(8,128)S(1)}, u32[]{:S(2)}, u32[]{:S(2)}) collective-permute-start(f32[4,1,64,256]{3,2,1,0:T(8,128)S(1)} %pad_maximum_fusion.45), channel_id=1, source_target_pairs={{2,0},{4,2},{6,4},{8,6},{10,8},{12,10},{14,12},{3,1},{5,3},{7,5},{... | collective-permute-start | bytes 786440 | tf_op jit(solution)/shard_map/ppermute | solution.py:133
  67.5 5.0 %collective-permute-start.14 = (f32[4,1,64,256]{3,2,1,0:T(8,128)S(1)}, f32[4,1,64,256]{3,2,1,0:T(8,128)S(1)}, u32[]{:S(2)}, u32[]{:S(2)}) collective-permute-start(f32[4,1,64,256]{3,2,1,0:T(8,128)S(1)} %pad_maximum_fusion.46), channel_id=1, source_target_pairs={{0,2},{2,4},{4,6},{6,8},{8,10},{10,12},{12,14},{1,3},{3,5},{5,7},{... | collective-permute-start | bytes 786440 | tf_op jit(solution)/shard_map/ppermute | solution.py:132
  72.6 4.8 %collective-permute-done.13 = f32[4,1,64,256]{3,2,1,0:T(8,128)S(1)} collective-permute-done((f32[4,1,64,256]{3,2,1,0:T(8,128)S(1)}, f32[4,1,64,256]{3,2,1,0:T(8,128)S(1)}, u32[]{:S(2)}, u32[]{:S(2)}) %collective-permute-start.13) | collective-permute-done | bytes 262176 | tf_op jit(solution)/shard_map/ppermute | solution.py:133
  77.4 5.7 %collective-permute-done.14 = f32[4,1,64,256]{3,2,1,0:T(8,128)S(1)} collective-permute-done((f32[4,1,64,256]{3,2,1,0:T(8,128)S(1)}, f32[4,1,64,256]{3,2,1,0:T(8,128)S(1)}, u32[]{:S(2)}, u32[]{:S(2)}) %collective-permute-start.14) | collective-permute-done | bytes 262176 | tf_op jit(solution)/shard_map/ppermute | solution.py:132
  83.2 0.4 fusion.20
  84.1 0.6 compare_reduce_fusion
  84.8 0.5 collective-permute-done.15
  85.3 0.3 fusion.23
  85.9 1.1 multiply_reduce_fusion
  87.2 0.5 copy-done.3
  88.2 1.1 collective-permute-done.16
  91.1 2.5 %collective-permute-start.17 = (f32[65,256]{1,0:T(8,128)S(1)}, f32[65,256]{1,0:T(8,128)S(1)}, u32[]{:S(2)}, u32[]{:S(2)}) collective-permute-start(f32[65,256]{1,0:T(8,128)S(1)} %select_maximum_fusion), channel_id=1, source_target_pairs={{0,2},{2,0},{4,6},{6,4},{8,10},{10,8},{12,14},{14,12},{1,3},{3,1},... | collective-permute-start | bytes 199688 | tf_op jit(solution)/shard_map/ppermute | solution.py:28
  93.6 2.6 %collective-permute-done.17 = f32[65,256]{1,0:T(8,128)S(1)} collective-permute-done((f32[65,256]{1,0:T(8,128)S(1)}, f32[65,256]{1,0:T(8,128)S(1)}, u32[]{:S(2)}, u32[]{:S(2)}) %collective-permute-start.17) | collective-permute-done | bytes 66592 | tf_op jit(solution)/shard_map/ppermute | solution.py:28
  96.3 2.7 %collective-permute-start.20 = (f32[65,256]{1,0:T(8,128)S(1)}, f32[65,256]{1,0:T(8,128)S(1)}, u32[]{:S(2)}, u32[]{:S(2)}) collective-permute-start(f32[65,256]{1,0:T(8,128)S(1)} %fusion.286), channel_id=1, source_target_pairs={{0,12},{2,14},{4,8},{6,10},{8,4},{10,6},{12,0},{14,2},{1,13},{3,15... | collective-permute-start | bytes 199688 | tf_op jit(solution)/shard_map/ppermute | solution.py:33
  98.9 0.4 collective-permute-start.19
  99.4 1.3 %collective-permute-start.18 = (f32[65,256]{1,0:T(8,128)S(1)}, f32[65,256]{1,0:T(8,128)S(1)}, u32[]{:S(2)}, u32[]{:S(2)}) collective-permute-start(f32[65,256]{1,0:T(8,128)S(1)} %fusion.286), channel_id=1, source_target_pairs={{0,4},{2,6},{4,0},{6,2},{8,12},{10,14},{12,8},{14,10},{1,5},{3,7},... | collective-permute-start | bytes 199688 | tf_op jit(solution)/shard_map/ppermute | solution.py:33
  100.7 2.6 %collective-permute-done.20 = f32[65,256]{1,0:T(8,128)S(1)} collective-permute-done((f32[65,256]{1,0:T(8,128)S(1)}, f32[65,256]{1,0:T(8,128)S(1)}, u32[]{:S(2)}, u32[]{:S(2)}) %collective-permute-start.20) | collective-permute-done | bytes 66592 | tf_op jit(solution)/shard_map/ppermute | solution.py:33
  103.3 2.5 %collective-permute-done.19 = f32[65,256]{1,0:T(8,128)S(1)} collective-permute-done((f32[65,256]{1,0:T(8,128)S(1)}, f32[65,256]{1,0:T(8,128)S(1)}, u32[]{:S(2)}, u32[]{:S(2)}) %collective-permute-start.19) | collective-permute-done | bytes 66592 | tf_op jit(solution)/shard_map/ppermute | solution.py:33
  105.9 0.6 slice_reduce_fusion
  107.2 0.5 slice.1282
  107.8 0.6 slice_divide_fusion
  (122 shorter events, 6.8 us)
Async XLA Ops:
  0.6 2.5 %copy-start.1 = (f32[2,4,64,256]{3,2,1,0:T(8,128)S(1)}, f32[2,4,64,256]{3,2,1,0:T(8,128)}, u32[]{:S(2)}) copy-start(f32[2,4,64,256]{3,2,1,0:T(8,128)} %param.9) | copy-start | bytes 1572868
  1.6 3.2 %collective-permute-start = (f32[2,4,1,256]{3,2,1,0:T(1,128)S(1)}, f32[2,4,1,256]{3,2,1,0:T(1,128)S(1)}, u32[]{:S(2)}, u32[]{:S(2)}) collective-permute-start(f32[2,4,1,256]{3,2,1,0:T(1,128)S(1)} %constant_dynamic-slice_fusion.17), channel_id=1, source_target_pairs={{0,1},{1,0},{2,3},{3,2},{4,5},{5,4},{6,7},{7,6},{8,9},{9,8},{10,11... | collective-permute-start | bytes 24584 | tf_op jit(solution)/shard_map/ppermute | solution.py:50
  3.1 1.5 %copy-start = (f32[2,4,64,256]{3,2,1,0:T(8,128)S(1)}, f32[2,4,64,256]{3,2,1,0:T(8,128)}, u32[]{:S(2)}) copy-start(f32[2,4,64,256]{3,2,1,0:T(8,128)} %param.7) | copy-start | bytes 1572868
  4.5 19.9 %collective-permute-start.4 = (f32[3,4,1,256]{3,2,1,0:T(1,128)S(1)}, f32[3,4,1,256]{3,2,1,0:T(1,128)S(1)}, u32[]{:S(2)}, u32[]{:S(2)}) collective-permute-start(f32[3,4,1,256]{3,2,1,0:T(1,128)S(1)} %pad_maximum_fusion.53), channel_id=1, source_target_pairs={{0,1},{1,0},{2,3},{3,2},{4,5},{5,4},{6,7},{7,6},{8,9},{9,8},{10,11... | collective-permute-start | bytes 36872 | tf_op jit(solution)/shard_map/ppermute | solution.py:116
  5.1 11.4 %collective-permute-start.1 = (f32[4,1,64,256]{3,2,1,0:T(8,128)S(1)}, f32[4,1,64,256]{3,2,1,0:T(8,128)S(1)}, u32[]{:S(2)}, u32[]{:S(2)}) collective-permute-start(f32[4,1,64,256]{3,2,1,0:T(8,128)S(1)} %pad_maximum_fusion.39), channel_id=1, source_target_pairs={{2,0},{4,2},{6,4},{8,6},{10,8},{12,10},{14,12},{3,1},{5,3},{7,5},{... | collective-permute-start | bytes 786440 | tf_op jit(solution)/shard_map/ppermute | solution.py:133
  6.5 15.8 %collective-permute-start.2 = (f32[4,1,64,256]{3,2,1,0:T(8,128)S(1)}, f32[4,1,64,256]{3,2,1,0:T(8,128)S(1)}, u32[]{:S(2)}, u32[]{:S(2)}) collective-permute-start(f32[4,1,64,256]{3,2,1,0:T(8,128)S(1)} %pad_maximum_fusion.40), channel_id=1, source_target_pairs={{0,2},{2,4},{4,6},{6,8},{8,10},{10,12},{12,14},{1,3},{3,5},{5,7},{... | collective-permute-start | bytes 786440 | tf_op jit(solution)/shard_map/ppermute | solution.py:132
  23.0 1.3 %collective-permute-start.3 = (f32[2,10,1,256]{3,2,1,0:T(1,128)S(1)}, f32[2,10,1,256]{3,2,1,0:T(1,128)S(1)}, u32[]{:S(2)}, u32[]{:S(2)}) collective-permute-start(f32[2,10,1,256]{3,2,1,0:T(1,128)S(1)} %pad_maximum_fusion.51), channel_id=1, source_target_pairs={{0,1},{1,0},{2,3},{3,2},{4,5},{5,4},{6,7},{7,6},{8,9},{9,8},{10,11... | collective-permute-start | bytes 61448 | tf_op jit(solution)/shard_map/ppermute | solution.py:152
  25.5 11.0 %collective-permute-start.5 = (f32[4,1,64,256]{3,2,1,0:T(8,128)S(1)}, f32[4,1,64,256]{3,2,1,0:T(8,128)S(1)}, u32[]{:S(2)}, u32[]{:S(2)}) collective-permute-start(f32[4,1,64,256]{3,2,1,0:T(8,128)S(1)} %pad_maximum_fusion.41), channel_id=1, source_target_pairs={{2,0},{4,2},{6,4},{8,6},{10,8},{12,10},{14,12},{3,1},{5,3},{7,5},{... | collective-permute-start | bytes 786440 | tf_op jit(solution)/shard_map/ppermute | solution.py:133
  26.8 15.5 %collective-permute-start.6 = (f32[4,1,64,256]{3,2,1,0:T(8,128)S(1)}, f32[4,1,64,256]{3,2,1,0:T(8,128)S(1)}, u32[]{:S(2)}, u32[]{:S(2)}) collective-permute-start(f32[4,1,64,256]{3,2,1,0:T(8,128)S(1)} %pad_maximum_fusion.42), channel_id=1, source_target_pairs={{0,2},{2,4},{4,6},{6,8},{8,10},{10,12},{12,14},{1,3},{3,5},{5,7},{... | collective-permute-start | bytes 786440 | tf_op jit(solution)/shard_map/ppermute | solution.py:132
  43.0 1.2 %collective-permute-start.7 = (f32[2,4,1,256]{3,2,1,0:T(1,128)S(1)}, f32[2,4,1,256]{3,2,1,0:T(1,128)S(1)}, u32[]{:S(2)}, u32[]{:S(2)}) collective-permute-start(f32[2,4,1,256]{3,2,1,0:T(1,128)S(1)} %constant_dynamic-slice_fusion.9), channel_id=1, source_target_pairs={{0,1},{1,0},{2,3},{3,2},{4,5},{5,4},{6,7},{7,6},{8,9},{9,8},{10,11... | collective-permute-start | bytes 24584 | tf_op jit(solution)/shard_map/ppermute | solution.py:50
  45.0 1.2 %collective-permute-start.8 = (f32[2,4,1,256]{3,2,1,0:T(1,128)S(1)}, f32[2,4,1,256]{3,2,1,0:T(1,128)S(1)}, u32[]{:S(2)}, u32[]{:S(2)}) collective-permute-start(f32[2,4,1,256]{3,2,1,0:T(1,128)S(1)} %constant_dynamic-slice_fusion.8), channel_id=1, source_target_pairs={{0,1},{1,0},{2,3},{3,2},{4,5},{5,4},{6,7},{7,6},{8,9},{9,8},{10,11... | collective-permute-start | bytes 24584 | tf_op jit(solution)/shard_map/ppermute | solution.py:50
  46.6 15.9 %collective-permute-start.10 = (f32[4,1,64,256]{3,2,1,0:T(8,128)S(1)}, f32[4,1,64,256]{3,2,1,0:T(8,128)S(1)}, u32[]{:S(2)}, u32[]{:S(2)}) collective-permute-start(f32[4,1,64,256]{3,2,1,0:T(8,128)S(1)} %pad_maximum_fusion.44), channel_id=1, source_target_pairs={{0,2},{2,4},{4,6},{6,8},{8,10},{10,12},{12,14},{1,3},{3,5},{5,7},{... | collective-permute-start | bytes 786440 | tf_op jit(solution)/shard_map/ppermute | solution.py:132
  51.0 11.5 %collective-permute-start.9 = (f32[4,1,64,256]{3,2,1,0:T(8,128)S(1)}, f32[4,1,64,256]{3,2,1,0:T(8,128)S(1)}, u32[]{:S(2)}, u32[]{:S(2)}) collective-permute-start(f32[4,1,64,256]{3,2,1,0:T(8,128)S(1)} %pad_maximum_fusion.43), channel_id=1, source_target_pairs={{2,0},{4,2},{6,4},{8,6},{10,8},{12,10},{14,12},{3,1},{5,3},{7,5},{... | collective-permute-start | bytes 786440 | tf_op jit(solution)/shard_map/ppermute | solution.py:133
  63.4 1.3 %collective-permute-start.11 = (f32[2,10,1,256]{3,2,1,0:T(1,128)S(1)}, f32[2,10,1,256]{3,2,1,0:T(1,128)S(1)}, u32[]{:S(2)}, u32[]{:S(2)}) collective-permute-start(f32[2,10,1,256]{3,2,1,0:T(1,128)S(1)} %pad_maximum_fusion.52), channel_id=1, source_target_pairs={{0,1},{1,0},{2,3},{3,2},{4,5},{5,4},{6,7},{7,6},{8,9},{9,8},{10,11... | collective-permute-start | bytes 61448 | tf_op jit(solution)/shard_map/ppermute | solution.py:152
  63.5 1.4 %collective-permute-start.12 = (f32[3,4,1,256]{3,2,1,0:T(1,128)S(1)}, f32[3,4,1,256]{3,2,1,0:T(1,128)S(1)}, u32[]{:S(2)}, u32[]{:S(2)}) collective-permute-start(f32[3,4,1,256]{3,2,1,0:T(1,128)S(1)} %pad_maximum_fusion.54), channel_id=1, source_target_pairs={{0,1},{1,0},{2,3},{3,2},{4,5},{5,4},{6,7},{7,6},{8,9},{9,8},{10,11... | collective-permute-start | bytes 36872 | tf_op jit(solution)/shard_map/ppermute | solution.py:116
  66.2 11.2 %collective-permute-start.13 = (f32[4,1,64,256]{3,2,1,0:T(8,128)S(1)}, f32[4,1,64,256]{3,2,1,0:T(8,128)S(1)}, u32[]{:S(2)}, u32[]{:S(2)}) collective-permute-start(f32[4,1,64,256]{3,2,1,0:T(8,128)S(1)} %pad_maximum_fusion.45), channel_id=1, source_target_pairs={{2,0},{4,2},{6,4},{8,6},{10,8},{12,10},{14,12},{3,1},{5,3},{7,5},{... | collective-permute-start | bytes 786440 | tf_op jit(solution)/shard_map/ppermute | solution.py:133
  67.5 15.7 %collective-permute-start.14 = (f32[4,1,64,256]{3,2,1,0:T(8,128)S(1)}, f32[4,1,64,256]{3,2,1,0:T(8,128)S(1)}, u32[]{:S(2)}, u32[]{:S(2)}) collective-permute-start(f32[4,1,64,256]{3,2,1,0:T(8,128)S(1)} %pad_maximum_fusion.46), channel_id=1, source_target_pairs={{0,2},{2,4},{4,6},{6,8},{8,10},{10,12},{12,14},{1,3},{3,5},{5,7},{... | collective-permute-start | bytes 786440 | tf_op jit(solution)/shard_map/ppermute | solution.py:132
  84.0 1.2 %collective-permute-start.15 = (f32[2,4,1,256]{3,2,1,0:T(1,128)S(1)}, f32[2,4,1,256]{3,2,1,0:T(1,128)S(1)}, u32[]{:S(2)}, u32[]{:S(2)}) collective-permute-start(f32[2,4,1,256]{3,2,1,0:T(1,128)S(1)} %constant_dynamic-slice_fusion), channel_id=1, source_target_pairs={{0,1},{1,0},{2,3},{3,2},{4,5},{5,4},{6,7},{7,6},{8,9},{9,8},{10,11... | collective-permute-start | bytes 24584 | tf_op jit(solution)/shard_map/ppermute | solution.py:50
  85.8 1.1 copy-start.2
  86.9 0.8 copy-start.3
  87.8 1.5 %collective-permute-start.16 = (f32[]{:T(128)}, f32[]{:T(128)}, u32[]{:S(2)}, u32[]{:S(2)}) collective-permute-start(f32[]{:T(128)} %get-tuple-element.17), channel_id=1, source_target_pairs={{0,1},{1,0},{2,3},{3,2},{4,5},{5,4},{6,7},{7,6},{8,9},{9,8},{10,11... | collective-permute-start | bytes 20 | tf_op jit(solution)/shard_map/ppermute | solution.py:19
  91.1 5.1 %collective-permute-start.17 = (f32[65,256]{1,0:T(8,128)S(1)}, f32[65,256]{1,0:T(8,128)S(1)}, u32[]{:S(2)}, u32[]{:S(2)}) collective-permute-start(f32[65,256]{1,0:T(8,128)S(1)} %select_maximum_fusion), channel_id=1, source_target_pairs={{0,2},{2,0},{4,6},{6,4},{8,10},{10,8},{12,14},{14,12},{1,3},{3,1},... | collective-permute-start | bytes 199688 | tf_op jit(solution)/shard_map/ppermute | solution.py:28
  96.3 7.1 %collective-permute-start.20 = (f32[65,256]{1,0:T(8,128)S(1)}, f32[65,256]{1,0:T(8,128)S(1)}, u32[]{:S(2)}, u32[]{:S(2)}) collective-permute-start(f32[65,256]{1,0:T(8,128)S(1)} %fusion.286), channel_id=1, source_target_pairs={{0,12},{2,14},{4,8},{6,10},{8,4},{10,6},{12,0},{14,2},{1,13},{3,15... | collective-permute-start | bytes 199688 | tf_op jit(solution)/shard_map/ppermute | solution.py:33
  98.9 6.9 %collective-permute-start.19 = (f32[65,256]{1,0:T(8,128)S(1)}, f32[65,256]{1,0:T(8,128)S(1)}, u32[]{:S(2)}, u32[]{:S(2)}) collective-permute-start(f32[65,256]{1,0:T(8,128)S(1)} %fusion.286), channel_id=1, source_target_pairs={{0,8},{2,10},{4,12},{6,14},{8,0},{10,2},{12,4},{14,6},{1,9},{3,11}... | collective-permute-start | bytes 199688 | tf_op jit(solution)/shard_map/ppermute | solution.py:33
  99.4 6.5 %collective-permute-start.18 = (f32[65,256]{1,0:T(8,128)S(1)}, f32[65,256]{1,0:T(8,128)S(1)}, u32[]{:S(2)}, u32[]{:S(2)}) collective-permute-start(f32[65,256]{1,0:T(8,128)S(1)} %fusion.286), channel_id=1, source_target_pairs={{0,4},{2,6},{4,0},{6,2},{8,12},{10,14},{12,8},{14,10},{1,5},{3,7},... | collective-permute-start | bytes 199688 | tf_op jit(solution)/shard_map/ppermute | solution.py:33

commit v17 on v15

--- a/solution.py
+++ b/solution.py
@@ -23,7 +23,7 @@
 
 def gx_total(value):
     count = lax.axis_size("gx")
-    if count > 8 or count % 2:
+    if count > 4 or count % 2:
         return axis_sum(value, "gx")
     pair = value + lax.ppermute(value, "gx", [(i, i ^ 1) for i in range(count)])
     groups = count // 2

time: 109 us -> 109 us (level)
    ppermute x1 -> x4, waiting for transfers between devices: 1.05 us -> 8.96 us  [axis_sum(): value = value + lax.ppermute(value, axis, pairs)]
    ppermute x4 -> x0, waiting for transfers between devices: 7.73 us -> none  [the longest x3 5.13 us: gx_total(): lax.ppermute(pair, 'gx', [(i, i ^ 2 * k) for i in range(count)])]
    ppermute x4 -> x0, starting transfers between devices: 6.98 us -> none  [the longest x3 4.45 us: gx_total(): lax.ppermute(pair, 'gx', [(i, i ^ 2 * k) for i in range(count)])]
    ppermute x1 -> x4, starting transfers between devices: 0.23 us -> 7.05 us  [axis_sum(): value = value + lax.ppermute(value, axis, pairs)]
  transfers between devices with their start and end apart: 21 -> 20, of which waited for: 16 -> 16; matrix products, arithmetic and copies ran while one was open for 5% -> 5% of each run, Pallas kernels for 0% -> 0%
where the time goes in v17:
time: 109 us
  waiting for transfers between devices  54.6 us (50%)
  starting transfers between devices  34 us (31%)
  other arithmetic  12 us (11%)
  between operations  5.25 us (5%)
  local copies, waits for them, and re-layouts  3.26 us (3%)
    ppermute x4, waiting for transfers between devices, stage_pair(): lax.ppermute(jnp.concatenate([stage[:, X - 1:], part_top]), 'gx', up)  27.3 us
    ppermute x4, starting transfers between devices, stage_pair(): lax.ppermute(jnp.concatenate([stage[:, X - 1:], part_top]), 'gx', up)  20 us
    ppermute x4, waiting for transfers between devices, stage_pair(): lax.ppermute(jnp.concatenate([stage[:, :1], part_bottom]), 'gx', down)  13.9 us
    ppermute x4, waiting for transfers between devices, axis_sum(): value = value + lax.ppermute(value, axis, pairs)  8.96 us
    ppermute x4, starting transfers between devices, axis_sum(): value = value + lax.ppermute(value, axis, pairs)  7.05 us
    ppermute x4, starting transfers between devices, stage_pair(): lax.ppermute(jnp.concatenate([stage[:, :1], part_bottom]), 'gx', down)  5.17 us
    sub x14, other arithmetic, operator(): lapl = total - 6.0 * field  3.83 us
    ppermute x4, waiting for transfers between devices, y_extended(): other = lax.ppermute(strip, 'gy', [(0, 1), (1, 0)])  2.62 us
  transfers between devices with their start and end apart: 20, of which 16 were waited for; matrix products, arithmetic and copies ran while one was open for 5% of the time, Pallas kernels for 0%

profile of v17, /device:TPU:0, one launch (start us, length us, event | category | flops | bytes accessed | tf_op | source)
XLA Modules:
  0.0 109.0 jit_solution(17518294662191653183)
XLA Ops:
  0.6 0.9 constant_dynamic-slice_fusion.17
  1.6 0.6 collective-permute-start
  2.2 0.8 slice_bitcast_fusion.18
  3.1 1.3 %multiply_add_fusion.6 = (f32[4,64,256]{2,1,0:T(8,128)S(1)}, f32[4,64,256]{2,1,0:T(8,128)S(1)}, f32[4,64,256]{2,1,0:T(8,128)S(1)}, f32[4,64,256]{2,1,0:T(8,128)S(1)}) fusion(f32[4,64,256]{2,1,0:T(8,128)} %param.10, f32[2,4,64,256]{3,2,1,0:T(8,128)} %param.8, f32[64,256]{1,0:T(8,128)S(1)} %mul.964, f32[4]{0:T(128)S(1)} %multiply_add_fusion.7, ...), kind=kLoop, calls=%fused_computation.256 | loop fusion | flops 1114112 | bytes 2490384 | tf_op jit(solution)/shard_map/add | solution.py:65
  5.1 1.3 %collective-permute-start.1 = (f32[4,1,64,256]{3,2,1,0:T(8,128)S(1)}, f32[4,1,64,256]{3,2,1,0:T(8,128)S(1)}, u32[]{:S(2)}, u32[]{:S(2)}) collective-permute-start(f32[4,1,64,256]{3,2,1,0:T(8,128)S(1)} %pad_maximum_fusion.38), channel_id=1, source_target_pairs={{2,0},{4,2},{6,4},{8,6},{10,8},{12,10},{14,12},{3,1},{5,3},{7,5},{... | collective-permute-start | bytes 786440 | tf_op jit(solution)/shard_map/ppermute | solution.py:133
  6.5 5.5 %collective-permute-start.2 = (f32[4,1,64,256]{3,2,1,0:T(8,128)S(1)}, f32[4,1,64,256]{3,2,1,0:T(8,128)S(1)}, u32[]{:S(2)}, u32[]{:S(2)}) collective-permute-start(f32[4,1,64,256]{3,2,1,0:T(8,128)S(1)} %pad_maximum_fusion.39), channel_id=1, source_target_pairs={{0,2},{2,4},{4,6},{6,8},{8,10},{10,12},{12,14},{1,3},{3,5},{5,7},{... | collective-permute-start | bytes 786440 | tf_op jit(solution)/shard_map/ppermute | solution.py:132
  12.0 4.5 %collective-permute-done.1 = f32[4,1,64,256]{3,2,1,0:T(8,128)S(1)} collective-permute-done((f32[4,1,64,256]{3,2,1,0:T(8,128)S(1)}, f32[4,1,64,256]{3,2,1,0:T(8,128)S(1)}, u32[]{:S(2)}, u32[]{:S(2)}) %collective-permute-start.1) | collective-permute-done | bytes 262176 | tf_op jit(solution)/shard_map/ppermute | solution.py:133
  16.5 5.7 %collective-permute-done.2 = f32[4,1,64,256]{3,2,1,0:T(8,128)S(1)} collective-permute-done((f32[4,1,64,256]{3,2,1,0:T(8,128)S(1)}, f32[4,1,64,256]{3,2,1,0:T(8,128)S(1)}, u32[]{:S(2)}, u32[]{:S(2)}) %collective-permute-start.2) | collective-permute-done | bytes 262176 | tf_op jit(solution)/shard_map/ppermute | solution.py:132
  22.3 0.4 fusion.2
  23.1 1.2 %collective-permute-done.3 = f32[2,10,1,256]{3,2,1,0:T(1,128)S(1)} collective-permute-done((f32[2,10,1,256]{3,2,1,0:T(1,128)S(1)}, f32[2,10,1,256]{3,2,1,0:T(1,128)S(1)}, u32[]{:S(2)}, u32[]{:S(2)}) %collective-permute-start.3) | collective-permute-done | bytes 20512 | tf_op jit(solution)/shard_map/ppermute | solution.py:152
  24.5 0.3 fusion.5
  25.5 1.3 %collective-permute-start.5 = (f32[4,1,64,256]{3,2,1,0:T(8,128)S(1)}, f32[4,1,64,256]{3,2,1,0:T(8,128)S(1)}, u32[]{:S(2)}, u32[]{:S(2)}) collective-permute-start(f32[4,1,64,256]{3,2,1,0:T(8,128)S(1)} %pad_maximum_fusion.40), channel_id=1, source_target_pairs={{2,0},{4,2},{6,4},{8,6},{10,8},{12,10},{14,12},{3,1},{5,3},{7,5},{... | collective-permute-start | bytes 786440 | tf_op jit(solution)/shard_map/ppermute | solution.py:133
  26.8 5.0 %collective-permute-start.6 = (f32[4,1,64,256]{3,2,1,0:T(8,128)S(1)}, f32[4,1,64,256]{3,2,1,0:T(8,128)S(1)}, u32[]{:S(2)}, u32[]{:S(2)}) collective-permute-start(f32[4,1,64,256]{3,2,1,0:T(8,128)S(1)} %pad_maximum_fusion.41), channel_id=1, source_target_pairs={{0,2},{2,4},{4,6},{6,8},{8,10},{10,12},{12,14},{1,3},{3,5},{5,7},{... | collective-permute-start | bytes 786440 | tf_op jit(solution)/shard_map/ppermute | solution.py:132
  31.9 4.6 %collective-permute-done.5 = f32[4,1,64,256]{3,2,1,0:T(8,128)S(1)} collective-permute-done((f32[4,1,64,256]{3,2,1,0:T(8,128)S(1)}, f32[4,1,64,256]{3,2,1,0:T(8,128)S(1)}, u32[]{:S(2)}, u32[]{:S(2)}) %collective-permute-start.5) | collective-permute-done | bytes 262176 | tf_op jit(solution)/shard_map/ppermute | solution.py:133
  36.5 5.7 %collective-permute-done.6 = f32[4,1,64,256]{3,2,1,0:T(8,128)S(1)} collective-permute-done((f32[4,1,64,256]{3,2,1,0:T(8,128)S(1)}, f32[4,1,64,256]{3,2,1,0:T(8,128)S(1)}, u32[]{:S(2)}, u32[]{:S(2)}) %collective-permute-start.6) | collective-permute-done | bytes 262176 | tf_op jit(solution)/shard_map/ppermute | solution.py:132
  42.3 0.4 fusion.8
  43.1 1.1 %collective-permute-done.7 = f32[2,4,1,256]{3,2,1,0:T(1,128)S(1)} collective-permute-done((f32[2,4,1,256]{3,2,1,0:T(1,128)S(1)}, f32[2,4,1,256]{3,2,1,0:T(1,128)S(1)}, u32[]{:S(2)}, u32[]{:S(2)}) %collective-permute-start.7) | collective-permute-done | bytes 8224 | tf_op jit(solution)/shard_map/ppermute | solution.py:50
  44.2 0.3 fusion.11
  45.2 1.0 collective-permute-done.8
  46.6 4.4 %collective-permute-start.10 = (f32[4,1,64,256]{3,2,1,0:T(8,128)S(1)}, f32[4,1,64,256]{3,2,1,0:T(8,128)S(1)}, u32[]{:S(2)}, u32[]{:S(2)}) collective-permute-start(f32[4,1,64,256]{3,2,1,0:T(8,128)S(1)} %pad_maximum_fusion.43), channel_id=1, source_target_pairs={{0,2},{2,4},{4,6},{6,8},{8,10},{10,12},{12,14},{1,3},{3,5},{5,7},{... | collective-permute-start | bytes 786440 | tf_op jit(solution)/shard_map/ppermute | solution.py:132
  51.0 1.3 %collective-permute-start.9 = (f32[4,1,64,256]{3,2,1,0:T(8,128)S(1)}, f32[4,1,64,256]{3,2,1,0:T(8,128)S(1)}, u32[]{:S(2)}, u32[]{:S(2)}) collective-permute-start(f32[4,1,64,256]{3,2,1,0:T(8,128)S(1)} %pad_maximum_fusion.42), channel_id=1, source_target_pairs={{2,0},{4,2},{6,4},{8,6},{10,8},{12,10},{14,12},{3,1},{5,3},{7,5},{... | collective-permute-start | bytes 786440 | tf_op jit(solution)/shard_map/ppermute | solution.py:133
  52.3 10.1 %collective-permute-done.10 = f32[4,1,64,256]{3,2,1,0:T(8,128)S(1)} collective-permute-done((f32[4,1,64,256]{3,2,1,0:T(8,128)S(1)}, f32[4,1,64,256]{3,2,1,0:T(8,128)S(1)}, u32[]{:S(2)}, u32[]{:S(2)}) %collective-permute-start.10) | collective-permute-done | bytes 262176 | tf_op jit(solution)/shard_map/ppermute | solution.py:132
  62.5 0.3 fusion.14
  63.1 0.3 multiply_add_fusion.2
  63.5 0.6 collective-permute-start.12
  64.1 0.6 collective-permute-done.11
  65.0 0.3 fusion.17
  65.5 0.3 multiply_add_fusion.1
  66.2 1.3 %collective-permute-start.13 = (f32[4,1,64,256]{3,2,1,0:T(8,128)S(1)}, f32[4,1,64,256]{3,2,1,0:T(8,128)S(1)}, u32[]{:S(2)}, u32[]{:S(2)}) collective-permute-start(f32[4,1,64,256]{3,2,1,0:T(8,128)S(1)} %pad_maximum_fusion.44), channel_id=1, source_target_pairs={{2,0},{4,2},{6,4},{8,6},{10,8},{12,10},{14,12},{3,1},{5,3},{7,5},{... | collective-permute-start | bytes 786440 | tf_op jit(solution)/shard_map/ppermute | solution.py:133
  67.5 5.0 %collective-permute-start.14 = (f32[4,1,64,256]{3,2,1,0:T(8,128)S(1)}, f32[4,1,64,256]{3,2,1,0:T(8,128)S(1)}, u32[]{:S(2)}, u32[]{:S(2)}) collective-permute-start(f32[4,1,64,256]{3,2,1,0:T(8,128)S(1)} %pad_maximum_fusion.45), channel_id=1, source_target_pairs={{0,2},{2,4},{4,6},{6,8},{8,10},{10,12},{12,14},{1,3},{3,5},{5,7},{... | collective-permute-start | bytes 786440 | tf_op jit(solution)/shard_map/ppermute | solution.py:132
  72.6 4.8 %collective-permute-done.13 = f32[4,1,64,256]{3,2,1,0:T(8,128)S(1)} collective-permute-done((f32[4,1,64,256]{3,2,1,0:T(8,128)S(1)}, f32[4,1,64,256]{3,2,1,0:T(8,128)S(1)}, u32[]{:S(2)}, u32[]{:S(2)}) %collective-permute-start.13) | collective-permute-done | bytes 262176 | tf_op jit(solution)/shard_map/ppermute | solution.py:133
  77.4 5.7 %collective-permute-done.14 = f32[4,1,64,256]{3,2,1,0:T(8,128)S(1)} collective-permute-done((f32[4,1,64,256]{3,2,1,0:T(8,128)S(1)}, f32[4,1,64,256]{3,2,1,0:T(8,128)S(1)}, u32[]{:S(2)}, u32[]{:S(2)}) %collective-permute-start.14) | collective-permute-done | bytes 262176 | tf_op jit(solution)/shard_map/ppermute | solution.py:132
  83.2 0.4 fusion.20
  83.8 0.3 multiply_add_fusion
  84.1 0.6 compare_reduce_fusion
  84.8 0.5 collective-permute-done.15
  85.3 0.3 fusion.23
  85.9 1.1 multiply_reduce_fusion
  87.2 0.5 copy-done.3
  88.2 0.9 collective-permute-done.16
  91.1 2.5 %collective-permute-start.17 = (f32[65,256]{1,0:T(8,128)S(1)}, f32[65,256]{1,0:T(8,128)S(1)}, u32[]{:S(2)}, u32[]{:S(2)}) collective-permute-start(f32[65,256]{1,0:T(8,128)S(1)} %select_maximum_fusion), channel_id=1, source_target_pairs={{0,2},{2,0},{4,6},{6,4},{8,10},{10,8},{12,14},{14,12},{1,3},{3,1},... | collective-permute-start | bytes 199688 | tf_op jit(solution)/shard_map/ppermute | solution.py:19
  93.6 2.6 %collective-permute-done.17 = f32[65,256]{1,0:T(8,128)S(1)} collective-permute-done((f32[65,256]{1,0:T(8,128)S(1)}, f32[65,256]{1,0:T(8,128)S(1)}, u32[]{:S(2)}, u32[]{:S(2)}) %collective-permute-start.17) | collective-permute-done | bytes 66592 | tf_op jit(solution)/shard_map/ppermute | solution.py:19
  96.3 1.6 %collective-permute-start.18 = (f32[65,256]{1,0:T(8,128)S(1)}, f32[65,256]{1,0:T(8,128)S(1)}, u32[]{:S(2)}, u32[]{:S(2)}) collective-permute-start(f32[65,256]{1,0:T(8,128)S(1)} %fusion.286), channel_id=1, source_target_pairs={{0,4},{2,6},{4,0},{6,2},{8,12},{10,14},{12,8},{14,10},{1,5},{3,7},... | collective-permute-start | bytes 199688 | tf_op jit(solution)/shard_map/ppermute | solution.py:19
  97.9 2.8 %collective-permute-done.18 = f32[65,256]{1,0:T(8,128)S(1)} collective-permute-done((f32[65,256]{1,0:T(8,128)S(1)}, f32[65,256]{1,0:T(8,128)S(1)}, u32[]{:S(2)}, u32[]{:S(2)}) %collective-permute-start.18) | collective-permute-done | bytes 66592 | tf_op jit(solution)/shard_map/ppermute | solution.py:19
  100.7 2.7 %collective-permute-start.19 = (f32[65,256]{1,0:T(8,128)S(1)}, f32[65,256]{1,0:T(8,128)S(1)}, u32[]{:S(2)}, u32[]{:S(2)}) collective-permute-start(f32[65,256]{1,0:T(8,128)S(1)} %add.948), channel_id=1, source_target_pairs={{0,8},{2,10},{4,12},{6,14},{8,0},{10,2},{12,4},{14,6},{1,9},{3,11}... | collective-permute-start | bytes 199688 | tf_op jit(solution)/shard_map/ppermute | solution.py:19
  103.3 2.7 %collective-permute-done.19 = f32[65,256]{1,0:T(8,128)S(1)} collective-permute-done((f32[65,256]{1,0:T(8,128)S(1)}, f32[65,256]{1,0:T(8,128)S(1)}, u32[]{:S(2)}, u32[]{:S(2)}) %collective-permute-start.19) | collective-permute-done | bytes 66592 | tf_op jit(solution)/shard_map/ppermute | solution.py:19
  106.0 0.5 slice.1275
  107.2 0.6 slice_divide_fusion
  (118 shorter events, 6.2 us)
Async XLA Ops:
  0.6 2.5 %copy-start.1 = (f32[2,4,64,256]{3,2,1,0:T(8,128)S(1)}, f32[2,4,64,256]{3,2,1,0:T(8,128)}, u32[]{:S(2)}) copy-start(f32[2,4,64,256]{3,2,1,0:T(8,128)} %param.9) | copy-start | bytes 1572868
  1.6 3.2 %collective-permute-start = (f32[2,4,1,256]{3,2,1,0:T(1,128)S(1)}, f32[2,4,1,256]{3,2,1,0:T(1,128)S(1)}, u32[]{:S(2)}, u32[]{:S(2)}) collective-permute-start(f32[2,4,1,256]{3,2,1,0:T(1,128)S(1)} %constant_dynamic-slice_fusion.17), channel_id=1, source_target_pairs={{0,1},{1,0},{2,3},{3,2},{4,5},{5,4},{6,7},{7,6},{8,9},{9,8},{10,11... | collective-permute-start | bytes 24584 | tf_op jit(solution)/shard_map/ppermute | solution.py:50
  3.1 1.5 %copy-start = (f32[2,4,64,256]{3,2,1,0:T(8,128)S(1)}, f32[2,4,64,256]{3,2,1,0:T(8,128)}, u32[]{:S(2)}) copy-start(f32[2,4,64,256]{3,2,1,0:T(8,128)} %param.7) | copy-start | bytes 1572868
  4.5 19.9 %collective-permute-start.4 = (f32[3,4,1,256]{3,2,1,0:T(1,128)S(1)}, f32[3,4,1,256]{3,2,1,0:T(1,128)S(1)}, u32[]{:S(2)}, u32[]{:S(2)}) collective-permute-start(f32[3,4,1,256]{3,2,1,0:T(1,128)S(1)} %pad_maximum_fusion.52), channel_id=1, source_target_pairs={{0,1},{1,0},{2,3},{3,2},{4,5},{5,4},{6,7},{7,6},{8,9},{9,8},{10,11... | collective-permute-start | bytes 36872 | tf_op jit(solution)/shard_map/ppermute | solution.py:116
  5.1 11.4 %collective-permute-start.1 = (f32[4,1,64,256]{3,2,1,0:T(8,128)S(1)}, f32[4,1,64,256]{3,2,1,0:T(8,128)S(1)}, u32[]{:S(2)}, u32[]{:S(2)}) collective-permute-start(f32[4,1,64,256]{3,2,1,0:T(8,128)S(1)} %pad_maximum_fusion.38), channel_id=1, source_target_pairs={{2,0},{4,2},{6,4},{8,6},{10,8},{12,10},{14,12},{3,1},{5,3},{7,5},{... | collective-permute-start | bytes 786440 | tf_op jit(solution)/shard_map/ppermute | solution.py:133
  6.5 15.8 %collective-permute-start.2 = (f32[4,1,64,256]{3,2,1,0:T(8,128)S(1)}, f32[4,1,64,256]{3,2,1,0:T(8,128)S(1)}, u32[]{:S(2)}, u32[]{:S(2)}) collective-permute-start(f32[4,1,64,256]{3,2,1,0:T(8,128)S(1)} %pad_maximum_fusion.39), channel_id=1, source_target_pairs={{0,2},{2,4},{4,6},{6,8},{8,10},{10,12},{12,14},{1,3},{3,5},{5,7},{... | collective-permute-start | bytes 786440 | tf_op jit(solution)/shard_map/ppermute | solution.py:132
  23.0 1.3 %collective-permute-start.3 = (f32[2,10,1,256]{3,2,1,0:T(1,128)S(1)}, f32[2,10,1,256]{3,2,1,0:T(1,128)S(1)}, u32[]{:S(2)}, u32[]{:S(2)}) collective-permute-start(f32[2,10,1,256]{3,2,1,0:T(1,128)S(1)} %pad_maximum_fusion.50), channel_id=1, source_target_pairs={{0,1},{1,0},{2,3},{3,2},{4,5},{5,4},{6,7},{7,6},{8,9},{9,8},{10,11... | collective-permute-start | bytes 61448 | tf_op jit(solution)/shard_map/ppermute | solution.py:152
  25.5 11.0 %collective-permute-start.5 = (f32[4,1,64,256]{3,2,1,0:T(8,128)S(1)}, f32[4,1,64,256]{3,2,1,0:T(8,128)S(1)}, u32[]{:S(2)}, u32[]{:S(2)}) collective-permute-start(f32[4,1,64,256]{3,2,1,0:T(8,128)S(1)} %pad_maximum_fusion.40), channel_id=1, source_target_pairs={{2,0},{4,2},{6,4},{8,6},{10,8},{12,10},{14,12},{3,1},{5,3},{7,5},{... | collective-permute-start | bytes 786440 | tf_op jit(solution)/shard_map/ppermute | solution.py:133
  26.8 15.5 %collective-permute-start.6 = (f32[4,1,64,256]{3,2,1,0:T(8,128)S(1)}, f32[4,1,64,256]{3,2,1,0:T(8,128)S(1)}, u32[]{:S(2)}, u32[]{:S(2)}) collective-permute-start(f32[4,1,64,256]{3,2,1,0:T(8,128)S(1)} %pad_maximum_fusion.41), channel_id=1, source_target_pairs={{0,2},{2,4},{4,6},{6,8},{8,10},{10,12},{12,14},{1,3},{3,5},{5,7},{... | collective-permute-start | bytes 786440 | tf_op jit(solution)/shard_map/ppermute | solution.py:132
  43.0 1.2 %collective-permute-start.7 = (f32[2,4,1,256]{3,2,1,0:T(1,128)S(1)}, f32[2,4,1,256]{3,2,1,0:T(1,128)S(1)}, u32[]{:S(2)}, u32[]{:S(2)}) collective-permute-start(f32[2,4,1,256]{3,2,1,0:T(1,128)S(1)} %constant_dynamic-slice_fusion.9), channel_id=1, source_target_pairs={{0,1},{1,0},{2,3},{3,2},{4,5},{5,4},{6,7},{7,6},{8,9},{9,8},{10,11... | collective-permute-start | bytes 24584 | tf_op jit(solution)/shard_map/ppermute | solution.py:50
  45.0 1.2 %collective-permute-start.8 = (f32[2,4,1,256]{3,2,1,0:T(1,128)S(1)}, f32[2,4,1,256]{3,2,1,0:T(1,128)S(1)}, u32[]{:S(2)}, u32[]{:S(2)}) collective-permute-start(f32[2,4,1,256]{3,2,1,0:T(1,128)S(1)} %constant_dynamic-slice_fusion.8), channel_id=1, source_target_pairs={{0,1},{1,0},{2,3},{3,2},{4,5},{5,4},{6,7},{7,6},{8,9},{9,8},{10,11... | collective-permute-start | bytes 24584 | tf_op jit(solution)/shard_map/ppermute | solution.py:50
  46.6 15.9 %collective-permute-start.10 = (f32[4,1,64,256]{3,2,1,0:T(8,128)S(1)}, f32[4,1,64,256]{3,2,1,0:T(8,128)S(1)}, u32[]{:S(2)}, u32[]{:S(2)}) collective-permute-start(f32[4,1,64,256]{3,2,1,0:T(8,128)S(1)} %pad_maximum_fusion.43), channel_id=1, source_target_pairs={{0,2},{2,4},{4,6},{6,8},{8,10},{10,12},{12,14},{1,3},{3,5},{5,7},{... | collective-permute-start | bytes 786440 | tf_op jit(solution)/shard_map/ppermute | solution.py:132
  51.0 11.5 %collective-permute-start.9 = (f32[4,1,64,256]{3,2,1,0:T(8,128)S(1)}, f32[4,1,64,256]{3,2,1,0:T(8,128)S(1)}, u32[]{:S(2)}, u32[]{:S(2)}) collective-permute-start(f32[4,1,64,256]{3,2,1,0:T(8,128)S(1)} %pad_maximum_fusion.42), channel_id=1, source_target_pairs={{2,0},{4,2},{6,4},{8,6},{10,8},{12,10},{14,12},{3,1},{5,3},{7,5},{... | collective-permute-start | bytes 786440 | tf_op jit(solution)/shard_map/ppermute | solution.py:133
  63.4 1.3 %collective-permute-start.11 = (f32[2,10,1,256]{3,2,1,0:T(1,128)S(1)}, f32[2,10,1,256]{3,2,1,0:T(1,128)S(1)}, u32[]{:S(2)}, u32[]{:S(2)}) collective-permute-start(f32[2,10,1,256]{3,2,1,0:T(1,128)S(1)} %pad_maximum_fusion.51), channel_id=1, source_target_pairs={{0,1},{1,0},{2,3},{3,2},{4,5},{5,4},{6,7},{7,6},{8,9},{9,8},{10,11... | collective-permute-start | bytes 61448 | tf_op jit(solution)/shard_map/ppermute | solution.py:152
  63.5 1.4 %collective-permute-start.12 = (f32[3,4,1,256]{3,2,1,0:T(1,128)S(1)}, f32[3,4,1,256]{3,2,1,0:T(1,128)S(1)}, u32[]{:S(2)}, u32[]{:S(2)}) collective-permute-start(f32[3,4,1,256]{3,2,1,0:T(1,128)S(1)} %pad_maximum_fusion.53), channel_id=1, source_target_pairs={{0,1},{1,0},{2,3},{3,2},{4,5},{5,4},{6,7},{7,6},{8,9},{9,8},{10,11... | collective-permute-start | bytes 36872 | tf_op jit(solution)/shard_map/ppermute | solution.py:116
  66.2 11.2 %collective-permute-start.13 = (f32[4,1,64,256]{3,2,1,0:T(8,128)S(1)}, f32[4,1,64,256]{3,2,1,0:T(8,128)S(1)}, u32[]{:S(2)}, u32[]{:S(2)}) collective-permute-start(f32[4,1,64,256]{3,2,1,0:T(8,128)S(1)} %pad_maximum_fusion.44), channel_id=1, source_target_pairs={{2,0},{4,2},{6,4},{8,6},{10,8},{12,10},{14,12},{3,1},{5,3},{7,5},{... | collective-permute-start | bytes 786440 | tf_op jit(solution)/shard_map/ppermute | solution.py:133
  67.5 15.7 %collective-permute-start.14 = (f32[4,1,64,256]{3,2,1,0:T(8,128)S(1)}, f32[4,1,64,256]{3,2,1,0:T(8,128)S(1)}, u32[]{:S(2)}, u32[]{:S(2)}) collective-permute-start(f32[4,1,64,256]{3,2,1,0:T(8,128)S(1)} %pad_maximum_fusion.45), channel_id=1, source_target_pairs={{0,2},{2,4},{4,6},{6,8},{8,10},{10,12},{12,14},{1,3},{3,5},{5,7},{... | collective-permute-start | bytes 786440 | tf_op jit(solution)/shard_map/ppermute | solution.py:132
  84.0 1.2 %collective-permute-start.15 = (f32[2,4,1,256]{3,2,1,0:T(1,128)S(1)}, f32[2,4,1,256]{3,2,1,0:T(1,128)S(1)}, u32[]{:S(2)}, u32[]{:S(2)}) collective-permute-start(f32[2,4,1,256]{3,2,1,0:T(1,128)S(1)} %constant_dynamic-slice_fusion), channel_id=1, source_target_pairs={{0,1},{1,0},{2,3},{3,2},{4,5},{5,4},{6,7},{7,6},{8,9},{9,8},{10,11... | collective-permute-start | bytes 24584 | tf_op jit(solution)/shard_map/ppermute | solution.py:50
  85.8 1.1 copy-start.2
  86.9 0.8 copy-start.3
  87.8 1.3 %collective-permute-start.16 = (f32[]{:T(128)}, f32[]{:T(128)}, u32[]{:S(2)}, u32[]{:S(2)}) collective-permute-start(f32[]{:T(128)} %get-tuple-element.17), channel_id=1, source_target_pairs={{0,1},{1,0},{2,3},{3,2},{4,5},{5,4},{6,7},{7,6},{8,9},{9,8},{10,11... | collective-permute-start | bytes 20 | tf_op jit(solution)/shard_map/ppermute | solution.py:19
  91.1 5.1 %collective-permute-start.17 = (f32[65,256]{1,0:T(8,128)S(1)}, f32[65,256]{1,0:T(8,128)S(1)}, u32[]{:S(2)}, u32[]{:S(2)}) collective-permute-start(f32[65,256]{1,0:T(8,128)S(1)} %select_maximum_fusion), channel_id=1, source_target_pairs={{0,2},{2,0},{4,6},{6,4},{8,10},{10,8},{12,14},{14,12},{1,3},{3,1},... | collective-permute-start | bytes 199688 | tf_op jit(solution)/shard_map/ppermute | solution.py:19
  96.3 4.4 %collective-permute-start.18 = (f32[65,256]{1,0:T(8,128)S(1)}, f32[65,256]{1,0:T(8,128)S(1)}, u32[]{:S(2)}, u32[]{:S(2)}) collective-permute-start(f32[65,256]{1,0:T(8,128)S(1)} %fusion.286), channel_id=1, source_target_pairs={{0,4},{2,6},{4,0},{6,2},{8,12},{10,14},{12,8},{14,10},{1,5},{3,7},... | collective-permute-start | bytes 199688 | tf_op jit(solution)/shard_map/ppermute | solution.py:19
  100.7 5.3 %collective-permute-start.19 = (f32[65,256]{1,0:T(8,128)S(1)}, f32[65,256]{1,0:T(8,128)S(1)}, u32[]{:S(2)}, u32[]{:S(2)}) collective-permute-start(f32[65,256]{1,0:T(8,128)S(1)} %add.948), channel_id=1, source_target_pairs={{0,8},{2,10},{4,12},{6,14},{8,0},{10,2},{12,4},{14,6},{1,9},{3,11}... | collective-permute-start | bytes 199688 | tf_op jit(solution)/shard_map/ppermute | solution.py:19
